TPU v7x, 32 devices: a whole 2x2x4 slice. The times are simulated.
32 devices in a mesh: gx: 8 (over y, x, core), gy: 4 (over z).
Axes of the slice: x: 2, y: 2, z: 4, core: 2. Of those that a mesh axis runs over, the one named last changes fastest.
Arguments:
- offsets: float32 [3, 16, 8, 4, 128], P(None, 'gx', 'gy'), may hold values from 0 to 1
- charges: float32 [16, 8, 4, 128], P('gx', 'gy'), may hold values from -0.12 to 0.12
- counts: int32 [16, 8, 4], P('gx', 'gy'), may hold values from 16 to 128, as said below
- c2e_leaf_up: float32 [256, 256], replicated, may hold values from -0.09375 to 0.09375
- c2e_leaf_down: float32 [256, 256], replicated, may hold values from -0.09375 to 0.09375
- c2e_top_up: float32 [256, 256], replicated, may hold values from -0.046875 to 0.046875
- c2e_top_down: float32 [256, 256], replicated, may hold values from -0.046875 to 0.046875
Outputs:
- potential: float32 [16, 8, 4, 128], P('gx', 'gy')
Inputs may be any that keep to these rules, and one draw needn't show every extreme that they name: The first counts slots of a leaf box hold its particles, the rest are padding.
All inputs are finite; a program needn't handle non-finite values.
Results may differ from a plain program's by a relative error of at most 0.0003.
Values sent between devices are 32-bit elements; how exact they have to be, the bound alone decides.
No kernel may reach another device: no remote copies, remote signals or barrier semaphores. Data moves between devices by JAX's collectives and lax.ppermute only.
A program may use at most 64 MiB of HBM per device.

v0:
```python
import jax
import jax.numpy as jnp
from jax import lax
from jax.sharding import PartitionSpec as P

softening_sq = 0.0004
golden_turn = 2.399963229728653
highest = lax.Precision.HIGHEST


def padded(cells, sides, width):
    for axis, dim in sides:
        count = lax.axis_size(axis)
        head = lax.slice_in_dim(cells, 0, width, axis=dim)
        tail = lax.slice_in_dim(cells, cells.shape[dim] - width, cells.shape[dim], axis=dim)
        cells = jnp.concatenate(
            [
                lax.ppermute(tail, axis, [(i, (i + 1) % count) for i in range(count)]),
                cells,
                lax.ppermute(head, axis, [((i + 1) % count, i) for i in range(count)]),
            ],
            axis=dim,
        )
    return cells


def sphere(point_count):
    middle = jnp.arange(point_count).astype(jnp.float32) + 0.5
    height = 1.0 - 2.0 * middle / point_count
    radial = jnp.sqrt(jnp.maximum(1.0 - height * height, 0.0))
    angle_turn = middle * golden_turn
    return jnp.stack([radial * jnp.cos(angle_turn), radial * jnp.sin(angle_turn), height])


def point_sum(targets, sources, weights):
    delta_x = targets[0][..., :, None] - sources[0][..., None, :]
    delta_y = targets[1][..., :, None] - sources[1][..., None, :]
    delta_z = targets[2][..., :, None] - sources[2][..., None, :]
    kernel = lax.rsqrt(delta_x * delta_x + delta_y * delta_y + delta_z * delta_z + softening_sq)
    return jnp.sum(kernel * weights[..., None, :], axis=-1)


def translation(unit_sphere, shift_x, shift_y, shift_z, radius):
    delta_x = (
        radius * (unit_sphere[0][:, None] - unit_sphere[0][None, :]) - shift_x[..., None, None]
    )
    delta_y = (
        radius * (unit_sphere[1][:, None] - unit_sphere[1][None, :]) - shift_y[..., None, None]
    )
    delta_z = (
        radius * (unit_sphere[2][:, None] - unit_sphere[2][None, :]) - shift_z[..., None, None]
    )
    return lax.rsqrt(delta_x * delta_x + delta_y * delta_y + delta_z * delta_z + softening_sq)


def child_points(unit_sphere):
    centre = jnp.arange(2).astype(jnp.float32) + 0.5
    point_count = unit_sphere.shape[1]
    box_shape = (2, 2, 2, point_count)
    along_x = jnp.broadcast_to(centre[:, None, None, None] + 0.9 * unit_sphere[0], box_shape)
    along_y = jnp.broadcast_to(centre[None, :, None, None] + 0.9 * unit_sphere[1], box_shape)
    along_z = jnp.broadcast_to(centre[None, None, :, None] + 0.9 * unit_sphere[2], box_shape)
    return jnp.stack([along_x, along_y, along_z]).reshape(3, 8 * point_count)


def shards(offsets, charges, counts, c2e_leaf_up, c2e_leaf_down, c2e_top_up, c2e_top_down):
    slot_count = offsets.shape[-1]
    layers = offsets.shape[3]
    parent_layers = layers // 2
    points = c2e_leaf_up.shape[0]
    unit_sphere = sphere(points)
    slot_index = jnp.arange(slot_count)
    weights = jnp.where(slot_index < counts[..., None], charges, 0.0)
    packed = jnp.concatenate([offsets, weights[None]], axis=0)
    beside_all = padded(packed, (("gx", 1), ("gy", 2)), 1)
    leaf_check_pts = 0.5 + 1.8 * unit_sphere
    leaf_check = point_sum(leaf_check_pts[:, None, None, None, :], offsets, weights)
    leaf_eq = jnp.einsum("ec,xyzc->xyze", c2e_leaf_up, leaf_check, precision=highest)
    children = child_points(unit_sphere)
    parent_weights = (
        leaf_eq.reshape(2, 2, parent_layers, 2, points)
        .transpose(2, 0, 1, 3, 4)
        .reshape(parent_layers, 8 * points)
    )
    parent_check_pts = 1.0 + 3.6 * unit_sphere
    parent_check = point_sum(parent_check_pts[:, None, :], children[:, None, :], parent_weights)
    parent_eq = jnp.einsum("ec,mc->me", c2e_top_up, parent_check, precision=highest)
    count_x = lax.axis_size("gx")
    count_y = lax.axis_size("gy")
    own_x = lax.axis_index("gx")
    own_y = lax.axis_index("gy")
    layer_float = jnp.arange(parent_layers).astype(jnp.float32)
    depth_pairs = 2.0 * (layer_float[None, :] - layer_float[:, None])
    pair_ones = jnp.ones((parent_layers, parent_layers), jnp.float32)
    local_index = jnp.arange(2)
    layer_index = jnp.arange(layers)
    depth_shift = jnp.arange(7) - 3
    depth_float = depth_shift.astype(jnp.float32)
    seven_ones = jnp.ones((7,), jnp.float32)
    valid_z = (layer_index[None, :] + depth_shift[:, None] >= 0) & (
        layer_index[None, :] + depth_shift[:, None] <= layers - 1
    )

    def far_term(target_x, target_y, source_x, source_y, density):
        off_x = (source_x - target_x + count_x // 2) % count_x - count_x // 2
        off_y = (source_y - target_y + count_y // 2) % count_y - count_y // 2
        keep = ((jnp.abs(off_x) > 1) | (jnp.abs(off_y) > 1)).astype(jnp.float32)
        matrices = translation(
            unit_sphere,
            2.0 * off_x.astype(jnp.float32) * pair_ones,
            2.0 * off_y.astype(jnp.float32) * pair_ones,
            depth_pairs,
            1.8,
        )
        return keep * jnp.sum(matrices * density[None, :, None, :], axis=(1, 3))

    def one_target(member, collected):
        term = far_term(member // count_y, member % count_y, own_x, own_y, parent_eq)
        return lax.dynamic_update_index_in_dim(collected, term, member, 0)

    far_check = lax.psum_scatter(
        lax.fori_loop(
            0,
            1 * lax.axis_size(("gx", "gy")),
            one_target,
            jnp.zeros((1 * lax.axis_size(("gx", "gy")), parent_layers, points), jnp.float32),
        ),
        ("gx", "gy"),
        scatter_dimension=0,
        tiled=True,
    )[0]
    cycle = padded(leaf_eq, (("gx", 0), ("gy", 1)), 2)
    framed = jnp.pad(cycle, ((1, 1), (1, 1), (3, 3), (0, 0)))

    def list_row(offset_x, running):
        shift_x = offset_x - 3
        valid_x = (local_index + shift_x >= -2) & (local_index + shift_x <= 3)
        for offset_y in range(7):
            shift_y = offset_y - 3
            valid_y = (local_index + shift_y >= -2) & (local_index + shift_y <= 3)
            block = lax.dynamic_slice(
                framed, (offset_x, offset_y, 0, 0), (2, 2, layers + 6, points)
            )
            stacked = jnp.stack([block[:, :, depth : depth + layers] for depth in range(7)])
            far_enough = (jnp.abs(shift_x) > 1) | (abs(shift_y) > 1) | (jnp.abs(depth_shift) > 1)
            keep = (
                valid_x[None, :, None, None]
                & valid_y[None, None, :, None]
                & valid_z[:, None, None, :]
                & far_enough[:, None, None, None]
            )
            matrices = translation(
                unit_sphere,
                shift_x.astype(jnp.float32) * seven_ones,
                float(shift_y) * seven_ones,
                depth_float,
                0.9,
            )
            sources = jnp.where(keep[..., None], stacked, 0.0)
            running = running + jnp.einsum("zce,zijke->ijkc", matrices, sources, precision=highest)
        return running

    leaf_down_check = lax.fori_loop(0, 7, list_row, jnp.zeros((2, 2, layers, points), jnp.float32))
    parent_local = jnp.einsum("ec,mc->me", c2e_top_down, far_check, precision=highest)
    leaf_local = jnp.einsum("ec,xyzc->xyze", c2e_leaf_down, leaf_down_check, precision=highest)
    padded_around = jnp.pad(beside_all, ((0, 0), (0, 0), (0, 0), (1, 1), (0, 0)))
    diagonal = jnp.arange(slot_count)[:, None] == jnp.arange(slot_count)[None, :]

    def near_box(target_index):
        box_x = target_index // (2 * layers)
        box_y = target_index // layers % 2
        box_z = target_index % layers
        own_block = lax.dynamic_slice(
            packed, (0, box_x, box_y, box_z, 0), (4, 1, 1, 1, slot_count)
        ).reshape(4, slot_count)

        def stencil_term(stencil, running):
            move_x = stencil // 9 - 1
            move_y = stencil // 3 % 3 - 1
            move_z = stencil % 3 - 1
            source = lax.dynamic_slice(
                padded_around,
                (0, box_x + 1 + move_x, box_y + 1 + move_y, box_z + 1 + move_z, 0),
                (4, 1, 1, 1, slot_count),
            ).reshape(4, slot_count)
            delta_x = own_block[0][:, None] - source[0][None, :] - move_x.astype(jnp.float32)
            delta_y = own_block[1][:, None] - source[1][None, :] - move_y.astype(jnp.float32)
            delta_z = own_block[2][:, None] - source[2][None, :] - move_z.astype(jnp.float32)
            kernel = lax.rsqrt(
                delta_x * delta_x + delta_y * delta_y + delta_z * delta_z + softening_sq
            )
            kernel = jnp.where(diagonal & (stencil == 13), 0.0, kernel)
            return running + jnp.sum(kernel * source[3][None, :], axis=1)

        return lax.fori_loop(0, 27, stencil_term, jnp.zeros((slot_count,), jnp.float32))

    near = lax.map(near_box, jnp.arange(4 * layers)).reshape(2, 2, layers, slot_count)
    leaf_down_pts = 0.5 + 1.8 * unit_sphere
    leaf_far = point_sum(offsets, leaf_down_pts[:, None, None, None, :], leaf_local)
    parent_down_pts = 1.0 + 3.6 * unit_sphere
    local_float = local_index.astype(jnp.float32)
    layer_parity = (layer_index % 2).astype(jnp.float32)
    in_parent = jnp.stack(
        [
            local_float[:, None, None, None] + offsets[0],
            local_float[None, :, None, None] + offsets[1],
            layer_parity[None, None, :, None] + offsets[2],
        ]
    )
    spread_local = jnp.repeat(parent_local, 2, axis=0)[None, None]
    parent_far = point_sum(in_parent, parent_down_pts[:, None, None, None, :], spread_local)
    total = near + leaf_far + parent_far
    return jnp.where(slot_index < counts[..., None], total, 0.0)


def solution(mesh):
    return jax.shard_map(
        shards,
        mesh=mesh,
        in_specs=(
            P(None, "gx", "gy", None, None),
            P("gx", "gy", None, None),
            P("gx", "gy", None),
            P(),
            P(),
            P(),
            P(),
        ),
        out_specs=P("gx", "gy", None, None),
        check_vma=False,
    )
```

profile of v0, /device:TPU:0, one launch (start us, length us, event | category | flops | bytes accessed | tf_op | source)
XLA Modules:
  0.0 514.2 jit_solution(7946859668413390378)
XLA Ops:
  9.6 3.4 collective-permute-start.5
  13.9 2.7 collective-permute-start.1
  18.4 48.2 %while.76 = (s32[]{:T(128)}, f32[32,2,256]{2,1,0:T(2,128)}, s32[]{:T(128)}, s32[]{:T(128)}, f32[2,256]{1,0:T(2,128)S(1)}, /*index=5*/f32[2]{0:T(128)S(1)}, s32[]...) while((s32[]{:T(128)}, f32[32,2,256]{2,1,0:T(2,128)}, ...), condition=%wide.region_12.13_spmd.clone, body=%wide.region_10.12_spmd.clone.sunk | while | flops 2303036 | bytes 1069764 | solution.py:122
  66.8 3.7 collective-permute-start.7
  70.6 3.9 collective-permute-start.3
  74.5 109.3 %all-reduce.5.cloned.1.call-done = f32[32,2,256]{2,1,0:T(2,128)} async-done(((f32[32,2,256]{2,1,0:T(2,128)}), f32[32,2,256]{2,1,0:T(2,128)}) %all-reduce.5.cloned.1.call-update) | async-done | bytes 65552
  186.2 212.3 %while.75 = (s32[]{:T(128)}, f32[16,128]{1,0:T(8,128)S(1)}, s32[16]{0:T(128)S(1)}, f32[4,2,2,4,128]{4,0,3,2,1:T(4,128)S(1)}, f32[4,4,4,6,128]{4,3,2,1,0:T(8,128)...) while((s32[]{:T(128)}, f32[16,128]{1,0:T(8,128)S(1)}, ...), condition=%wide.region_4.5_spmd.clone, body=%wide.region_0.4_spmd.clone.sunk | while | flops 278759 | bytes 52331 | solution.py:197
  189.2 10.2 %while.78 = (s32[]{:T(128)}, f32[128]{0:T(128)S(1)}, pred[128,128]{1,0:T(8,128)(4,1)S(1)}, f32[4,128]{1,0:T(4,128)S(1)}, s32[]{:T(128)}, /*index=5*/s32[]{:T(128...) while((s32[]{:T(128)}, f32[128]{0:T(128)S(1)}, ...), condition=%wide.region_3.3_spmd.clone, body=%wide.region_1.2_spmd.clone.sunk | while | flops 262321 | bytes 29889 | solution.py:195
  202.5 10.2 %while.78 = (s32[]{:T(128)}, f32[128]{0:T(128)S(1)}, pred[128,128]{1,0:T(8,128)(4,1)S(1)}, f32[4,128]{1,0:T(4,128)S(1)}, s32[]{:T(128)}, /*index=5*/s32[]{:T(128...) while((s32[]{:T(128)}, f32[128]{0:T(128)S(1)}, ...), condition=%wide.region_3.3_spmd.clone, body=%wide.region_1.2_spmd.clone.sunk | while | flops 262321 | bytes 29889 | solution.py:195
  215.7 10.2 %while.78 = (s32[]{:T(128)}, f32[128]{0:T(128)S(1)}, pred[128,128]{1,0:T(8,128)(4,1)S(1)}, f32[4,128]{1,0:T(4,128)S(1)}, s32[]{:T(128)}, /*index=5*/s32[]{:T(128...) while((s32[]{:T(128)}, f32[128]{0:T(128)S(1)}, ...), condition=%wide.region_3.3_spmd.clone, body=%wide.region_1.2_spmd.clone.sunk | while | flops 262321 | bytes 29889 | solution.py:195
  229.0 10.2 %while.78 = (s32[]{:T(128)}, f32[128]{0:T(128)S(1)}, pred[128,128]{1,0:T(8,128)(4,1)S(1)}, f32[4,128]{1,0:T(4,128)S(1)}, s32[]{:T(128)}, /*index=5*/s32[]{:T(128...) while((s32[]{:T(128)}, f32[128]{0:T(128)S(1)}, ...), condition=%wide.region_3.3_spmd.clone, body=%wide.region_1.2_spmd.clone.sunk | while | flops 262321 | bytes 29889 | solution.py:195
  242.3 10.2 %while.78 = (s32[]{:T(128)}, f32[128]{0:T(128)S(1)}, pred[128,128]{1,0:T(8,128)(4,1)S(1)}, f32[4,128]{1,0:T(4,128)S(1)}, s32[]{:T(128)}, /*index=5*/s32[]{:T(128...) while((s32[]{:T(128)}, f32[128]{0:T(128)S(1)}, ...), condition=%wide.region_3.3_spmd.clone, body=%wide.region_1.2_spmd.clone.sunk | while | flops 262321 | bytes 29889 | solution.py:195
  255.6 10.2 %while.78 = (s32[]{:T(128)}, f32[128]{0:T(128)S(1)}, pred[128,128]{1,0:T(8,128)(4,1)S(1)}, f32[4,128]{1,0:T(4,128)S(1)}, s32[]{:T(128)}, /*index=5*/s32[]{:T(128...) while((s32[]{:T(128)}, f32[128]{0:T(128)S(1)}, ...), condition=%wide.region_3.3_spmd.clone, body=%wide.region_1.2_spmd.clone.sunk | while | flops 262321 | bytes 29889 | solution.py:195
  268.8 10.2 %while.78 = (s32[]{:T(128)}, f32[128]{0:T(128)S(1)}, pred[128,128]{1,0:T(8,128)(4,1)S(1)}, f32[4,128]{1,0:T(4,128)S(1)}, s32[]{:T(128)}, /*index=5*/s32[]{:T(128...) while((s32[]{:T(128)}, f32[128]{0:T(128)S(1)}, ...), condition=%wide.region_3.3_spmd.clone, body=%wide.region_1.2_spmd.clone.sunk | while | flops 262321 | bytes 29889 | solution.py:195
  282.1 10.2 %while.78 = (s32[]{:T(128)}, f32[128]{0:T(128)S(1)}, pred[128,128]{1,0:T(8,128)(4,1)S(1)}, f32[4,128]{1,0:T(4,128)S(1)}, s32[]{:T(128)}, /*index=5*/s32[]{:T(128...) while((s32[]{:T(128)}, f32[128]{0:T(128)S(1)}, ...), condition=%wide.region_3.3_spmd.clone, body=%wide.region_1.2_spmd.clone.sunk | while | flops 262321 | bytes 29889 | solution.py:195
  295.4 10.2 %while.78 = (s32[]{:T(128)}, f32[128]{0:T(128)S(1)}, pred[128,128]{1,0:T(8,128)(4,1)S(1)}, f32[4,128]{1,0:T(4,128)S(1)}, s32[]{:T(128)}, /*index=5*/s32[]{:T(128...) while((s32[]{:T(128)}, f32[128]{0:T(128)S(1)}, ...), condition=%wide.region_3.3_spmd.clone, body=%wide.region_1.2_spmd.clone.sunk | while | flops 262321 | bytes 29889 | solution.py:195
  308.6 10.2 %while.78 = (s32[]{:T(128)}, f32[128]{0:T(128)S(1)}, pred[128,128]{1,0:T(8,128)(4,1)S(1)}, f32[4,128]{1,0:T(4,128)S(1)}, s32[]{:T(128)}, /*index=5*/s32[]{:T(128...) while((s32[]{:T(128)}, f32[128]{0:T(128)S(1)}, ...), condition=%wide.region_3.3_spmd.clone, body=%wide.region_1.2_spmd.clone.sunk | while | flops 262321 | bytes 29889 | solution.py:195
  321.9 10.2 %while.78 = (s32[]{:T(128)}, f32[128]{0:T(128)S(1)}, pred[128,128]{1,0:T(8,128)(4,1)S(1)}, f32[4,128]{1,0:T(4,128)S(1)}, s32[]{:T(128)}, /*index=5*/s32[]{:T(128...) while((s32[]{:T(128)}, f32[128]{0:T(128)S(1)}, ...), condition=%wide.region_3.3_spmd.clone, body=%wide.region_1.2_spmd.clone.sunk | while | flops 262321 | bytes 29889 | solution.py:195
  335.2 10.2 %while.78 = (s32[]{:T(128)}, f32[128]{0:T(128)S(1)}, pred[128,128]{1,0:T(8,128)(4,1)S(1)}, f32[4,128]{1,0:T(4,128)S(1)}, s32[]{:T(128)}, /*index=5*/s32[]{:T(128...) while((s32[]{:T(128)}, f32[128]{0:T(128)S(1)}, ...), condition=%wide.region_3.3_spmd.clone, body=%wide.region_1.2_spmd.clone.sunk | while | flops 262321 | bytes 29889 | solution.py:195
  348.4 10.2 %while.78 = (s32[]{:T(128)}, f32[128]{0:T(128)S(1)}, pred[128,128]{1,0:T(8,128)(4,1)S(1)}, f32[4,128]{1,0:T(4,128)S(1)}, s32[]{:T(128)}, /*index=5*/s32[]{:T(128...) while((s32[]{:T(128)}, f32[128]{0:T(128)S(1)}, ...), condition=%wide.region_3.3_spmd.clone, body=%wide.region_1.2_spmd.clone.sunk | while | flops 262321 | bytes 29889 | solution.py:195
  361.7 10.2 %while.78 = (s32[]{:T(128)}, f32[128]{0:T(128)S(1)}, pred[128,128]{1,0:T(8,128)(4,1)S(1)}, f32[4,128]{1,0:T(4,128)S(1)}, s32[]{:T(128)}, /*index=5*/s32[]{:T(128...) while((s32[]{:T(128)}, f32[128]{0:T(128)S(1)}, ...), condition=%wide.region_3.3_spmd.clone, body=%wide.region_1.2_spmd.clone.sunk | while | flops 262321 | bytes 29889 | solution.py:195
  375.0 10.2 %while.78 = (s32[]{:T(128)}, f32[128]{0:T(128)S(1)}, pred[128,128]{1,0:T(8,128)(4,1)S(1)}, f32[4,128]{1,0:T(4,128)S(1)}, s32[]{:T(128)}, /*index=5*/s32[]{:T(128...) while((s32[]{:T(128)}, f32[128]{0:T(128)S(1)}, ...), condition=%wide.region_3.3_spmd.clone, body=%wide.region_1.2_spmd.clone.sunk | while | flops 262321 | bytes 29889 | solution.py:195
  388.3 10.2 %while.78 = (s32[]{:T(128)}, f32[128]{0:T(128)S(1)}, pred[128,128]{1,0:T(8,128)(4,1)S(1)}, f32[4,128]{1,0:T(4,128)S(1)}, s32[]{:T(128)}, /*index=5*/s32[]{:T(128...) while((s32[]{:T(128)}, f32[128]{0:T(128)S(1)}, ...), condition=%wide.region_3.3_spmd.clone, body=%wide.region_1.2_spmd.clone.sunk | while | flops 262321 | bytes 29889 | solution.py:195
  398.7 106.3 %while.77 = (s32[]{:T(128)}, f32[2,2,4,256]{3,2,1,0:T(4,128)S(1)}, f32[8,8,10,256]{3,2,1,0:T(8,128)S(1)}, s32[7]{0:T(128)S(1)}, s32[]{:T(128)}, /*index=5*/s32[]...) while((s32[]{:T(128)}, f32[2,2,4,256]{3,2,1,0:T(4,128)S(1)}, ...), condition=%wide.region_7.8_spmd.clone.clone, body=%wide.region_6.7_spmd.clone.clone.sunk | while | flops 631486848 | bytes 9828623 | solution.py:163
  400.7 1.9 fusion.200
  402.6 1.9 fusion.199
  404.5 1.9 fusion.198
  406.4 1.9 fusion.197
  408.3 1.9 fusion.196
  410.2 1.9 fusion.194
  412.1 1.9 fusion.195
  415.8 1.9 fusion.200
  417.8 1.9 fusion.199
  421.6 1.9 fusion.197
  425.4 1.9 fusion.194
  431.0 1.9 fusion.200
  432.9 1.9 fusion.199
  434.8 1.9 fusion.198
  436.7 1.9 fusion.197
  438.6 1.9 fusion.196
  440.5 1.9 fusion.194
  442.4 1.9 fusion.195
  446.2 1.9 fusion.200
  450.0 1.9 fusion.198
  453.8 1.9 fusion.196
  457.6 1.9 fusion.195
  461.3 1.9 fusion.200
  463.2 1.9 fusion.199
  465.1 1.9 fusion.198
  467.0 1.9 fusion.197
  468.9 1.9 fusion.196
  470.8 1.9 fusion.194
  472.8 1.9 fusion.195
  476.5 1.9 fusion.200
  478.4 1.9 fusion.199
  482.2 1.9 fusion.197
  486.0 1.9 fusion.194
  491.6 1.9 fusion.200
  493.5 1.9 fusion.199
  495.5 1.9 fusion.198
  497.4 1.9 fusion.197
  499.3 1.9 fusion.196
  501.2 1.9 fusion.194
  503.1 1.9 fusion.195
  (2439 shorter events, 203.9 us)
Async XLA Ops:
  6.5 2.7 copy-start
  6.5 177.2 %all-reduce.5.cloned.1.call-start = ((), (), s32[]{:S(2)}) async-start(), calls=%async_computation | async-start | bytes 131072
  9.6 57.1 %collective-permute-start.5 = (f32[2,2,4,256]{3,2,1,0:T(4,128)S(1)}, f32[2,2,4,256]{3,2,1,0:T(4,128)S(1)}, u32[]{:S(2)}, u32[]{:S(2)}) collective-permute-start(f32[2,2,4,256]{3,2,1,0:T(4,128)S(1)} %fusion.133), channel_id=1, source_target_pairs={{4,0},{8,4},{12,8},{16,12},{20,16},{24,20},{28,24},{0,28},{5,1},{9... | collective-permute-start | bytes 49160 | tf_op jit(solution)/shard_map/ppermute | solution.py:20
  13.0 53.8 %collective-permute-start.4 = (f32[2,2,4,256]{3,2,1,0:T(4,128)S(1)}, f32[2,2,4,256]{3,2,1,0:T(4,128)S(1)}, u32[]{:S(2)}, u32[]{:S(2)}) collective-permute-start(f32[2,2,4,256]{3,2,1,0:T(4,128)S(1)} %fusion.133), channel_id=1, source_target_pairs={{0,4},{4,8},{8,12},{12,16},{16,20},{20,24},{24,28},{28,0},{1,5},{5... | collective-permute-start | bytes 49160 | tf_op jit(solution)/shard_map/ppermute | solution.py:18
  13.8 56.7 %collective-permute-start = (f32[4,1,2,4,128]{4,3,2,1,0:T(4,128)S(1)}, f32[4,1,2,4,128]{4,3,2,1,0:T(4,128)S(1)}, u32[]{:S(2)}, u32[]{:S(2)}) collective-permute-start(f32[4,1,2,4,128]{4,3,2,1,0:T(4,128)S(1)} %copy.96), channel_id=1, source_target_pairs={{0,4},{4,8},{8,12},{12,16},{16,20},{20,24},{24,28},{28,0},{1,5},{5... | collective-permute-start | bytes 49160 | tf_op jit(solution)/shard_map/ppermute | solution.py:18
  13.9 56.6 %collective-permute-start.1 = (f32[4,1,2,4,128]{4,3,2,1,0:T(4,128)S(1)}, f32[4,1,2,4,128]{4,3,2,1,0:T(4,128)S(1)}, u32[]{:S(2)}, u32[]{:S(2)}) collective-permute-start(f32[4,1,2,4,128]{4,3,2,1,0:T(4,128)S(1)} %copy.97), channel_id=1, source_target_pairs={{4,0},{8,4},{12,8},{16,12},{20,16},{24,20},{28,24},{0,28},{5,1},{9... | collective-permute-start | bytes 49160 | tf_op jit(solution)/shard_map/ppermute | solution.py:20
  16.9 1.2 copy-start.2
  18.4 48.3 %copy-start.4 = (f32[3,2,2,4,128]{4,3,2,1,0:T(4,128)S(1)}, f32[3,2,2,4,128]{4,3,2,1,0:T(4,128)}, u32[]{:S(2)}) copy-start(f32[3,2,2,4,128]{4,3,2,1,0:T(4,128)} %param.15) | copy-start | bytes 73732
  18.4 165.4 %copy-start.3 = (f32[256,256]{1,0:T(8,128)S(1)}, f32[256,256]{1,0:T(8,128)}, u32[]{:S(2)}) copy-start(f32[256,256]{1,0:T(8,128)} %param.21) | copy-start | bytes 786436
  66.8 331.7 %collective-permute-start.7 = (f32[6,2,4,256]{3,2,1,0:T(4,128)S(1)}, f32[6,2,4,256]{3,2,1,0:T(4,128)S(1)}, u32[]{:S(2)}, u32[]{:S(2)}) collective-permute-start(f32[6,2,4,256]{3,2,1,0:T(4,128)S(1)} %pad_maximum_fusion), channel_id=1, source_target_pairs={{1,0},{2,1},{3,2},{0,3},{5,4},{6,5},{7,6},{4,7},{9,8},{10,9},{11,1... | collective-permute-start | bytes 147464 | tf_op jit(solution)/shard_map/ppermute | solution.py:20
  70.5 328.1 %collective-permute-start.6 = (f32[6,2,4,256]{3,2,1,0:T(4,128)S(1)}, f32[6,2,4,256]{3,2,1,0:T(4,128)S(1)}, u32[]{:S(2)}, u32[]{:S(2)}) collective-permute-start(f32[6,2,4,256]{3,2,1,0:T(4,128)S(1)} %pad_maximum_fusion), channel_id=1, source_target_pairs={{0,1},{1,2},{2,3},{3,0},{4,5},{5,6},{6,7},{7,4},{8,9},{9,10},{10,1... | collective-permute-start | bytes 147464 | tf_op jit(solution)/shard_map/ppermute | solution.py:18
  70.6 115.6 %collective-permute-start.2 = (f32[4,4,1,4,128]{4,3,2,1,0:T(4,128)S(1)}, f32[4,4,1,4,128]{4,3,2,1,0:T(4,128)S(1)}, u32[]{:S(2)}, u32[]{:S(2)}) collective-permute-start(f32[4,4,1,4,128]{4,3,2,1,0:T(4,128)S(1)} %get-tuple-element.1490), channel_id=1, source_target_pairs={{0,1},{1,2},{2,3},{3,0},{4,5},{5,6},{6,7},{7,4},{8,9},{9,10},{10,1... | collective-permute-start | bytes 98312 | tf_op jit(solution)/shard_map/ppermute | solution.py:18
  70.6 115.5 %collective-permute-start.3 = (f32[4,4,1,4,128]{4,3,2,1,0:T(4,128)S(1)}, f32[4,4,1,4,128]{4,3,2,1,0:T(4,128)S(1)}, u32[]{:S(2)}, u32[]{:S(2)}) collective-permute-start(f32[4,4,1,4,128]{4,3,2,1,0:T(4,128)S(1)} %get-tuple-element.1491), channel_id=1, source_target_pairs={{1,0},{2,1},{3,2},{0,3},{5,4},{6,5},{7,6},{4,7},{9,8},{10,9},{11,1... | collective-permute-start | bytes 98312 | tf_op jit(solution)/shard_map/ppermute | solution.py:20
  398.7 106.3 %copy-start.1 = (f32[256,256]{1,0:T(8,128)S(1)}, f32[256,256]{1,0:T(8,128)}, u32[]{:S(2)}) copy-start(f32[256,256]{1,0:T(8,128)} %param.19) | copy-start | bytes 786436
  398.7 108.0 %copy-start.5 = (s32[2,2,4]{2,1,0:T(2,128)S(1)}, s32[2,2,4]{2,1,0:T(2,128)}, u32[]{:S(2)}) copy-start(s32[2,2,4]{2,1,0:T(2,128)} %param.17) | copy-start | bytes 196
Sparse Core Ops, SparseCore 0:
  66.8 116.9 all-reduce.4
where the time goes:
time: 517 us; the launch traced here: 514 us
  other arithmetic  159 us (31%)
  waiting for transfers between devices  109 us (21%)
  loops' own time  97.8 us (19%)
  matrix products  94.8 us (18%)
  local copies, waits for them, and re-layouts  25.7 us (5%)
  between operations  13.8 us (3%)
  starting transfers between devices  13.7 us (3%)
    unnamed x2, waiting for transfers between devices  109 us
    dot_general x49, matrix products, list_row(): jnp.einsum('zce,zijke->ijkc', matrices, sources, precision=highest)  93 us
    reduce_sum x432, other arithmetic, stencil_term(): return running + jnp.sum(kernel * source[3][None, :], axis=1)  90 us
    another operation x16, loops' own time, near_box(): lax.fori_loop(0, 27, stencil_term, jnp.zeros((slot_count,), jnp.float32))  56.6 us
    another operation x1, loops' own time, shards(): lax.map(near_box, jnp.arange(4 * layers)).reshape(2, 2, layers, slot_count)  38.4 us
    dynamic_update_slice x32, other arithmetic, one_target(): return lax.dynamic_update_index_in_dim(collected, term, member, 0)  18.9 us
    ppermute x4, starting transfers between devices, padded(): lax.ppermute(head, axis, [((i + 1) % count, i) for i in range(count)])  13.6 us
    reduce_sum x32, other arithmetic, far_term(): return keep * jnp.sum(matrices * density[None, :, None, :], axis=(1, 3))  12.4 us
  transfers between devices with their start and end apart: 9, of which 1 were waited for; matrix products, arithmetic and copies ran while one was open for 33% of the time, Pallas kernels for 0%

commit v1 on v0

--- a/solution.py
+++ b/solution.py
@@ -1,4 +1,5 @@
 import jax
+import numpy as np
 import jax.numpy as jnp
 from jax import lax
 from jax.sharding import PartitionSpec as P
@@ -61,6 +62,18 @@
     along_y = jnp.broadcast_to(centre[None, :, None, None] + 0.9 * unit_sphere[1], box_shape)
     along_z = jnp.broadcast_to(centre[None, None, :, None] + 0.9 * unit_sphere[2], box_shape)
     return jnp.stack([along_x, along_y, along_z]).reshape(3, 8 * point_count)
+
+
+def rel_gather(buf, axis, dim):
+    count = lax.axis_size(axis)
+    have = 1
+    while have < count:
+        step = min(have, count - have)
+        part = lax.slice_in_dim(buf, 0, step, axis=dim)
+        got = lax.ppermute(part, axis, [(j, (j - have) % count) for j in range(count)])
+        buf = jnp.concatenate([buf, got], axis=dim)
+        have += step
+    return buf
 
 
 def shards(offsets, charges, counts, c2e_leaf_up, c2e_leaf_down, c2e_top_up, c2e_top_down):
@@ -87,11 +100,35 @@
     parent_eq = jnp.einsum("ec,mc->me", c2e_top_up, parent_check, precision=highest)
     count_x = lax.axis_size("gx")
     count_y = lax.axis_size("gy")
-    own_x = lax.axis_index("gx")
-    own_y = lax.axis_index("gy")
+
+    gathered = rel_gather(rel_gather(parent_eq[None, None], "gy", 1), "gx", 0)
+    kept = []
+    for rel_x in range(count_x):
+        for rel_y in range(count_y):
+            off_x = (rel_x + count_x // 2) % count_x - count_x // 2
+            off_y = (rel_y + count_y // 2) % count_y - count_y // 2
+            if abs(off_x) > 1 or abs(off_y) > 1:
+                kept.append((rel_x * count_y + rel_y, off_x, off_y))
+    kept_index = np.array([k[0] for k in kept], np.int32)
+    kept_x = np.array([2.0 * k[1] for k in kept], np.float32)
+    kept_y = np.array([2.0 * k[2] for k in kept], np.float32)
+    far_sources = jnp.take(gathered.reshape(count_x * count_y, parent_layers, points), kept_index, axis=0)
     layer_float = jnp.arange(parent_layers).astype(jnp.float32)
     depth_pairs = 2.0 * (layer_float[None, :] - layer_float[:, None])
-    pair_ones = jnp.ones((parent_layers, parent_layers), jnp.float32)
+    far_shape = (parent_layers, len(kept), parent_layers, points)
+    source_pts = jnp.stack(
+        [
+            jnp.broadcast_to(kept_x[None, :, None, None] + 1.8 * unit_sphere[0], far_shape),
+            jnp.broadcast_to(kept_y[None, :, None, None] + 1.8 * unit_sphere[1], far_shape),
+            jnp.broadcast_to(depth_pairs[:, None, :, None] + 1.8 * unit_sphere[2], far_shape),
+        ]
+    ).reshape(3, parent_layers, -1)
+    far_check = point_sum(
+        jnp.broadcast_to(1.8 * unit_sphere[:, None, :], (3, parent_layers, points)),
+        source_pts,
+        far_sources.reshape(-1),
+    )
+
     local_index = jnp.arange(2)
     layer_index = jnp.arange(layers)
     depth_shift = jnp.arange(7) - 3
@@ -100,35 +137,6 @@
     valid_z = (layer_index[None, :] + depth_shift[:, None] >= 0) & (
         layer_index[None, :] + depth_shift[:, None] <= layers - 1
     )
-
-    def far_term(target_x, target_y, source_x, source_y, density):
-        off_x = (source_x - target_x + count_x // 2) % count_x - count_x // 2
-        off_y = (source_y - target_y + count_y // 2) % count_y - count_y // 2
-        keep = ((jnp.abs(off_x) > 1) | (jnp.abs(off_y) > 1)).astype(jnp.float32)
-        matrices = translation(
-            unit_sphere,
-            2.0 * off_x.astype(jnp.float32) * pair_ones,
-            2.0 * off_y.astype(jnp.float32) * pair_ones,
-            depth_pairs,
-            1.8,
-        )
-        return keep * jnp.sum(matrices * density[None, :, None, :], axis=(1, 3))
-
-    def one_target(member, collected):
-        term = far_term(member // count_y, member % count_y, own_x, own_y, parent_eq)
-        return lax.dynamic_update_index_in_dim(collected, term, member, 0)
-
-    far_check = lax.psum_scatter(
-        lax.fori_loop(
-            0,
-            1 * lax.axis_size(("gx", "gy")),
-            one_target,
-            jnp.zeros((1 * lax.axis_size(("gx", "gy")), parent_layers, points), jnp.float32),
-        ),
-        ("gx", "gy"),
-        scatter_dimension=0,
-        tiled=True,
-    )[0]
     cycle = padded(leaf_eq, (("gx", 0), ("gy", 1)), 2)
     framed = jnp.pad(cycle, ((1, 1), (1, 1), (3, 3), (0, 0)))
 
@@ -163,43 +171,41 @@
     leaf_down_check = lax.fori_loop(0, 7, list_row, jnp.zeros((2, 2, layers, points), jnp.float32))
     parent_local = jnp.einsum("ec,mc->me", c2e_top_down, far_check, precision=highest)
     leaf_local = jnp.einsum("ec,xyzc->xyze", c2e_leaf_down, leaf_down_check, precision=highest)
+
     padded_around = jnp.pad(beside_all, ((0, 0), (0, 0), (0, 0), (1, 1), (0, 0)))
+    around_shape = padded_around.shape[1:4]
+    moves = [(mx, my, mz) for mx in (-1, 0, 1) for my in (-1, 0, 1) for mz in (-1, 0, 1)]
+    box_rows = np.array(
+        [
+            [
+                np.ravel_multi_index((bx + 1 + mx, by + 1 + my, bz + 1 + mz), around_shape)
+                for bx in range(2)
+                for by in range(2)
+                for bz in range(layers)
+            ]
+            for mx, my, mz in moves
+        ],
+        np.int32,
+    )
+    source = jnp.take(
+        padded_around.reshape(4, -1, slot_count), box_rows, axis=1
+    ).reshape(4, len(moves), 2, 2, layers, slot_count)
+    move = jnp.array(moves, jnp.float32)
+    shape6 = (len(moves), 1, 1, 1, 1, 1)
+    delta_x = packed[0][None, ..., :, None] - source[0][..., None, :] - move[:, 0].reshape(shape6)
+    delta_y = packed[1][None, ..., :, None] - source[1][..., None, :] - move[:, 1].reshape(shape6)
+    delta_z = packed[2][None, ..., :, None] - source[2][..., None, :] - move[:, 2].reshape(shape6)
+    kernel = lax.rsqrt(delta_x * delta_x + delta_y * delta_y + delta_z * delta_z + softening_sq)
     diagonal = jnp.arange(slot_count)[:, None] == jnp.arange(slot_count)[None, :]
-
-    def near_box(target_index):
-        box_x = target_index // (2 * layers)
-        box_y = target_index // layers % 2
-        box_z = target_index % layers
-        own_block = lax.dynamic_slice(
-            packed, (0, box_x, box_y, box_z, 0), (4, 1, 1, 1, slot_count)
-        ).reshape(4, slot_count)
-
-        def stencil_term(stencil, running):
-            move_x = stencil // 9 - 1
-            move_y = stencil // 3 % 3 - 1
-            move_z = stencil % 3 - 1
-            source = lax.dynamic_slice(
-                padded_around,
-                (0, box_x + 1 + move_x, box_y + 1 + move_y, box_z + 1 + move_z, 0),
-                (4, 1, 1, 1, slot_count),
-            ).reshape(4, slot_count)
-            delta_x = own_block[0][:, None] - source[0][None, :] - move_x.astype(jnp.float32)
-            delta_y = own_block[1][:, None] - source[1][None, :] - move_y.astype(jnp.float32)
-            delta_z = own_block[2][:, None] - source[2][None, :] - move_z.astype(jnp.float32)
-            kernel = lax.rsqrt(
-                delta_x * delta_x + delta_y * delta_y + delta_z * delta_z + softening_sq
-            )
-            kernel = jnp.where(diagonal & (stencil == 13), 0.0, kernel)
-            return running + jnp.sum(kernel * source[3][None, :], axis=1)
-
-        return lax.fori_loop(0, 27, stencil_term, jnp.zeros((slot_count,), jnp.float32))
-
-    near = lax.map(near_box, jnp.arange(4 * layers)).reshape(2, 2, layers, slot_count)
+    centre = (jnp.arange(len(moves)) == 13).reshape(shape6)
+    kernel = jnp.where(centre & diagonal, 0.0, kernel)
+    near = jnp.sum(jnp.sum(kernel * source[3][..., None, :], axis=-1), axis=0)
+
     leaf_down_pts = 0.5 + 1.8 * unit_sphere
     leaf_far = point_sum(offsets, leaf_down_pts[:, None, None, None, :], leaf_local)
     parent_down_pts = 1.0 + 3.6 * unit_sphere
-    local_float = local_index.astype(jnp.float32)
-    layer_parity = (layer_index % 2).astype(jnp.float32)
+    local_float = jnp.arange(2).astype(jnp.float32)
+    layer_parity = (jnp.arange(layers) % 2).astype(jnp.float32)
     in_parent = jnp.stack(
         [
             local_float[:, None, None, None] + offsets[0],

time: 517 us -> 184 us (0.36)
  other arithmetic: 159 us -> 53 us
  waiting for transfers between devices: 109 us -> 6.17 us
  loops' own time: 97.8 us -> 1.83 us
  local copies, waits for them, and re-layouts: 25.7 us -> 7.32 us
  between operations: 13.8 us -> 0.56 us
  starting transfers between devices: 13.7 us -> 20.3 us
    unnamed x2 -> x0, waiting for transfers between devices: 109 us -> none
    another operation x18 -> x0, loops' own time: 96.1 us -> none  [the longest x16 56.6 us: near_box(): lax.fori_loop(0, 27, stencil_term, jnp.zeros((slot_count,), jnp.float32))]
    reduce_sum x464 -> x1, other arithmetic: 102 us -> 22.8 us  [shards(): near = jnp.sum(jnp.sum(kernel * source[3][..., None, :], axis=-1), axis=0)]
    dynamic_update_slice x32 -> x0, other arithmetic: 18.9 us -> none  [one_target(): return lax.dynamic_update_index_in_dim(collected, term, member, 0)]
    reduce_sum x4 -> x5, other arithmetic: 4.15 us -> 15.8 us  [point_sum(): return jnp.sum(kernel * weights[..., None, :], axis=-1)]
    sub x865 -> x1, local copies, waits for them, and re-layouts: 12.1 us -> 0.74 us  [shards(): packed[0][None, ..., :, None] - source[0][..., None, :]]
    dynamic_slice x16 -> x0, local copies, waits for them, and re-layouts: 9.42 us -> none  [shards(): lax.map(near_box, jnp.arange(4 * layers)).reshape(2, 2, layers, slot_count)]
    ppermute x0 -> x5, starting transfers between devices: none -> 5.89 us  [rel_gather(): lax.ppermute(part, axis, [(j, (j - have) % count) for j in range(count)])]
  transfers between devices with their start and end apart: 9 -> 13, of which waited for: 1 -> 4; matrix products, arithmetic and copies ran while one was open for 33% -> 24% of each run, Pallas kernels for 0% -> 0%
where the time goes in v1:
time: 184 us; the launch traced here: 183 us
  matrix products  94 us (51%)
  other arithmetic  53 us (29%)
  starting transfers between devices  20.3 us (11%)
  local copies, waits for them, and re-layouts  7.32 us (4%)
  waiting for transfers between devices  6.17 us (3%)
    dot_general x49, matrix products, list_row(): jnp.einsum('zce,zijke->ijkc', matrices, sources, precision=highest)  92.8 us
    reduce_sum x1, other arithmetic, shards(): near = jnp.sum(jnp.sum(kernel * source[3][..., None, :], axis=-1), axis=0)  22.8 us
    reduce_sum x5, other arithmetic, point_sum(): return jnp.sum(kernel * weights[..., None, :], axis=-1)  15.8 us
    ppermute x4, starting transfers between devices, padded(): lax.ppermute(head, axis, [((i + 1) % count, i) for i in range(count)])  14.3 us
    ppermute x5, starting transfers between devices, rel_gather(): lax.ppermute(part, axis, [(j, (j - have) % count) for j in range(count)])  5.89 us
    ppermute x5, waiting for transfers between devices, rel_gather(): lax.ppermute(part, axis, [(j, (j - have) % count) for j in range(count)])  4.63 us
  transfers between devices with their start and end apart: 13, of which 4 were waited for; matrix products, arithmetic and copies ran while one was open for 24% of the time, Pallas kernels for 0%

profile of v1, /device:TPU:0, one launch (start us, length us, event | category | flops | bytes accessed | tf_op | source)
XLA Modules:
  0.0 183.1 jit_solution(15204385450991539228)
XLA Ops:
  1.7 1.1 multiply_reduce_fusion.4
  3.1 3.4 %collective-permute-start.5 = (f32[2,2,4,256]{3,2,1,0:T(4,128)S(1)}, f32[2,2,4,256]{3,2,1,0:T(4,128)S(1)}, u32[]{:S(2)}, u32[]{:S(2)}) collective-permute-start(f32[2,2,4,256]{3,2,1,0:T(4,128)S(1)} %fusion.112), channel_id=1, source_target_pairs={{4,0},{8,4},{12,8},{16,12},{20,16},{24,20},{28,24},{0,28},{5,1},{9... | collective-permute-start | bytes 49160 | tf_op jit(solution)/shard_map/ppermute | solution.py:21
  8.0 2.7 %collective-permute-start.1 = (f32[4,1,2,4,128]{4,3,2,1,0:T(4,128)S(1)}, f32[4,1,2,4,128]{4,3,2,1,0:T(4,128)S(1)}, u32[]{:S(2)}, u32[]{:S(2)}) collective-permute-start(f32[4,1,2,4,128]{4,3,2,1,0:T(4,128)S(1)} %get-tuple-element.670), channel_id=1, source_target_pairs={{4,0},{8,4},{12,8},{16,12},{20,16},{24,20},{28,24},{0,28},{5,1},{9... | collective-permute-start | bytes 49160 | tf_op jit(solution)/shard_map/ppermute | solution.py:21
  12.6 3.7 %collective-permute-start.8 = (f32[1,1,2,256]{3,2,1,0:T(2,128)S(1)}, f32[1,1,2,256]{3,2,1,0:T(2,128)S(1)}, u32[]{:S(2)}, u32[]{:S(2)}) collective-permute-start(f32[1,1,2,256]{3,2,1,0:T(2,128)S(1)} %convolution_bitcast_fusion), channel_id=1, source_target_pairs={{0,3},{1,0},{2,1},{3,2},{4,7},{5,4},{6,5},{7,6},{8,11},{9,8},{10,9... | collective-permute-start | bytes 6152 | tf_op jit(solution)/shard_map/ppermute | solution.py:73
  17.6 1.3 collective-permute-start.9
  18.9 3.2 %collective-permute-done.9 = f32[1,2,2,256]{3,2,1,0:T(2,128)S(1)} collective-permute-done((f32[1,2,2,256]{3,2,1,0:T(2,128)S(1)}, f32[1,2,2,256]{3,2,1,0:T(2,128)S(1)}, u32[]{:S(2)}, u32[]{:S(2)}) %collective-permute-start.9) | collective-permute-done | bytes 4128 | tf_op jit(solution)/shard_map/ppermute | solution.py:73
  23.9 4.1 %collective-permute-start.7 = (f32[6,2,4,256]{3,2,1,0:T(4,128)S(1)}, f32[6,2,4,256]{3,2,1,0:T(4,128)S(1)}, u32[]{:S(2)}, u32[]{:S(2)}) collective-permute-start(f32[6,2,4,256]{3,2,1,0:T(4,128)S(1)} %pad_maximum_fusion.4), channel_id=1, source_target_pairs={{1,0},{2,1},{3,2},{0,3},{5,4},{6,5},{7,6},{4,7},{9,8},{10,9},{11,1... | collective-permute-start | bytes 147464 | tf_op jit(solution)/shard_map/ppermute | solution.py:21
  28.2 4.0 %collective-permute-start.3 = (f32[4,4,1,4,128]{4,3,2,1,0:T(4,128)S(1)}, f32[4,4,1,4,128]{4,3,2,1,0:T(4,128)S(1)}, u32[]{:S(2)}, u32[]{:S(2)}) collective-permute-start(f32[4,4,1,4,128]{4,3,2,1,0:T(4,128)S(1)} %get-tuple-element.668), channel_id=1, source_target_pairs={{1,0},{2,1},{3,2},{0,3},{5,4},{6,5},{7,6},{4,7},{9,8},{10,9},{11,1... | collective-permute-start | bytes 98312 | tf_op jit(solution)/shard_map/ppermute | solution.py:21
  32.8 1.5 collective-permute-done.2
  34.5 2.3 %gather_fusion = f32[432,4,128]{2,1,0:T(4,128)S(1)} fusion(f32[4,96,128]{2,0,1:T(4,128)S(1)} %bitcast.384, s32[1024]{0:T(1024)S(1)} %pad_clamp_fusion.1), kind=kCustom, calls=%fused_computation | custom fusion | bytes 1771200 | tf_op jit(solution)/shard_map/jit(_take)/gather | solution.py:190
  37.5 22.8 %fusion.108 = f32[2,2,4,128]{3,2,1,0:T(4,128)S(1)} fusion(f32[27]{0:T(128)S(1)} %copy-done.10, f32[27]{0:T(128)S(1)} %copy-done.11, f32[27]{0:T(128)S(1)} %copy-done.12, f32[27,2,2,4,128]{4,3,2,1,0:T(4,128)S(1)} %bitcast.388, f32[27,2,2,4,128]{4,3,2,1,0:T(4,128)S(1)} %bitcast.389, f32[2,2,4,128]{3,2,1,0:T(4,128)S(1)} %get-tuple-element.675, ...), kind=kLoop, calls=%fused_computation.267 | loop fusion | flops 106166272 | bytes 1360196 | tf_op jit(solution)/shard_map/reduce_sum | solution.py:202
  61.0 11.6 %multiply_reduce_fusion = f32[2,256]{1,0:T(2,128)S(1)} fusion(f32[11776]{0:T(1024)S(1)} %select_n.139, f32[2,11776]{1,0:T(2,128)S(1)} %stack_broadcast_in_dim.41, f32[256]{0:T(256)S(1)} %bitcast.414, f32[11776]{0:T(1024)S(1)} %stack_broadcast_in_dim.39, f32[256]{0:T(256)S(1)} %bitcast.415, f32[11776]{0:T(1024)S(1)} %stack_broadcast_in_dim.37, ...), kind=kLoop, calls=%fused_computation.271 | loop fusion | flops 66321920 | bytes 240640 | tf_op jit(solution)/shard_map/reduce_sum | solution.py:41
  73.0 1.3 multiply_reduce_fusion.2
  74.5 106.2 %while.17 = (s32[]{:T(128)}, f32[2,2,4,256]{3,2,0,1:T(4,128)S(1)}, f32[8,8,10,256]{3,2,0,1:T(8,128)S(1)}, s32[7]{0:T(128)S(1)}, s32[]{:T(128)}, /*index=5*/s32[]...) while((s32[]{:T(128)}, f32[2,2,4,256]{3,2,0,1:T(4,128)S(1)}, ...), condition=%wide.region_3.4_spmd.clone.clone, body=%wide.region_2.3_spmd.clone.clone.sunk | while | flops 631486848 | bytes 9828623 | solution.py:171
  76.6 1.9 %fusion.182 = f32[2,2,4,256,1]{3,2,1,0,4:T(4,128)S(1)} fusion(f32[7]{0:T(128)S(1)} %add_convert_fusion.2, f32[256,256]{1,0:T(8,128)S(1)} %subtract_multiply_fusion.13, f32[256,256]{1,0:T(8,128)S(1)} %get-tuple-element.874, f32[7,2,2,4,256]{4,3,1,2,0:T(4,128)S(1)} %get-tuple-element.875, pred[7,2,2,4]{3,1,2,0:T(4,128)(4,1)S(1)} %get-tuple-element.876), kind=kOutput, calls=%fused_computation.24.clone.1 | convolution fusion | flops 89944064 | bytes 655500 | tf_op jit(solution)/shard_map/while/body/eval_jaxpr/zce,zijke->ijkc/dot_general | solution.py:168
  78.5 1.9 %fusion.181 = f32[2,2,4,256,1]{3,2,1,0,4:T(4,128)S(1)} fusion(f32[256,256]{1,0:T(8,128)S(1)} %get-tuple-element.872, f32[7]{0:T(128)S(1)} %add_convert_fusion.2, f32[256,256]{1,0:T(8,128)S(1)} %subtract_multiply_fusion.13, f32[7,2,2,4,256]{4,3,1,2,0:T(4,128)S(1)} %get-tuple-element.873), kind=kOutput, calls=%fused_computation.22.clone.1 | convolution fusion | flops 89915392 | bytes 655388 | tf_op jit(solution)/shard_map/while/body/eval_jaxpr/zce,zijke->ijkc/dot_general | solution.py:168
  80.4 1.9 %fusion.180 = f32[2,2,4,256,1]{3,2,1,0,4:T(4,128)S(1)} fusion(f32[256,256]{1,0:T(8,128)S(1)} %get-tuple-element.866, f32[7]{0:T(128)S(1)} %add_convert_fusion.2, f32[256,256]{1,0:T(8,128)S(1)} %subtract_multiply_fusion.13, f32[7,2,2,4,256]{4,3,1,2,0:T(4,128)S(1)} %get-tuple-element.871), kind=kOutput, calls=%fused_computation.20.clone.1 | convolution fusion | flops 89915392 | bytes 655388 | tf_op jit(solution)/shard_map/while/body/eval_jaxpr/zce,zijke->ijkc/dot_general | solution.py:168
  82.3 1.9 %fusion.179 = f32[2,2,4,256,1]{3,2,1,0,4:T(4,128)S(1)} fusion(f32[256,256]{1,0:T(8,128)S(1)} %get-tuple-element.864, f32[7]{0:T(128)S(1)} %add_convert_fusion.2, f32[256,256]{1,0:T(8,128)S(1)} %subtract_multiply_fusion.13, f32[7,2,2,4,256]{4,3,1,2,0:T(4,128)S(1)} %get-tuple-element.865), kind=kOutput, calls=%fused_computation.18.clone.1 | convolution fusion | flops 89915392 | bytes 655388 | tf_op jit(solution)/shard_map/while/body/eval_jaxpr/zce,zijke->ijkc/dot_general | solution.py:168
  84.2 1.9 %fusion.178 = f32[2,2,4,256,1]{3,2,1,0,4:T(4,128)S(1)} fusion(f32[256,256]{1,0:T(8,128)S(1)} %get-tuple-element.858, f32[7]{0:T(128)S(1)} %add_convert_fusion.2, f32[256,256]{1,0:T(8,128)S(1)} %subtract_multiply_fusion.13, f32[7,2,2,4,256]{4,3,1,2,0:T(4,128)S(1)} %get-tuple-element.863), kind=kOutput, calls=%fused_computation.16.clone.1 | convolution fusion | flops 89915392 | bytes 655388 | tf_op jit(solution)/shard_map/while/body/eval_jaxpr/zce,zijke->ijkc/dot_general | solution.py:168
  86.1 1.9 %fusion.176 = f32[2,2,4,256,1]{3,2,1,0,4:T(4,128)S(1)} fusion(f32[256,256]{1,0:T(8,128)S(1)} %get-tuple-element.802, f32[7]{0:T(128)S(1)} %add_convert_fusion.2, f32[256,256]{1,0:T(8,128)S(1)} %subtract_multiply_fusion.13, f32[7,2,2,4,256]{4,3,1,2,0:T(4,128)S(1)} %get-tuple-element.855), kind=kOutput, calls=%fused_computation.12.clone.1 | convolution fusion | flops 89915392 | bytes 655388 | tf_op jit(solution)/shard_map/while/body/eval_jaxpr/zce,zijke->ijkc/dot_general | solution.py:168
  88.0 1.9 %fusion.177 = f32[2,2,4,256,1]{3,2,1,0,4:T(4,128)S(1)} fusion(f32[256,256]{1,0:T(8,128)S(1)} %get-tuple-element.856, f32[7]{0:T(128)S(1)} %add_convert_fusion.2, f32[256,256]{1,0:T(8,128)S(1)} %subtract_multiply_fusion.13, f32[7,2,2,4,256]{4,3,1,2,0:T(4,128)S(1)} %get-tuple-element.857), kind=kOutput, calls=%fused_computation.14.clone.1 | convolution fusion | flops 89915392 | bytes 655388 | tf_op jit(solution)/shard_map/while/body/eval_jaxpr/zce,zijke->ijkc/dot_general | solution.py:168
  91.7 1.9 %fusion.182 = f32[2,2,4,256,1]{3,2,1,0,4:T(4,128)S(1)} fusion(f32[7]{0:T(128)S(1)} %add_convert_fusion.2, f32[256,256]{1,0:T(8,128)S(1)} %subtract_multiply_fusion.13, f32[256,256]{1,0:T(8,128)S(1)} %get-tuple-element.874, f32[7,2,2,4,256]{4,3,1,2,0:T(4,128)S(1)} %get-tuple-element.875, pred[7,2,2,4]{3,1,2,0:T(4,128)(4,1)S(1)} %get-tuple-element.876), kind=kOutput, calls=%fused_computation.24.clone.1 | convolution fusion | flops 89944064 | bytes 655500 | tf_op jit(solution)/shard_map/while/body/eval_jaxpr/zce,zijke->ijkc/dot_general | solution.py:168
  93.6 1.9 %fusion.181 = f32[2,2,4,256,1]{3,2,1,0,4:T(4,128)S(1)} fusion(f32[256,256]{1,0:T(8,128)S(1)} %get-tuple-element.872, f32[7]{0:T(128)S(1)} %add_convert_fusion.2, f32[256,256]{1,0:T(8,128)S(1)} %subtract_multiply_fusion.13, f32[7,2,2,4,256]{4,3,1,2,0:T(4,128)S(1)} %get-tuple-element.873), kind=kOutput, calls=%fused_computation.22.clone.1 | convolution fusion | flops 89915392 | bytes 655388 | tf_op jit(solution)/shard_map/while/body/eval_jaxpr/zce,zijke->ijkc/dot_general | solution.py:168
  95.5 1.9 %fusion.180 = f32[2,2,4,256,1]{3,2,1,0,4:T(4,128)S(1)} fusion(f32[256,256]{1,0:T(8,128)S(1)} %get-tuple-element.866, f32[7]{0:T(128)S(1)} %add_convert_fusion.2, f32[256,256]{1,0:T(8,128)S(1)} %subtract_multiply_fusion.13, f32[7,2,2,4,256]{4,3,1,2,0:T(4,128)S(1)} %get-tuple-element.871), kind=kOutput, calls=%fused_computation.20.clone.1 | convolution fusion | flops 89915392 | bytes 655388 | tf_op jit(solution)/shard_map/while/body/eval_jaxpr/zce,zijke->ijkc/dot_general | solution.py:168
  97.4 1.9 %fusion.179 = f32[2,2,4,256,1]{3,2,1,0,4:T(4,128)S(1)} fusion(f32[256,256]{1,0:T(8,128)S(1)} %get-tuple-element.864, f32[7]{0:T(128)S(1)} %add_convert_fusion.2, f32[256,256]{1,0:T(8,128)S(1)} %subtract_multiply_fusion.13, f32[7,2,2,4,256]{4,3,1,2,0:T(4,128)S(1)} %get-tuple-element.865), kind=kOutput, calls=%fused_computation.18.clone.1 | convolution fusion | flops 89915392 | bytes 655388 | tf_op jit(solution)/shard_map/while/body/eval_jaxpr/zce,zijke->ijkc/dot_general | solution.py:168
  99.3 1.9 %fusion.178 = f32[2,2,4,256,1]{3,2,1,0,4:T(4,128)S(1)} fusion(f32[256,256]{1,0:T(8,128)S(1)} %get-tuple-element.858, f32[7]{0:T(128)S(1)} %add_convert_fusion.2, f32[256,256]{1,0:T(8,128)S(1)} %subtract_multiply_fusion.13, f32[7,2,2,4,256]{4,3,1,2,0:T(4,128)S(1)} %get-tuple-element.863), kind=kOutput, calls=%fused_computation.16.clone.1 | convolution fusion | flops 89915392 | bytes 655388 | tf_op jit(solution)/shard_map/while/body/eval_jaxpr/zce,zijke->ijkc/dot_general | solution.py:168
  101.2 1.9 %fusion.176 = f32[2,2,4,256,1]{3,2,1,0,4:T(4,128)S(1)} fusion(f32[256,256]{1,0:T(8,128)S(1)} %get-tuple-element.802, f32[7]{0:T(128)S(1)} %add_convert_fusion.2, f32[256,256]{1,0:T(8,128)S(1)} %subtract_multiply_fusion.13, f32[7,2,2,4,256]{4,3,1,2,0:T(4,128)S(1)} %get-tuple-element.855), kind=kOutput, calls=%fused_computation.12.clone.1 | convolution fusion | flops 89915392 | bytes 655388 | tf_op jit(solution)/shard_map/while/body/eval_jaxpr/zce,zijke->ijkc/dot_general | solution.py:168
  103.1 1.9 %fusion.177 = f32[2,2,4,256,1]{3,2,1,0,4:T(4,128)S(1)} fusion(f32[256,256]{1,0:T(8,128)S(1)} %get-tuple-element.856, f32[7]{0:T(128)S(1)} %add_convert_fusion.2, f32[256,256]{1,0:T(8,128)S(1)} %subtract_multiply_fusion.13, f32[7,2,2,4,256]{4,3,1,2,0:T(4,128)S(1)} %get-tuple-element.857), kind=kOutput, calls=%fused_computation.14.clone.1 | convolution fusion | flops 89915392 | bytes 655388 | tf_op jit(solution)/shard_map/while/body/eval_jaxpr/zce,zijke->ijkc/dot_general | solution.py:168
  106.8 1.9 %fusion.182 = f32[2,2,4,256,1]{3,2,1,0,4:T(4,128)S(1)} fusion(f32[7]{0:T(128)S(1)} %add_convert_fusion.2, f32[256,256]{1,0:T(8,128)S(1)} %subtract_multiply_fusion.13, f32[256,256]{1,0:T(8,128)S(1)} %get-tuple-element.874, f32[7,2,2,4,256]{4,3,1,2,0:T(4,128)S(1)} %get-tuple-element.875, pred[7,2,2,4]{3,1,2,0:T(4,128)(4,1)S(1)} %get-tuple-element.876), kind=kOutput, calls=%fused_computation.24.clone.1 | convolution fusion | flops 89944064 | bytes 655500 | tf_op jit(solution)/shard_map/while/body/eval_jaxpr/zce,zijke->ijkc/dot_general | solution.py:168
  108.7 1.9 %fusion.181 = f32[2,2,4,256,1]{3,2,1,0,4:T(4,128)S(1)} fusion(f32[256,256]{1,0:T(8,128)S(1)} %get-tuple-element.872, f32[7]{0:T(128)S(1)} %add_convert_fusion.2, f32[256,256]{1,0:T(8,128)S(1)} %subtract_multiply_fusion.13, f32[7,2,2,4,256]{4,3,1,2,0:T(4,128)S(1)} %get-tuple-element.873), kind=kOutput, calls=%fused_computation.22.clone.1 | convolution fusion | flops 89915392 | bytes 655388 | tf_op jit(solution)/shard_map/while/body/eval_jaxpr/zce,zijke->ijkc/dot_general | solution.py:168
  110.6 1.9 %fusion.180 = f32[2,2,4,256,1]{3,2,1,0,4:T(4,128)S(1)} fusion(f32[256,256]{1,0:T(8,128)S(1)} %get-tuple-element.866, f32[7]{0:T(128)S(1)} %add_convert_fusion.2, f32[256,256]{1,0:T(8,128)S(1)} %subtract_multiply_fusion.13, f32[7,2,2,4,256]{4,3,1,2,0:T(4,128)S(1)} %get-tuple-element.871), kind=kOutput, calls=%fused_computation.20.clone.1 | convolution fusion | flops 89915392 | bytes 655388 | tf_op jit(solution)/shard_map/while/body/eval_jaxpr/zce,zijke->ijkc/dot_general | solution.py:168
  112.5 1.9 %fusion.179 = f32[2,2,4,256,1]{3,2,1,0,4:T(4,128)S(1)} fusion(f32[256,256]{1,0:T(8,128)S(1)} %get-tuple-element.864, f32[7]{0:T(128)S(1)} %add_convert_fusion.2, f32[256,256]{1,0:T(8,128)S(1)} %subtract_multiply_fusion.13, f32[7,2,2,4,256]{4,3,1,2,0:T(4,128)S(1)} %get-tuple-element.865), kind=kOutput, calls=%fused_computation.18.clone.1 | convolution fusion | flops 89915392 | bytes 655388 | tf_op jit(solution)/shard_map/while/body/eval_jaxpr/zce,zijke->ijkc/dot_general | solution.py:168
  114.4 1.9 %fusion.178 = f32[2,2,4,256,1]{3,2,1,0,4:T(4,128)S(1)} fusion(f32[256,256]{1,0:T(8,128)S(1)} %get-tuple-element.858, f32[7]{0:T(128)S(1)} %add_convert_fusion.2, f32[256,256]{1,0:T(8,128)S(1)} %subtract_multiply_fusion.13, f32[7,2,2,4,256]{4,3,1,2,0:T(4,128)S(1)} %get-tuple-element.863), kind=kOutput, calls=%fused_computation.16.clone.1 | convolution fusion | flops 89915392 | bytes 655388 | tf_op jit(solution)/shard_map/while/body/eval_jaxpr/zce,zijke->ijkc/dot_general | solution.py:168
  116.3 1.9 %fusion.176 = f32[2,2,4,256,1]{3,2,1,0,4:T(4,128)S(1)} fusion(f32[256,256]{1,0:T(8,128)S(1)} %get-tuple-element.802, f32[7]{0:T(128)S(1)} %add_convert_fusion.2, f32[256,256]{1,0:T(8,128)S(1)} %subtract_multiply_fusion.13, f32[7,2,2,4,256]{4,3,1,2,0:T(4,128)S(1)} %get-tuple-element.855), kind=kOutput, calls=%fused_computation.12.clone.1 | convolution fusion | flops 89915392 | bytes 655388 | tf_op jit(solution)/shard_map/while/body/eval_jaxpr/zce,zijke->ijkc/dot_general | solution.py:168
  118.2 1.9 %fusion.177 = f32[2,2,4,256,1]{3,2,1,0,4:T(4,128)S(1)} fusion(f32[256,256]{1,0:T(8,128)S(1)} %get-tuple-element.856, f32[7]{0:T(128)S(1)} %add_convert_fusion.2, f32[256,256]{1,0:T(8,128)S(1)} %subtract_multiply_fusion.13, f32[7,2,2,4,256]{4,3,1,2,0:T(4,128)S(1)} %get-tuple-element.857), kind=kOutput, calls=%fused_computation.14.clone.1 | convolution fusion | flops 89915392 | bytes 655388 | tf_op jit(solution)/shard_map/while/body/eval_jaxpr/zce,zijke->ijkc/dot_general | solution.py:168
  122.0 1.9 %fusion.182 = f32[2,2,4,256,1]{3,2,1,0,4:T(4,128)S(1)} fusion(f32[7]{0:T(128)S(1)} %add_convert_fusion.2, f32[256,256]{1,0:T(8,128)S(1)} %subtract_multiply_fusion.13, f32[256,256]{1,0:T(8,128)S(1)} %get-tuple-element.874, f32[7,2,2,4,256]{4,3,1,2,0:T(4,128)S(1)} %get-tuple-element.875, pred[7,2,2,4]{3,1,2,0:T(4,128)(4,1)S(1)} %get-tuple-element.876), kind=kOutput, calls=%fused_computation.24.clone.1 | convolution fusion | flops 89944064 | bytes 655500 | tf_op jit(solution)/shard_map/while/body/eval_jaxpr/zce,zijke->ijkc/dot_general | solution.py:168
  123.9 1.9 %fusion.181 = f32[2,2,4,256,1]{3,2,1,0,4:T(4,128)S(1)} fusion(f32[256,256]{1,0:T(8,128)S(1)} %get-tuple-element.872, f32[7]{0:T(128)S(1)} %add_convert_fusion.2, f32[256,256]{1,0:T(8,128)S(1)} %subtract_multiply_fusion.13, f32[7,2,2,4,256]{4,3,1,2,0:T(4,128)S(1)} %get-tuple-element.873), kind=kOutput, calls=%fused_computation.22.clone.1 | convolution fusion | flops 89915392 | bytes 655388 | tf_op jit(solution)/shard_map/while/body/eval_jaxpr/zce,zijke->ijkc/dot_general | solution.py:168
  125.8 1.9 %fusion.180 = f32[2,2,4,256,1]{3,2,1,0,4:T(4,128)S(1)} fusion(f32[256,256]{1,0:T(8,128)S(1)} %get-tuple-element.866, f32[7]{0:T(128)S(1)} %add_convert_fusion.2, f32[256,256]{1,0:T(8,128)S(1)} %subtract_multiply_fusion.13, f32[7,2,2,4,256]{4,3,1,2,0:T(4,128)S(1)} %get-tuple-element.871), kind=kOutput, calls=%fused_computation.20.clone.1 | convolution fusion | flops 89915392 | bytes 655388 | tf_op jit(solution)/shard_map/while/body/eval_jaxpr/zce,zijke->ijkc/dot_general | solution.py:168
  127.7 1.9 %fusion.179 = f32[2,2,4,256,1]{3,2,1,0,4:T(4,128)S(1)} fusion(f32[256,256]{1,0:T(8,128)S(1)} %get-tuple-element.864, f32[7]{0:T(128)S(1)} %add_convert_fusion.2, f32[256,256]{1,0:T(8,128)S(1)} %subtract_multiply_fusion.13, f32[7,2,2,4,256]{4,3,1,2,0:T(4,128)S(1)} %get-tuple-element.865), kind=kOutput, calls=%fused_computation.18.clone.1 | convolution fusion | flops 89915392 | bytes 655388 | tf_op jit(solution)/shard_map/while/body/eval_jaxpr/zce,zijke->ijkc/dot_general | solution.py:168
  129.6 1.9 %fusion.178 = f32[2,2,4,256,1]{3,2,1,0,4:T(4,128)S(1)} fusion(f32[256,256]{1,0:T(8,128)S(1)} %get-tuple-element.858, f32[7]{0:T(128)S(1)} %add_convert_fusion.2, f32[256,256]{1,0:T(8,128)S(1)} %subtract_multiply_fusion.13, f32[7,2,2,4,256]{4,3,1,2,0:T(4,128)S(1)} %get-tuple-element.863), kind=kOutput, calls=%fused_computation.16.clone.1 | convolution fusion | flops 89915392 | bytes 655388 | tf_op jit(solution)/shard_map/while/body/eval_jaxpr/zce,zijke->ijkc/dot_general | solution.py:168
  131.5 1.9 %fusion.176 = f32[2,2,4,256,1]{3,2,1,0,4:T(4,128)S(1)} fusion(f32[256,256]{1,0:T(8,128)S(1)} %get-tuple-element.802, f32[7]{0:T(128)S(1)} %add_convert_fusion.2, f32[256,256]{1,0:T(8,128)S(1)} %subtract_multiply_fusion.13, f32[7,2,2,4,256]{4,3,1,2,0:T(4,128)S(1)} %get-tuple-element.855), kind=kOutput, calls=%fused_computation.12.clone.1 | convolution fusion | flops 89915392 | bytes 655388 | tf_op jit(solution)/shard_map/while/body/eval_jaxpr/zce,zijke->ijkc/dot_general | solution.py:168
  133.4 1.9 %fusion.177 = f32[2,2,4,256,1]{3,2,1,0,4:T(4,128)S(1)} fusion(f32[256,256]{1,0:T(8,128)S(1)} %get-tuple-element.856, f32[7]{0:T(128)S(1)} %add_convert_fusion.2, f32[256,256]{1,0:T(8,128)S(1)} %subtract_multiply_fusion.13, f32[7,2,2,4,256]{4,3,1,2,0:T(4,128)S(1)} %get-tuple-element.857), kind=kOutput, calls=%fused_computation.14.clone.1 | convolution fusion | flops 89915392 | bytes 655388 | tf_op jit(solution)/shard_map/while/body/eval_jaxpr/zce,zijke->ijkc/dot_general | solution.py:168
  137.1 1.9 %fusion.182 = f32[2,2,4,256,1]{3,2,1,0,4:T(4,128)S(1)} fusion(f32[7]{0:T(128)S(1)} %add_convert_fusion.2, f32[256,256]{1,0:T(8,128)S(1)} %subtract_multiply_fusion.13, f32[256,256]{1,0:T(8,128)S(1)} %get-tuple-element.874, f32[7,2,2,4,256]{4,3,1,2,0:T(4,128)S(1)} %get-tuple-element.875, pred[7,2,2,4]{3,1,2,0:T(4,128)(4,1)S(1)} %get-tuple-element.876), kind=kOutput, calls=%fused_computation.24.clone.1 | convolution fusion | flops 89944064 | bytes 655500 | tf_op jit(solution)/shard_map/while/body/eval_jaxpr/zce,zijke->ijkc/dot_general | solution.py:168
  139.0 1.9 %fusion.181 = f32[2,2,4,256,1]{3,2,1,0,4:T(4,128)S(1)} fusion(f32[256,256]{1,0:T(8,128)S(1)} %get-tuple-element.872, f32[7]{0:T(128)S(1)} %add_convert_fusion.2, f32[256,256]{1,0:T(8,128)S(1)} %subtract_multiply_fusion.13, f32[7,2,2,4,256]{4,3,1,2,0:T(4,128)S(1)} %get-tuple-element.873), kind=kOutput, calls=%fused_computation.22.clone.1 | convolution fusion | flops 89915392 | bytes 655388 | tf_op jit(solution)/shard_map/while/body/eval_jaxpr/zce,zijke->ijkc/dot_general | solution.py:168
  140.9 1.9 %fusion.180 = f32[2,2,4,256,1]{3,2,1,0,4:T(4,128)S(1)} fusion(f32[256,256]{1,0:T(8,128)S(1)} %get-tuple-element.866, f32[7]{0:T(128)S(1)} %add_convert_fusion.2, f32[256,256]{1,0:T(8,128)S(1)} %subtract_multiply_fusion.13, f32[7,2,2,4,256]{4,3,1,2,0:T(4,128)S(1)} %get-tuple-element.871), kind=kOutput, calls=%fused_computation.20.clone.1 | convolution fusion | flops 89915392 | bytes 655388 | tf_op jit(solution)/shard_map/while/body/eval_jaxpr/zce,zijke->ijkc/dot_general | solution.py:168
  142.8 1.9 %fusion.179 = f32[2,2,4,256,1]{3,2,1,0,4:T(4,128)S(1)} fusion(f32[256,256]{1,0:T(8,128)S(1)} %get-tuple-element.864, f32[7]{0:T(128)S(1)} %add_convert_fusion.2, f32[256,256]{1,0:T(8,128)S(1)} %subtract_multiply_fusion.13, f32[7,2,2,4,256]{4,3,1,2,0:T(4,128)S(1)} %get-tuple-element.865), kind=kOutput, calls=%fused_computation.18.clone.1 | convolution fusion | flops 89915392 | bytes 655388 | tf_op jit(solution)/shard_map/while/body/eval_jaxpr/zce,zijke->ijkc/dot_general | solution.py:168
  144.7 1.9 %fusion.178 = f32[2,2,4,256,1]{3,2,1,0,4:T(4,128)S(1)} fusion(f32[256,256]{1,0:T(8,128)S(1)} %get-tuple-element.858, f32[7]{0:T(128)S(1)} %add_convert_fusion.2, f32[256,256]{1,0:T(8,128)S(1)} %subtract_multiply_fusion.13, f32[7,2,2,4,256]{4,3,1,2,0:T(4,128)S(1)} %get-tuple-element.863), kind=kOutput, calls=%fused_computation.16.clone.1 | convolution fusion | flops 89915392 | bytes 655388 | tf_op jit(solution)/shard_map/while/body/eval_jaxpr/zce,zijke->ijkc/dot_general | solution.py:168
  146.6 1.9 %fusion.176 = f32[2,2,4,256,1]{3,2,1,0,4:T(4,128)S(1)} fusion(f32[256,256]{1,0:T(8,128)S(1)} %get-tuple-element.802, f32[7]{0:T(128)S(1)} %add_convert_fusion.2, f32[256,256]{1,0:T(8,128)S(1)} %subtract_multiply_fusion.13, f32[7,2,2,4,256]{4,3,1,2,0:T(4,128)S(1)} %get-tuple-element.855), kind=kOutput, calls=%fused_computation.12.clone.1 | convolution fusion | flops 89915392 | bytes 655388 | tf_op jit(solution)/shard_map/while/body/eval_jaxpr/zce,zijke->ijkc/dot_general | solution.py:168
  148.5 1.9 %fusion.177 = f32[2,2,4,256,1]{3,2,1,0,4:T(4,128)S(1)} fusion(f32[256,256]{1,0:T(8,128)S(1)} %get-tuple-element.856, f32[7]{0:T(128)S(1)} %add_convert_fusion.2, f32[256,256]{1,0:T(8,128)S(1)} %subtract_multiply_fusion.13, f32[7,2,2,4,256]{4,3,1,2,0:T(4,128)S(1)} %get-tuple-element.857), kind=kOutput, calls=%fused_computation.14.clone.1 | convolution fusion | flops 89915392 | bytes 655388 | tf_op jit(solution)/shard_map/while/body/eval_jaxpr/zce,zijke->ijkc/dot_general | solution.py:168
  152.2 1.9 %fusion.182 = f32[2,2,4,256,1]{3,2,1,0,4:T(4,128)S(1)} fusion(f32[7]{0:T(128)S(1)} %add_convert_fusion.2, f32[256,256]{1,0:T(8,128)S(1)} %subtract_multiply_fusion.13, f32[256,256]{1,0:T(8,128)S(1)} %get-tuple-element.874, f32[7,2,2,4,256]{4,3,1,2,0:T(4,128)S(1)} %get-tuple-element.875, pred[7,2,2,4]{3,1,2,0:T(4,128)(4,1)S(1)} %get-tuple-element.876), kind=kOutput, calls=%fused_computation.24.clone.1 | convolution fusion | flops 89944064 | bytes 655500 | tf_op jit(solution)/shard_map/while/body/eval_jaxpr/zce,zijke->ijkc/dot_general | solution.py:168
  154.1 1.9 %fusion.181 = f32[2,2,4,256,1]{3,2,1,0,4:T(4,128)S(1)} fusion(f32[256,256]{1,0:T(8,128)S(1)} %get-tuple-element.872, f32[7]{0:T(128)S(1)} %add_convert_fusion.2, f32[256,256]{1,0:T(8,128)S(1)} %subtract_multiply_fusion.13, f32[7,2,2,4,256]{4,3,1,2,0:T(4,128)S(1)} %get-tuple-element.873), kind=kOutput, calls=%fused_computation.22.clone.1 | convolution fusion | flops 89915392 | bytes 655388 | tf_op jit(solution)/shard_map/while/body/eval_jaxpr/zce,zijke->ijkc/dot_general | solution.py:168
  156.0 1.9 %fusion.180 = f32[2,2,4,256,1]{3,2,1,0,4:T(4,128)S(1)} fusion(f32[256,256]{1,0:T(8,128)S(1)} %get-tuple-element.866, f32[7]{0:T(128)S(1)} %add_convert_fusion.2, f32[256,256]{1,0:T(8,128)S(1)} %subtract_multiply_fusion.13, f32[7,2,2,4,256]{4,3,1,2,0:T(4,128)S(1)} %get-tuple-element.871), kind=kOutput, calls=%fused_computation.20.clone.1 | convolution fusion | flops 89915392 | bytes 655388 | tf_op jit(solution)/shard_map/while/body/eval_jaxpr/zce,zijke->ijkc/dot_general | solution.py:168
  157.9 1.9 %fusion.179 = f32[2,2,4,256,1]{3,2,1,0,4:T(4,128)S(1)} fusion(f32[256,256]{1,0:T(8,128)S(1)} %get-tuple-element.864, f32[7]{0:T(128)S(1)} %add_convert_fusion.2, f32[256,256]{1,0:T(8,128)S(1)} %subtract_multiply_fusion.13, f32[7,2,2,4,256]{4,3,1,2,0:T(4,128)S(1)} %get-tuple-element.865), kind=kOutput, calls=%fused_computation.18.clone.1 | convolution fusion | flops 89915392 | bytes 655388 | tf_op jit(solution)/shard_map/while/body/eval_jaxpr/zce,zijke->ijkc/dot_general | solution.py:168
  159.8 1.9 %fusion.178 = f32[2,2,4,256,1]{3,2,1,0,4:T(4,128)S(1)} fusion(f32[256,256]{1,0:T(8,128)S(1)} %get-tuple-element.858, f32[7]{0:T(128)S(1)} %add_convert_fusion.2, f32[256,256]{1,0:T(8,128)S(1)} %subtract_multiply_fusion.13, f32[7,2,2,4,256]{4,3,1,2,0:T(4,128)S(1)} %get-tuple-element.863), kind=kOutput, calls=%fused_computation.16.clone.1 | convolution fusion | flops 89915392 | bytes 655388 | tf_op jit(solution)/shard_map/while/body/eval_jaxpr/zce,zijke->ijkc/dot_general | solution.py:168
  161.8 1.9 %fusion.176 = f32[2,2,4,256,1]{3,2,1,0,4:T(4,128)S(1)} fusion(f32[256,256]{1,0:T(8,128)S(1)} %get-tuple-element.802, f32[7]{0:T(128)S(1)} %add_convert_fusion.2, f32[256,256]{1,0:T(8,128)S(1)} %subtract_multiply_fusion.13, f32[7,2,2,4,256]{4,3,1,2,0:T(4,128)S(1)} %get-tuple-element.855), kind=kOutput, calls=%fused_computation.12.clone.1 | convolution fusion | flops 89915392 | bytes 655388 | tf_op jit(solution)/shard_map/while/body/eval_jaxpr/zce,zijke->ijkc/dot_general | solution.py:168
  163.7 1.9 %fusion.177 = f32[2,2,4,256,1]{3,2,1,0,4:T(4,128)S(1)} fusion(f32[256,256]{1,0:T(8,128)S(1)} %get-tuple-element.856, f32[7]{0:T(128)S(1)} %add_convert_fusion.2, f32[256,256]{1,0:T(8,128)S(1)} %subtract_multiply_fusion.13, f32[7,2,2,4,256]{4,3,1,2,0:T(4,128)S(1)} %get-tuple-element.857), kind=kOutput, calls=%fused_computation.14.clone.1 | convolution fusion | flops 89915392 | bytes 655388 | tf_op jit(solution)/shard_map/while/body/eval_jaxpr/zce,zijke->ijkc/dot_general | solution.py:168
  167.4 1.9 %fusion.182 = f32[2,2,4,256,1]{3,2,1,0,4:T(4,128)S(1)} fusion(f32[7]{0:T(128)S(1)} %add_convert_fusion.2, f32[256,256]{1,0:T(8,128)S(1)} %subtract_multiply_fusion.13, f32[256,256]{1,0:T(8,128)S(1)} %get-tuple-element.874, f32[7,2,2,4,256]{4,3,1,2,0:T(4,128)S(1)} %get-tuple-element.875, pred[7,2,2,4]{3,1,2,0:T(4,128)(4,1)S(1)} %get-tuple-element.876), kind=kOutput, calls=%fused_computation.24.clone.1 | convolution fusion | flops 89944064 | bytes 655500 | tf_op jit(solution)/shard_map/while/body/eval_jaxpr/zce,zijke->ijkc/dot_general | solution.py:168
  169.3 1.9 %fusion.181 = f32[2,2,4,256,1]{3,2,1,0,4:T(4,128)S(1)} fusion(f32[256,256]{1,0:T(8,128)S(1)} %get-tuple-element.872, f32[7]{0:T(128)S(1)} %add_convert_fusion.2, f32[256,256]{1,0:T(8,128)S(1)} %subtract_multiply_fusion.13, f32[7,2,2,4,256]{4,3,1,2,0:T(4,128)S(1)} %get-tuple-element.873), kind=kOutput, calls=%fused_computation.22.clone.1 | convolution fusion | flops 89915392 | bytes 655388 | tf_op jit(solution)/shard_map/while/body/eval_jaxpr/zce,zijke->ijkc/dot_general | solution.py:168
  171.2 1.9 %fusion.180 = f32[2,2,4,256,1]{3,2,1,0,4:T(4,128)S(1)} fusion(f32[256,256]{1,0:T(8,128)S(1)} %get-tuple-element.866, f32[7]{0:T(128)S(1)} %add_convert_fusion.2, f32[256,256]{1,0:T(8,128)S(1)} %subtract_multiply_fusion.13, f32[7,2,2,4,256]{4,3,1,2,0:T(4,128)S(1)} %get-tuple-element.871), kind=kOutput, calls=%fused_computation.20.clone.1 | convolution fusion | flops 89915392 | bytes 655388 | tf_op jit(solution)/shard_map/while/body/eval_jaxpr/zce,zijke->ijkc/dot_general | solution.py:168
  173.1 1.9 %fusion.179 = f32[2,2,4,256,1]{3,2,1,0,4:T(4,128)S(1)} fusion(f32[256,256]{1,0:T(8,128)S(1)} %get-tuple-element.864, f32[7]{0:T(128)S(1)} %add_convert_fusion.2, f32[256,256]{1,0:T(8,128)S(1)} %subtract_multiply_fusion.13, f32[7,2,2,4,256]{4,3,1,2,0:T(4,128)S(1)} %get-tuple-element.865), kind=kOutput, calls=%fused_computation.18.clone.1 | convolution fusion | flops 89915392 | bytes 655388 | tf_op jit(solution)/shard_map/while/body/eval_jaxpr/zce,zijke->ijkc/dot_general | solution.py:168
  175.0 1.9 %fusion.178 = f32[2,2,4,256,1]{3,2,1,0,4:T(4,128)S(1)} fusion(f32[256,256]{1,0:T(8,128)S(1)} %get-tuple-element.858, f32[7]{0:T(128)S(1)} %add_convert_fusion.2, f32[256,256]{1,0:T(8,128)S(1)} %subtract_multiply_fusion.13, f32[7,2,2,4,256]{4,3,1,2,0:T(4,128)S(1)} %get-tuple-element.863), kind=kOutput, calls=%fused_computation.16.clone.1 | convolution fusion | flops 89915392 | bytes 655388 | tf_op jit(solution)/shard_map/while/body/eval_jaxpr/zce,zijke->ijkc/dot_general | solution.py:168
  176.9 1.9 %fusion.176 = f32[2,2,4,256,1]{3,2,1,0,4:T(4,128)S(1)} fusion(f32[256,256]{1,0:T(8,128)S(1)} %get-tuple-element.802, f32[7]{0:T(128)S(1)} %add_convert_fusion.2, f32[256,256]{1,0:T(8,128)S(1)} %subtract_multiply_fusion.13, f32[7,2,2,4,256]{4,3,1,2,0:T(4,128)S(1)} %get-tuple-element.855), kind=kOutput, calls=%fused_computation.12.clone.1 | convolution fusion | flops 89915392 | bytes 655388 | tf_op jit(solution)/shard_map/while/body/eval_jaxpr/zce,zijke->ijkc/dot_general | solution.py:168
  178.8 1.9 %fusion.177 = f32[2,2,4,256,1]{3,2,1,0,4:T(4,128)S(1)} fusion(f32[256,256]{1,0:T(8,128)S(1)} %get-tuple-element.856, f32[7]{0:T(128)S(1)} %add_convert_fusion.2, f32[256,256]{1,0:T(8,128)S(1)} %subtract_multiply_fusion.13, f32[7,2,2,4,256]{4,3,1,2,0:T(4,128)S(1)} %get-tuple-element.857), kind=kOutput, calls=%fused_computation.14.clone.1 | convolution fusion | flops 89915392 | bytes 655388 | tf_op jit(solution)/shard_map/while/body/eval_jaxpr/zce,zijke->ijkc/dot_general | solution.py:168
  181.1 1.3 multiply_reduce_fusion.3
  (343 shorter events, 23.6 us)
Async XLA Ops:
  0.0 2.8 %copy-start = (f32[256,256]{1,0:T(8,128)S(1)}, f32[256,256]{1,0:T(8,128)}, u32[]{:S(2)}) copy-start(f32[256,256]{1,0:T(8,128)} %param.17) | copy-start | bytes 786436
  3.1 20.8 %collective-permute-start.5 = (f32[2,2,4,256]{3,2,1,0:T(4,128)S(1)}, f32[2,2,4,256]{3,2,1,0:T(4,128)S(1)}, u32[]{:S(2)}, u32[]{:S(2)}) collective-permute-start(f32[2,2,4,256]{3,2,1,0:T(4,128)S(1)} %fusion.112), channel_id=1, source_target_pairs={{4,0},{8,4},{12,8},{16,12},{20,16},{24,20},{28,24},{0,28},{5,1},{9... | collective-permute-start | bytes 49160 | tf_op jit(solution)/shard_map/ppermute | solution.py:21
  6.5 17.4 %collective-permute-start.4 = (f32[2,2,4,256]{3,2,1,0:T(4,128)S(1)}, f32[2,2,4,256]{3,2,1,0:T(4,128)S(1)}, u32[]{:S(2)}, u32[]{:S(2)}) collective-permute-start(f32[2,2,4,256]{3,2,1,0:T(4,128)S(1)} %fusion.112), channel_id=1, source_target_pairs={{0,4},{4,8},{8,12},{12,16},{16,20},{20,24},{24,28},{28,0},{1,5},{5... | collective-permute-start | bytes 49160 | tf_op jit(solution)/shard_map/ppermute | solution.py:19
  8.0 20.1 %collective-permute-start = (f32[4,1,2,4,128]{4,3,2,1,0:T(4,128)S(1)}, f32[4,1,2,4,128]{4,3,2,1,0:T(4,128)S(1)}, u32[]{:S(2)}, u32[]{:S(2)}) collective-permute-start(f32[4,1,2,4,128]{4,3,2,1,0:T(4,128)S(1)} %get-tuple-element.669), channel_id=1, source_target_pairs={{0,4},{4,8},{8,12},{12,16},{16,20},{20,24},{24,28},{28,0},{1,5},{5... | collective-permute-start | bytes 49160 | tf_op jit(solution)/shard_map/ppermute | solution.py:19
  8.0 20.0 %collective-permute-start.1 = (f32[4,1,2,4,128]{4,3,2,1,0:T(4,128)S(1)}, f32[4,1,2,4,128]{4,3,2,1,0:T(4,128)S(1)}, u32[]{:S(2)}, u32[]{:S(2)}) collective-permute-start(f32[4,1,2,4,128]{4,3,2,1,0:T(4,128)S(1)} %get-tuple-element.670), channel_id=1, source_target_pairs={{4,0},{8,4},{12,8},{16,12},{20,16},{24,20},{28,24},{0,28},{5,1},{9... | collective-permute-start | bytes 49160 | tf_op jit(solution)/shard_map/ppermute | solution.py:21
  11.0 1.3 copy-start.3
  11.1 5.6 %copy-start.1 = (f32[3,2,2,4,128]{4,3,2,1,0:T(4,128)S(1)}, f32[3,2,2,4,128]{4,3,2,1,0:T(4,128)}, u32[]{:S(2)}) copy-start(f32[3,2,2,4,128]{4,3,2,1,0:T(4,128)} %param.14) | copy-start | bytes 73732
  11.1 5.7 %copy-start.8 = (f32[23]{0:T(128)S(1)}, f32[23]{0:T(128)}, u32[]{:S(2)}) copy-start(f32[23]{0:T(128)} %constant.325) | copy-start | bytes 280
  11.1 5.8 %copy-start.9 = (f32[23]{0:T(128)S(1)}, f32[23]{0:T(128)}, u32[]{:S(2)}) copy-start(f32[23]{0:T(128)} %constant.324) | copy-start | bytes 280
  11.1 6.1 %copy-start.6 = (s32[432]{0:T(512)S(1)}, s32[432]{0:T(512)}, u32[]{:S(2)}) copy-start(s32[432]{0:T(512)} %constant.338) | copy-start | bytes 5188
  11.1 7.8 %copy-start.7 = (s32[23]{0:T(128)S(1)}, s32[23]{0:T(128)}, u32[]{:S(2)}) copy-start(s32[23]{0:T(128)} %constant.339) | copy-start | bytes 280
  12.6 5.0 %collective-permute-start.8 = (f32[1,1,2,256]{3,2,1,0:T(2,128)S(1)}, f32[1,1,2,256]{3,2,1,0:T(2,128)S(1)}, u32[]{:S(2)}, u32[]{:S(2)}) collective-permute-start(f32[1,1,2,256]{3,2,1,0:T(2,128)S(1)} %convolution_bitcast_fusion), channel_id=1, source_target_pairs={{0,3},{1,0},{2,1},{3,2},{4,7},{5,4},{6,5},{7,6},{8,11},{9,8},{10,9... | collective-permute-start | bytes 6152 | tf_op jit(solution)/shard_map/ppermute | solution.py:73
  17.6 4.5 %collective-permute-start.9 = (f32[1,2,2,256]{3,2,1,0:T(2,128)S(1)}, f32[1,2,2,256]{3,2,1,0:T(2,128)S(1)}, u32[]{:S(2)}, u32[]{:S(2)}) collective-permute-start(f32[1,2,2,256]{3,2,1,0:T(2,128)S(1)} %pad_maximum_fusion.10), channel_id=1, source_target_pairs={{0,2},{1,3},{2,0},{3,1},{4,6},{5,7},{6,4},{7,5},{8,10},{9,11},{10,... | collective-permute-start | bytes 12296 | tf_op jit(solution)/shard_map/ppermute | solution.py:73
  22.1 1.4 collective-permute-start.10
  23.5 8.7 %collective-permute-start.11 = (f32[2,4,2,256]{3,2,1,0:T(2,128)S(1)}, f32[2,4,2,256]{3,2,1,0:T(2,128)S(1)}, u32[]{:S(2)}, u32[]{:S(2)}) collective-permute-start(f32[2,4,2,256]{3,2,1,0:T(2,128)S(1)} %pad_maximum_fusion.7), channel_id=1, source_target_pairs={{0,24},{4,28},{8,0},{12,4},{16,8},{20,12},{24,16},{28,20},{1,25},{... | collective-permute-start | bytes 49160 | tf_op jit(solution)/shard_map/ppermute | solution.py:73
  23.9 50.4 %collective-permute-start.7 = (f32[6,2,4,256]{3,2,1,0:T(4,128)S(1)}, f32[6,2,4,256]{3,2,1,0:T(4,128)S(1)}, u32[]{:S(2)}, u32[]{:S(2)}) collective-permute-start(f32[6,2,4,256]{3,2,1,0:T(4,128)S(1)} %pad_maximum_fusion.4), channel_id=1, source_target_pairs={{1,0},{2,1},{3,2},{0,3},{5,4},{6,5},{7,6},{4,7},{9,8},{10,9},{11,1... | collective-permute-start | bytes 147464 | tf_op jit(solution)/shard_map/ppermute | solution.py:21
  28.0 46.3 %collective-permute-start.6 = (f32[6,2,4,256]{3,2,1,0:T(4,128)S(1)}, f32[6,2,4,256]{3,2,1,0:T(4,128)S(1)}, u32[]{:S(2)}, u32[]{:S(2)}) collective-permute-start(f32[6,2,4,256]{3,2,1,0:T(4,128)S(1)} %pad_maximum_fusion.4), channel_id=1, source_target_pairs={{0,1},{1,2},{2,3},{3,0},{4,5},{5,6},{6,7},{7,4},{8,9},{9,10},{10,1... | collective-permute-start | bytes 147464 | tf_op jit(solution)/shard_map/ppermute | solution.py:19
  28.1 6.2 %collective-permute-start.2 = (f32[4,4,1,4,128]{4,3,2,1,0:T(4,128)S(1)}, f32[4,4,1,4,128]{4,3,2,1,0:T(4,128)S(1)}, u32[]{:S(2)}, u32[]{:S(2)}) collective-permute-start(f32[4,4,1,4,128]{4,3,2,1,0:T(4,128)S(1)} %get-tuple-element.667), channel_id=1, source_target_pairs={{0,1},{1,2},{2,3},{3,0},{4,5},{5,6},{6,7},{7,4},{8,9},{9,10},{10,1... | collective-permute-start | bytes 98312 | tf_op jit(solution)/shard_map/ppermute | solution.py:19
  28.2 6.2 %collective-permute-start.3 = (f32[4,4,1,4,128]{4,3,2,1,0:T(4,128)S(1)}, f32[4,4,1,4,128]{4,3,2,1,0:T(4,128)S(1)}, u32[]{:S(2)}, u32[]{:S(2)}) collective-permute-start(f32[4,4,1,4,128]{4,3,2,1,0:T(4,128)S(1)} %get-tuple-element.668), channel_id=1, source_target_pairs={{1,0},{2,1},{3,2},{0,3},{5,4},{6,5},{7,6},{4,7},{9,8},{10,9},{11,1... | collective-permute-start | bytes 98312 | tf_op jit(solution)/shard_map/ppermute | solution.py:21
  32.2 28.0 %collective-permute-start.12 = (f32[4,4,2,256]{3,2,1,0:T(2,128)S(1)}, f32[4,4,2,256]{3,2,1,0:T(2,128)S(1)}, u32[]{:S(2)}, u32[]{:S(2)}) collective-permute-start(f32[4,4,2,256]{3,2,1,0:T(2,128)S(1)} %pad_maximum_fusion.5), channel_id=1, source_target_pairs={{0,16},{4,20},{8,24},{12,28},{16,0},{20,4},{24,8},{28,12},{1,17},{... | collective-permute-start | bytes 98312 | tf_op jit(solution)/shard_map/ppermute | solution.py:73
  34.4 3.1 %copy-start.10 = (f32[27]{0:T(128)S(1)}, f32[27]{0:T(128)}, u32[]{:S(2)}) copy-start(f32[27]{0:T(128)} %constant.337) | copy-start | bytes 328
  34.4 3.1 %copy-start.11 = (f32[27]{0:T(128)S(1)}, f32[27]{0:T(128)}, u32[]{:S(2)}) copy-start(f32[27]{0:T(128)} %constant.336) | copy-start | bytes 328
  34.4 3.1 %copy-start.12 = (f32[27]{0:T(128)S(1)}, f32[27]{0:T(128)}, u32[]{:S(2)}) copy-start(f32[27]{0:T(128)} %constant.335) | copy-start | bytes 328
  61.0 11.7 %copy-start.4 = (f32[256,256]{1,0:T(8,128)S(1)}, f32[256,256]{1,0:T(8,128)}, u32[]{:S(2)}) copy-start(f32[256,256]{1,0:T(8,128)} %param.20) | copy-start | bytes 786436
  74.5 106.2 %copy-start.2 = (f32[256,256]{1,0:T(8,128)S(1)}, f32[256,256]{1,0:T(8,128)}, u32[]{:S(2)}) copy-start(f32[256,256]{1,0:T(8,128)} %param.18) | copy-start | bytes 786436
  74.5 107.9 %copy-start.5 = (s32[2,2,4]{2,1,0:T(2,128)S(1)}, s32[2,2,4]{2,1,0:T(2,128)}, u32[]{:S(2)}) copy-start(s32[2,2,4]{2,1,0:T(2,128)} %param.16) | copy-start | bytes 196

commit v2 on v1

--- a/solution.py
+++ b/solution.py
@@ -1,28 +1,16 @@
+import functools
+
 import jax
 import numpy as np
 import jax.numpy as jnp
 from jax import lax
+from jax.experimental import pallas as pl
+from jax.experimental.pallas import tpu as pltpu
 from jax.sharding import PartitionSpec as P
 
 softening_sq = 0.0004
 golden_turn = 2.399963229728653
 highest = lax.Precision.HIGHEST
-
-
-def padded(cells, sides, width):
-    for axis, dim in sides:
-        count = lax.axis_size(axis)
-        head = lax.slice_in_dim(cells, 0, width, axis=dim)
-        tail = lax.slice_in_dim(cells, cells.shape[dim] - width, cells.shape[dim], axis=dim)
-        cells = jnp.concatenate(
-            [
-                lax.ppermute(tail, axis, [(i, (i + 1) % count) for i in range(count)]),
-                cells,
-                lax.ppermute(head, axis, [((i + 1) % count, i) for i in range(count)]),
-            ],
-            axis=dim,
-        )
-    return cells
 
 
 def sphere(point_count):
@@ -76,6 +64,92 @@
     return buf
 
 
+def exchange(items, axis):
+    count = lax.axis_size(axis)
+    heads, tails = [], []
+    for cells, dim, width in items:
+        heads.append(lax.slice_in_dim(cells, 0, width, axis=dim))
+        tails.append(lax.slice_in_dim(cells, cells.shape[dim] - width, cells.shape[dim], axis=dim))
+    sent_tail = jnp.concatenate([t.reshape(-1) for t in tails])
+    sent_head = jnp.concatenate([h.reshape(-1) for h in heads])
+    from_left = lax.ppermute(sent_tail, axis, [(i, (i + 1) % count) for i in range(count)])
+    from_right = lax.ppermute(sent_head, axis, [((i + 1) % count, i) for i in range(count)])
+    out, start = [], 0
+    for (cells, dim, width), head, tail in zip(items, heads, tails):
+        size = head.size
+        before = from_left[start : start + size].reshape(tail.shape)
+        after = from_right[start : start + size].reshape(head.shape)
+        out.append(jnp.concatenate([before, cells, after], axis=dim))
+        start += size
+    return out
+
+
+def m2l_kernel(shift_count, rows, table_ref, base_ref, plus_ref, minus_ref, out_ref):
+    out_ref[...] = jnp.zeros_like(out_ref)
+
+    def body(index, carry):
+        shift_x = table_ref[3 * index]
+        shift_y = table_ref[3 * index + 1]
+        shift_z = table_ref[3 * index + 2]
+        fwd = plus_ref[index]
+        back = minus_ref[index]
+        for row in range(0, base_ref.shape[1], rows):
+            delta_x = base_ref[0, row : row + rows, :] - shift_x
+            delta_y = base_ref[1, row : row + rows, :] - shift_y
+            delta_z = base_ref[2, row : row + rows, :] - shift_z
+            matrix = lax.rsqrt(
+                delta_x * delta_x + delta_y * delta_y + delta_z * delta_z + softening_sq
+            )
+            out_ref[:, row : row + rows] += lax.dot_general(
+                fwd,
+                matrix,
+                (((1,), (1,)), ((), ())),
+                precision=highest,
+                preferred_element_type=jnp.float32,
+            )
+            out_ref[...] += lax.dot_general(
+                back[:, row : row + rows],
+                matrix,
+                (((1,), (0,)), ((), ())),
+                precision=highest,
+                preferred_element_type=jnp.float32,
+            )
+        return carry
+
+    lax.fori_loop(0, shift_count, body, 0)
+
+
+def m2l(table, base, plus, minus):
+    shift_count, vectors, points = plus.shape
+    return pl.pallas_call(
+        functools.partial(m2l_kernel, shift_count, 128),
+        out_shape=jax.ShapeDtypeStruct((vectors, points), jnp.float32),
+        in_specs=[
+            pl.BlockSpec(memory_space=pltpu.SMEM),
+            pl.BlockSpec(memory_space=pltpu.VMEM),
+            pl.BlockSpec(memory_space=pltpu.VMEM),
+            pl.BlockSpec(memory_space=pltpu.VMEM),
+        ],
+        out_specs=pl.BlockSpec(memory_space=pltpu.VMEM),
+        compiler_params=pltpu.CompilerParams(vmem_limit_bytes=48 * 1024 * 1024),
+        cost_estimate=pl.CostEstimate(
+            flops=4 * shift_count * vectors * points * points + 10 * shift_count * points * points,
+            transcendentals=shift_count * points * points,
+            bytes_accessed=4 * (2 * plus.size + base.size + vectors * points),
+        ),
+    )(table, base, plus, minus)
+
+
+def far_shifts(span):
+    shifts = []
+    for dx in range(-span, span + 1):
+        for dy in range(-span, span + 1):
+            for dz in range(-span, span + 1):
+                if max(abs(dx), abs(dy), abs(dz)) >= 2 and (dx, dy, dz) > (0, 0, 0):
+                    shifts.append((dx, dy, dz))
+    return shifts
+
+
 def shards(offsets, charges, counts, c2e_leaf_up, c2e_leaf_down, c2e_top_up, c2e_top_down):
     slot_count = offsets.shape[-1]
     layers = offsets.shape[3]
@@ -85,10 +159,11 @@
     slot_index = jnp.arange(slot_count)
     weights = jnp.where(slot_index < counts[..., None], charges, 0.0)
     packed = jnp.concatenate([offsets, weights[None]], axis=0)
-    beside_all = padded(packed, (("gx", 1), ("gy", 2)), 1)
     leaf_check_pts = 0.5 + 1.8 * unit_sphere
     leaf_check = point_sum(leaf_check_pts[:, None, None, None, :], offsets, weights)
     leaf_eq = jnp.einsum("ec,xyzc->xyze", c2e_leaf_up, leaf_check, precision=highest)
+    packed_x, eq_x = exchange([(packed, 1, 1), (leaf_eq, 0, 2)], "gx")
+    beside_all, cycle = exchange([(packed_x, 2, 1), (eq_x, 1, 2)], "gy")
     children = child_points(unit_sphere)
     parent_weights = (
         leaf_eq.reshape(2, 2, parent_layers, 2, points)
@@ -129,46 +204,32 @@
         far_sources.reshape(-1),
     )
 
-    local_index = jnp.arange(2)
-    layer_index = jnp.arange(layers)
-    depth_shift = jnp.arange(7) - 3
-    depth_float = depth_shift.astype(jnp.float32)
-    seven_ones = jnp.ones((7,), jnp.float32)
-    valid_z = (layer_index[None, :] + depth_shift[:, None] >= 0) & (
-        layer_index[None, :] + depth_shift[:, None] <= layers - 1
-    )
-    cycle = padded(leaf_eq, (("gx", 0), ("gy", 1)), 2)
     framed = jnp.pad(cycle, ((1, 1), (1, 1), (3, 3), (0, 0)))
-
-    def list_row(offset_x, running):
-        shift_x = offset_x - 3
-        valid_x = (local_index + shift_x >= -2) & (local_index + shift_x <= 3)
-        for offset_y in range(7):
-            shift_y = offset_y - 3
-            valid_y = (local_index + shift_y >= -2) & (local_index + shift_y <= 3)
-            block = lax.dynamic_slice(
-                framed, (offset_x, offset_y, 0, 0), (2, 2, layers + 6, points)
-            )
-            stacked = jnp.stack([block[:, :, depth : depth + layers] for depth in range(7)])
-            far_enough = (jnp.abs(shift_x) > 1) | (abs(shift_y) > 1) | (jnp.abs(depth_shift) > 1)
-            keep = (
-                valid_x[None, :, None, None]
-                & valid_y[None, None, :, None]
-                & valid_z[:, None, None, :]
-                & far_enough[:, None, None, None]
-            )
-            matrices = translation(
-                unit_sphere,
-                shift_x.astype(jnp.float32) * seven_ones,
-                float(shift_y) * seven_ones,
-                depth_float,
-                0.9,
-            )
-            sources = jnp.where(keep[..., None], stacked, 0.0)
-            running = running + jnp.einsum("zce,zijke->ijkc", matrices, sources, precision=highest)
-        return running
-
-    leaf_down_check = lax.fori_loop(0, 7, list_row, jnp.zeros((2, 2, layers, points), jnp.float32))
+    shifts = far_shifts(3)
+    targets = [(ix, iy, k) for ix in range(2) for iy in range(2) for k in range(layers)]
+
+    def rows_for(sign):
+        return np.array(
+            [
+                [
+                    np.ravel_multi_index(
+                        (ix + sign * dx + 3, iy + sign * dy + 3, k + sign * dz + 3), framed.shape[:3]
+                    )
+                    for ix, iy, k in targets
+                ]
+                for dx, dy, dz in shifts
+            ],
+            np.int32,
+        )
+
+    framed_rows = framed.reshape(-1, points)
+    plus = jnp.take(framed_rows, rows_for(1), axis=0)
+    minus = jnp.take(framed_rows, rows_for(-1), axis=0)
+    base = jnp.stack(
+        [0.9 * (unit_sphere[i][:, None] - unit_sphere[i][None, :]) for i in range(3)]
+    )
+    table = jnp.asarray(np.array(shifts, np.float32).reshape(-1))
+    leaf_down_check = m2l(table, base, plus, minus).reshape(2, 2, layers, points)
     parent_local = jnp.einsum("ec,mc->me", c2e_top_down, far_check, precision=highest)
     leaf_local = jnp.einsum("ec,xyzc->xyze", c2e_leaf_down, leaf_down_check, precision=highest)
 

time: 184 us -> 171 us (0.929)
  matrix products: 94 us -> 2.14 us
  Pallas kernels: 0 us -> 76 us
  local copies, waits for them, and re-layouts: 7.32 us -> 22 us
  other arithmetic: 53 us -> 47.2 us
  starting transfers between devices: 20.3 us -> 14.9 us
    dot_general x49 -> x0, matrix products: 92.8 us -> none  [list_row(): jnp.einsum('zce,zijke->ijkc', matrices, sources, precision=highest)]
    pallas_call x0 -> x1, Pallas kernels: none -> 76 us  [m2l(): pl.pallas_call(functools.partial(m2l_kernel, shift_count, 128), out_shape...]
    gather x0 -> x2, local copies, waits for them, and re-layouts: none -> 13 us  [the longest x1 7.03 us: shards(): plus = jnp.take(framed_rows, rows_for(1), axis=0)]
    ppermute x8 -> x4, starting transfers between devices: 14.4 us -> 7.32 us  [the longest x2 6.76 us: exchange(): lax.ppermute(sent_head, axis, [((i + 1) % count, i) for i in range(count)])]
    ppermute x5, waiting for transfers between devices: 4.63 us -> 7.69 us  [rel_gather(): lax.ppermute(part, axis, [(j, (j - have) % count) for j in range(count)])]
    unnamed x31 -> x50, local copies, waits for them, and re-layouts: 0.2 us -> 3.12 us
    select_n x21 -> x0, other arithmetic: 2.65 us -> none  [list_row(): sources = jnp.where(keep[..., None], stacked, 0.0)]
    and x77 -> x0, other arithmetic: 2.37 us -> none  [the longest x14 1.42 us: list_row(): valid_x[None, :, None, None] & valid_y[None, None, :, None]]
  transfers between devices with their start and end apart: 13 -> 9, of which waited for: 4 -> 3; matrix products, arithmetic and copies ran while one was open for 24% -> 11% of each run, Pallas kernels for 0% -> 0%
where the time goes in v2:
time: 171 us
  Pallas kernels  76 us (44%)
  other arithmetic  47.2 us (28%)
  local copies, waits for them, and re-layouts  22 us (13%)
  starting transfers between devices  14.9 us (9%)
  waiting for transfers between devices  7.7 us (5%)
  matrix products  2.14 us (1%)
    pallas_call x1, Pallas kernels, m2l(): pl.pallas_call(functools.partial(m2l_kernel, shift_count, 128), out_shape...  76 us
    reduce_sum x1, other arithmetic, shards(): near = jnp.sum(jnp.sum(kernel * source[3][..., None, :], axis=-1), axis=0)  23.4 us
    reduce_sum x5, other arithmetic, point_sum(): return jnp.sum(kernel * weights[..., None, :], axis=-1)  16.5 us
    ppermute x5, waiting for transfers between devices, rel_gather(): lax.ppermute(part, axis, [(j, (j - have) % count) for j in range(count)])  7.69 us
    ppermute x5, starting transfers between devices, rel_gather(): lax.ppermute(part, axis, [(j, (j - have) % count) for j in range(count)])  7.62 us
    gather x1, local copies, waits for them, and re-layouts, shards(): plus = jnp.take(framed_rows, rows_for(1), axis=0)  7.03 us
    ppermute x2, starting transfers between devices, exchange(): lax.ppermute(sent_head, axis, [((i + 1) % count, i) for i in range(count)])  6.76 us
    gather x1, local copies, waits for them, and re-layouts, shards(): minus = jnp.take(framed_rows, rows_for(-1), axis=0)  5.98 us
  transfers between devices with their start and end apart: 9, of which 3 were waited for; matrix products, arithmetic and copies ran while one was open for 11% of the time, Pallas kernels for 0%

profile of v2, /device:TPU:0, one launch (start us, length us, event | category | flops | bytes accessed | tf_op | source)
XLA Modules:
  0.0 170.7 jit_solution(12456212092895139477)
XLA Ops:
  0.0 0.1 cosine_multiply_fusion.1
  0.1 0.1 sine_multiply_fusion.1
  0.1 0.8 fusion.38
  0.9 0.8 fusion.17
  1.7 0.7 slice_bitcast_fusion.2
  2.5 1.1 multiply_reduce_fusion.4
  3.6 0.3 fusion.14
  3.9 0.7 fusion.16
  4.7 0.5 collective-permute-start
  5.2 2.9 %collective-permute-start.1 = (f32[8192]{0:T(1024)S(1)}, f32[8192]{0:T(1024)S(1)}, u32[]{:S(2)}, u32[]{:S(2)}) collective-permute-start(f32[8192]{0:T(1024)S(1)} %get-tuple-element.27), channel_id=1, source_target_pairs={{4,0},{8,4},{12,8},{16,12},{20,16},{24,20},{28,24},{0,28},{5,1},{9... | collective-permute-start | bytes 98312 | tf_op jit(solution)/shard_map/ppermute | solution.py:76
  8.2 0.1 broadcast_add_fusion.8
  8.4 0.0 copy-start.6
  8.4 0.0 copy-start.4
  8.4 0.0 copy-start.20
  8.5 0.0 copy-start.21
  8.5 0.8 add_rsqrt_fusion
  9.3 0.4 multiply_reduce_fusion.1
  9.7 0.0 copy-start.11
  9.8 0.0 copy-start.10
  9.8 0.0 copy-start.14
  9.8 0.0 copy-start.19
  9.8 0.3 convolution_bitcast_fusion
  10.1 4.4 %collective-permute-start.4 = (f32[1,1,2,256]{3,2,1,0:T(2,128)S(1)}, f32[1,1,2,256]{3,2,1,0:T(2,128)S(1)}, u32[]{:S(2)}, u32[]{:S(2)}) collective-permute-start(f32[1,1,2,256]{3,2,1,0:T(2,128)S(1)} %convolution_bitcast_fusion), channel_id=1, source_target_pairs={{0,3},{1,0},{2,1},{3,2},{4,7},{5,4},{6,5},{7,6},{8,11},{9,8},{10,9... | collective-permute-start | bytes 6152 | tf_op jit(solution)/shard_map/ppermute | solution.py:61
  14.4 0.1 fusion.23
  14.7 0.1 fusion.21
  14.8 0.1 subtract_multiply_fusion.3
  14.9 0.1 broadcast_add_fusion.4
  15.0 0.1 subtract_multiply_fusion.2
  15.1 0.1 broadcast_add_fusion.5
  15.1 0.1 broadcast_add_fusion
  15.2 0.1 broadcast_add_fusion.1
  15.3 1.0 broadcast_and_fusion
  16.3 0.1 subtract_multiply_fusion
  16.5 1.0 pad_maximum_fusion.base_ref
  17.5 0.1 collective-permute-start.5
  17.6 4.5 %collective-permute-done.5 = f32[1,2,2,256]{3,2,1,0:T(2,128)S(1)} collective-permute-done((f32[1,2,2,256]{3,2,1,0:T(2,128)S(1)}, f32[1,2,2,256]{3,2,1,0:T(2,128)S(1)}, u32[]{:S(2)}, u32[]{:S(2)}) %collective-permute-start.5) | collective-permute-done | bytes 4128 | tf_op jit(solution)/shard_map/ppermute | solution.py:61
  22.1 1.3 collective-permute-done.6
  23.4 1.6 collective-permute-start.7
  25.2 0.1 stack_broadcast_in_dim.41
  25.3 1.9 %collective-permute-done.7 = f32[2,4,2,256]{3,2,1,0:T(2,128)S(1)} collective-permute-done((f32[2,4,2,256]{3,2,1,0:T(2,128)S(1)}, f32[2,4,2,256]{3,2,1,0:T(2,128)S(1)}, u32[]{:S(2)}, u32[]{:S(2)}) %collective-permute-start.7) | collective-permute-done | bytes 16416 | tf_op jit(solution)/shard_map/ppermute | solution.py:61
  27.2 1.6 collective-permute-start.8
  29.0 0.1 collective-permute-start.2
  29.1 3.8 %collective-permute-start.3 = (f32[20480]{0:T(1024)S(1)}, f32[20480]{0:T(1024)S(1)}, u32[]{:S(2)}, u32[]{:S(2)}) collective-permute-start(f32[20480]{0:T(1024)S(1)} %get-tuple-element.13), channel_id=1, source_target_pairs={{1,0},{2,1},{3,2},{0,3},{5,4},{6,5},{7,6},{4,7},{9,8},{10,9},{11,1... | collective-permute-start | bytes 245768 | tf_op jit(solution)/shard_map/ppermute | solution.py:76
  32.9 0.6 gather_fusion.1
  33.6 0.0 copy-start.7
  33.6 11.7 %multiply_reduce_fusion = f32[2,256]{1,0:T(2,128)S(1)} fusion(f32[11776]{0:T(1024)S(1)} %select_n.61, f32[2,11776]{1,0:T(2,128)S(1)} %stack_broadcast_in_dim.41, f32[256]{0:T(256)S(1)} %bitcast.128, f32[11776]{0:T(1024)S(1)} %stack_broadcast_in_dim.39, f32[256]{0:T(256)S(1)} %bitcast.129, f32[11776]{0:T(1024)S(1)} %stack_broadcast_in_dim.37, f32[256]{0:T(256)S(1)} %bitcast.127), kind=kLoop, calls=%fused_computation.14 | loop fusion | flops 66321920 | bytes 240640 | tf_op jit(solution)/shard_map/reduce_sum | solution.py:29
  45.3 0.3 fusion.31
  45.5 0.1 mul.507
  45.6 1.3 multiply_reduce_fusion.2
  47.1 0.1 copy.22
  47.3 2.3 %gather_fusion = f32[432,4,128]{2,1,0:T(4,128)S(1)} fusion(f32[4,96,128]{2,0,1:T(4,128)S(1)} %bitcast.87, s32[1024]{0:T(1024)S(1)} %pad_clamp_fusion.3), kind=kCustom, calls=%fused_computation.2 | custom fusion | bytes 1771200 | tf_op jit(solution)/shard_map/jit(_take)/gather | solution.py:251
  49.5 1.5 fusion.24
  51.1 0.1 select_maximum_fusion
  51.2 0.1 reshape.846
  51.3 6.0 %gather_fusion.3 = f32[2528,256]{1,0:T(8,128)S(1)} fusion(f32[640,256]{1,0:T(8,128)S(1)} %reshape.846, s32[3072]{0:T(1024)S(1)} %pad_clamp_fusion), kind=kCustom, calls=%fused_computation.1.clone | custom fusion | bytes 5187456 | tf_op jit(solution)/shard_map/jit(_take)/gather | solution.py:227
  57.3 0.0 copy-start.3
  57.3 7.0 %gather_fusion.2 = f32[2528,256]{1,0:T(8,128)} fusion(f32[640,256]{1,0:T(8,128)S(1)} %reshape.846, s32[3072]{0:T(1024)S(1)} %pad_clamp_fusion.1), kind=kCustom, calls=%fused_computation.clone | custom fusion | bytes 5187456 | tf_op jit(solution)/shard_map/jit(_take)/gather | solution.py:226
  64.3 1.7 %copy-done.1 = f32[2528,256]{1,0:T(8,128)S(1)} copy-done((f32[2528,256]{1,0:T(8,128)S(1)}, f32[2528,256]{1,0:T(8,128)}, u32[]{:S(2)}) %copy-start.1) | copy-done | bytes 2588696
  66.1 1.1 copy-done.2
  67.2 76.0 %shard_map.145 = f32[16,256]{1,0:T(8,128)S(1)} custom-call(f32[474]{0:T(512)S(1)} %copy-done.3, f32[3,256,256]{2,1,0:T(8,128)S(1)} %copy-done.2, f32[158,16,256]{2,1,0:T(8,128)S(1)} %bitcast.86, f32[158,16,256]{2,1,0:T(8,128)S(1)} %bitcast.85), custom_call_target="tpu_custom_call" | custom-call | flops 766246912 | bytes 5980160 | tf_op jit(solution)/shard_map/pallas_call | solution.py:124
  143.2 1.3 fusion.12
  144.5 2.0 %multiply_reduce_fusion.3 = f32[2,2,4,128]{3,2,1,0:T(4,128)S(1)} fusion(f32[2,2,4,256]{3,2,1,0:T(4,128)S(1)} %fusion.12, f32[256]{0:T(256)} %bitcast.124, f32[2,2,4,128]{3,2,1,0:T(4,128)} %copy-done.12, f32[256]{0:T(256)S(1)} %bitcast.122, f32[2,2,4,128]{3,2,1,0:T(4,128)} %copy-done.13, f32[256]{0:T(256)} %bitcast.126, f32[2,2,4,128]{3,2,1,0:T(4,128)S(1)} %get-tuple-element.23), kind=kLoop, calls=%fused_computation.18 | loop fusion | flops 5765120 | bytes 52224 | tf_op jit(solution)/shard_map/reduce_sum | solution.py:29
  146.6 23.4 %fusion.5 = f32[2,2,4,128]{3,2,1,0:T(4,128)S(1)} fusion(f32[27]{0:T(128)} %constant.177, f32[27]{0:T(128)} %constant.176, f32[27]{0:T(128)} %constant.175, f32[27,2,2,4,128]{4,3,2,1,0:T(4,128)} %bitcast.92, f32[27,2,2,4,128]{4,3,2,1,0:T(4,128)} %bitcast.93, f32[2,2,4,128]{3,2,1,0:T(4,128)} %copy-done.12, f32[27,2,2,4,128]{4,3,2,1,0:T(4,128)} %bitcast.91, ...), kind=kLoop, calls=%fused_computation.10 | loop fusion | flops 106166272 | bytes 1360196 | tf_op jit(solution)/shard_map/reduce_sum | solution.py:263
  170.0 0.7 add_select_fusion
  (102 shorter events, 1.1 us)
Async XLA Ops:
  0.0 3.5 %copy-start = (f32[256,256]{1,0:T(8,128)S(1)}, f32[256,256]{1,0:T(8,128)}, u32[]{:S(2)}) copy-start(f32[256,256]{1,0:T(8,128)} %param.20) | copy-start | bytes 786436
  2.4 6.9 %copy-start.12 = (f32[2,2,4,128]{3,2,1,0:T(4,128)}, f32[2,2,4,128]{3,2,1,0:T(4,128)S(1)}, u32[]{:S(2)}) copy-start(f32[2,2,4,128]{3,2,1,0:T(4,128)S(1)} %get-tuple-element.24) | copy-start | bytes 24580
  2.4 7.3 %copy-start.13 = (f32[2,2,4,128]{3,2,1,0:T(4,128)}, f32[2,2,4,128]{3,2,1,0:T(4,128)S(1)}, u32[]{:S(2)}) copy-start(f32[2,2,4,128]{3,2,1,0:T(4,128)S(1)} %get-tuple-element.25) | copy-start | bytes 24580
  2.4 7.3 %copy-start.15 = (f32[1,256]{1,0:T(1,128)}, f32[1,256]{1,0:T(1,128)S(1)}, u32[]{:S(2)}) copy-start(f32[1,256]{1,0:T(1,128)S(1)} %get-tuple-element.42) | copy-start | bytes 3076
  2.4 7.3 %copy-start.17 = (f32[1,256]{1,0:T(1,128)}, f32[1,256]{1,0:T(1,128)S(1)}, u32[]{:S(2)}) copy-start(f32[1,256]{1,0:T(1,128)S(1)} %get-tuple-element.43) | copy-start | bytes 3076
  2.5 7.3 %copy-start.18 = (f32[1,256]{1,0:T(1,128)}, f32[1,256]{1,0:T(1,128)S(1)}, u32[]{:S(2)}) copy-start(f32[1,256]{1,0:T(1,128)S(1)} %get-tuple-element.44) | copy-start | bytes 3076
  4.7 24.2 %collective-permute-start = (f32[8192]{0:T(1024)S(1)}, f32[8192]{0:T(1024)S(1)}, u32[]{:S(2)}, u32[]{:S(2)}) collective-permute-start(f32[8192]{0:T(1024)S(1)} %get-tuple-element.26), channel_id=1, source_target_pairs={{0,4},{4,8},{8,12},{12,16},{16,20},{20,24},{24,28},{28,0},{1,5},{5... | collective-permute-start | bytes 98312 | tf_op jit(solution)/shard_map/ppermute | solution.py:75
  5.2 23.7 %collective-permute-start.1 = (f32[8192]{0:T(1024)S(1)}, f32[8192]{0:T(1024)S(1)}, u32[]{:S(2)}, u32[]{:S(2)}) collective-permute-start(f32[8192]{0:T(1024)S(1)} %get-tuple-element.27), channel_id=1, source_target_pairs={{4,0},{8,4},{12,8},{16,12},{20,16},{24,20},{28,24},{0,28},{5,1},{9... | collective-permute-start | bytes 98312 | tf_op jit(solution)/shard_map/ppermute | solution.py:76
  8.4 1.3 copy-start.6
  8.4 6.5 %copy-start.4 = (f32[3,2,2,4,128]{4,3,2,1,0:T(4,128)S(1)}, f32[3,2,2,4,128]{4,3,2,1,0:T(4,128)}, u32[]{:S(2)}) copy-start(f32[3,2,2,4,128]{4,3,2,1,0:T(4,128)} %param.17) | copy-start | bytes 73732
  8.4 6.7 %copy-start.20 = (f32[23]{0:T(128)S(1)}, f32[23]{0:T(128)}, u32[]{:S(2)}) copy-start(f32[23]{0:T(128)} %constant.149) | copy-start | bytes 280
  8.5 6.8 %copy-start.21 = (f32[23]{0:T(128)S(1)}, f32[23]{0:T(128)}, u32[]{:S(2)}) copy-start(f32[23]{0:T(128)} %constant.148) | copy-start | bytes 280
  9.7 7.7 %copy-start.11 = (s32[2528]{0:T(1024)S(1)}, s32[2528]{0:T(1024)}, u32[]{:S(2)}) copy-start(s32[2528]{0:T(1024)} %constant.182) | copy-start | bytes 30340
  9.8 7.8 %copy-start.10 = (s32[2528]{0:T(1024)S(1)}, s32[2528]{0:T(1024)}, u32[]{:S(2)}) copy-start(s32[2528]{0:T(1024)} %constant.183) | copy-start | bytes 30340
  9.8 12.3 %copy-start.14 = (s32[432]{0:T(512)S(1)}, s32[432]{0:T(512)}, u32[]{:S(2)}) copy-start(s32[432]{0:T(512)} %constant.178) | copy-start | bytes 5188
  9.8 15.2 %copy-start.19 = (s32[23]{0:T(128)S(1)}, s32[23]{0:T(128)}, u32[]{:S(2)}) copy-start(s32[23]{0:T(128)} %constant.179) | copy-start | bytes 280
  10.1 7.4 %collective-permute-start.4 = (f32[1,1,2,256]{3,2,1,0:T(2,128)S(1)}, f32[1,1,2,256]{3,2,1,0:T(2,128)S(1)}, u32[]{:S(2)}, u32[]{:S(2)}) collective-permute-start(f32[1,1,2,256]{3,2,1,0:T(2,128)S(1)} %convolution_bitcast_fusion), channel_id=1, source_target_pairs={{0,3},{1,0},{2,1},{3,2},{4,7},{5,4},{6,5},{7,6},{8,11},{9,8},{10,9... | collective-permute-start | bytes 6152 | tf_op jit(solution)/shard_map/ppermute | solution.py:61
  17.5 4.6 %collective-permute-start.5 = (f32[1,2,2,256]{3,2,1,0:T(2,128)S(1)}, f32[1,2,2,256]{3,2,1,0:T(2,128)S(1)}, u32[]{:S(2)}, u32[]{:S(2)}) collective-permute-start(f32[1,2,2,256]{3,2,1,0:T(2,128)S(1)} %pad_maximum_fusion.14), channel_id=1, source_target_pairs={{0,2},{1,3},{2,0},{3,1},{4,6},{5,7},{6,4},{7,5},{8,10},{9,11},{10,... | collective-permute-start | bytes 12296 | tf_op jit(solution)/shard_map/ppermute | solution.py:61
  22.0 1.4 collective-permute-start.6
  23.4 3.8 %collective-permute-start.7 = (f32[2,4,2,256]{3,2,1,0:T(2,128)S(1)}, f32[2,4,2,256]{3,2,1,0:T(2,128)S(1)}, u32[]{:S(2)}, u32[]{:S(2)}) collective-permute-start(f32[2,4,2,256]{3,2,1,0:T(2,128)S(1)} %pad_maximum_fusion.11), channel_id=1, source_target_pairs={{0,24},{4,28},{8,0},{12,4},{16,8},{20,12},{24,16},{28,20},{1,25},{... | collective-permute-start | bytes 49160 | tf_op jit(solution)/shard_map/ppermute | solution.py:61
  27.2 5.7 %collective-permute-start.8 = (f32[4,4,2,256]{3,2,1,0:T(2,128)S(1)}, f32[4,4,2,256]{3,2,1,0:T(2,128)S(1)}, u32[]{:S(2)}, u32[]{:S(2)}) collective-permute-start(f32[4,4,2,256]{3,2,1,0:T(2,128)S(1)} %pad_maximum_fusion.9), channel_id=1, source_target_pairs={{0,16},{4,20},{8,24},{12,28},{16,0},{20,4},{24,8},{28,12},{1,17},{... | collective-permute-start | bytes 98312 | tf_op jit(solution)/shard_map/ppermute | solution.py:61
  29.0 17.9 %collective-permute-start.2 = (f32[20480]{0:T(1024)S(1)}, f32[20480]{0:T(1024)S(1)}, u32[]{:S(2)}, u32[]{:S(2)}) collective-permute-start(f32[20480]{0:T(1024)S(1)} %get-tuple-element.12), channel_id=1, source_target_pairs={{0,1},{1,2},{2,3},{3,0},{4,5},{5,6},{6,7},{7,4},{8,9},{9,10},{10,1... | collective-permute-start | bytes 245768 | tf_op jit(solution)/shard_map/ppermute | solution.py:75
  29.1 17.9 %collective-permute-start.3 = (f32[20480]{0:T(1024)S(1)}, f32[20480]{0:T(1024)S(1)}, u32[]{:S(2)}, u32[]{:S(2)}) collective-permute-start(f32[20480]{0:T(1024)S(1)} %get-tuple-element.13), channel_id=1, source_target_pairs={{1,0},{2,1},{3,2},{0,3},{5,4},{6,5},{7,6},{4,7},{9,8},{10,9},{11,1... | collective-permute-start | bytes 245768 | tf_op jit(solution)/shard_map/ppermute | solution.py:76
  33.6 11.7 %copy-start.7 = (f32[256,256]{1,0:T(8,128)S(1)}, f32[256,256]{1,0:T(8,128)}, u32[]{:S(2)}) copy-start(f32[256,256]{1,0:T(8,128)} %param.23) | copy-start | bytes 786436
  57.3 7.0 %copy-start.3 = (f32[474]{0:T(512)S(1)}, f32[474]{0:T(512)}, u32[]{:S(2)}) copy-start(f32[474]{0:T(512)} %constant.125.clone.table_ref) | copy-start | bytes 5692
  64.3 1.7 %copy-start.1 = (f32[2528,256]{1,0:T(8,128)S(1)}, f32[2528,256]{1,0:T(8,128)}, u32[]{:S(2)}) copy-start(f32[2528,256]{1,0:T(8,128)} %gather_fusion.2) | copy-start | bytes 7766020
  66.1 1.1 copy-start.2
  67.2 77.3 %copy-start.16 = (f32[1,256]{1,0:T(1,128)S(1)}, f32[1,256]{1,0:T(1,128)}, u32[]{:S(2)}) copy-start(f32[1,256]{1,0:T(1,128)} %copy-done.15) | copy-start | bytes 3076
  67.2 79.4 %copy-start.5 = (pred[27,128,128]{2,1,0:T(8,128)(4,1)S(1)}, pred[27,128,128]{2,1,0:T(8,128)(4,1)}, u32[]{:S(2)}) copy-start(pred[27,128,128]{2,1,0:T(8,128)(4,1)} %broadcast_and_fusion) | copy-start | bytes 1327108
  67.2 79.4 %copy-start.8 = (f32[1,27,16,128]{3,0,2,1:T(1,128)S(1)}, f32[1,27,16,128]{3,0,2,1:T(1,128)}, u32[]{:S(2)}) copy-start(f32[1,27,16,128]{3,0,2,1:T(1,128)} %get-tuple-element.6) | copy-start | bytes 663556
  146.6 23.4 %copy-start.9 = (s32[2,2,4]{2,1,0:T(2,128)S(1)}, s32[2,2,4]{2,1,0:T(2,128)}, u32[]{:S(2)}) copy-start(s32[2,2,4]{2,1,0:T(2,128)} %param.19) | copy-start | bytes 196

commit v3 on v2

--- a/solution.py
+++ b/solution.py
@@ -84,15 +84,15 @@
     return out
 
 
-def m2l_kernel(shift_count, rows, table_ref, base_ref, plus_ref, minus_ref, out_ref):
+def m2l_kernel(shift_count, rows, table_ref, base_ref, sources_ref, out_ref):
     out_ref[...] = jnp.zeros_like(out_ref)
 
     def body(index, carry):
         shift_x = table_ref[3 * index]
         shift_y = table_ref[3 * index + 1]
         shift_z = table_ref[3 * index + 2]
-        fwd = plus_ref[index]
-        back = minus_ref[index]
+        fwd = sources_ref[0, index]
+        back = sources_ref[1, index]
         for row in range(0, base_ref.shape[1], rows):
             delta_x = base_ref[0, row : row + rows, :] - shift_x
             delta_y = base_ref[1, row : row + rows, :] - shift_y
@@ -119,14 +119,13 @@
     lax.fori_loop(0, shift_count, body, 0)
 
 
-def m2l(table, base, plus, minus):
-    shift_count, vectors, points = plus.shape
+def m2l(table, base, sources):
+    shift_count, vectors, points = sources.shape[1:]
     return pl.pallas_call(
         functools.partial(m2l_kernel, shift_count, 128),
         out_shape=jax.ShapeDtypeStruct((vectors, points), jnp.float32),
         in_specs=[
             pl.BlockSpec(memory_space=pltpu.SMEM),
-            pl.BlockSpec(memory_space=pltpu.VMEM),
             pl.BlockSpec(memory_space=pltpu.VMEM),
             pl.BlockSpec(memory_space=pltpu.VMEM),
         ],
@@ -135,9 +134,9 @@
         cost_estimate=pl.CostEstimate(
             flops=4 * shift_count * vectors * points * points + 10 * shift_count * points * points,
             transcendentals=shift_count * points * points,
-            bytes_accessed=4 * (2 * plus.size + base.size + vectors * points),
+            bytes_accessed=4 * (sources.size + base.size + vectors * points),
         ),
-    )(table, base, plus, minus)
+    )(table, base, sources)
 
 
 def far_shifts(span):
@@ -206,30 +205,31 @@
 
     framed = jnp.pad(cycle, ((1, 1), (1, 1), (3, 3), (0, 0)))
     shifts = far_shifts(3)
-    targets = [(ix, iy, k) for ix in range(2) for iy in range(2) for k in range(layers)]
-
-    def rows_for(sign):
-        return np.array(
+    depth_windows = jnp.stack(
+        [framed[:, :, depth : depth + layers] for depth in range(7)], axis=2
+    ).reshape(-1, layers * points)
+    window_rows = np.array(
+        [
             [
                 [
                     np.ravel_multi_index(
-                        (ix + sign * dx + 3, iy + sign * dy + 3, k + sign * dz + 3), framed.shape[:3]
+                        (ix + sign * dx + 3, iy + sign * dy + 3, sign * dz + 3), framed.shape[:2] + (7,)
                     )
-                    for ix, iy, k in targets
+                    for ix in range(2)
+                    for iy in range(2)
                 ]
                 for dx, dy, dz in shifts
-            ],
-            np.int32,
-        )
-
-    framed_rows = framed.reshape(-1, points)
-    plus = jnp.take(framed_rows, rows_for(1), axis=0)
-    minus = jnp.take(framed_rows, rows_for(-1), axis=0)
+            ]
+            for sign in (1, -1)
+        ],
+        np.int32,
+    )
+    sources = jnp.take(depth_windows, window_rows, axis=0).reshape(2, len(shifts), 4 * layers, points)
     base = jnp.stack(
         [0.9 * (unit_sphere[i][:, None] - unit_sphere[i][None, :]) for i in range(3)]
     )
     table = jnp.asarray(np.array(shifts, np.float32).reshape(-1))
-    leaf_down_check = m2l(table, base, plus, minus).reshape(2, 2, layers, points)
+    leaf_down_check = m2l(table, base, sources).reshape(2, 2, layers, points)
     parent_local = jnp.einsum("ec,mc->me", c2e_top_down, far_check, precision=highest)
     leaf_local = jnp.einsum("ec,xyzc->xyze", c2e_leaf_down, leaf_down_check, precision=highest)
 

time: 171 us -> 167 us (0.977)
  other arithmetic: 47.2 us -> 44.2 us
    unnamed x50 -> x47, local copies, waits for them, and re-layouts: 3.12 us -> 4.14 us
  transfers between devices with their start and end apart: 9 -> 9, of which waited for: 3 -> 3; matrix products, arithmetic and copies ran while one was open for 11% -> 10% of each run, Pallas kernels for 0% -> 0%
where the time goes in v3:
time: 167 us
  Pallas kernels  75.1 us (45%)
  other arithmetic  44.2 us (26%)
  local copies, waits for them, and re-layouts  22.4 us (13%)
  starting transfers between devices  16.4 us (10%)
  waiting for transfers between devices  6.6 us (4%)
    pallas_call x1, Pallas kernels, m2l(): pl.pallas_call(functools.partial(m2l_kernel, shift_count, 128), out_shape...  75.1 us
    reduce_sum x1, other arithmetic, shards(): near = jnp.sum(jnp.sum(kernel * source[3][..., None, :], axis=-1), axis=0)  22.8 us
    reduce_sum x5, other arithmetic, point_sum(): return jnp.sum(kernel * weights[..., None, :], axis=-1)  15.8 us
    gather x2, local copies, waits for them, and re-layouts, shards(): jnp.take(depth_windows, window_rows, axis=0)  12.3 us
    ppermute x5, starting transfers between devices, rel_gather(): lax.ppermute(part, axis, [(j, (j - have) % count) for j in range(count)])  8.73 us
    ppermute x5, waiting for transfers between devices, rel_gather(): lax.ppermute(part, axis, [(j, (j - have) % count) for j in range(count)])  6.59 us
    ppermute x2, starting transfers between devices, exchange(): lax.ppermute(sent_head, axis, [((i + 1) % count, i) for i in range(count)])  5.55 us
    unnamed x47, local copies, waits for them, and re-layouts  4.14 us
  transfers between devices with their start and end apart: 9, of which 3 were waited for; matrix products, arithmetic and copies ran while one was open for 10% of the time, Pallas kernels for 0%

profile of v3, /device:TPU:0, one launch (start us, length us, event | category | flops | bytes accessed | tf_op | source)
XLA Modules:
  0.0 166.7 jit_solution(11674499280089346017)
XLA Ops:
  0.0 0.1 cosine_multiply_fusion.1
  0.1 0.1 sine_multiply_fusion.1
  0.1 0.8 fusion.24
  0.9 0.8 fusion.45
  1.7 0.7 slice_bitcast_fusion.9
  2.4 1.1 multiply_reduce_fusion.4
  3.5 0.3 fusion.21
  3.9 0.7 fusion.23
  4.6 0.5 collective-permute-start
  5.1 2.9 %collective-permute-start.1 = (f32[8192]{0:T(1024)S(1)}, f32[8192]{0:T(1024)S(1)}, u32[]{:S(2)}, u32[]{:S(2)}) collective-permute-start(f32[8192]{0:T(1024)S(1)} %get-tuple-element.26), channel_id=1, source_target_pairs={{4,0},{8,4},{12,8},{16,12},{20,16},{24,20},{28,24},{0,28},{5,1},{9... | collective-permute-start | bytes 98312 | tf_op jit(solution)/shard_map/ppermute | solution.py:76
  8.3 0.1 broadcast_add_fusion.8
  8.4 0.8 add_rsqrt_fusion
  9.2 0.0 copy-start.13
  9.2 0.4 multiply_reduce_fusion.1
  9.7 0.0 copy-start.9
  9.7 0.3 convolution_bitcast_fusion
  10.0 4.4 %collective-permute-start.4 = (f32[1,1,2,256]{3,2,1,0:T(2,128)S(1)}, f32[1,1,2,256]{3,2,1,0:T(2,128)S(1)}, u32[]{:S(2)}, u32[]{:S(2)}) collective-permute-start(f32[1,1,2,256]{3,2,1,0:T(2,128)S(1)} %convolution_bitcast_fusion), channel_id=1, source_target_pairs={{0,3},{1,0},{2,1},{3,2},{4,7},{5,4},{6,5},{7,6},{8,11},{9,8},{10,9... | collective-permute-start | bytes 6152 | tf_op jit(solution)/shard_map/ppermute | solution.py:61
  14.5 0.1 fusion.28
  14.5 0.1 fusion.30
  14.7 0.1 subtract_multiply_fusion.2
  14.9 0.1 subtract_multiply_fusion.3
  14.9 0.1 broadcast_add_fusion.4
  15.0 0.1 subtract_multiply_fusion
  15.1 0.3 broadcast_and_fusion
  15.4 0.1 broadcast_add_fusion.5
  15.5 0.1 broadcast_add_fusion.1
  15.6 0.1 broadcast_add_fusion
  15.6 0.1 pad_maximum_fusion.base_ref
  15.7 1.2 collective-permute-start.5
  16.9 3.4 %collective-permute-done.5 = f32[1,2,2,256]{3,2,1,0:T(2,128)S(1)} collective-permute-done((f32[1,2,2,256]{3,2,1,0:T(2,128)S(1)}, f32[1,2,2,256]{3,2,1,0:T(2,128)S(1)}, u32[]{:S(2)}, u32[]{:S(2)}) %collective-permute-start.5) | collective-permute-done | bytes 4128 | tf_op jit(solution)/shard_map/ppermute | solution.py:61
  20.3 1.3 collective-permute-done.6
  21.7 1.6 collective-permute-start.7
  23.3 0.1 stack_broadcast_in_dim.41
  23.6 1.9 %collective-permute-done.7 = f32[2,4,2,256]{3,2,1,0:T(2,128)S(1)} collective-permute-done((f32[2,4,2,256]{3,2,1,0:T(2,128)S(1)}, f32[2,4,2,256]{3,2,1,0:T(2,128)S(1)}, u32[]{:S(2)}, u32[]{:S(2)}) %collective-permute-start.7) | collective-permute-done | bytes 16416 | tf_op jit(solution)/shard_map/ppermute | solution.py:61
  25.5 1.6 collective-permute-start.8
  27.3 1.6 collective-permute-start.2
  28.9 2.6 %collective-permute-start.3 = (f32[20480]{0:T(1024)S(1)}, f32[20480]{0:T(1024)S(1)}, u32[]{:S(2)}, u32[]{:S(2)}) collective-permute-start(f32[20480]{0:T(1024)S(1)} %get-tuple-element.12), channel_id=1, source_target_pairs={{1,0},{2,1},{3,2},{0,3},{5,4},{6,5},{7,6},{4,7},{9,8},{10,9},{11,1... | collective-permute-start | bytes 245768 | tf_op jit(solution)/shard_map/ppermute | solution.py:76
  31.5 0.6 gather_fusion.2
  32.2 11.6 %multiply_reduce_fusion = f32[2,256]{1,0:T(2,128)S(1)} fusion(f32[11776]{0:T(1024)S(1)} %select_n.66, f32[2,11776]{1,0:T(2,128)S(1)} %stack_broadcast_in_dim.41, f32[256]{0:T(256)S(1)} %bitcast.157, f32[11776]{0:T(1024)S(1)} %stack_broadcast_in_dim.39, f32[256]{0:T(256)S(1)} %bitcast.158, f32[11776]{0:T(1024)S(1)} %stack_broadcast_in_dim.37, f32[256]{0:T(256)S(1)} %bitcast.156), kind=kLoop, calls=%fused_computation.13 | loop fusion | flops 66321920 | bytes 240640 | tf_op jit(solution)/shard_map/reduce_sum | solution.py:29
  43.9 0.3 fusion.38
  44.1 0.1 mul.507
  44.2 1.3 multiply_reduce_fusion.2
  45.7 0.6 copy-done.7
  46.2 0.1 select_maximum_fusion
  46.4 0.1 fusion.17
  46.5 0.1 fusion.16
  46.6 0.1 fusion.15
  46.7 0.1 fusion.14
  46.8 0.1 fusion.13
  46.9 0.1 fusion.12
  47.0 0.3 copy.19
  47.3 0.4 copy.26
  47.7 5.2 %gather_fusion.1 = f32[1264,1024]{1,0:T(8,128)} fusion(f32[448,1024]{1,0:T(8,128)S(1)} %bitcast.114, s32[2048]{0:T(1024)S(1)} %pad_clamp_fusion), kind=kCustom, calls=%fused_computation.1 | custom fusion | bytes 10359744 | tf_op jit(solution)/shard_map/jit(_take)/gather | solution.py:227
  52.9 7.1 %gather.16.sources_ref = f32[2,158,16,256]{3,2,1,0:T(8,128)} reshape(f32[1264,1024]{1,0:T(8,128)} %gather_fusion.1) | data formatting | bytes 10354688 | tf_op jit(solution)/shard_map/jit(_take)/gather | solution.py:227
  60.0 2.5 %copy-done.1 = f32[2,158,16,256]{3,2,1,0:T(8,128)S(1)} copy-done((f32[2,158,16,256]{3,2,1,0:T(8,128)S(1)}, f32[2,158,16,256]{3,2,1,0:T(8,128)}, u32[]{:S(2)}) %copy-start.1) | copy-done | bytes 5177368
  62.5 75.1 %shard_map.136 = f32[16,256]{1,0:T(8,128)S(1)} custom-call(f32[474]{0:T(512)S(1)} %copy-done.2, f32[3,256,256]{2,1,0:T(8,128)S(1)} %pad_maximum_fusion.base_ref, f32[2,158,16,256]{3,2,1,0:T(8,128)S(1)} %copy-done.1), custom_call_target="tpu_custom_call" | custom-call | flops 766246912 | bytes 5980160 | tf_op jit(solution)/shard_map/pallas_call | solution.py:124
  137.6 0.3 fusion.19
  138.0 1.3 multiply_reduce_fusion.3
  139.3 0.8 slice.304
  140.2 0.1 copy.23
  140.3 2.3 %gather_fusion = f32[432,4,128]{2,1,0:T(4,128)S(1)} fusion(f32[4,96,128]{2,0,1:T(4,128)S(1)} %bitcast.116, s32[1024]{0:T(1024)S(1)} %pad_clamp_fusion.2), kind=kCustom, calls=%fused_computation | custom fusion | bytes 1771200 | tf_op jit(solution)/shard_map/jit(_take)/gather | solution.py:251
  142.6 0.6 fusion.31
  143.3 22.8 %fusion.5 = f32[2,2,4,128]{3,2,1,0:T(4,128)S(1)} fusion(f32[27]{0:T(128)S(1)} %copy-done.16, f32[27]{0:T(128)S(1)} %copy-done.15, f32[27]{0:T(128)S(1)} %copy-done.14, f32[27,2,2,4,128]{4,3,2,1,0:T(4,128)S(1)} %bitcast.121, f32[27,2,2,4,128]{4,3,2,1,0:T(4,128)S(1)} %bitcast.122, f32[2,2,4,128]{3,2,1,0:T(4,128)S(1)} %get-tuple-element.23, ...), kind=kLoop, calls=%fused_computation.9 | loop fusion | flops 106166272 | bytes 1360196 | tf_op jit(solution)/shard_map/reduce_sum | solution.py:263
  166.1 0.7 add_select_fusion
  (99 shorter events, 1.1 us)
Async XLA Ops:
  0.0 3.5 %copy-start = (f32[256,256]{1,0:T(8,128)S(1)}, f32[256,256]{1,0:T(8,128)}, u32[]{:S(2)}) copy-start(f32[256,256]{1,0:T(8,128)} %param.17) | copy-start | bytes 786436
  4.6 22.5 %collective-permute-start = (f32[8192]{0:T(1024)S(1)}, f32[8192]{0:T(1024)S(1)}, u32[]{:S(2)}, u32[]{:S(2)}) collective-permute-start(f32[8192]{0:T(1024)S(1)} %get-tuple-element.25), channel_id=1, source_target_pairs={{0,4},{4,8},{8,12},{12,16},{16,20},{20,24},{24,28},{28,0},{1,5},{5... | collective-permute-start | bytes 98312 | tf_op jit(solution)/shard_map/ppermute | solution.py:75
  5.1 22.0 %collective-permute-start.1 = (f32[8192]{0:T(1024)S(1)}, f32[8192]{0:T(1024)S(1)}, u32[]{:S(2)}, u32[]{:S(2)}) collective-permute-start(f32[8192]{0:T(1024)S(1)} %get-tuple-element.26), channel_id=1, source_target_pairs={{4,0},{8,4},{12,8},{16,12},{20,16},{24,20},{28,24},{0,28},{5,1},{9... | collective-permute-start | bytes 98312 | tf_op jit(solution)/shard_map/ppermute | solution.py:76
  8.4 1.3 copy-start.5
  8.4 6.5 %copy-start.3 = (f32[3,2,2,4,128]{4,3,2,1,0:T(4,128)S(1)}, f32[3,2,2,4,128]{4,3,2,1,0:T(4,128)}, u32[]{:S(2)}) copy-start(f32[3,2,2,4,128]{4,3,2,1,0:T(4,128)} %param.14) | copy-start | bytes 73732
  9.2 6.3 %copy-start.12 = (f32[23]{0:T(128)S(1)}, f32[23]{0:T(128)}, u32[]{:S(2)}) copy-start(f32[23]{0:T(128)} %constant.156) | copy-start | bytes 280
  9.2 6.3 %copy-start.13 = (f32[23]{0:T(128)S(1)}, f32[23]{0:T(128)}, u32[]{:S(2)}) copy-start(f32[23]{0:T(128)} %constant.157) | copy-start | bytes 280
  9.7 7.2 %copy-start.9 = (s32[1264]{0:T(1024)S(1)}, s32[1264]{0:T(1024)}, u32[]{:S(2)}) copy-start(s32[1264]{0:T(1024)} %constant.172) | copy-start | bytes 15172
  9.7 10.6 %copy-start.10 = (s32[432]{0:T(512)S(1)}, s32[432]{0:T(512)}, u32[]{:S(2)}) copy-start(s32[432]{0:T(512)} %constant.171) | copy-start | bytes 5188
  9.7 13.6 %copy-start.11 = (s32[23]{0:T(128)S(1)}, s32[23]{0:T(128)}, u32[]{:S(2)}) copy-start(s32[23]{0:T(128)} %constant.173) | copy-start | bytes 280
  10.0 5.7 %collective-permute-start.4 = (f32[1,1,2,256]{3,2,1,0:T(2,128)S(1)}, f32[1,1,2,256]{3,2,1,0:T(2,128)S(1)}, u32[]{:S(2)}, u32[]{:S(2)}) collective-permute-start(f32[1,1,2,256]{3,2,1,0:T(2,128)S(1)} %convolution_bitcast_fusion), channel_id=1, source_target_pairs={{0,3},{1,0},{2,1},{3,2},{4,7},{5,4},{6,5},{7,6},{8,11},{9,8},{10,9... | collective-permute-start | bytes 6152 | tf_op jit(solution)/shard_map/ppermute | solution.py:61
  15.7 4.6 %collective-permute-start.5 = (f32[1,2,2,256]{3,2,1,0:T(2,128)S(1)}, f32[1,2,2,256]{3,2,1,0:T(2,128)S(1)}, u32[]{:S(2)}, u32[]{:S(2)}) collective-permute-start(f32[1,2,2,256]{3,2,1,0:T(2,128)S(1)} %pad_maximum_fusion.14), channel_id=1, source_target_pairs={{0,2},{1,3},{2,0},{3,1},{4,6},{5,7},{6,4},{7,5},{8,10},{9,11},{10,... | collective-permute-start | bytes 12296 | tf_op jit(solution)/shard_map/ppermute | solution.py:61
  20.3 1.4 collective-permute-start.6
  21.7 3.8 %collective-permute-start.7 = (f32[2,4,2,256]{3,2,1,0:T(2,128)S(1)}, f32[2,4,2,256]{3,2,1,0:T(2,128)S(1)}, u32[]{:S(2)}, u32[]{:S(2)}) collective-permute-start(f32[2,4,2,256]{3,2,1,0:T(2,128)S(1)} %pad_maximum_fusion.11), channel_id=1, source_target_pairs={{0,24},{4,28},{8,0},{12,4},{16,8},{20,12},{24,16},{28,20},{1,25},{... | collective-permute-start | bytes 49160 | tf_op jit(solution)/shard_map/ppermute | solution.py:61
  25.5 6.0 %collective-permute-start.8 = (f32[4,4,2,256]{3,2,1,0:T(2,128)S(1)}, f32[4,4,2,256]{3,2,1,0:T(2,128)S(1)}, u32[]{:S(2)}, u32[]{:S(2)}) collective-permute-start(f32[4,4,2,256]{3,2,1,0:T(2,128)S(1)} %pad_maximum_fusion.9), channel_id=1, source_target_pairs={{0,16},{4,20},{8,24},{12,28},{16,0},{20,4},{24,8},{28,12},{1,17},{... | collective-permute-start | bytes 98312 | tf_op jit(solution)/shard_map/ppermute | solution.py:61
  27.3 18.3 %collective-permute-start.2 = (f32[20480]{0:T(1024)S(1)}, f32[20480]{0:T(1024)S(1)}, u32[]{:S(2)}, u32[]{:S(2)}) collective-permute-start(f32[20480]{0:T(1024)S(1)} %get-tuple-element.11), channel_id=1, source_target_pairs={{0,1},{1,2},{2,3},{3,0},{4,5},{5,6},{6,7},{7,4},{8,9},{9,10},{10,1... | collective-permute-start | bytes 245768 | tf_op jit(solution)/shard_map/ppermute | solution.py:75
  28.9 16.7 %collective-permute-start.3 = (f32[20480]{0:T(1024)S(1)}, f32[20480]{0:T(1024)S(1)}, u32[]{:S(2)}, u32[]{:S(2)}) collective-permute-start(f32[20480]{0:T(1024)S(1)} %get-tuple-element.12), channel_id=1, source_target_pairs={{1,0},{2,1},{3,2},{0,3},{5,4},{6,5},{7,6},{4,7},{9,8},{10,9},{11,1... | collective-permute-start | bytes 245768 | tf_op jit(solution)/shard_map/ppermute | solution.py:76
  32.2 11.7 %copy-start.6 = (f32[256,256]{1,0:T(8,128)S(1)}, f32[256,256]{1,0:T(8,128)}, u32[]{:S(2)}) copy-start(f32[256,256]{1,0:T(8,128)} %param.20) | copy-start | bytes 786436
  45.6 0.6 copy-start.7
  52.9 7.1 %copy-start.2 = (f32[474]{0:T(512)S(1)}, f32[474]{0:T(512)}, u32[]{:S(2)}) copy-start(f32[474]{0:T(512)} %constant.126.clone.table_ref) | copy-start | bytes 5692
  60.0 2.5 %copy-start.1 = (f32[2,158,16,256]{3,2,1,0:T(8,128)S(1)}, f32[2,158,16,256]{3,2,1,0:T(8,128)}, u32[]{:S(2)}) copy-start(f32[2,158,16,256]{3,2,1,0:T(8,128)} %gather.16.sources_ref) | copy-start | bytes 15532036
  62.5 75.2 %copy-start.4 = (f32[256,256]{1,0:T(8,128)S(1)}, f32[256,256]{1,0:T(8,128)}, u32[]{:S(2)}) copy-start(f32[256,256]{1,0:T(8,128)} %param.18) | copy-start | bytes 786436
  140.1 3.1 %copy-start.14 = (f32[27]{0:T(128)S(1)}, f32[27]{0:T(128)}, u32[]{:S(2)}) copy-start(f32[27]{0:T(128)} %constant.168) | copy-start | bytes 328
  140.1 3.1 %copy-start.15 = (f32[27]{0:T(128)S(1)}, f32[27]{0:T(128)}, u32[]{:S(2)}) copy-start(f32[27]{0:T(128)} %constant.169) | copy-start | bytes 328
  140.1 3.1 %copy-start.16 = (f32[27]{0:T(128)S(1)}, f32[27]{0:T(128)}, u32[]{:S(2)}) copy-start(f32[27]{0:T(128)} %constant.170) | copy-start | bytes 328
  143.2 22.8 %copy-start.8 = (s32[2,2,4]{2,1,0:T(2,128)S(1)}, s32[2,2,4]{2,1,0:T(2,128)}, u32[]{:S(2)}) copy-start(s32[2,2,4]{2,1,0:T(2,128)} %param.16) | copy-start | bytes 196

commit v4 on v3

--- a/solution.py
+++ b/solution.py
@@ -84,8 +84,21 @@
     return out
 
 
+def split_top(values):
+    scaled = values * 65537.0
+    return scaled - (scaled - values)
+
+
 def m2l_kernel(shift_count, rows, table_ref, base_ref, sources_ref, out_ref):
     out_ref[...] = jnp.zeros_like(out_ref)
+    vectors = out_ref.shape[0]
+
+    def split_dot(left, matrix_high, matrix_low, dims):
+        both = lax.dot_general(left, matrix_high, dims, preferred_element_type=jnp.float32)
+        cross = lax.dot_general(
+            left[:vectors], matrix_low, dims, preferred_element_type=jnp.float32
+        )
+        return both[:vectors] + both[vectors:] + cross
 
     def body(index, carry):
         shift_x = table_ref[3 * index]
@@ -100,19 +113,14 @@
             matrix = lax.rsqrt(
                 delta_x * delta_x + delta_y * delta_y + delta_z * delta_z + softening_sq
             )
-            out_ref[:, row : row + rows] += lax.dot_general(
-                fwd,
-                matrix,
-                (((1,), (1,)), ((), ())),
-                precision=highest,
-                preferred_element_type=jnp.float32,
+            matrix_top = split_top(matrix)
+            matrix_high = matrix_top.astype(jnp.bfloat16)
+            matrix_low = (matrix - matrix_top).astype(jnp.bfloat16)
+            out_ref[:, row : row + rows] += split_dot(
+                fwd, matrix_high, matrix_low, (((1,), (1,)), ((), ()))
             )
-            out_ref[...] += lax.dot_general(
-                back[:, row : row + rows],
-                matrix,
-                (((1,), (0,)), ((), ())),
-                precision=highest,
-                preferred_element_type=jnp.float32,
+            out_ref[...] += split_dot(
+                back[:, row : row + rows], matrix_high, matrix_low, (((1,), (0,)), ((), ()))
             )
         return carry
 
@@ -120,6 +128,8 @@
 
 
 def m2l(table, base, sources):
+    top = split_top(sources)
+    split = jnp.concatenate([top, sources - top], axis=2).astype(jnp.bfloat16)
     shift_count, vectors, points = sources.shape[1:]
     return pl.pallas_call(
         functools.partial(m2l_kernel, shift_count, 128),
@@ -132,11 +142,11 @@
         out_specs=pl.BlockSpec(memory_space=pltpu.VMEM),
         compiler_params=pltpu.CompilerParams(vmem_limit_bytes=48 * 1024 * 1024),
         cost_estimate=pl.CostEstimate(
-            flops=4 * shift_count * vectors * points * points + 10 * shift_count * points * points,
+            flops=12 * shift_count * vectors * points * points + 14 * shift_count * points * points,
             transcendentals=shift_count * points * points,
             bytes_accessed=4 * (sources.size + base.size + vectors * points),
         ),
-    )(table, base, sources)
+    )(table, base, split)
 
 
 def far_shifts(span):

time: 167 us -> 141 us (0.84)
  Pallas kernels: 75.1 us -> 46.7 us
  other arithmetic: 44.2 us -> 48.5 us
  local copies, waits for them, and re-layouts: 22.4 us -> 20 us
    pallas_call x1, Pallas kernels: 75.1 us -> 46.7 us  [m2l(): pl.pallas_call(functools.partial(m2l_kernel, shift_count, 128), out_shape...]
    another operation x0 -> x1, other arithmetic: none -> 3.38 us
    unnamed x47 -> x45, local copies, waits for them, and re-layouts: 4.14 us -> 1.67 us
  transfers between devices with their start and end apart: 9 -> 9, of which waited for: 3 -> 3; matrix products, arithmetic and copies ran while one was open for 10% -> 12% of each run, Pallas kernels for 0% -> 0%
where the time goes in v4:
time: 141 us; the launch traced here: 140 us
  other arithmetic  48.5 us (34%)
  Pallas kernels  46.7 us (33%)
  local copies, waits for them, and re-layouts  20 us (14%)
  starting transfers between devices  16.4 us (12%)
  waiting for transfers between devices  6.6 us (5%)
    pallas_call x1, Pallas kernels, m2l(): pl.pallas_call(functools.partial(m2l_kernel, shift_count, 128), out_shape...  46.7 us
    reduce_sum x1, other arithmetic, shards(): near = jnp.sum(jnp.sum(kernel * source[3][..., None, :], axis=-1), axis=0)  23 us
    reduce_sum x5, other arithmetic, point_sum(): return jnp.sum(kernel * weights[..., None, :], axis=-1)  15.8 us
    gather x2, local copies, waits for them, and re-layouts, shards(): jnp.take(depth_windows, window_rows, axis=0)  12.2 us
    ppermute x5, starting transfers between devices, rel_gather(): lax.ppermute(part, axis, [(j, (j - have) % count) for j in range(count)])  8.73 us
    ppermute x5, waiting for transfers between devices, rel_gather(): lax.ppermute(part, axis, [(j, (j - have) % count) for j in range(count)])  6.59 us
    ppermute x2, starting transfers between devices, exchange(): lax.ppermute(sent_head, axis, [((i + 1) % count, i) for i in range(count)])  5.55 us
    another operation x1, other arithmetic  3.38 us
  transfers between devices with their start and end apart: 9, of which 3 were waited for; matrix products, arithmetic and copies ran while one was open for 12% of the time, Pallas kernels for 0%

profile of v4, /device:TPU:0, one launch (start us, length us, event | category | flops | bytes accessed | tf_op | source)
XLA Modules:
  0.0 140.2 jit_solution(1642578064792314285)
XLA Ops:
  0.0 0.1 cosine_multiply_fusion.1
  0.1 0.1 sine_multiply_fusion.1
  0.1 0.8 fusion.27
  0.9 0.8 fusion.48
  1.7 0.7 slice_bitcast_fusion.9
  2.4 1.1 multiply_reduce_fusion.4
  3.5 0.3 fusion.24
  3.9 0.7 fusion.26
  4.6 0.5 collective-permute-start
  5.1 2.9 %collective-permute-start.1 = (f32[8192]{0:T(1024)S(1)}, f32[8192]{0:T(1024)S(1)}, u32[]{:S(2)}, u32[]{:S(2)}) collective-permute-start(f32[8192]{0:T(1024)S(1)} %get-tuple-element.28), channel_id=1, source_target_pairs={{4,0},{8,4},{12,8},{16,12},{20,16},{24,20},{28,24},{0,28},{5,1},{9... | collective-permute-start | bytes 98312 | tf_op jit(solution)/shard_map/ppermute | solution.py:76
  8.3 0.1 broadcast_add_fusion.8
  8.4 0.8 add_rsqrt_fusion
  9.2 0.0 copy-start.12
  9.2 0.4 multiply_reduce_fusion.1
  9.7 0.3 convolution_bitcast_fusion
  10.0 4.4 %collective-permute-start.4 = (f32[1,1,2,256]{3,2,1,0:T(2,128)S(1)}, f32[1,1,2,256]{3,2,1,0:T(2,128)S(1)}, u32[]{:S(2)}, u32[]{:S(2)}) collective-permute-start(f32[1,1,2,256]{3,2,1,0:T(2,128)S(1)} %convolution_bitcast_fusion), channel_id=1, source_target_pairs={{0,3},{1,0},{2,1},{3,2},{4,7},{5,4},{6,5},{7,6},{8,11},{9,8},{10,9... | collective-permute-start | bytes 6152 | tf_op jit(solution)/shard_map/ppermute | solution.py:61
  14.5 0.1 fusion.31
  14.5 0.1 fusion.33
  14.7 0.1 subtract_multiply_fusion.2
  14.9 0.1 subtract_multiply_fusion.3
  14.9 0.1 broadcast_add_fusion.4
  15.0 0.1 subtract_multiply_fusion
  15.1 0.3 broadcast_and_fusion
  15.4 0.1 broadcast_add_fusion.5
  15.5 0.1 broadcast_add_fusion.1
  15.6 0.1 broadcast_add_fusion
  15.6 0.1 pad_maximum_fusion.1.base_ref
  15.7 1.2 collective-permute-start.5
  16.9 3.4 %collective-permute-done.5 = f32[1,2,2,256]{3,2,1,0:T(2,128)S(1)} collective-permute-done((f32[1,2,2,256]{3,2,1,0:T(2,128)S(1)}, f32[1,2,2,256]{3,2,1,0:T(2,128)S(1)}, u32[]{:S(2)}, u32[]{:S(2)}) %collective-permute-start.5) | collective-permute-done | bytes 4128 | tf_op jit(solution)/shard_map/ppermute | solution.py:61
  20.3 1.3 collective-permute-done.6
  21.7 1.6 %collective-permute-start.7 = (f32[2,4,2,256]{3,2,1,0:T(2,128)S(1)}, f32[2,4,2,256]{3,2,1,0:T(2,128)S(1)}, u32[]{:S(2)}, u32[]{:S(2)}) collective-permute-start(f32[2,4,2,256]{3,2,1,0:T(2,128)S(1)} %pad_maximum_fusion.12), channel_id=1, source_target_pairs={{0,24},{4,28},{8,0},{12,4},{16,8},{20,12},{24,16},{28,20},{1,25},{... | collective-permute-start | bytes 49160 | tf_op jit(solution)/shard_map/ppermute | solution.py:61
  23.3 0.1 stack_broadcast_in_dim.41
  23.6 1.9 %collective-permute-done.7 = f32[2,4,2,256]{3,2,1,0:T(2,128)S(1)} collective-permute-done((f32[2,4,2,256]{3,2,1,0:T(2,128)S(1)}, f32[2,4,2,256]{3,2,1,0:T(2,128)S(1)}, u32[]{:S(2)}, u32[]{:S(2)}) %collective-permute-start.7) | collective-permute-done | bytes 16416 | tf_op jit(solution)/shard_map/ppermute | solution.py:61
  25.5 1.6 %collective-permute-start.8 = (f32[4,4,2,256]{3,2,1,0:T(2,128)S(1)}, f32[4,4,2,256]{3,2,1,0:T(2,128)S(1)}, u32[]{:S(2)}, u32[]{:S(2)}) collective-permute-start(f32[4,4,2,256]{3,2,1,0:T(2,128)S(1)} %pad_maximum_fusion.10), channel_id=1, source_target_pairs={{0,16},{4,20},{8,24},{12,28},{16,0},{20,4},{24,8},{28,12},{1,17},{... | collective-permute-start | bytes 98312 | tf_op jit(solution)/shard_map/ppermute | solution.py:61
  27.3 1.6 %collective-permute-start.2 = (f32[20480]{0:T(1024)S(1)}, f32[20480]{0:T(1024)S(1)}, u32[]{:S(2)}, u32[]{:S(2)}) collective-permute-start(f32[20480]{0:T(1024)S(1)} %get-tuple-element.13), channel_id=1, source_target_pairs={{0,1},{1,2},{2,3},{3,0},{4,5},{5,6},{6,7},{7,4},{8,9},{9,10},{10,1... | collective-permute-start | bytes 245768 | tf_op jit(solution)/shard_map/ppermute | solution.py:75
  28.9 2.6 %collective-permute-start.3 = (f32[20480]{0:T(1024)S(1)}, f32[20480]{0:T(1024)S(1)}, u32[]{:S(2)}, u32[]{:S(2)}) collective-permute-start(f32[20480]{0:T(1024)S(1)} %get-tuple-element.14), channel_id=1, source_target_pairs={{1,0},{2,1},{3,2},{0,3},{5,4},{6,5},{7,6},{4,7},{9,8},{10,9},{11,1... | collective-permute-start | bytes 245768 | tf_op jit(solution)/shard_map/ppermute | solution.py:76
  31.5 0.6 gather_fusion.2
  32.2 11.6 %multiply_reduce_fusion = f32[2,256]{1,0:T(2,128)S(1)} fusion(f32[11776]{0:T(1024)S(1)} %select_n.66, f32[2,11776]{1,0:T(2,128)S(1)} %stack_broadcast_in_dim.41, f32[256]{0:T(256)S(1)} %bitcast.157, f32[11776]{0:T(1024)S(1)} %stack_broadcast_in_dim.39, f32[256]{0:T(256)S(1)} %bitcast.158, f32[11776]{0:T(1024)S(1)} %stack_broadcast_in_dim.37, f32[256]{0:T(256)S(1)} %bitcast.156), kind=kLoop, calls=%fused_computation.13 | loop fusion | flops 66321920 | bytes 240640 | tf_op jit(solution)/shard_map/reduce_sum | solution.py:29
  43.9 0.3 fusion.41
  44.1 0.1 mul.515
  44.2 1.3 multiply_reduce_fusion.2
  45.7 0.6 copy-done.6
  46.2 0.1 select_maximum_fusion
  46.4 0.1 fusion.20
  46.5 0.1 fusion.19
  46.6 0.1 fusion.18
  46.7 0.1 fusion.17
  46.8 0.1 fusion.16
  46.9 0.1 fusion.15
  47.0 0.3 copy.19
  47.3 0.4 copy.26
  47.7 5.2 %gather_fusion.1 = f32[1264,1024]{1,0:T(8,128)} fusion(f32[448,1024]{1,0:T(8,128)S(1)} %bitcast.114, s32[2048]{0:T(1024)S(1)} %pad_clamp_fusion), kind=kCustom, calls=%fused_computation.1 | custom fusion | bytes 10359744 | tf_op jit(solution)/shard_map/jit(_take)/gather | solution.py:237
  52.9 7.1 %gather.16 = f32[2,158,16,256]{3,2,1,0:T(8,128)} reshape(f32[1264,1024]{1,0:T(8,128)} %gather_fusion.1) | data formatting | bytes 10354688 | tf_op jit(solution)/shard_map/jit(_take)/gather | solution.py:237
  60.0 3.4 %fusion.8 = (bf16[2,158,16,256]{3,2,1,0:T(8,128)(2,1)S(1)}, bf16[2,158,16,256]{3,2,1,0:T(8,128)(2,1)S(1)}) fusion(f32[2,158,16,256]{3,2,1,0:T(8,128)} %gather.16), kind=kLoop, calls=%fused_computation.16 | loop fusion | flops 7766016 | bytes 10354688 | tf_op jit(solution)/shard_map/convert
  63.4 0.7 pad_maximum_fusion.sources_ref
  64.1 46.7 %shard_map.136 = f32[16,256]{1,0:T(8,128)S(1)} custom-call(f32[474]{0:T(512)S(1)} %copy-done.1, f32[3,256,256]{2,1,0:T(8,128)S(1)} %pad_maximum_fusion.1.base_ref, bf16[2,158,32,256]{3,2,1,0:T(8,128)(2,1)S(1)} %pad_maximum_fusion.sources_ref), custom_call_target="tpu_custom_call" | custom-call | flops 2133065728 | bytes 5980160 | tf_op jit(solution)/shard_map/pallas_call | solution.py:134
  110.8 0.3 fusion.22
  111.2 1.3 multiply_reduce_fusion.3
  112.5 0.8 slice.304
  113.4 0.1 copy.23
  113.5 2.3 %gather_fusion = f32[432,4,128]{2,1,0:T(4,128)S(1)} fusion(f32[4,96,128]{2,0,1:T(4,128)S(1)} %bitcast.116, s32[1024]{0:T(1024)S(1)} %pad_clamp_fusion.2), kind=kCustom, calls=%fused_computation | custom fusion | bytes 1771200 | tf_op jit(solution)/shard_map/jit(_take)/gather | solution.py:261
  115.8 0.6 fusion.34
  116.5 23.0 %fusion.5 = f32[2,2,4,128]{3,2,1,0:T(4,128)S(1)} fusion(f32[27]{0:T(128)S(1)} %copy-done.15, f32[27]{0:T(128)S(1)} %copy-done.14, f32[27]{0:T(128)S(1)} %copy-done.13, f32[27,2,2,4,128]{4,3,2,1,0:T(4,128)S(1)} %bitcast.121, f32[27,2,2,4,128]{4,3,2,1,0:T(4,128)S(1)} %bitcast.122, f32[2,2,4,128]{3,2,1,0:T(4,128)S(1)} %get-tuple-element.25, ...), kind=kLoop, calls=%fused_computation.9 | loop fusion | flops 106166272 | bytes 1360196 | tf_op jit(solution)/shard_map/reduce_sum | solution.py:273
  139.5 0.7 add_select_fusion
  (99 shorter events, 1.2 us)
Async XLA Ops:
  0.0 3.5 %copy-start = (f32[256,256]{1,0:T(8,128)S(1)}, f32[256,256]{1,0:T(8,128)}, u32[]{:S(2)}) copy-start(f32[256,256]{1,0:T(8,128)} %param.17) | copy-start | bytes 786436
  4.6 22.5 %collective-permute-start = (f32[8192]{0:T(1024)S(1)}, f32[8192]{0:T(1024)S(1)}, u32[]{:S(2)}, u32[]{:S(2)}) collective-permute-start(f32[8192]{0:T(1024)S(1)} %get-tuple-element.27), channel_id=1, source_target_pairs={{0,4},{4,8},{8,12},{12,16},{16,20},{20,24},{24,28},{28,0},{1,5},{5... | collective-permute-start | bytes 98312 | tf_op jit(solution)/shard_map/ppermute | solution.py:75
  5.1 22.0 %collective-permute-start.1 = (f32[8192]{0:T(1024)S(1)}, f32[8192]{0:T(1024)S(1)}, u32[]{:S(2)}, u32[]{:S(2)}) collective-permute-start(f32[8192]{0:T(1024)S(1)} %get-tuple-element.28), channel_id=1, source_target_pairs={{4,0},{8,4},{12,8},{16,12},{20,16},{24,20},{28,24},{0,28},{5,1},{9... | collective-permute-start | bytes 98312 | tf_op jit(solution)/shard_map/ppermute | solution.py:76
  8.4 1.3 copy-start.4
  8.4 6.5 %copy-start.2 = (f32[3,2,2,4,128]{4,3,2,1,0:T(4,128)S(1)}, f32[3,2,2,4,128]{4,3,2,1,0:T(4,128)}, u32[]{:S(2)}) copy-start(f32[3,2,2,4,128]{4,3,2,1,0:T(4,128)} %param.14) | copy-start | bytes 73732
  9.2 6.3 %copy-start.11 = (f32[23]{0:T(128)S(1)}, f32[23]{0:T(128)}, u32[]{:S(2)}) copy-start(f32[23]{0:T(128)} %constant.158) | copy-start | bytes 280
  9.2 6.3 %copy-start.12 = (f32[23]{0:T(128)S(1)}, f32[23]{0:T(128)}, u32[]{:S(2)}) copy-start(f32[23]{0:T(128)} %constant.159) | copy-start | bytes 280
  9.7 7.2 %copy-start.8 = (s32[1264]{0:T(1024)S(1)}, s32[1264]{0:T(1024)}, u32[]{:S(2)}) copy-start(s32[1264]{0:T(1024)} %constant.174) | copy-start | bytes 15172
  9.7 10.6 %copy-start.9 = (s32[432]{0:T(512)S(1)}, s32[432]{0:T(512)}, u32[]{:S(2)}) copy-start(s32[432]{0:T(512)} %constant.173) | copy-start | bytes 5188
  9.7 13.6 %copy-start.10 = (s32[23]{0:T(128)S(1)}, s32[23]{0:T(128)}, u32[]{:S(2)}) copy-start(s32[23]{0:T(128)} %constant.175) | copy-start | bytes 280
  10.0 5.7 %collective-permute-start.4 = (f32[1,1,2,256]{3,2,1,0:T(2,128)S(1)}, f32[1,1,2,256]{3,2,1,0:T(2,128)S(1)}, u32[]{:S(2)}, u32[]{:S(2)}) collective-permute-start(f32[1,1,2,256]{3,2,1,0:T(2,128)S(1)} %convolution_bitcast_fusion), channel_id=1, source_target_pairs={{0,3},{1,0},{2,1},{3,2},{4,7},{5,4},{6,5},{7,6},{8,11},{9,8},{10,9... | collective-permute-start | bytes 6152 | tf_op jit(solution)/shard_map/ppermute | solution.py:61
  15.7 4.6 %collective-permute-start.5 = (f32[1,2,2,256]{3,2,1,0:T(2,128)S(1)}, f32[1,2,2,256]{3,2,1,0:T(2,128)S(1)}, u32[]{:S(2)}, u32[]{:S(2)}) collective-permute-start(f32[1,2,2,256]{3,2,1,0:T(2,128)S(1)} %pad_maximum_fusion.15), channel_id=1, source_target_pairs={{0,2},{1,3},{2,0},{3,1},{4,6},{5,7},{6,4},{7,5},{8,10},{9,11},{10,... | collective-permute-start | bytes 12296 | tf_op jit(solution)/shard_map/ppermute | solution.py:61
  20.3 1.4 collective-permute-start.6
  21.7 3.8 %collective-permute-start.7 = (f32[2,4,2,256]{3,2,1,0:T(2,128)S(1)}, f32[2,4,2,256]{3,2,1,0:T(2,128)S(1)}, u32[]{:S(2)}, u32[]{:S(2)}) collective-permute-start(f32[2,4,2,256]{3,2,1,0:T(2,128)S(1)} %pad_maximum_fusion.12), channel_id=1, source_target_pairs={{0,24},{4,28},{8,0},{12,4},{16,8},{20,12},{24,16},{28,20},{1,25},{... | collective-permute-start | bytes 49160 | tf_op jit(solution)/shard_map/ppermute | solution.py:61
  25.5 6.0 %collective-permute-start.8 = (f32[4,4,2,256]{3,2,1,0:T(2,128)S(1)}, f32[4,4,2,256]{3,2,1,0:T(2,128)S(1)}, u32[]{:S(2)}, u32[]{:S(2)}) collective-permute-start(f32[4,4,2,256]{3,2,1,0:T(2,128)S(1)} %pad_maximum_fusion.10), channel_id=1, source_target_pairs={{0,16},{4,20},{8,24},{12,28},{16,0},{20,4},{24,8},{28,12},{1,17},{... | collective-permute-start | bytes 98312 | tf_op jit(solution)/shard_map/ppermute | solution.py:61
  27.3 18.3 %collective-permute-start.2 = (f32[20480]{0:T(1024)S(1)}, f32[20480]{0:T(1024)S(1)}, u32[]{:S(2)}, u32[]{:S(2)}) collective-permute-start(f32[20480]{0:T(1024)S(1)} %get-tuple-element.13), channel_id=1, source_target_pairs={{0,1},{1,2},{2,3},{3,0},{4,5},{5,6},{6,7},{7,4},{8,9},{9,10},{10,1... | collective-permute-start | bytes 245768 | tf_op jit(solution)/shard_map/ppermute | solution.py:75
  28.9 16.7 %collective-permute-start.3 = (f32[20480]{0:T(1024)S(1)}, f32[20480]{0:T(1024)S(1)}, u32[]{:S(2)}, u32[]{:S(2)}) collective-permute-start(f32[20480]{0:T(1024)S(1)} %get-tuple-element.14), channel_id=1, source_target_pairs={{1,0},{2,1},{3,2},{0,3},{5,4},{6,5},{7,6},{4,7},{9,8},{10,9},{11,1... | collective-permute-start | bytes 245768 | tf_op jit(solution)/shard_map/ppermute | solution.py:76
  32.2 11.7 %copy-start.5 = (f32[256,256]{1,0:T(8,128)S(1)}, f32[256,256]{1,0:T(8,128)}, u32[]{:S(2)}) copy-start(f32[256,256]{1,0:T(8,128)} %param.20) | copy-start | bytes 786436
  45.6 0.6 copy-start.6
  63.4 0.7 copy-start.1
  64.1 46.7 %copy-start.3 = (f32[256,256]{1,0:T(8,128)S(1)}, f32[256,256]{1,0:T(8,128)}, u32[]{:S(2)}) copy-start(f32[256,256]{1,0:T(8,128)} %param.18) | copy-start | bytes 786436
  113.3 3.1 %copy-start.13 = (f32[27]{0:T(128)S(1)}, f32[27]{0:T(128)}, u32[]{:S(2)}) copy-start(f32[27]{0:T(128)} %constant.170) | copy-start | bytes 328
  113.3 3.1 %copy-start.14 = (f32[27]{0:T(128)S(1)}, f32[27]{0:T(128)}, u32[]{:S(2)}) copy-start(f32[27]{0:T(128)} %constant.171) | copy-start | bytes 328
  113.3 3.1 %copy-start.15 = (f32[27]{0:T(128)S(1)}, f32[27]{0:T(128)}, u32[]{:S(2)}) copy-start(f32[27]{0:T(128)} %constant.172) | copy-start | bytes 328
  116.4 23.0 %copy-start.7 = (s32[2,2,4]{2,1,0:T(2,128)S(1)}, s32[2,2,4]{2,1,0:T(2,128)}, u32[]{:S(2)}) copy-start(s32[2,2,4]{2,1,0:T(2,128)} %param.16) | copy-start | bytes 196

commit v5 on v4

--- a/solution.py
+++ b/solution.py
@@ -89,9 +89,10 @@
     return scaled - (scaled - values)
 
 
-def m2l_kernel(shift_count, rows, table_ref, base_ref, sources_ref, out_ref):
+def m2l_kernel(shift_count, rows, table_ref, index_ref, base_ref, windows_ref, out_ref):
     out_ref[...] = jnp.zeros_like(out_ref)
     vectors = out_ref.shape[0]
+    pieces = index_ref.shape[0] // (2 * shift_count)
 
     def split_dot(left, matrix_high, matrix_low, dims):
         both = lax.dot_general(left, matrix_high, dims, preferred_element_type=jnp.float32)
@@ -100,12 +101,20 @@
         )
         return both[:vectors] + both[vectors:] + cross
 
+    def gathered(sign, index):
+        first = (sign * shift_count + index) * pieces
+        block = jnp.concatenate(
+            [windows_ref[index_ref[first + piece]] for piece in range(pieces)], axis=0
+        )
+        top = split_top(block)
+        return jnp.concatenate([top, block - top], axis=0).astype(jnp.bfloat16)
+
     def body(index, carry):
         shift_x = table_ref[3 * index]
         shift_y = table_ref[3 * index + 1]
         shift_z = table_ref[3 * index + 2]
-        fwd = sources_ref[0, index]
-        back = sources_ref[1, index]
+        fwd = gathered(0, index)
+        back = gathered(1, index)
         for row in range(0, base_ref.shape[1], rows):
             delta_x = base_ref[0, row : row + rows, :] - shift_x
             delta_y = base_ref[1, row : row + rows, :] - shift_y
@@ -127,14 +136,14 @@
     lax.fori_loop(0, shift_count, body, 0)
 
 
-def m2l(table, base, sources):
-    top = split_top(sources)
-    split = jnp.concatenate([top, sources - top], axis=2).astype(jnp.bfloat16)
-    shift_count, vectors, points = sources.shape[1:]
+def m2l(table, window_index, base, windows, vectors):
+    shift_count = table.shape[0] // 3
+    points = windows.shape[-1]
     return pl.pallas_call(
         functools.partial(m2l_kernel, shift_count, 128),
         out_shape=jax.ShapeDtypeStruct((vectors, points), jnp.float32),
         in_specs=[
+            pl.BlockSpec(memory_space=pltpu.SMEM),
             pl.BlockSpec(memory_space=pltpu.SMEM),
             pl.BlockSpec(memory_space=pltpu.VMEM),
             pl.BlockSpec(memory_space=pltpu.VMEM),
@@ -144,9 +153,9 @@
         cost_estimate=pl.CostEstimate(
             flops=12 * shift_count * vectors * points * points + 14 * shift_count * points * points,
             transcendentals=shift_count * points * points,
-            bytes_accessed=4 * (sources.size + base.size + vectors * points),
+            bytes_accessed=4 * (windows.size + base.size + vectors * points),
         ),
-    )(table, base, split)
+    )(table, window_index, base, windows)
 
 
 def far_shifts(span):
@@ -217,29 +226,26 @@
     shifts = far_shifts(3)
     depth_windows = jnp.stack(
         [framed[:, :, depth : depth + layers] for depth in range(7)], axis=2
-    ).reshape(-1, layers * points)
-    window_rows = np.array(
+    ).reshape(-1, layers, points)
+    window_index = np.array(
         [
-            [
-                [
-                    np.ravel_multi_index(
-                        (ix + sign * dx + 3, iy + sign * dy + 3, sign * dz + 3), framed.shape[:2] + (7,)
-                    )
-                    for ix in range(2)
-                    for iy in range(2)
-                ]
-                for dx, dy, dz in shifts
-            ]
+            np.ravel_multi_index(
+                (ix + sign * dx + 3, iy + sign * dy + 3, sign * dz + 3), framed.shape[:2] + (7,)
+            )
             for sign in (1, -1)
+            for dx, dy, dz in shifts
+            for ix in range(2)
+            for iy in range(2)
         ],
         np.int32,
     )
-    sources = jnp.take(depth_windows, window_rows, axis=0).reshape(2, len(shifts), 4 * layers, points)
     base = jnp.stack(
         [0.9 * (unit_sphere[i][:, None] - unit_sphere[i][None, :]) for i in range(3)]
     )
     table = jnp.asarray(np.array(shifts, np.float32).reshape(-1))
-    leaf_down_check = m2l(table, base, sources).reshape(2, 2, layers, points)
+    leaf_down_check = m2l(table, jnp.asarray(window_index), base, depth_windows, 4 * layers).reshape(
+        2, 2, layers, points
+    )
     parent_local = jnp.einsum("ec,mc->me", c2e_top_down, far_check, precision=highest)
     leaf_local = jnp.einsum("ec,xyzc->xyze", c2e_leaf_down, leaf_down_check, precision=highest)
 

time: 141 us -> 123 us (0.87)
  local copies, waits for them, and re-layouts: 20 us -> 6.23 us
  other arithmetic: 48.5 us -> 44.2 us
    gather x2 -> x0, local copies, waits for them, and re-layouts: 12.2 us -> none  [shards(): jnp.take(depth_windows, window_rows, axis=0)]
    another operation x1 -> x0, other arithmetic: 3.38 us -> none
  transfers between devices with their start and end apart: 9 -> 9, of which waited for: 3 -> 3; matrix products, arithmetic and copies ran while one was open for 12% -> 14% of each run, Pallas kernels for 0% -> 0%
where the time goes in v5:
time: 123 us
  Pallas kernels  47.3 us (38%)
  other arithmetic  44.2 us (36%)
  starting transfers between devices  16.5 us (13%)
  waiting for transfers between devices  6.5 us (5%)
  local copies, waits for them, and re-layouts  6.23 us (5%)
    pallas_call x1, Pallas kernels, m2l(): pl.pallas_call(functools.partial(m2l_kernel, shift_count, 128), out_shape...  47.3 us
    reduce_sum x1, other arithmetic, shards(): near = jnp.sum(jnp.sum(kernel * source[3][..., None, :], axis=-1), axis=0)  22.8 us
    reduce_sum x5, other arithmetic, point_sum(): return jnp.sum(kernel * weights[..., None, :], axis=-1)  15.8 us
    ppermute x5, starting transfers between devices, rel_gather(): lax.ppermute(part, axis, [(j, (j - have) % count) for j in range(count)])  8.8 us
    ppermute x5, waiting for transfers between devices, rel_gather(): lax.ppermute(part, axis, [(j, (j - have) % count) for j in range(count)])  6.49 us
    ppermute x2, starting transfers between devices, exchange(): lax.ppermute(sent_head, axis, [((i + 1) % count, i) for i in range(count)])  5.55 us
  transfers between devices with their start and end apart: 9, of which 3 were waited for; matrix products, arithmetic and copies ran while one was open for 14% of the time, Pallas kernels for 0%

profile of v5, /device:TPU:0, one launch (start us, length us, event | category | flops | bytes accessed | tf_op | source)
XLA Modules:
  0.0 122.7 jit_solution(9713203947134381303)
XLA Ops:
  0.0 0.1 cosine_multiply_fusion.1
  0.1 0.1 sine_multiply_fusion.1
  0.1 0.8 fusion.24
  0.9 0.8 fusion.45
  1.7 0.7 slice_bitcast_fusion.9
  2.4 1.1 multiply_reduce_fusion.4
  3.5 0.3 fusion.21
  3.9 0.7 fusion.23
  4.6 0.5 collective-permute-start
  5.1 2.9 %collective-permute-start.1 = (f32[8192]{0:T(1024)S(1)}, f32[8192]{0:T(1024)S(1)}, u32[]{:S(2)}, u32[]{:S(2)}) collective-permute-start(f32[8192]{0:T(1024)S(1)} %get-tuple-element.26), channel_id=1, source_target_pairs={{4,0},{8,4},{12,8},{16,12},{20,16},{24,20},{28,24},{0,28},{5,1},{9... | collective-permute-start | bytes 98312 | tf_op jit(solution)/shard_map/ppermute | solution.py:76
  8.2 0.1 broadcast_add_fusion.8
  8.4 0.8 add_rsqrt_fusion
  9.2 0.0 copy-start.10
  9.2 0.0 copy-start.11
  9.2 0.4 multiply_reduce_fusion.1
  9.7 0.0 copy-start.8
  9.7 0.0 copy-start.9
  9.7 0.3 convolution_bitcast_fusion
  9.9 4.4 %collective-permute-start.4 = (f32[1,1,2,256]{3,2,1,0:T(2,128)S(1)}, f32[1,1,2,256]{3,2,1,0:T(2,128)S(1)}, u32[]{:S(2)}, u32[]{:S(2)}) collective-permute-start(f32[1,1,2,256]{3,2,1,0:T(2,128)S(1)} %convolution_bitcast_fusion), channel_id=1, source_target_pairs={{0,3},{1,0},{2,1},{3,2},{4,7},{5,4},{6,5},{7,6},{8,11},{9,8},{10,9... | collective-permute-start | bytes 6152 | tf_op jit(solution)/shard_map/ppermute | solution.py:61
  14.4 0.1 fusion.28
  14.5 0.1 fusion.30
  14.7 0.1 subtract_multiply_fusion.2
  14.8 0.1 subtract_multiply_fusion.3
  14.9 0.1 broadcast_add_fusion.4
  14.9 0.1 subtract_multiply_fusion
  15.1 0.3 broadcast_and_fusion
  15.4 0.1 broadcast_add_fusion.5
  15.4 0.1 broadcast_add_fusion.1
  15.5 0.1 broadcast_add_fusion
  15.6 0.0 collective-permute-done.4
  15.6 1.3 %collective-permute-start.5 = (f32[1,2,2,256]{3,2,1,0:T(2,128)S(1)}, f32[1,2,2,256]{3,2,1,0:T(2,128)S(1)}, u32[]{:S(2)}, u32[]{:S(2)}) collective-permute-start(f32[1,2,2,256]{3,2,1,0:T(2,128)S(1)} %pad_maximum_fusion.14), channel_id=1, source_target_pairs={{0,2},{1,3},{2,0},{3,1},{4,6},{5,7},{6,4},{7,5},{8,10},{9,11},{10,... | collective-permute-start | bytes 12296 | tf_op jit(solution)/shard_map/ppermute | solution.py:61
  16.9 0.1 pad_maximum_fusion.base_ref
  16.9 3.3 %collective-permute-done.5 = f32[1,2,2,256]{3,2,1,0:T(2,128)S(1)} collective-permute-done((f32[1,2,2,256]{3,2,1,0:T(2,128)S(1)}, f32[1,2,2,256]{3,2,1,0:T(2,128)S(1)}, u32[]{:S(2)}, u32[]{:S(2)}) %collective-permute-start.5) | collective-permute-done | bytes 4128 | tf_op jit(solution)/shard_map/ppermute | solution.py:61
  20.2 1.3 %collective-permute-done.6 = f32[1,4,2,256]{3,2,1,0:T(2,128)S(1)} collective-permute-done((f32[1,4,2,256]{3,2,1,0:T(2,128)S(1)}, f32[1,4,2,256]{3,2,1,0:T(2,128)S(1)}, u32[]{:S(2)}, u32[]{:S(2)}) %collective-permute-start.6) | collective-permute-done | bytes 8224 | tf_op jit(solution)/shard_map/ppermute | solution.py:61
  21.6 1.6 %collective-permute-start.7 = (f32[2,4,2,256]{3,2,1,0:T(2,128)S(1)}, f32[2,4,2,256]{3,2,1,0:T(2,128)S(1)}, u32[]{:S(2)}, u32[]{:S(2)}) collective-permute-start(f32[2,4,2,256]{3,2,1,0:T(2,128)S(1)} %pad_maximum_fusion.11), channel_id=1, source_target_pairs={{0,24},{4,28},{8,0},{12,4},{16,8},{20,12},{24,16},{28,20},{1,25},{... | collective-permute-start | bytes 49160 | tf_op jit(solution)/shard_map/ppermute | solution.py:61
  23.2 0.1 stack_broadcast_in_dim.41
  23.5 1.9 %collective-permute-done.7 = f32[2,4,2,256]{3,2,1,0:T(2,128)S(1)} collective-permute-done((f32[2,4,2,256]{3,2,1,0:T(2,128)S(1)}, f32[2,4,2,256]{3,2,1,0:T(2,128)S(1)}, u32[]{:S(2)}, u32[]{:S(2)}) %collective-permute-start.7) | collective-permute-done | bytes 16416 | tf_op jit(solution)/shard_map/ppermute | solution.py:61
  25.4 1.6 %collective-permute-start.8 = (f32[4,4,2,256]{3,2,1,0:T(2,128)S(1)}, f32[4,4,2,256]{3,2,1,0:T(2,128)S(1)}, u32[]{:S(2)}, u32[]{:S(2)}) collective-permute-start(f32[4,4,2,256]{3,2,1,0:T(2,128)S(1)} %pad_maximum_fusion.9), channel_id=1, source_target_pairs={{0,16},{4,20},{8,24},{12,28},{16,0},{20,4},{24,8},{28,12},{1,17},{... | collective-permute-start | bytes 98312 | tf_op jit(solution)/shard_map/ppermute | solution.py:61
  27.2 1.7 %collective-permute-start.2 = (f32[20480]{0:T(1024)S(1)}, f32[20480]{0:T(1024)S(1)}, u32[]{:S(2)}, u32[]{:S(2)}) collective-permute-start(f32[20480]{0:T(1024)S(1)} %get-tuple-element.11), channel_id=1, source_target_pairs={{0,1},{1,2},{2,3},{3,0},{4,5},{5,6},{6,7},{7,4},{8,9},{9,10},{10,1... | collective-permute-start | bytes 245768 | tf_op jit(solution)/shard_map/ppermute | solution.py:75
  28.9 2.6 %collective-permute-start.3 = (f32[20480]{0:T(1024)S(1)}, f32[20480]{0:T(1024)S(1)}, u32[]{:S(2)}, u32[]{:S(2)}) collective-permute-start(f32[20480]{0:T(1024)S(1)} %get-tuple-element.12), channel_id=1, source_target_pairs={{1,0},{2,1},{3,2},{0,3},{5,4},{6,5},{7,6},{4,7},{9,8},{10,9},{11,1... | collective-permute-start | bytes 245768 | tf_op jit(solution)/shard_map/ppermute | solution.py:76
  31.5 0.6 gather_fusion.1
  32.2 11.7 %multiply_reduce_fusion = f32[2,256]{1,0:T(2,128)S(1)} fusion(f32[11776]{0:T(1024)S(1)} %select_n.54, f32[2,11776]{1,0:T(2,128)S(1)} %stack_broadcast_in_dim.41, f32[256]{0:T(256)S(1)} %bitcast.154, f32[11776]{0:T(1024)S(1)} %stack_broadcast_in_dim.39, f32[256]{0:T(256)S(1)} %bitcast.155, f32[11776]{0:T(1024)S(1)} %stack_broadcast_in_dim.37, f32[256]{0:T(256)S(1)} %bitcast.153), kind=kLoop, calls=%fused_computation.12 | loop fusion | flops 66321920 | bytes 240640 | tf_op jit(solution)/shard_map/reduce_sum | solution.py:29
  43.8 0.3 fusion.38
  44.1 0.1 mul.507
  44.2 1.3 %multiply_reduce_fusion.2 = f32[2,2,4,128]{3,2,1,0:T(4,128)S(1)} fusion(f32[4,256]{1,0:T(4,128)S(1)} %mul.507, f32[256]{0:T(256)S(1)} %bitcast.144, f32[2,2,4,128]{3,2,1,0:T(4,128)S(1)} %get-tuple-element.21, f32[256]{0:T(256)S(1)} %bitcast.146, f32[2,2,4,128]{3,2,1,0:T(4,128)S(1)} %get-tuple-element.20, f32[256]{0:T(256)S(1)} %bitcast.142, ...), kind=kLoop, calls=%fused_computation.14 | loop fusion | flops 5765120 | bytes 39936 | tf_op jit(solution)/shard_map/reduce_sum | solution.py:29
  45.6 0.1 select_maximum_fusion
  45.8 0.1 fusion.17
  45.9 0.1 fusion.16
  46.0 0.1 fusion.15
  46.1 0.1 fusion.14
  46.2 0.1 fusion.13
  46.3 0.0 copy-start.1
  46.3 0.1 fusion.12
  46.4 0.3 copy.20
  46.7 0.2 copy-done.1
  47.0 47.3 %shard_map.136 = f32[16,256]{1,0:T(8,128)S(1)} custom-call(f32[474]{0:T(512)S(1)} %copy-done.2, s32[1264]{0:T(1024)S(1)} %copy-done.1, f32[3,256,256]{2,1,0:T(8,128)S(1)} %pad_maximum_fusion.base_ref, f32[448,4,256]{2,1,0:T(4,128)S(1)} %bitcast.112), custom_call_target="tpu_custom_call" | custom-call | flops 2133065728 | bytes 2637824 | tf_op jit(solution)/shard_map/pallas_call | solution.py:142
  94.3 0.3 fusion.19
  94.7 1.3 %multiply_reduce_fusion.3 = f32[2,2,4,128]{3,2,1,0:T(4,128)S(1)} fusion(f32[2,2,4,256]{3,2,1,0:T(4,128)S(1)} %fusion.19, f32[256]{0:T(256)S(1)} %bitcast.150, f32[2,2,4,128]{3,2,1,0:T(4,128)S(1)} %get-tuple-element.23, f32[256]{0:T(256)S(1)} %bitcast.148, f32[2,2,4,128]{3,2,1,0:T(4,128)S(1)} %get-tuple-element.24, f32[256]{0:T(256)S(1)} %bitcast.152, ...), kind=kLoop, calls=%fused_computation.16 | loop fusion | flops 5765120 | bytes 52224 | tf_op jit(solution)/shard_map/reduce_sum | solution.py:29
  96.1 0.0 copy-start.12
  96.1 0.1 copy.24
  96.2 2.3 %gather_fusion = f32[432,4,128]{2,1,0:T(4,128)S(1)} fusion(f32[4,96,128]{2,0,1:T(4,128)S(1)} %bitcast.113, s32[1024]{0:T(1024)S(1)} %pad_clamp_fusion.1), kind=kCustom, calls=%fused_computation | custom fusion | bytes 1771200 | tf_op jit(solution)/shard_map/jit(_take)/gather | solution.py:267
  98.5 0.6 fusion.31
  99.2 22.8 %fusion.5 = f32[2,2,4,128]{3,2,1,0:T(4,128)S(1)} fusion(f32[27]{0:T(128)S(1)} %copy-done.14, f32[27]{0:T(128)S(1)} %copy-done.13, f32[27]{0:T(128)S(1)} %copy-done.12, f32[27,2,2,4,128]{4,3,2,1,0:T(4,128)S(1)} %bitcast.118, f32[27,2,2,4,128]{4,3,2,1,0:T(4,128)S(1)} %bitcast.119, f32[2,2,4,128]{3,2,1,0:T(4,128)S(1)} %get-tuple-element.23, ...), kind=kLoop, calls=%fused_computation.8 | loop fusion | flops 106166272 | bytes 1360196 | tf_op jit(solution)/shard_map/reduce_sum | solution.py:279
  122.0 0.7 add_select_fusion
  (91 shorter events, 1.1 us)
Async XLA Ops:
  0.0 3.5 %copy-start = (f32[256,256]{1,0:T(8,128)S(1)}, f32[256,256]{1,0:T(8,128)}, u32[]{:S(2)}) copy-start(f32[256,256]{1,0:T(8,128)} %param.17) | copy-start | bytes 786436
  4.6 22.4 %collective-permute-start = (f32[8192]{0:T(1024)S(1)}, f32[8192]{0:T(1024)S(1)}, u32[]{:S(2)}, u32[]{:S(2)}) collective-permute-start(f32[8192]{0:T(1024)S(1)} %get-tuple-element.25), channel_id=1, source_target_pairs={{0,4},{4,8},{8,12},{12,16},{16,20},{20,24},{24,28},{28,0},{1,5},{5... | collective-permute-start | bytes 98312 | tf_op jit(solution)/shard_map/ppermute | solution.py:75
  5.1 21.9 %collective-permute-start.1 = (f32[8192]{0:T(1024)S(1)}, f32[8192]{0:T(1024)S(1)}, u32[]{:S(2)}, u32[]{:S(2)}) collective-permute-start(f32[8192]{0:T(1024)S(1)} %get-tuple-element.26), channel_id=1, source_target_pairs={{4,0},{8,4},{12,8},{16,12},{20,16},{24,20},{28,24},{0,28},{5,1},{9... | collective-permute-start | bytes 98312 | tf_op jit(solution)/shard_map/ppermute | solution.py:76
  8.4 1.3 %copy-start.5 = (f32[256,256]{1,0:T(8,128)S(1)}, f32[256,256]{1,0:T(8,128)}, u32[]{:S(2)}) copy-start(f32[256,256]{1,0:T(8,128)} %param.19) | copy-start | bytes 786436
  8.4 6.5 %copy-start.3 = (f32[3,2,2,4,128]{4,3,2,1,0:T(4,128)S(1)}, f32[3,2,2,4,128]{4,3,2,1,0:T(4,128)}, u32[]{:S(2)}) copy-start(f32[3,2,2,4,128]{4,3,2,1,0:T(4,128)} %param.14) | copy-start | bytes 73732
  9.2 6.2 %copy-start.10 = (f32[23]{0:T(128)S(1)}, f32[23]{0:T(128)}, u32[]{:S(2)}) copy-start(f32[23]{0:T(128)} %constant.135) | copy-start | bytes 280
  9.2 6.3 %copy-start.11 = (f32[23]{0:T(128)S(1)}, f32[23]{0:T(128)}, u32[]{:S(2)}) copy-start(f32[23]{0:T(128)} %constant.136) | copy-start | bytes 280
  9.7 10.6 %copy-start.8 = (s32[432]{0:T(512)S(1)}, s32[432]{0:T(512)}, u32[]{:S(2)}) copy-start(s32[432]{0:T(512)} %constant.149) | copy-start | bytes 5188
  9.7 13.5 %copy-start.9 = (s32[23]{0:T(128)S(1)}, s32[23]{0:T(128)}, u32[]{:S(2)}) copy-start(s32[23]{0:T(128)} %constant.150) | copy-start | bytes 280
  9.9 5.7 %collective-permute-start.4 = (f32[1,1,2,256]{3,2,1,0:T(2,128)S(1)}, f32[1,1,2,256]{3,2,1,0:T(2,128)S(1)}, u32[]{:S(2)}, u32[]{:S(2)}) collective-permute-start(f32[1,1,2,256]{3,2,1,0:T(2,128)S(1)} %convolution_bitcast_fusion), channel_id=1, source_target_pairs={{0,3},{1,0},{2,1},{3,2},{4,7},{5,4},{6,5},{7,6},{8,11},{9,8},{10,9... | collective-permute-start | bytes 6152 | tf_op jit(solution)/shard_map/ppermute | solution.py:61
  15.6 4.6 %collective-permute-start.5 = (f32[1,2,2,256]{3,2,1,0:T(2,128)S(1)}, f32[1,2,2,256]{3,2,1,0:T(2,128)S(1)}, u32[]{:S(2)}, u32[]{:S(2)}) collective-permute-start(f32[1,2,2,256]{3,2,1,0:T(2,128)S(1)} %pad_maximum_fusion.14), channel_id=1, source_target_pairs={{0,2},{1,3},{2,0},{3,1},{4,6},{5,7},{6,4},{7,5},{8,10},{9,11},{10,... | collective-permute-start | bytes 12296 | tf_op jit(solution)/shard_map/ppermute | solution.py:61
  20.2 1.4 %collective-permute-start.6 = (f32[1,4,2,256]{3,2,1,0:T(2,128)S(1)}, f32[1,4,2,256]{3,2,1,0:T(2,128)S(1)}, u32[]{:S(2)}, u32[]{:S(2)}) collective-permute-start(f32[1,4,2,256]{3,2,1,0:T(2,128)S(1)} %pad_maximum_fusion.12), channel_id=1, source_target_pairs={{0,28},{4,0},{8,4},{12,8},{16,12},{20,16},{24,20},{28,24},{1,29},{... | collective-permute-start | bytes 24584 | tf_op jit(solution)/shard_map/ppermute | solution.py:61
  21.6 3.8 %collective-permute-start.7 = (f32[2,4,2,256]{3,2,1,0:T(2,128)S(1)}, f32[2,4,2,256]{3,2,1,0:T(2,128)S(1)}, u32[]{:S(2)}, u32[]{:S(2)}) collective-permute-start(f32[2,4,2,256]{3,2,1,0:T(2,128)S(1)} %pad_maximum_fusion.11), channel_id=1, source_target_pairs={{0,24},{4,28},{8,0},{12,4},{16,8},{20,12},{24,16},{28,20},{1,25},{... | collective-permute-start | bytes 49160 | tf_op jit(solution)/shard_map/ppermute | solution.py:61
  25.4 6.1 %collective-permute-start.8 = (f32[4,4,2,256]{3,2,1,0:T(2,128)S(1)}, f32[4,4,2,256]{3,2,1,0:T(2,128)S(1)}, u32[]{:S(2)}, u32[]{:S(2)}) collective-permute-start(f32[4,4,2,256]{3,2,1,0:T(2,128)S(1)} %pad_maximum_fusion.9), channel_id=1, source_target_pairs={{0,16},{4,20},{8,24},{12,28},{16,0},{20,4},{24,8},{28,12},{1,17},{... | collective-permute-start | bytes 98312 | tf_op jit(solution)/shard_map/ppermute | solution.py:61
  27.2 18.3 %collective-permute-start.2 = (f32[20480]{0:T(1024)S(1)}, f32[20480]{0:T(1024)S(1)}, u32[]{:S(2)}, u32[]{:S(2)}) collective-permute-start(f32[20480]{0:T(1024)S(1)} %get-tuple-element.11), channel_id=1, source_target_pairs={{0,1},{1,2},{2,3},{3,0},{4,5},{5,6},{6,7},{7,4},{8,9},{9,10},{10,1... | collective-permute-start | bytes 245768 | tf_op jit(solution)/shard_map/ppermute | solution.py:75
  28.9 16.7 %collective-permute-start.3 = (f32[20480]{0:T(1024)S(1)}, f32[20480]{0:T(1024)S(1)}, u32[]{:S(2)}, u32[]{:S(2)}) collective-permute-start(f32[20480]{0:T(1024)S(1)} %get-tuple-element.12), channel_id=1, source_target_pairs={{1,0},{2,1},{3,2},{0,3},{5,4},{6,5},{7,6},{4,7},{9,8},{10,9},{11,1... | collective-permute-start | bytes 245768 | tf_op jit(solution)/shard_map/ppermute | solution.py:76
  32.2 11.7 %copy-start.6 = (f32[256,256]{1,0:T(8,128)S(1)}, f32[256,256]{1,0:T(8,128)}, u32[]{:S(2)}) copy-start(f32[256,256]{1,0:T(8,128)} %param.20) | copy-start | bytes 786436
  46.3 0.7 copy-start.1
  46.3 0.7 copy-start.2
  47.0 47.3 %copy-start.4 = (f32[256,256]{1,0:T(8,128)S(1)}, f32[256,256]{1,0:T(8,128)}, u32[]{:S(2)}) copy-start(f32[256,256]{1,0:T(8,128)} %param.18) | copy-start | bytes 786436
  96.1 3.1 %copy-start.12 = (f32[27]{0:T(128)S(1)}, f32[27]{0:T(128)}, u32[]{:S(2)}) copy-start(f32[27]{0:T(128)} %constant.146) | copy-start | bytes 328
  96.1 3.1 %copy-start.13 = (f32[27]{0:T(128)S(1)}, f32[27]{0:T(128)}, u32[]{:S(2)}) copy-start(f32[27]{0:T(128)} %constant.147) | copy-start | bytes 328
  96.1 3.1 %copy-start.14 = (f32[27]{0:T(128)S(1)}, f32[27]{0:T(128)}, u32[]{:S(2)}) copy-start(f32[27]{0:T(128)} %constant.148) | copy-start | bytes 328
  99.2 22.8 %copy-start.7 = (s32[2,2,4]{2,1,0:T(2,128)S(1)}, s32[2,2,4]{2,1,0:T(2,128)}, u32[]{:S(2)}) copy-start(s32[2,2,4]{2,1,0:T(2,128)} %param.16) | copy-start | bytes 196

commit v6 on v5

--- a/solution.py
+++ b/solution.py
@@ -267,16 +267,19 @@
     source = jnp.take(
         padded_around.reshape(4, -1, slot_count), box_rows, axis=1
     ).reshape(4, len(moves), 2, 2, layers, slot_count)
-    move = jnp.array(moves, jnp.float32)
-    shape6 = (len(moves), 1, 1, 1, 1, 1)
-    delta_x = packed[0][None, ..., :, None] - source[0][..., None, :] - move[:, 0].reshape(shape6)
-    delta_y = packed[1][None, ..., :, None] - source[1][..., None, :] - move[:, 1].reshape(shape6)
-    delta_z = packed[2][None, ..., :, None] - source[2][..., None, :] - move[:, 2].reshape(shape6)
+    source = source.reshape(4, len(moves), 4 * layers, slot_count).transpose(0, 2, 1, 3)
+    source = source.reshape(4, 4 * layers, len(moves) * slot_count)
+    move = np.repeat(np.array(moves, np.float32), slot_count, axis=0)
+    own = packed.reshape(4, 4 * layers, slot_count)
+    delta_x = own[0][..., :, None] - source[0][..., None, :] - move[:, 0]
+    delta_y = own[1][..., :, None] - source[1][..., None, :] - move[:, 1]
+    delta_z = own[2][..., :, None] - source[2][..., None, :] - move[:, 2]
     kernel = lax.rsqrt(delta_x * delta_x + delta_y * delta_y + delta_z * delta_z + softening_sq)
-    diagonal = jnp.arange(slot_count)[:, None] == jnp.arange(slot_count)[None, :]
-    centre = (jnp.arange(len(moves)) == 13).reshape(shape6)
-    kernel = jnp.where(centre & diagonal, 0.0, kernel)
-    near = jnp.sum(jnp.sum(kernel * source[3][..., None, :], axis=-1), axis=0)
+    centre = moves.index((0, 0, 0))
+    column = jnp.arange(len(moves) * slot_count)[None, :]
+    itself = column == jnp.arange(slot_count)[:, None] + centre * slot_count
+    kernel = jnp.where(itself, 0.0, kernel)
+    near = jnp.sum(kernel * source[3][..., None, :], axis=-1).reshape(2, 2, layers, slot_count)
 
     leaf_down_pts = 0.5 + 1.8 * unit_sphere
     leaf_far = point_sum(offsets, leaf_down_pts[:, None, None, None, :], leaf_local)

time: 123 us -> 121 us (0.984)
  other arithmetic: 44.2 us -> 41.4 us
    reduce_sum x1, other arithmetic: 22.8 us -> 20 us  [shards(): jnp.sum(kernel * source[3][..., None, :], axis=-1)]
    gather x1 -> x2, local copies, waits for them, and re-layouts: 2.27 us -> 2.79 us  [shards(): jnp.take(padded_around.reshape(4, -1, slot_count), box_rows, axis=1)]
where the time goes in v6:
time: 121 us; the launch traced here: 120 us
  Pallas kernels  47.3 us (39%)
  other arithmetic  41.4 us (34%)
  starting transfers between devices  16.5 us (14%)
  local copies, waits for them, and re-layouts  6.79 us (6%)
  waiting for transfers between devices  6.51 us (5%)
    pallas_call x1, Pallas kernels, m2l(): pl.pallas_call(functools.partial(m2l_kernel, shift_count, 128), out_shape...  47.3 us
    reduce_sum x1, other arithmetic, shards(): jnp.sum(kernel * source[3][..., None, :], axis=-1)  20 us
    reduce_sum x5, other arithmetic, point_sum(): return jnp.sum(kernel * weights[..., None, :], axis=-1)  15.8 us
    ppermute x5, starting transfers between devices, rel_gather(): lax.ppermute(part, axis, [(j, (j - have) % count) for j in range(count)])  8.79 us
    ppermute x5, waiting for transfers between devices, rel_gather(): lax.ppermute(part, axis, [(j, (j - have) % count) for j in range(count)])  6.49 us
    ppermute x2, starting transfers between devices, exchange(): lax.ppermute(sent_head, axis, [((i + 1) % count, i) for i in range(count)])  5.55 us
    gather x2, local copies, waits for them, and re-layouts, shards(): jnp.take(padded_around.reshape(4, -1, slot_count), box_rows, axis=1)  2.79 us
  transfers between devices with their start and end apart: 9, of which 3 were waited for; matrix products, arithmetic and copies ran while one was open for 14% of the time, Pallas kernels for 0%

profile of v6, /device:TPU:0, one launch (start us, length us, event | category | flops | bytes accessed | tf_op | source)
XLA Modules:
  0.0 120.4 jit_solution(16549963247376388334)
XLA Ops:
  0.0 0.1 cosine_multiply_fusion.1
  0.1 0.1 sine_multiply_fusion.1
  0.1 0.8 fusion.24
  0.9 0.8 fusion.46
  1.7 0.7 fusion.35
  2.4 1.1 multiply_reduce_fusion.4
  3.5 0.3 fusion.21
  3.9 0.7 fusion.23
  4.6 0.5 collective-permute-start
  5.1 2.9 %collective-permute-start.1 = (f32[8192]{0:T(1024)S(1)}, f32[8192]{0:T(1024)S(1)}, u32[]{:S(2)}, u32[]{:S(2)}) collective-permute-start(f32[8192]{0:T(1024)S(1)} %get-tuple-element.29), channel_id=1, source_target_pairs={{4,0},{8,4},{12,8},{16,12},{20,16},{24,20},{28,24},{0,28},{5,1},{9... | collective-permute-start | bytes 98312 | tf_op jit(solution)/shard_map/ppermute | solution.py:76
  8.3 0.1 broadcast_add_fusion.8
  8.4 0.8 add_rsqrt_fusion
  9.2 0.4 multiply_reduce_fusion.1
  9.7 0.3 convolution_bitcast_fusion
  10.0 4.4 %collective-permute-start.4 = (f32[1,1,2,256]{3,2,1,0:T(2,128)S(1)}, f32[1,1,2,256]{3,2,1,0:T(2,128)S(1)}, u32[]{:S(2)}, u32[]{:S(2)}) collective-permute-start(f32[1,1,2,256]{3,2,1,0:T(2,128)S(1)} %convolution_bitcast_fusion), channel_id=1, source_target_pairs={{0,3},{1,0},{2,1},{3,2},{4,7},{5,4},{6,5},{7,6},{8,11},{9,8},{10,9... | collective-permute-start | bytes 6152 | tf_op jit(solution)/shard_map/ppermute | solution.py:61
  14.4 0.1 fusion.28
  14.5 0.1 fusion.30
  14.7 0.1 subtract_multiply_fusion.2
  14.8 0.3 iota_compare_fusion
  15.1 0.1 subtract_multiply_fusion.3
  15.2 0.1 broadcast_add_fusion.4
  15.2 0.1 subtract_multiply_fusion
  15.4 0.1 broadcast_add_fusion.5
  15.4 0.1 broadcast_add_fusion.1
  15.5 0.1 broadcast_add_fusion
  15.6 1.2 %collective-permute-start.5 = (f32[1,2,2,256]{3,2,1,0:T(2,128)S(1)}, f32[1,2,2,256]{3,2,1,0:T(2,128)S(1)}, u32[]{:S(2)}, u32[]{:S(2)}) collective-permute-start(f32[1,2,2,256]{3,2,1,0:T(2,128)S(1)} %pad_maximum_fusion.14), channel_id=1, source_target_pairs={{0,2},{1,3},{2,0},{3,1},{4,6},{5,7},{6,4},{7,5},{8,10},{9,11},{10,... | collective-permute-start | bytes 12296 | tf_op jit(solution)/shard_map/ppermute | solution.py:61
  16.9 0.1 pad_maximum_fusion.base_ref
  16.9 3.3 %collective-permute-done.5 = f32[1,2,2,256]{3,2,1,0:T(2,128)S(1)} collective-permute-done((f32[1,2,2,256]{3,2,1,0:T(2,128)S(1)}, f32[1,2,2,256]{3,2,1,0:T(2,128)S(1)}, u32[]{:S(2)}, u32[]{:S(2)}) %collective-permute-start.5) | collective-permute-done | bytes 4128 | tf_op jit(solution)/shard_map/ppermute | solution.py:61
  20.3 1.3 %collective-permute-done.6 = f32[1,4,2,256]{3,2,1,0:T(2,128)S(1)} collective-permute-done((f32[1,4,2,256]{3,2,1,0:T(2,128)S(1)}, f32[1,4,2,256]{3,2,1,0:T(2,128)S(1)}, u32[]{:S(2)}, u32[]{:S(2)}) %collective-permute-start.6) | collective-permute-done | bytes 8224 | tf_op jit(solution)/shard_map/ppermute | solution.py:61
  21.6 1.6 %collective-permute-start.7 = (f32[2,4,2,256]{3,2,1,0:T(2,128)S(1)}, f32[2,4,2,256]{3,2,1,0:T(2,128)S(1)}, u32[]{:S(2)}, u32[]{:S(2)}) collective-permute-start(f32[2,4,2,256]{3,2,1,0:T(2,128)S(1)} %pad_maximum_fusion.11), channel_id=1, source_target_pairs={{0,24},{4,28},{8,0},{12,4},{16,8},{20,12},{24,16},{28,20},{1,25},{... | collective-permute-start | bytes 49160 | tf_op jit(solution)/shard_map/ppermute | solution.py:61
  23.2 0.1 stack_broadcast_in_dim.41
  23.5 1.9 %collective-permute-done.7 = f32[2,4,2,256]{3,2,1,0:T(2,128)S(1)} collective-permute-done((f32[2,4,2,256]{3,2,1,0:T(2,128)S(1)}, f32[2,4,2,256]{3,2,1,0:T(2,128)S(1)}, u32[]{:S(2)}, u32[]{:S(2)}) %collective-permute-start.7) | collective-permute-done | bytes 16416 | tf_op jit(solution)/shard_map/ppermute | solution.py:61
  25.4 1.6 %collective-permute-start.8 = (f32[4,4,2,256]{3,2,1,0:T(2,128)S(1)}, f32[4,4,2,256]{3,2,1,0:T(2,128)S(1)}, u32[]{:S(2)}, u32[]{:S(2)}) collective-permute-start(f32[4,4,2,256]{3,2,1,0:T(2,128)S(1)} %pad_maximum_fusion.9), channel_id=1, source_target_pairs={{0,16},{4,20},{8,24},{12,28},{16,0},{20,4},{24,8},{28,12},{1,17},{... | collective-permute-start | bytes 98312 | tf_op jit(solution)/shard_map/ppermute | solution.py:61
  27.2 1.7 %collective-permute-start.2 = (f32[20480]{0:T(1024)S(1)}, f32[20480]{0:T(1024)S(1)}, u32[]{:S(2)}, u32[]{:S(2)}) collective-permute-start(f32[20480]{0:T(1024)S(1)} %get-tuple-element.11), channel_id=1, source_target_pairs={{0,1},{1,2},{2,3},{3,0},{4,5},{5,6},{6,7},{7,4},{8,9},{9,10},{10,1... | collective-permute-start | bytes 245768 | tf_op jit(solution)/shard_map/ppermute | solution.py:75
  28.9 2.6 %collective-permute-start.3 = (f32[20480]{0:T(1024)S(1)}, f32[20480]{0:T(1024)S(1)}, u32[]{:S(2)}, u32[]{:S(2)}) collective-permute-start(f32[20480]{0:T(1024)S(1)} %get-tuple-element.12), channel_id=1, source_target_pairs={{1,0},{2,1},{3,2},{0,3},{5,4},{6,5},{7,6},{4,7},{9,8},{10,9},{11,1... | collective-permute-start | bytes 245768 | tf_op jit(solution)/shard_map/ppermute | solution.py:76
  31.5 0.6 gather_fusion.1
  32.2 11.7 %multiply_reduce_fusion = f32[2,256]{1,0:T(2,128)S(1)} fusion(f32[11776]{0:T(1024)S(1)} %select_n.55, f32[2,11776]{1,0:T(2,128)S(1)} %stack_broadcast_in_dim.41, f32[256]{0:T(256)S(1)} %bitcast.181, f32[11776]{0:T(1024)S(1)} %stack_broadcast_in_dim.39, f32[256]{0:T(256)S(1)} %bitcast.182, f32[11776]{0:T(1024)S(1)} %stack_broadcast_in_dim.37, f32[256]{0:T(256)S(1)} %bitcast.180), kind=kLoop, calls=%fused_computation.12 | loop fusion | flops 66321920 | bytes 240640 | tf_op jit(solution)/shard_map/reduce_sum | solution.py:29
  43.9 0.3 fusion.39
  44.1 0.1 mul.507
  44.2 1.3 %multiply_reduce_fusion.2 = f32[2,2,4,128]{3,2,1,0:T(4,128)S(1)} fusion(f32[4,256]{1,0:T(4,128)S(1)} %mul.507, f32[256]{0:T(256)S(1)} %bitcast.171, f32[2,2,4,128]{3,2,1,0:T(4,128)S(1)} %get-tuple-element.27, f32[256]{0:T(256)S(1)} %bitcast.173, f32[2,2,4,128]{3,2,1,0:T(4,128)S(1)} %get-tuple-element.20, f32[256]{0:T(256)S(1)} %bitcast.169, ...), kind=kLoop, calls=%fused_computation.14 | loop fusion | flops 5765120 | bytes 39936 | tf_op jit(solution)/shard_map/reduce_sum | solution.py:29
  45.6 0.1 select_maximum_fusion
  45.8 0.1 fusion.17
  45.9 0.1 fusion.16
  46.0 0.1 fusion.15
  46.1 0.1 fusion.14
  46.2 0.1 fusion.13
  46.3 0.1 fusion.12
  46.4 0.3 copy.24
  46.8 0.2 copy-done.1
  47.0 47.3 %shard_map.154 = f32[16,256]{1,0:T(8,128)S(1)} custom-call(f32[474]{0:T(512)S(1)} %copy-done.2, s32[1264]{0:T(1024)S(1)} %copy-done.1, f32[3,256,256]{2,1,0:T(8,128)S(1)} %pad_maximum_fusion.base_ref, f32[448,4,256]{2,1,0:T(4,128)S(1)} %bitcast.130), custom_call_target="tpu_custom_call" | custom-call | flops 2133065728 | bytes 2637824 | tf_op jit(solution)/shard_map/pallas_call | solution.py:142
  94.3 0.3 fusion.19
  94.7 1.3 %multiply_reduce_fusion.3 = f32[2,2,4,128]{3,2,1,0:T(4,128)S(1)} fusion(f32[2,2,4,256]{3,2,1,0:T(4,128)S(1)} %fusion.19, f32[256]{0:T(256)S(1)} %bitcast.177, f32[2,2,4,128]{3,2,1,0:T(4,128)S(1)} %get-tuple-element.24, f32[256]{0:T(256)S(1)} %bitcast.175, f32[2,2,4,128]{3,2,1,0:T(4,128)S(1)} %get-tuple-element.23, f32[256]{0:T(256)S(1)} %bitcast.179, ...), kind=kLoop, calls=%fused_computation.16 | loop fusion | flops 5765120 | bytes 52224 | tf_op jit(solution)/shard_map/reduce_sum | solution.py:29
  96.1 0.1 copy.28
  96.2 2.3 %gather_fusion = f32[432,4,128]{2,1,0:T(4,128)S(1)} fusion(f32[4,96,128]{2,0,1:T(4,128)S(1)} %bitcast.131, s32[1024]{0:T(1024)S(1)} %pad_clamp_fusion.1), kind=kCustom, calls=%fused_computation | custom fusion | bytes 1771200 | tf_op jit(solution)/shard_map/jit(_take)/gather | solution.py:267
  98.5 0.5 copy.50
  99.0 0.1 fusion.31
  99.1 0.1 copy.51
  99.3 0.1 copy.52
  99.4 0.1 copy.53
  99.5 0.1 copy.54
  99.7 0.0 copy-done.12
  99.7 0.0 copy-done.13
  99.8 20.0 %fusion.5 = f32[16,128]{1,0:T(8,128)S(1)} fusion(f32[3456]{0:T(1024)S(1)} %copy-done.14, f32[3456]{0:T(1024)S(1)} %copy-done.13, f32[3456]{0:T(1024)S(1)} %copy-done.12, f32[16,3456]{1,0:T(8,128)S(1)} %bitcast.139, f32[16,3456]{1,0:T(8,128)S(1)} %bitcast.140, f32[16,128]{1,0:T(8,128)S(1)} %bitcast.165, f32[16,3456]{1,0:T(8,128)S(1)} %bitcast.141, ...), kind=kLoop, calls=%fused_computation.8 | loop fusion | flops 106166272 | bytes 1401344 | tf_op jit(solution)/shard_map/reduce_sum | solution.py:282
  119.8 0.7 add_select_fusion
  (95 shorter events, 1.1 us)
Async XLA Ops:
  0.0 3.5 %copy-start = (f32[256,256]{1,0:T(8,128)S(1)}, f32[256,256]{1,0:T(8,128)}, u32[]{:S(2)}) copy-start(f32[256,256]{1,0:T(8,128)} %param.19) | copy-start | bytes 786436
  4.6 22.4 %collective-permute-start = (f32[8192]{0:T(1024)S(1)}, f32[8192]{0:T(1024)S(1)}, u32[]{:S(2)}, u32[]{:S(2)}) collective-permute-start(f32[8192]{0:T(1024)S(1)} %get-tuple-element.28), channel_id=1, source_target_pairs={{0,4},{4,8},{8,12},{12,16},{16,20},{20,24},{24,28},{28,0},{1,5},{5... | collective-permute-start | bytes 98312 | tf_op jit(solution)/shard_map/ppermute | solution.py:75
  5.1 21.9 %collective-permute-start.1 = (f32[8192]{0:T(1024)S(1)}, f32[8192]{0:T(1024)S(1)}, u32[]{:S(2)}, u32[]{:S(2)}) collective-permute-start(f32[8192]{0:T(1024)S(1)} %get-tuple-element.29), channel_id=1, source_target_pairs={{4,0},{8,4},{12,8},{16,12},{20,16},{24,20},{28,24},{0,28},{5,1},{9... | collective-permute-start | bytes 98312 | tf_op jit(solution)/shard_map/ppermute | solution.py:76
  8.4 1.3 %copy-start.5 = (f32[256,256]{1,0:T(8,128)S(1)}, f32[256,256]{1,0:T(8,128)}, u32[]{:S(2)}) copy-start(f32[256,256]{1,0:T(8,128)} %param.21) | copy-start | bytes 786436
  8.4 6.7 %copy-start.3 = (f32[3,2,2,4,128]{4,3,2,1,0:T(4,128)S(1)}, f32[3,2,2,4,128]{4,3,2,1,0:T(4,128)}, u32[]{:S(2)}) copy-start(f32[3,2,2,4,128]{4,3,2,1,0:T(4,128)} %param.16) | copy-start | bytes 73732
  9.2 6.2 %copy-start.10 = (f32[23]{0:T(128)S(1)}, f32[23]{0:T(128)}, u32[]{:S(2)}) copy-start(f32[23]{0:T(128)} %constant.139) | copy-start | bytes 280
  9.2 6.3 %copy-start.11 = (f32[23]{0:T(128)S(1)}, f32[23]{0:T(128)}, u32[]{:S(2)}) copy-start(f32[23]{0:T(128)} %constant.140) | copy-start | bytes 280
  9.7 10.6 %copy-start.8 = (s32[432]{0:T(512)S(1)}, s32[432]{0:T(512)}, u32[]{:S(2)}) copy-start(s32[432]{0:T(512)} %constant.150) | copy-start | bytes 5188
  9.7 13.5 %copy-start.9 = (s32[23]{0:T(128)S(1)}, s32[23]{0:T(128)}, u32[]{:S(2)}) copy-start(s32[23]{0:T(128)} %constant.151) | copy-start | bytes 280
  10.0 5.7 %collective-permute-start.4 = (f32[1,1,2,256]{3,2,1,0:T(2,128)S(1)}, f32[1,1,2,256]{3,2,1,0:T(2,128)S(1)}, u32[]{:S(2)}, u32[]{:S(2)}) collective-permute-start(f32[1,1,2,256]{3,2,1,0:T(2,128)S(1)} %convolution_bitcast_fusion), channel_id=1, source_target_pairs={{0,3},{1,0},{2,1},{3,2},{4,7},{5,4},{6,5},{7,6},{8,11},{9,8},{10,9... | collective-permute-start | bytes 6152 | tf_op jit(solution)/shard_map/ppermute | solution.py:61
  15.6 4.6 %collective-permute-start.5 = (f32[1,2,2,256]{3,2,1,0:T(2,128)S(1)}, f32[1,2,2,256]{3,2,1,0:T(2,128)S(1)}, u32[]{:S(2)}, u32[]{:S(2)}) collective-permute-start(f32[1,2,2,256]{3,2,1,0:T(2,128)S(1)} %pad_maximum_fusion.14), channel_id=1, source_target_pairs={{0,2},{1,3},{2,0},{3,1},{4,6},{5,7},{6,4},{7,5},{8,10},{9,11},{10,... | collective-permute-start | bytes 12296 | tf_op jit(solution)/shard_map/ppermute | solution.py:61
  20.2 1.4 %collective-permute-start.6 = (f32[1,4,2,256]{3,2,1,0:T(2,128)S(1)}, f32[1,4,2,256]{3,2,1,0:T(2,128)S(1)}, u32[]{:S(2)}, u32[]{:S(2)}) collective-permute-start(f32[1,4,2,256]{3,2,1,0:T(2,128)S(1)} %pad_maximum_fusion.12), channel_id=1, source_target_pairs={{0,28},{4,0},{8,4},{12,8},{16,12},{20,16},{24,20},{28,24},{1,29},{... | collective-permute-start | bytes 24584 | tf_op jit(solution)/shard_map/ppermute | solution.py:61
  21.6 3.8 %collective-permute-start.7 = (f32[2,4,2,256]{3,2,1,0:T(2,128)S(1)}, f32[2,4,2,256]{3,2,1,0:T(2,128)S(1)}, u32[]{:S(2)}, u32[]{:S(2)}) collective-permute-start(f32[2,4,2,256]{3,2,1,0:T(2,128)S(1)} %pad_maximum_fusion.11), channel_id=1, source_target_pairs={{0,24},{4,28},{8,0},{12,4},{16,8},{20,12},{24,16},{28,20},{1,25},{... | collective-permute-start | bytes 49160 | tf_op jit(solution)/shard_map/ppermute | solution.py:61
  25.4 6.1 %collective-permute-start.8 = (f32[4,4,2,256]{3,2,1,0:T(2,128)S(1)}, f32[4,4,2,256]{3,2,1,0:T(2,128)S(1)}, u32[]{:S(2)}, u32[]{:S(2)}) collective-permute-start(f32[4,4,2,256]{3,2,1,0:T(2,128)S(1)} %pad_maximum_fusion.9), channel_id=1, source_target_pairs={{0,16},{4,20},{8,24},{12,28},{16,0},{20,4},{24,8},{28,12},{1,17},{... | collective-permute-start | bytes 98312 | tf_op jit(solution)/shard_map/ppermute | solution.py:61
  27.2 18.3 %collective-permute-start.2 = (f32[20480]{0:T(1024)S(1)}, f32[20480]{0:T(1024)S(1)}, u32[]{:S(2)}, u32[]{:S(2)}) collective-permute-start(f32[20480]{0:T(1024)S(1)} %get-tuple-element.11), channel_id=1, source_target_pairs={{0,1},{1,2},{2,3},{3,0},{4,5},{5,6},{6,7},{7,4},{8,9},{9,10},{10,1... | collective-permute-start | bytes 245768 | tf_op jit(solution)/shard_map/ppermute | solution.py:75
  28.9 16.7 %collective-permute-start.3 = (f32[20480]{0:T(1024)S(1)}, f32[20480]{0:T(1024)S(1)}, u32[]{:S(2)}, u32[]{:S(2)}) collective-permute-start(f32[20480]{0:T(1024)S(1)} %get-tuple-element.12), channel_id=1, source_target_pairs={{1,0},{2,1},{3,2},{0,3},{5,4},{6,5},{7,6},{4,7},{9,8},{10,9},{11,1... | collective-permute-start | bytes 245768 | tf_op jit(solution)/shard_map/ppermute | solution.py:76
  32.2 11.7 %copy-start.6 = (f32[256,256]{1,0:T(8,128)S(1)}, f32[256,256]{1,0:T(8,128)}, u32[]{:S(2)}) copy-start(f32[256,256]{1,0:T(8,128)} %param.22) | copy-start | bytes 786436
  46.3 0.7 copy-start.1
  46.3 0.7 copy-start.2
  47.0 47.3 %copy-start.4 = (f32[256,256]{1,0:T(8,128)S(1)}, f32[256,256]{1,0:T(8,128)}, u32[]{:S(2)}) copy-start(f32[256,256]{1,0:T(8,128)} %param.20) | copy-start | bytes 786436
  99.0 0.7 copy-start.12
  99.0 0.7 copy-start.13
  99.0 0.7 copy-start.14
  99.8 20.0 %copy-start.7 = (s32[2,2,4]{2,1,0:T(2,128)S(1)}, s32[2,2,4]{2,1,0:T(2,128)}, u32[]{:S(2)}) copy-start(s32[2,2,4]{2,1,0:T(2,128)} %param.18) | copy-start | bytes 196

commit v7 on v6

--- a/solution.py
+++ b/solution.py
@@ -194,7 +194,16 @@
     count_x = lax.axis_size("gx")
     count_y = lax.axis_size("gy")
 
-    gathered = rel_gather(rel_gather(parent_eq[None, None], "gy", 1), "gx", 0)
+    own_x = lax.axis_index("gx")
+    own_y = lax.axis_index("gy")
+    every = lax.all_gather(parent_eq, ("gx", "gy"), axis=0, tiled=False).reshape(
+        count_x, count_y, parent_layers, points
+    )
+    twice = jnp.concatenate([every, every], axis=0)
+    twice = jnp.concatenate([twice, twice], axis=1)
+    gathered = lax.dynamic_slice(
+        twice, (own_x, own_y, 0, 0), (count_x, count_y, parent_layers, points)
+    )
     kept = []
     for rel_x in range(count_x):
         for rel_y in range(count_y):

time: 121 us -> 176 us (1.45)
  blocking collectives: 0 us -> 67.6 us
  starting transfers between devices: 16.5 us -> 7.32 us
  waiting for transfers between devices: 6.51 us -> 2.37 us
    all_gather x0 -> x1, blocking collectives: none -> 67.6 us  [shards(): lax.all_gather(parent_eq, ('gx', 'gy'), axis=0, tiled=False)]
    ppermute x5 -> x0, starting transfers between devices: 8.79 us -> none  [rel_gather(): lax.ppermute(part, axis, [(j, (j - have) % count) for j in range(count)])]
    ppermute x5 -> x0, waiting for transfers between devices: 6.49 us -> none  [rel_gather(): lax.ppermute(part, axis, [(j, (j - have) % count) for j in range(count)])]
    ppermute x2, waiting for transfers between devices: 0.01 us -> 2.36 us  [exchange(): lax.ppermute(sent_tail, axis, [(i, (i + 1) % count) for i in range(count)])]
  transfers between devices with their start and end apart: 9 -> 4, of which waited for: 3 -> 1; matrix products, arithmetic and copies ran while one was open for 14% -> 10% of each run, Pallas kernels for 0% -> 0%
where the time goes in v7:
time: 176 us; the launch traced here: 175 us
  blocking collectives  67.6 us (38%)
  Pallas kernels  47.3 us (27%)
  other arithmetic  41.7 us (24%)
  starting transfers between devices  7.32 us (4%)
  local copies, waits for them, and re-layouts  6.8 us (4%)
  waiting for transfers between devices  2.37 us (1%)
    all_gather x1, blocking collectives, shards(): lax.all_gather(parent_eq, ('gx', 'gy'), axis=0, tiled=False)  67.6 us
    pallas_call x1, Pallas kernels, m2l(): pl.pallas_call(functools.partial(m2l_kernel, shift_count, 128), out_shape...  47.3 us
    reduce_sum x1, other arithmetic, shards(): jnp.sum(kernel * source[3][..., None, :], axis=-1)  20 us
    reduce_sum x5, other arithmetic, point_sum(): return jnp.sum(kernel * weights[..., None, :], axis=-1)  15.8 us
    ppermute x2, starting transfers between devices, exchange(): lax.ppermute(sent_head, axis, [((i + 1) % count, i) for i in range(count)])  6.76 us
  transfers between devices with their start and end apart: 4, of which 1 were waited for; matrix products, arithmetic and copies ran while one was open for 10% of the time, Pallas kernels for 0%

profile of v7, /device:TPU:0, one launch (start us, length us, event | category | flops | bytes accessed | tf_op | source)
XLA Modules:
  0.0 174.9 jit_solution(2645948322804720586)
XLA Ops:
  0.0 0.1 cosine_multiply_fusion.1
  0.1 0.1 sine_multiply_fusion.1
  0.1 0.8 fusion.27
  0.9 0.8 fusion.49
  1.7 0.7 fusion.38
  2.4 1.1 multiply_reduce_fusion.4
  3.5 0.3 fusion.21
  3.9 0.7 fusion.26
  4.6 0.5 collective-permute-start
  5.1 2.9 %collective-permute-start.1 = (f32[8192]{0:T(1024)S(1)}, f32[8192]{0:T(1024)S(1)}, u32[]{:S(2)}, u32[]{:S(2)}) collective-permute-start(f32[8192]{0:T(1024)S(1)} %get-tuple-element.29), channel_id=1, source_target_pairs={{4,0},{8,4},{12,8},{16,12},{20,16},{24,20},{28,24},{0,28},{5,1},{9... | collective-permute-start | bytes 98312 | tf_op jit(solution)/shard_map/ppermute | solution.py:76
  8.3 0.1 fusion.31
  8.4 0.1 fusion.33
  8.6 0.3 iota_compare_fusion
  8.9 0.1 broadcast_add_fusion.8
  9.1 0.0 copy-start.8
  9.1 0.0 copy-start.11
  9.1 0.0 copy-start.10
  9.1 0.8 add_rsqrt_fusion
  9.9 0.4 multiply_reduce_fusion.1
  10.3 0.3 convolution_bitcast_fusion
  10.6 67.6 %all-gather.1 = f32[32,2,256]{2,1,0:T(2,128)S(1)} all-gather(f32[1,2,256]{2,1,0:T(2,128)S(1)} %convolution_bitcast_fusion), channel_id=2, replica_groups=mesh['gx'=8,'gy'=4] {'gx','gy'}, dimensions={0}, use_global_device_ids=true | all-gather | bytes 67584 | tf_op jit(solution)/shard_map/all_gather | solution.py:199
  78.2 0.3 fusion.25
  78.5 0.6 gather_fusion.1
  79.2 0.1 subtract_multiply_fusion.3
  79.3 0.1 broadcast_add_fusion.5
  79.4 0.1 stack_broadcast_in_dim.41
  79.5 0.1 broadcast_add_fusion.1
  79.7 0.1 broadcast_add_fusion
  79.9 11.6 %multiply_reduce_fusion = f32[2,256]{1,0:T(2,128)S(1)} fusion(f32[11776]{0:T(1024)S(1)} %select_n.63, f32[2,11776]{1,0:T(2,128)S(1)} %stack_broadcast_in_dim.41, f32[256]{0:T(256)S(1)} %bitcast.183, f32[11776]{0:T(1024)S(1)} %stack_broadcast_in_dim.39, f32[256]{0:T(256)S(1)} %bitcast.184, f32[11776]{0:T(1024)S(1)} %stack_broadcast_in_dim.37, f32[256]{0:T(256)S(1)} %bitcast.182), kind=kLoop, calls=%fused_computation.12 | loop fusion | flops 66321920 | bytes 240640 | tf_op jit(solution)/shard_map/reduce_sum | solution.py:29
  91.5 0.3 fusion.42
  91.8 0.1 mul.507
  91.9 0.1 broadcast_add_fusion.4
  91.9 0.1 subtract_multiply_fusion
  92.1 1.3 multiply_reduce_fusion.2
  93.4 0.1 subtract_multiply_fusion.2
  93.7 0.1 collective-permute-start.2
  93.8 3.8 %collective-permute-start.3 = (f32[20480]{0:T(1024)S(1)}, f32[20480]{0:T(1024)S(1)}, u32[]{:S(2)}, u32[]{:S(2)}) collective-permute-start(f32[20480]{0:T(1024)S(1)} %get-tuple-element.12), channel_id=1, source_target_pairs={{1,0},{2,1},{3,2},{0,3},{5,4},{6,5},{7,6},{4,7},{9,8},{10,9},{11,1... | collective-permute-start | bytes 245768 | tf_op jit(solution)/shard_map/ppermute | solution.py:76
  97.6 0.1 pad_maximum_fusion.base_ref
  97.7 2.4 %collective-permute-done.2 = f32[20480]{0:T(1024)S(1)} collective-permute-done((f32[20480]{0:T(1024)S(1)}, f32[20480]{0:T(1024)S(1)}, u32[]{:S(2)}, u32[]{:S(2)}) %collective-permute-start.2) | collective-permute-done | bytes 81952 | tf_op jit(solution)/shard_map/ppermute | solution.py:75
  100.1 0.1 select_maximum_fusion
  100.3 0.1 fusion.17
  100.4 0.1 fusion.16
  100.5 0.1 fusion.15
  100.6 0.1 fusion.14
  100.7 0.1 fusion.13
  100.8 0.1 fusion.12
  100.9 0.3 copy.28
  101.2 0.2 copy-done.1
  101.5 47.3 %shard_map.154 = f32[16,256]{1,0:T(8,128)S(1)} custom-call(f32[474]{0:T(512)S(1)} %copy-done.2, s32[1264]{0:T(1024)S(1)} %copy-done.1, f32[3,256,256]{2,1,0:T(8,128)S(1)} %pad_maximum_fusion.base_ref, f32[448,4,256]{2,1,0:T(4,128)S(1)} %bitcast.131), custom_call_target="tpu_custom_call" | custom-call | flops 2133065728 | bytes 2637824 | tf_op jit(solution)/shard_map/pallas_call | solution.py:142
  148.8 0.3 fusion.19
  149.2 1.3 multiply_reduce_fusion.3
  150.5 0.1 copy.32
  150.7 2.3 %gather_fusion = f32[432,4,128]{2,1,0:T(4,128)S(1)} fusion(f32[4,96,128]{2,0,1:T(4,128)S(1)} %bitcast.132, s32[1024]{0:T(1024)S(1)} %get-tuple-element.48), kind=kCustom, calls=%fused_computation | custom fusion | bytes 1771200 | tf_op jit(solution)/shard_map/jit(_take)/gather | solution.py:276
  153.0 0.5 copy.54
  153.5 0.1 fusion.34
  153.6 0.1 copy.55
  153.7 0.1 copy.56
  153.9 0.1 copy.57
  154.0 0.1 copy.58
  154.2 0.0 copy-done.12
  154.2 0.0 copy-done.13
  154.2 0.0 copy-done.14
  154.2 20.0 %fusion.5 = f32[16,128]{1,0:T(8,128)S(1)} fusion(f32[3456]{0:T(1024)S(1)} %copy-done.14, f32[3456]{0:T(1024)S(1)} %copy-done.13, f32[3456]{0:T(1024)S(1)} %copy-done.12, f32[16,3456]{1,0:T(8,128)S(1)} %bitcast.141, f32[16,3456]{1,0:T(8,128)S(1)} %bitcast.142, f32[16,128]{1,0:T(8,128)S(1)} %bitcast.167, f32[16,3456]{1,0:T(8,128)S(1)} %bitcast.143, ...), kind=kLoop, calls=%fused_computation.8 | loop fusion | flops 106166272 | bytes 1401344 | tf_op jit(solution)/shard_map/reduce_sum | solution.py:291
  174.3 0.7 add_select_fusion
  (81 shorter events, 1.0 us)
Async XLA Ops:
  0.0 3.5 %copy-start = (f32[256,256]{1,0:T(8,128)S(1)}, f32[256,256]{1,0:T(8,128)}, u32[]{:S(2)}) copy-start(f32[256,256]{1,0:T(8,128)} %param.19) | copy-start | bytes 786436
  4.6 88.9 %collective-permute-start = (f32[8192]{0:T(1024)S(1)}, f32[8192]{0:T(1024)S(1)}, u32[]{:S(2)}, u32[]{:S(2)}) collective-permute-start(f32[8192]{0:T(1024)S(1)} %get-tuple-element.28), channel_id=1, source_target_pairs={{0,4},{4,8},{8,12},{12,16},{16,20},{20,24},{24,28},{28,0},{1,5},{5... | collective-permute-start | bytes 98312 | tf_op jit(solution)/shard_map/ppermute | solution.py:75
  5.1 88.4 %collective-permute-start.1 = (f32[8192]{0:T(1024)S(1)}, f32[8192]{0:T(1024)S(1)}, u32[]{:S(2)}, u32[]{:S(2)}) collective-permute-start(f32[8192]{0:T(1024)S(1)} %get-tuple-element.29), channel_id=1, source_target_pairs={{4,0},{8,4},{12,8},{16,12},{20,16},{24,20},{28,24},{0,28},{5,1},{9... | collective-permute-start | bytes 98312 | tf_op jit(solution)/shard_map/ppermute | solution.py:76
  9.1 1.3 copy-start.5
  9.1 69.1 %copy-start.8 = (s32[432]{0:T(512)S(1)}, s32[432]{0:T(512)}, u32[]{:S(2)}) copy-start(s32[432]{0:T(512)} %constant.163) | copy-start | bytes 5188
  9.1 69.1 %copy-start.11 = (s32[23]{0:T(128)S(1)}, s32[23]{0:T(128)}, u32[]{:S(2)}) copy-start(s32[23]{0:T(128)} %constant.164) | copy-start | bytes 280
  9.1 70.4 %copy-start.10 = (f32[23]{0:T(128)S(1)}, f32[23]{0:T(128)}, u32[]{:S(2)}) copy-start(f32[23]{0:T(128)} %constant.152) | copy-start | bytes 280
  9.9 69.8 %copy-start.9 = (f32[23]{0:T(128)S(1)}, f32[23]{0:T(128)}, u32[]{:S(2)}) copy-start(f32[23]{0:T(128)} %constant.153) | copy-start | bytes 280
  79.8 11.7 %copy-start.6 = (f32[256,256]{1,0:T(8,128)S(1)}, f32[256,256]{1,0:T(8,128)}, u32[]{:S(2)}) copy-start(f32[256,256]{1,0:T(8,128)} %param.22) | copy-start | bytes 786436
  79.8 12.0 %copy-start.3 = (f32[3,2,2,4,128]{4,3,2,1,0:T(4,128)S(1)}, f32[3,2,2,4,128]{4,3,2,1,0:T(4,128)}, u32[]{:S(2)}) copy-start(f32[3,2,2,4,128]{4,3,2,1,0:T(4,128)} %param.16) | copy-start | bytes 73732
  93.7 6.3 %collective-permute-start.2 = (f32[20480]{0:T(1024)S(1)}, f32[20480]{0:T(1024)S(1)}, u32[]{:S(2)}, u32[]{:S(2)}) collective-permute-start(f32[20480]{0:T(1024)S(1)} %get-tuple-element.11), channel_id=1, source_target_pairs={{0,1},{1,2},{2,3},{3,0},{4,5},{5,6},{6,7},{7,4},{8,9},{9,10},{10,1... | collective-permute-start | bytes 245768 | tf_op jit(solution)/shard_map/ppermute | solution.py:75
  93.8 6.3 %collective-permute-start.3 = (f32[20480]{0:T(1024)S(1)}, f32[20480]{0:T(1024)S(1)}, u32[]{:S(2)}, u32[]{:S(2)}) collective-permute-start(f32[20480]{0:T(1024)S(1)} %get-tuple-element.12), channel_id=1, source_target_pairs={{1,0},{2,1},{3,2},{0,3},{5,4},{6,5},{7,6},{4,7},{9,8},{10,9},{11,1... | collective-permute-start | bytes 245768 | tf_op jit(solution)/shard_map/ppermute | solution.py:76
  100.8 0.7 copy-start.1
  100.8 0.7 copy-start.2
  101.5 47.3 %copy-start.4 = (f32[256,256]{1,0:T(8,128)S(1)}, f32[256,256]{1,0:T(8,128)}, u32[]{:S(2)}) copy-start(f32[256,256]{1,0:T(8,128)} %param.20) | copy-start | bytes 786436
  153.5 0.7 copy-start.12
  153.5 0.7 copy-start.13
  153.5 0.7 copy-start.14
  154.2 20.0 %copy-start.7 = (s32[2,2,4]{2,1,0:T(2,128)S(1)}, s32[2,2,4]{2,1,0:T(2,128)}, u32[]{:S(2)}) copy-start(s32[2,2,4]{2,1,0:T(2,128)} %param.18) | copy-start | bytes 196

commit v8 on v6

--- a/solution.py
+++ b/solution.py
@@ -182,6 +182,7 @@
     leaf_eq = jnp.einsum("ec,xyzc->xyze", c2e_leaf_up, leaf_check, precision=highest)
     packed_x, eq_x = exchange([(packed, 1, 1), (leaf_eq, 0, 2)], "gx")
     beside_all, cycle = exchange([(packed_x, 2, 1), (eq_x, 1, 2)], "gy")
+    leaf_eq, beside_all, cycle = lax.optimization_barrier((leaf_eq, beside_all, cycle))
     children = child_points(unit_sphere)
     parent_weights = (
         leaf_eq.reshape(2, 2, parent_layers, 2, points)

time: 121 us -> 140 us (1.16)
  local copies, waits for them, and re-layouts: 6.79 us -> 20.8 us
  other arithmetic: 41.4 us -> 46 us
  waiting for transfers between devices: 6.51 us -> 8.74 us
  starting transfers between devices: 16.5 us -> 14.8 us
    unnamed x46 -> x120, local copies, waits for them, and re-layouts: 1.54 us -> 5.28 us
    ppermute x2, waiting for transfers between devices: 0.01 us -> 2.1 us  [exchange(): lax.ppermute(sent_tail, axis, [(i, (i + 1) % count) for i in range(count)])]
    reshape x2, local copies, waits for them, and re-layouts: 0.03 us -> 1.98 us  [shards(): leaf_eq.reshape(2, 2, parent_layers, 2, points).transpose(2, 0, 1, 3, 4)]
    another operation x6, local copies, waits for them, and re-layouts: 0.25 us -> 2.1 us  [shards(): jnp.stack([jnp.broadcast_to(kept_x[None, :, None, None] + 1.8 * unit_sphe...]
    ppermute x5, starting transfers between devices: 8.79 us -> 6.99 us  [rel_gather(): lax.ppermute(part, axis, [(j, (j - have) % count) for j in range(count)])]
    gather x2, local copies, waits for them, and re-layouts: 2.79 us -> 4.38 us  [shards(): jnp.take(padded_around.reshape(4, -1, slot_count), box_rows, axis=1)]
    slice x5, local copies, waits for them, and re-layouts: 0.05 us -> 1.6 us  [exchange(): after = from_right[start:start + size].reshape(head.shape)]
  transfers between devices with their start and end apart: 9 -> 9, of which waited for: 3 -> 5; matrix products, arithmetic and copies ran while one was open for 14% -> 22% of each run, Pallas kernels for 0% -> 34%
where the time goes in v8:
time: 140 us
  Pallas kernels  47.3 us (34%)
  other arithmetic  46 us (33%)
  local copies, waits for them, and re-layouts  20.8 us (15%)
  starting transfers between devices  14.8 us (11%)
  waiting for transfers between devices  8.74 us (6%)
    pallas_call x1, Pallas kernels, m2l(): pl.pallas_call(functools.partial(m2l_kernel, shift_count, 128), out_shape...  47.3 us
    reduce_sum x1, other arithmetic, shards(): jnp.sum(kernel * source[3][..., None, :], axis=-1)  20 us
    reduce_sum x5, other arithmetic, point_sum(): return jnp.sum(kernel * weights[..., None, :], axis=-1)  16.6 us
    ppermute x5, starting transfers between devices, rel_gather(): lax.ppermute(part, axis, [(j, (j - have) % count) for j in range(count)])  6.99 us
    ppermute x5, waiting for transfers between devices, rel_gather(): lax.ppermute(part, axis, [(j, (j - have) % count) for j in range(count)])  6.52 us
    unnamed x120, local copies, waits for them, and re-layouts  5.28 us
    ppermute x2, starting transfers between devices, exchange(): lax.ppermute(sent_head, axis, [((i + 1) % count, i) for i in range(count)])  4.97 us
    gather x2, local copies, waits for them, and re-layouts, shards(): jnp.take(padded_around.reshape(4, -1, slot_count), box_rows, axis=1)  4.38 us
  transfers between devices with their start and end apart: 9, of which 5 were waited for; matrix products, arithmetic and copies ran while one was open for 22% of the time, Pallas kernels for 34%

profile of v8, /device:TPU:0, one launch (start us, length us, event | category | flops | bytes accessed | tf_op | source)
XLA Modules:
  0.0 139.8 jit_solution(1436617784786649414)
XLA Ops:
  0.1 0.8 fusion.26
  0.9 0.8 fusion.48
  1.7 1.3 fusion.37
  3.1 1.1 multiply_reduce_fusion.4
  4.2 0.3 fusion.23
  4.6 0.7 fusion.25
  5.3 0.5 collective-permute-start
  5.9 2.9 %collective-permute-start.1 = (f32[8192]{0:T(1024)S(1)}, f32[8192]{0:T(1024)S(1)}, u32[]{:S(2)}, u32[]{:S(2)}) collective-permute-start(f32[8192]{0:T(1024)S(1)} %get-tuple-element.35), channel_id=1, source_target_pairs={{4,0},{8,4},{12,8},{16,12},{20,16},{24,20},{28,24},{0,28},{5,1},{9... | collective-permute-start | bytes 98312 | tf_op jit(solution)/shard_map/ppermute | solution.py:76
  9.3 0.1 subtract_multiply_fusion.2
  9.4 1.1 iota_compare_fusion
  10.6 0.6 fusion.40
  11.2 0.1 subtract_multiply_fusion.3
  11.3 0.7 broadcast_add_fusion.4
  12.0 0.1 subtract_multiply_fusion
  12.1 0.1 broadcast_add_fusion.5
  12.4 0.8 add_rsqrt_fusion
  13.2 0.6 pad_clamp_fusion.1
  13.8 0.7 stack_broadcast_in_dim.41
  14.6 0.7 stack_broadcast_in_dim.37
  15.3 0.7 stack_broadcast_in_dim.39
  16.1 0.6 pad_maximum_fusion.4
  16.7 2.3 %collective-permute-start.2 = (f32[20480]{0:T(1024)S(1)}, f32[20480]{0:T(1024)S(1)}, u32[]{:S(2)}, u32[]{:S(2)}) collective-permute-start(f32[20480]{0:T(1024)S(1)} %get-tuple-element.17), channel_id=1, source_target_pairs={{0,1},{1,2},{2,3},{3,0},{4,5},{5,6},{6,7},{7,4},{8,9},{9,10},{10,1... | collective-permute-start | bytes 245768 | tf_op jit(solution)/shard_map/ppermute | solution.py:75
  19.0 2.0 %collective-permute-start.3 = (f32[20480]{0:T(1024)}, f32[20480]{0:T(1024)}, u32[]{:S(2)}, u32[]{:S(2)}) collective-permute-start(f32[20480]{0:T(1024)} %get-tuple-element.18), channel_id=1, source_target_pairs={{1,0},{2,1},{3,2},{0,3},{5,4},{6,5},{7,6},{4,7},{9,8},{10,9},{11,1... | collective-permute-start | bytes 245768 | tf_op jit(solution)/shard_map/ppermute | solution.py:76
  21.0 1.3 pad_clamp_fusion
  22.3 2.1 %collective-permute-done.2 = f32[20480]{0:T(1024)S(1)} collective-permute-done((f32[20480]{0:T(1024)S(1)}, f32[20480]{0:T(1024)S(1)}, u32[]{:S(2)}, u32[]{:S(2)}) %collective-permute-start.2) | collective-permute-done | bytes 81952 | tf_op jit(solution)/shard_map/ppermute | solution.py:75
  24.4 0.1 collective-permute-done.3
  24.5 0.8 slice.298
  25.4 0.8 slice.294
  26.2 0.8 slice.296
  27.0 0.1 fusion.10
  27.1 0.1 fusion.12
  27.3 0.1 fusion.16
  27.4 1.2 copy-done.3
  28.6 0.1 copy.28
  28.7 2.7 %gather_fusion = f32[432,4,128]{2,1,0:T(4,128)} fusion(f32[4,96,128]{2,0,1:T(4,128)S(1)} %bitcast.131, s32[1024]{0:T(1024)} %pad_clamp_fusion.1), kind=kCustom, calls=%fused_computation | custom fusion | bytes 1771200 | tf_op jit(solution)/shard_map/jit(_take)/gather | solution.py:268
  31.4 1.7 %copy.50 = f32[27,16,4,128]{3,0,1,2:T(8,128)S(1)} copy(f32[27,16,4,128]{3,2,1,0:T(4,128)} %bitcast.133) | data formatting | bytes 1769472 | tf_op jit(solution)/shard_map/jit(_take)/gather | solution.py:268
  33.1 0.1 fusion.33
  33.2 0.8 copy.51
  34.0 0.8 copy.52
  34.8 0.8 copy.53
  35.6 0.8 copy.54
  36.5 0.6 reshape.836
  37.1 1.4 copy.55
  38.4 1.3 mul.502
  39.9 1.2 multiply_reduce_fusion.1
  41.1 0.3 convolution_bitcast_fusion
  41.4 3.1 %collective-permute-start.4 = (f32[1,1,2,256]{3,2,1,0:T(2,128)S(1)}, f32[1,1,2,256]{3,2,1,0:T(2,128)S(1)}, u32[]{:S(2)}, u32[]{:S(2)}) collective-permute-start(f32[1,1,2,256]{3,2,1,0:T(2,128)S(1)} %convolution_bitcast_fusion), channel_id=1, source_target_pairs={{0,3},{1,0},{2,1},{3,2},{4,7},{5,4},{6,5},{7,6},{8,11},{9,8},{10,9... | collective-permute-start | bytes 6152 | tf_op jit(solution)/shard_map/ppermute | solution.py:61
  44.6 20.0 %fusion.5 = f32[16,128]{1,0:T(8,128)S(1)} fusion(f32[3456]{0:T(1024)S(1)} %copy-done.51, f32[3456]{0:T(1024)S(1)} %copy-done.50, f32[3456]{0:T(1024)S(1)} %copy-done.49, f32[16,3456]{1,0:T(8,128)S(1)} %bitcast.139, f32[16,3456]{1,0:T(8,128)S(1)} %bitcast.140, f32[16,128]{1,0:T(8,128)S(1)} %bitcast.166, f32[16,3456]{1,0:T(8,128)S(1)} %bitcast.141, ...), kind=kLoop, calls=%fused_computation.8 | loop fusion | flops 106166272 | bytes 1401344 | tf_op jit(solution)/shard_map/reduce_sum | solution.py:283
  64.6 0.1 fusion.18
  64.8 0.1 fusion.20
  64.9 0.3 copy.24
  65.2 4.1 %collective-permute-done.5 = f32[1,2,2,256]{3,2,1,0:T(2,128)S(1)} collective-permute-done((f32[1,2,2,256]{3,2,1,0:T(2,128)S(1)}, f32[1,2,2,256]{3,2,1,0:T(2,128)S(1)}, u32[]{:S(2)}, u32[]{:S(2)}) %collective-permute-start.5) | collective-permute-done | bytes 4128 | tf_op jit(solution)/shard_map/ppermute | solution.py:61
  69.5 47.3 %shard_map.154 = f32[16,256]{1,0:T(8,128)S(1)} custom-call(f32[474]{0:T(512)S(1)} %copy-done.2, s32[1264]{0:T(1024)S(1)} %copy-done.1, f32[3,256,256]{2,1,0:T(8,128)S(1)} %pad_maximum_fusion.base_ref, f32[448,4,256]{2,1,0:T(4,128)S(1)} %bitcast.130), custom_call_target="tpu_custom_call" | custom-call | flops 2133065728 | bytes 2637824 | tf_op jit(solution)/shard_map/pallas_call | solution.py:142
  116.8 2.0 %collective-permute-start.7 = (f32[2,4,2,256]{3,2,1,0:T(2,128)S(1)}, f32[2,4,2,256]{3,2,1,0:T(2,128)S(1)}, u32[]{:S(2)}, u32[]{:S(2)}) collective-permute-start(f32[2,4,2,256]{3,2,1,0:T(2,128)S(1)} %pad_maximum_fusion.12), channel_id=1, source_target_pairs={{0,24},{4,28},{8,0},{12,4},{16,8},{20,12},{24,16},{28,20},{1,25},{... | collective-permute-start | bytes 49160 | tf_op jit(solution)/shard_map/ppermute | solution.py:61
  118.8 0.3 fusion.21
  119.2 1.6 %collective-permute-done.7 = f32[2,4,2,256]{3,2,1,0:T(2,128)S(1)} collective-permute-done((f32[2,4,2,256]{3,2,1,0:T(2,128)S(1)}, f32[2,4,2,256]{3,2,1,0:T(2,128)S(1)}, u32[]{:S(2)}, u32[]{:S(2)}) %collective-permute-start.7) | collective-permute-done | bytes 16416 | tf_op jit(solution)/shard_map/ppermute | solution.py:61
  120.8 1.8 %collective-permute-start.8 = (f32[4,4,2,256]{3,2,1,0:T(2,128)S(1)}, f32[4,4,2,256]{3,2,1,0:T(2,128)S(1)}, u32[]{:S(2)}, u32[]{:S(2)}) collective-permute-start(f32[4,4,2,256]{3,2,1,0:T(2,128)S(1)} %pad_maximum_fusion.10), channel_id=1, source_target_pairs={{0,16},{4,20},{8,24},{12,28},{16,0},{20,4},{24,8},{28,12},{1,17},{... | collective-permute-start | bytes 98312 | tf_op jit(solution)/shard_map/ppermute | solution.py:61
  122.7 1.3 multiply_reduce_fusion.3
  124.0 0.8 collective-permute-done.8
  124.8 0.7 gather_fusion.1
  125.8 11.7 %multiply_reduce_fusion = f32[2,256]{1,0:T(2,128)S(1)} fusion(f32[11776]{0:T(1024)S(1)} %select_n.55, f32[2,11776]{1,0:T(2,128)S(1)} %copy-done.14, f32[256]{0:T(256)S(1)} %bitcast.181, f32[11776]{0:T(1024)S(1)} %copy-done.17, f32[256]{0:T(256)S(1)} %bitcast.182, f32[11776]{0:T(1024)S(1)} %copy-done.16, f32[256]{0:T(256)S(1)} %bitcast.180), kind=kLoop, calls=%fused_computation.12 | loop fusion | flops 66321920 | bytes 240640 | tf_op jit(solution)/shard_map/reduce_sum | solution.py:29
  137.4 0.3 fusion.41
  137.8 1.3 multiply_reduce_fusion.2
  139.2 0.7 add_select_fusion
  (169 shorter events, 1.8 us)
Async XLA Ops:
  0.0 4.2 %copy-start = (f32[256,256]{1,0:T(8,128)S(1)}, f32[256,256]{1,0:T(8,128)}, u32[]{:S(2)}) copy-start(f32[256,256]{1,0:T(8,128)} %param.19) | copy-start | bytes 786436
  0.0 12.2 %copy-start.47 = (f32[23]{0:T(128)S(1)}, f32[23]{0:T(128)}, u32[]{:S(2)}) copy-start(f32[23]{0:T(128)} %constant.139) | copy-start | bytes 280
  0.0 12.2 %copy-start.48 = (f32[23]{0:T(128)S(1)}, f32[23]{0:T(128)}, u32[]{:S(2)}) copy-start(f32[23]{0:T(128)} %constant.140) | copy-start | bytes 280
  0.0 11.3 %copy-start.5 = (f32[3,2,2,4,128]{4,3,2,1,0:T(4,128)S(1)}, f32[3,2,2,4,128]{4,3,2,1,0:T(4,128)}, u32[]{:S(2)}) copy-start(f32[3,2,2,4,128]{4,3,2,1,0:T(4,128)} %param.16) | copy-start | bytes 73732
  3.0 1.5 %copy-start.19 = (f32[2,2,4,128]{3,2,1,0:T(4,128)}, f32[2,2,4,128]{3,2,1,0:T(4,128)S(1)}, u32[]{:S(2)}) copy-start(f32[2,2,4,128]{3,2,1,0:T(4,128)S(1)} %get-tuple-element.28) | copy-start | bytes 24580
  3.0 1.5 %copy-start.21 = (f32[2,2,4,128]{3,2,1,0:T(4,128)}, f32[2,2,4,128]{3,2,1,0:T(4,128)S(1)}, u32[]{:S(2)}) copy-start(f32[2,2,4,128]{3,2,1,0:T(4,128)S(1)} %get-tuple-element.29) | copy-start | bytes 24580
  3.0 1.5 %copy-start.23 = (f32[2,2,4,128]{3,2,1,0:T(4,128)}, f32[2,2,4,128]{3,2,1,0:T(4,128)S(1)}, u32[]{:S(2)}) copy-start(f32[2,2,4,128]{3,2,1,0:T(4,128)S(1)} %get-tuple-element.30) | copy-start | bytes 24580
  3.1 6.0 %copy-start.38 = (f32[1,256]{1,0:T(1,128)}, f32[1,256]{1,0:T(1,128)S(1)}, u32[]{:S(2)}) copy-start(f32[1,256]{1,0:T(1,128)S(1)} %get-tuple-element.50) | copy-start | bytes 3076
  3.1 6.0 %copy-start.40 = (f32[1,256]{1,0:T(1,128)}, f32[1,256]{1,0:T(1,128)S(1)}, u32[]{:S(2)}) copy-start(f32[1,256]{1,0:T(1,128)S(1)} %get-tuple-element.51) | copy-start | bytes 3076
  3.1 9.3 %copy-start.42 = (f32[1,256]{1,0:T(1,128)}, f32[1,256]{1,0:T(1,128)S(1)}, u32[]{:S(2)}) copy-start(f32[1,256]{1,0:T(1,128)S(1)} %get-tuple-element.52) | copy-start | bytes 3076
  3.1 9.3 %copy-start.31 = (f32[1,256]{1,0:T(1,128)}, f32[1,256]{1,0:T(1,128)S(1)}, u32[]{:S(2)}) copy-start(f32[1,256]{1,0:T(1,128)S(1)} %get-tuple-element.36) | copy-start | bytes 3076
  3.1 9.3 %copy-start.33 = (f32[1,256]{1,0:T(1,128)}, f32[1,256]{1,0:T(1,128)S(1)}, u32[]{:S(2)}) copy-start(f32[1,256]{1,0:T(1,128)S(1)} %get-tuple-element.37) | copy-start | bytes 3076
  3.1 9.3 %copy-start.35 = (f32[1,256]{1,0:T(1,128)}, f32[1,256]{1,0:T(1,128)S(1)}, u32[]{:S(2)}) copy-start(f32[1,256]{1,0:T(1,128)S(1)} %get-tuple-element.38) | copy-start | bytes 3076
  5.3 10.6 %collective-permute-start = (f32[8192]{0:T(1024)S(1)}, f32[8192]{0:T(1024)S(1)}, u32[]{:S(2)}, u32[]{:S(2)}) collective-permute-start(f32[8192]{0:T(1024)S(1)} %get-tuple-element.34), channel_id=1, source_target_pairs={{0,4},{4,8},{8,12},{12,16},{16,20},{20,24},{24,28},{28,0},{1,5},{5... | collective-permute-start | bytes 98312 | tf_op jit(solution)/shard_map/ppermute | solution.py:75
  5.9 10.1 %collective-permute-start.1 = (f32[8192]{0:T(1024)S(1)}, f32[8192]{0:T(1024)S(1)}, u32[]{:S(2)}, u32[]{:S(2)}) collective-permute-start(f32[8192]{0:T(1024)S(1)} %get-tuple-element.35), channel_id=1, source_target_pairs={{4,0},{8,4},{12,8},{16,12},{20,16},{24,20},{28,24},{0,28},{5,1},{9... | collective-permute-start | bytes 98312 | tf_op jit(solution)/shard_map/ppermute | solution.py:76
  12.0 1.3 copy-start.37
  16.7 7.6 %collective-permute-start.2 = (f32[20480]{0:T(1024)S(1)}, f32[20480]{0:T(1024)S(1)}, u32[]{:S(2)}, u32[]{:S(2)}) collective-permute-start(f32[20480]{0:T(1024)S(1)} %get-tuple-element.17), channel_id=1, source_target_pairs={{0,1},{1,2},{2,3},{3,0},{4,5},{5,6},{6,7},{7,4},{8,9},{9,10},{10,1... | collective-permute-start | bytes 245768 | tf_op jit(solution)/shard_map/ppermute | solution.py:75
  19.0 5.5 %collective-permute-start.3 = (f32[20480]{0:T(1024)}, f32[20480]{0:T(1024)}, u32[]{:S(2)}, u32[]{:S(2)}) collective-permute-start(f32[20480]{0:T(1024)} %get-tuple-element.18), channel_id=1, source_target_pairs={{1,0},{2,1},{3,2},{0,3},{5,4},{6,5},{7,6},{4,7},{9,8},{10,9},{11,1... | collective-permute-start | bytes 245768 | tf_op jit(solution)/shard_map/ppermute | solution.py:76
  24.4 1.0 copy-start.15
  27.4 1.2 copy-start.3
  37.1 4.0 %copy-start.8 = (f32[256,256]{1,0:T(8,128)S(1)}, f32[256,256]{1,0:T(8,128)}, u32[]{:S(2)}) copy-start(f32[256,256]{1,0:T(8,128)} %param.21) | copy-start | bytes 786436
  39.8 4.7 %copy-start.6 = (pred[128,3456]{1,0:T(8,128)(4,1)S(1)}, pred[128,3456]{1,0:T(8,128)(4,1)}, u32[]{:S(2)}) copy-start(pred[128,3456]{1,0:T(8,128)(4,1)} %iota_compare_fusion) | copy-start | bytes 1327108
  39.8 4.7 %copy-start.10 = (f32[2,8,27,128]{3,1,2,0:T(8,128)S(1)}, f32[2,8,27,128]{3,1,2,0:T(8,128)}, u32[]{:S(2)}) copy-start(f32[2,8,27,128]{3,1,2,0:T(8,128)} %copy.51) | copy-start | bytes 663556
  39.8 4.7 %copy-start.11 = (f32[2,8,27,128]{3,1,2,0:T(8,128)S(1)}, f32[2,8,27,128]{3,1,2,0:T(8,128)}, u32[]{:S(2)}) copy-start(f32[2,8,27,128]{3,1,2,0:T(8,128)} %copy.52) | copy-start | bytes 663556
  39.8 4.7 %copy-start.12 = (f32[2,8,27,128]{3,1,2,0:T(8,128)S(1)}, f32[2,8,27,128]{3,1,2,0:T(8,128)}, u32[]{:S(2)}) copy-start(f32[2,8,27,128]{3,1,2,0:T(8,128)} %copy.53) | copy-start | bytes 663556
  39.8 4.7 %copy-start.13 = (f32[2,8,27,128]{3,1,2,0:T(8,128)S(1)}, f32[2,8,27,128]{3,1,2,0:T(8,128)}, u32[]{:S(2)}) copy-start(f32[2,8,27,128]{3,1,2,0:T(8,128)} %copy.54) | copy-start | bytes 663556
  39.8 4.7 %copy-start.28 = (f32[1,2,2,4,128]{4,3,2,1,0:T(4,128)S(1)}, f32[1,2,2,4,128]{4,3,2,1,0:T(4,128)}, u32[]{:S(2)}) copy-start(f32[1,2,2,4,128]{4,3,2,1,0:T(4,128)} %get-tuple-element.27) | copy-start | bytes 24580
  39.8 4.7 %copy-start.29 = (f32[1,2,2,4,128]{4,3,2,1,0:T(4,128)S(1)}, f32[1,2,2,4,128]{4,3,2,1,0:T(4,128)}, u32[]{:S(2)}) copy-start(f32[1,2,2,4,128]{4,3,2,1,0:T(4,128)} %get-tuple-element.31) | copy-start | bytes 24580
  39.8 4.7 %copy-start.30 = (f32[1,2,2,4,128]{4,3,2,1,0:T(4,128)S(1)}, f32[1,2,2,4,128]{4,3,2,1,0:T(4,128)}, u32[]{:S(2)}) copy-start(f32[1,2,2,4,128]{4,3,2,1,0:T(4,128)} %get-tuple-element.32) | copy-start | bytes 24580
  39.8 4.7 %copy-start.49 = (f32[3456]{0:T(1024)S(1)}, f32[3456]{0:T(1024)}, u32[]{:S(2)}) copy-start(f32[3456]{0:T(1024)} %constant.136) | copy-start | bytes 41476
  39.8 4.7 %copy-start.50 = (f32[3456]{0:T(1024)S(1)}, f32[3456]{0:T(1024)}, u32[]{:S(2)}) copy-start(f32[3456]{0:T(1024)} %constant.137) | copy-start | bytes 41476
  39.9 4.7 %copy-start.51 = (f32[3456]{0:T(1024)S(1)}, f32[3456]{0:T(1024)}, u32[]{:S(2)}) copy-start(f32[3456]{0:T(1024)} %constant.138) | copy-start | bytes 41476
  41.4 23.4 %collective-permute-start.4 = (f32[1,1,2,256]{3,2,1,0:T(2,128)S(1)}, f32[1,1,2,256]{3,2,1,0:T(2,128)S(1)}, u32[]{:S(2)}, u32[]{:S(2)}) collective-permute-start(f32[1,1,2,256]{3,2,1,0:T(2,128)S(1)} %convolution_bitcast_fusion), channel_id=1, source_target_pairs={{0,3},{1,0},{2,1},{3,2},{4,7},{5,4},{6,5},{7,6},{8,11},{9,8},{10,9... | collective-permute-start | bytes 6152 | tf_op jit(solution)/shard_map/ppermute | solution.py:61
  44.6 20.0 %copy-start.4 = (f32[8,8,7,4,256]{4,3,1,0,2:T(4,128)S(1)}, f32[8,8,7,4,256]{4,3,1,0,2:T(4,128)}, u32[]{:S(2)}) copy-start(f32[8,8,7,4,256]{4,3,1,0,2:T(4,128)} %copy-done.3) | copy-start | bytes 5505028
  64.7 4.6 %copy-start.1 = (s32[1264]{0:T(1024)S(1)}, s32[1264]{0:T(1024)}, u32[]{:S(2)}) copy-start(s32[1264]{0:T(1024)} %constant.116.clone.index_ref) | copy-start | bytes 15172
  64.7 4.6 %copy-start.2 = (f32[474]{0:T(512)S(1)}, f32[474]{0:T(512)}, u32[]{:S(2)}) copy-start(f32[474]{0:T(512)} %constant.115.clone.table_ref) | copy-start | bytes 5692
  64.7 4.6 %collective-permute-start.5 = (f32[1,2,2,256]{3,2,1,0:T(2,128)S(1)}, f32[1,2,2,256]{3,2,1,0:T(2,128)S(1)}, u32[]{:S(2)}, u32[]{:S(2)}) collective-permute-start(f32[1,2,2,256]{3,2,1,0:T(2,128)S(1)} %pad_maximum_fusion.15), channel_id=1, source_target_pairs={{0,2},{1,3},{2,0},{3,1},{4,6},{5,7},{6,4},{7,5},{8,10},{9,11},{10,... | collective-permute-start | bytes 12296 | tf_op jit(solution)/shard_map/ppermute | solution.py:61
  69.3 47.5 %collective-permute-start.6 = (f32[1,4,2,256]{3,2,1,0:T(2,128)S(1)}, f32[1,4,2,256]{3,2,1,0:T(2,128)S(1)}, u32[]{:S(2)}, u32[]{:S(2)}) collective-permute-start(f32[1,4,2,256]{3,2,1,0:T(2,128)S(1)} %pad_maximum_fusion.13), channel_id=1, source_target_pairs={{0,28},{4,0},{8,4},{12,8},{16,12},{20,16},{24,20},{28,24},{1,29},{... | collective-permute-start | bytes 24584 | tf_op jit(solution)/shard_map/ppermute | solution.py:61
  69.3 49.5 %copy-start.7 = (f32[256,256]{1,0:T(8,128)S(1)}, f32[256,256]{1,0:T(8,128)}, u32[]{:S(2)}) copy-start(f32[256,256]{1,0:T(8,128)} %param.20) | copy-start | bytes 786436
  69.4 53.3 %copy-start.20 = (f32[2,2,4,128]{3,2,1,0:T(4,128)S(1)}, f32[2,2,4,128]{3,2,1,0:T(4,128)}, u32[]{:S(2)}) copy-start(f32[2,2,4,128]{3,2,1,0:T(4,128)} %copy-done.19) | copy-start | bytes 24580
  69.4 53.3 %copy-start.22 = (f32[2,2,4,128]{3,2,1,0:T(4,128)S(1)}, f32[2,2,4,128]{3,2,1,0:T(4,128)}, u32[]{:S(2)}) copy-start(f32[2,2,4,128]{3,2,1,0:T(4,128)} %copy-done.21) | copy-start | bytes 24580
  69.4 53.3 %copy-start.24 = (f32[2,2,4,128]{3,2,1,0:T(4,128)S(1)}, f32[2,2,4,128]{3,2,1,0:T(4,128)}, u32[]{:S(2)}) copy-start(f32[2,2,4,128]{3,2,1,0:T(4,128)} %copy-done.23) | copy-start | bytes 24580
  69.4 53.3 %copy-start.39 = (f32[1,256]{1,0:T(1,128)S(1)}, f32[1,256]{1,0:T(1,128)}, u32[]{:S(2)}) copy-start(f32[1,256]{1,0:T(1,128)} %copy-done.38) | copy-start | bytes 3076
  69.4 53.2 %copy-start.41 = (f32[1,256]{1,0:T(1,128)S(1)}, f32[1,256]{1,0:T(1,128)}, u32[]{:S(2)}) copy-start(f32[1,256]{1,0:T(1,128)} %copy-done.40) | copy-start | bytes 3076
  69.4 53.2 %copy-start.43 = (f32[1,256]{1,0:T(1,128)S(1)}, f32[1,256]{1,0:T(1,128)}, u32[]{:S(2)}) copy-start(f32[1,256]{1,0:T(1,128)} %copy-done.42) | copy-start | bytes 3076
  69.4 56.2 %copy-start.14 = (f32[2,11776]{1,0:T(2,128)S(1)}, f32[2,11776]{1,0:T(2,128)}, u32[]{:S(2)}) copy-start(f32[2,11776]{1,0:T(2,128)} %stack_broadcast_in_dim.41) | copy-start | bytes 282628
  69.4 56.2 %copy-start.16 = (f32[11776]{0:T(1024)S(1)}, f32[11776]{0:T(1024)}, u32[]{:S(2)}) copy-start(f32[11776]{0:T(1024)} %stack_broadcast_in_dim.37) | copy-start | bytes 141316
  69.4 56.2 %copy-start.17 = (f32[11776]{0:T(1024)S(1)}, f32[11776]{0:T(1024)}, u32[]{:S(2)}) copy-start(f32[11776]{0:T(1024)} %stack_broadcast_in_dim.39) | copy-start | bytes 141316
  69.4 56.2 %copy-start.44 = (f32[1,1,256]{2,1,0:T(1,128)S(1)}, f32[1,1,256]{2,1,0:T(1,128)}, u32[]{:S(2)}) copy-start(f32[1,1,256]{2,1,0:T(1,128)} %get-tuple-element.42) | copy-start | bytes 3076
  69.5 56.2 %copy-start.45 = (f32[1,1,256]{2,1,0:T(1,128)S(1)}, f32[1,1,256]{2,1,0:T(1,128)}, u32[]{:S(2)}) copy-start(f32[1,1,256]{2,1,0:T(1,128)} %get-tuple-element.43) | copy-start | bytes 3076
  69.5 56.2 %copy-start.46 = (f32[1,1,256]{2,1,0:T(1,128)S(1)}, f32[1,1,256]{2,1,0:T(1,128)}, u32[]{:S(2)}) copy-start(f32[1,1,256]{2,1,0:T(1,128)} %get-tuple-element.44) | copy-start | bytes 3076
  116.8 4.0 %collective-permute-start.7 = (f32[2,4,2,256]{3,2,1,0:T(2,128)S(1)}, f32[2,4,2,256]{3,2,1,0:T(2,128)S(1)}, u32[]{:S(2)}, u32[]{:S(2)}) collective-permute-start(f32[2,4,2,256]{3,2,1,0:T(2,128)S(1)} %pad_maximum_fusion.12), channel_id=1, source_target_pairs={{0,24},{4,28},{8,0},{12,4},{16,8},{20,12},{24,16},{28,20},{1,25},{... | collective-permute-start | bytes 49160 | tf_op jit(solution)/shard_map/ppermute | solution.py:61
  120.8 4.0 %collective-permute-start.8 = (f32[4,4,2,256]{3,2,1,0:T(2,128)S(1)}, f32[4,4,2,256]{3,2,1,0:T(2,128)S(1)}, u32[]{:S(2)}, u32[]{:S(2)}) collective-permute-start(f32[4,4,2,256]{3,2,1,0:T(2,128)S(1)} %pad_maximum_fusion.10), channel_id=1, source_target_pairs={{0,16},{4,20},{8,24},{12,28},{16,0},{20,4},{24,8},{28,12},{1,17},{... | collective-permute-start | bytes 98312 | tf_op jit(solution)/shard_map/ppermute | solution.py:61
  125.7 11.7 %copy-start.9 = (f32[256,256]{1,0:T(8,128)S(1)}, f32[256,256]{1,0:T(8,128)}, u32[]{:S(2)}) copy-start(f32[256,256]{1,0:T(8,128)} %param.22) | copy-start | bytes 786436
  125.7 12.1 %copy-start.25 = (f32[2,2,4,128]{3,2,1,0:T(4,128)S(1)}, f32[2,2,4,128]{3,2,1,0:T(4,128)}, u32[]{:S(2)}) copy-start(f32[2,2,4,128]{3,2,1,0:T(4,128)} %get-tuple-element.25) | copy-start | bytes 24580
  125.7 12.1 %copy-start.26 = (f32[2,2,4,128]{3,2,1,0:T(4,128)S(1)}, f32[2,2,4,128]{3,2,1,0:T(4,128)}, u32[]{:S(2)}) copy-start(f32[2,2,4,128]{3,2,1,0:T(4,128)} %get-tuple-element.26) | copy-start | bytes 24580
  125.7 12.1 %copy-start.27 = (f32[2,2,4,128]{3,2,1,0:T(4,128)S(1)}, f32[2,2,4,128]{3,2,1,0:T(4,128)}, u32[]{:S(2)}) copy-start(f32[2,2,4,128]{3,2,1,0:T(4,128)} %get-tuple-element.33) | copy-start | bytes 24580
  125.7 12.1 %copy-start.32 = (f32[1,256]{1,0:T(1,128)S(1)}, f32[1,256]{1,0:T(1,128)}, u32[]{:S(2)}) copy-start(f32[1,256]{1,0:T(1,128)} %copy-done.31) | copy-start | bytes 3076
  125.7 12.1 %copy-start.34 = (f32[1,256]{1,0:T(1,128)S(1)}, f32[1,256]{1,0:T(1,128)}, u32[]{:S(2)}) copy-start(f32[1,256]{1,0:T(1,128)} %copy-done.33) | copy-start | bytes 3076
  125.7 12.1 %copy-start.36 = (f32[1,256]{1,0:T(1,128)S(1)}, f32[1,256]{1,0:T(1,128)}, u32[]{:S(2)}) copy-start(f32[1,256]{1,0:T(1,128)} %copy-done.35) | copy-start | bytes 3076
  125.8 13.4 %copy-start.18 = (s32[2,2,4]{2,1,0:T(2,128)S(1)}, s32[2,2,4]{2,1,0:T(2,128)}, u32[]{:S(2)}) copy-start(s32[2,2,4]{2,1,0:T(2,128)} %param.18) | copy-start | bytes 196

commit v9 on v6

--- a/solution.py
+++ b/solution.py
@@ -50,18 +50,6 @@
     along_y = jnp.broadcast_to(centre[None, :, None, None] + 0.9 * unit_sphere[1], box_shape)
     along_z = jnp.broadcast_to(centre[None, None, :, None] + 0.9 * unit_sphere[2], box_shape)
     return jnp.stack([along_x, along_y, along_z]).reshape(3, 8 * point_count)
-
-
-def rel_gather(buf, axis, dim):
-    count = lax.axis_size(axis)
-    have = 1
-    while have < count:
-        step = min(have, count - have)
-        part = lax.slice_in_dim(buf, 0, step, axis=dim)
-        got = lax.ppermute(part, axis, [(j, (j - have) % count) for j in range(count)])
-        buf = jnp.concatenate([buf, got], axis=dim)
-        have += step
-    return buf
 
 
 def exchange(items, axis):
@@ -194,33 +182,48 @@
     count_x = lax.axis_size("gx")
     count_y = lax.axis_size("gy")
 
-    gathered = rel_gather(rel_gather(parent_eq[None, None], "gy", 1), "gx", 0)
     kept = []
     for rel_x in range(count_x):
         for rel_y in range(count_y):
-            off_x = (rel_x + count_x // 2) % count_x - count_x // 2
-            off_y = (rel_y + count_y // 2) % count_y - count_y // 2
+            off_x = (count_x // 2 - rel_x) % count_x - count_x // 2
+            off_y = (count_y // 2 - rel_y) % count_y - count_y // 2
             if abs(off_x) > 1 or abs(off_y) > 1:
                 kept.append((rel_x * count_y + rel_y, off_x, off_y))
     kept_index = np.array([k[0] for k in kept], np.int32)
     kept_x = np.array([2.0 * k[1] for k in kept], np.float32)
     kept_y = np.array([2.0 * k[2] for k in kept], np.float32)
-    far_sources = jnp.take(gathered.reshape(count_x * count_y, parent_layers, points), kept_index, axis=0)
     layer_float = jnp.arange(parent_layers).astype(jnp.float32)
-    depth_pairs = 2.0 * (layer_float[None, :] - layer_float[:, None])
-    far_shape = (parent_layers, len(kept), parent_layers, points)
-    source_pts = jnp.stack(
-        [
-            jnp.broadcast_to(kept_x[None, :, None, None] + 1.8 * unit_sphere[0], far_shape),
-            jnp.broadcast_to(kept_y[None, :, None, None] + 1.8 * unit_sphere[1], far_shape),
-            jnp.broadcast_to(depth_pairs[:, None, :, None] + 1.8 * unit_sphere[2], far_shape),
+    far_shape = (len(kept), parent_layers, points)
+    check_pts = jnp.stack(
+        [
+            jnp.broadcast_to(1.8 * unit_sphere[0] - kept_x[:, None, None], far_shape),
+            jnp.broadcast_to(1.8 * unit_sphere[1] - kept_y[:, None, None], far_shape),
+            jnp.broadcast_to(1.8 * unit_sphere[2] + 2.0 * layer_float[:, None], far_shape),
         ]
-    ).reshape(3, parent_layers, -1)
-    far_check = point_sum(
-        jnp.broadcast_to(1.8 * unit_sphere[:, None, :], (3, parent_layers, points)),
-        source_pts,
-        far_sources.reshape(-1),
-    )
+    ).reshape(3, -1)
+    equivalent_pts = jnp.stack(
+        [
+            jnp.broadcast_to(1.8 * unit_sphere[0], (parent_layers, points)),
+            jnp.broadcast_to(1.8 * unit_sphere[1], (parent_layers, points)),
+            2.0 * layer_float[:, None] + 1.8 * unit_sphere[2],
+        ]
+    ).reshape(3, -1)
+    outgoing = point_sum(check_pts, equivalent_pts, parent_eq.reshape(-1))
+    partial = (
+        jnp.zeros((count_x * count_y, parent_layers * points), jnp.float32)
+        .at[kept_index]
+        .set(outgoing.reshape(len(kept), -1))
+        .reshape(count_x, count_y, parent_layers, points)
+    )
+    for axis, dim, count in (("gy", 1, count_y), ("gx", 0, count_x)):
+        half = count // 2
+        while half >= 1:
+            keep_part = lax.slice_in_dim(partial, 0, half, axis=dim)
+            send_part = lax.slice_in_dim(partial, half, 2 * half, axis=dim)
+            got = lax.ppermute(send_part, axis, [(j, (j + half) % count) for j in range(count)])
+            partial = keep_part + got
+            half //= 2
+    far_check = partial[0, 0]
 
     framed = jnp.pad(cycle, ((1, 1), (1, 1), (3, 3), (0, 0)))
     shifts = far_shifts(3)

time: 121 us -> 127 us (1.050)
  waiting for transfers between devices: 6.51 us -> 12.2 us
  starting transfers between devices: 16.5 us -> 15.1 us
    ppermute x5, waiting for transfers between devices: 6.49 us -> 10.7 us  [shards(): lax.ppermute(send_part, axis, [(j, (j + half) % count) for j in range(cou...]
    ppermute x2, starting transfers between devices: 2.19 us -> 0.56 us  [exchange(): lax.ppermute(sent_tail, axis, [(i, (i + 1) % count) for i in range(count)])]
    ppermute x2, waiting for transfers between devices: 0.01 us -> 1.56 us  [exchange(): lax.ppermute(sent_tail, axis, [(i, (i + 1) % count) for i in range(count)])]
    reduce_sum x5, other arithmetic: 15.8 us -> 17.2 us  [point_sum(): return jnp.sum(kernel * weights[..., None, :], axis=-1)]
  transfers between devices with their start and end apart: 9 -> 9, of which waited for: 3 -> 5; matrix products, arithmetic and copies ran while one was open for 14% -> 15% of each run, Pallas kernels for 0% -> 0%
where the time goes in v9:
time: 127 us; the launch traced here: 126 us
  Pallas kernels  47.3 us (37%)
  other arithmetic  42.6 us (34%)
  starting transfers between devices  15.1 us (12%)
  waiting for transfers between devices  12.2 us (10%)
  local copies, waits for them, and re-layouts  7.03 us (6%)
    pallas_call x1, Pallas kernels, m2l(): pl.pallas_call(functools.partial(m2l_kernel, shift_count, 128), out_shape...  47.3 us
    reduce_sum x1, other arithmetic, shards(): jnp.sum(kernel * source[3][..., None, :], axis=-1)  20 us
    reduce_sum x5, other arithmetic, point_sum(): return jnp.sum(kernel * weights[..., None, :], axis=-1)  17.2 us
    ppermute x5, waiting for transfers between devices, shards(): lax.ppermute(send_part, axis, [(j, (j + half) % count) for j in range(cou...  10.7 us
    ppermute x5, starting transfers between devices, shards(): lax.ppermute(send_part, axis, [(j, (j + half) % count) for j in range(cou...  7.77 us
    ppermute x2, starting transfers between devices, exchange(): lax.ppermute(sent_head, axis, [((i + 1) % count, i) for i in range(count)])  6.76 us
    gather x2, local copies, waits for them, and re-layouts, shards(): jnp.take(padded_around.reshape(4, -1, slot_count), box_rows, axis=1)  2.79 us
  transfers between devices with their start and end apart: 9, of which 5 were waited for; matrix products, arithmetic and copies ran while one was open for 15% of the time, Pallas kernels for 0%

profile of v9, /device:TPU:0, one launch (start us, length us, event | category | flops | bytes accessed | tf_op | source)
XLA Modules:
  0.0 126.2 jit_solution(9118896249106152600)
XLA Ops:
  0.0 0.1 cosine_multiply_fusion.1
  0.1 0.1 sine_multiply_fusion.1
  0.1 0.8 fusion.26
  0.9 0.8 fusion.45
  1.7 0.7 fusion.37
  2.4 1.1 multiply_reduce_fusion.4
  3.5 0.3 fusion.21
  3.9 0.7 fusion.25
  4.6 0.5 collective-permute-start
  5.1 2.9 %collective-permute-start.1 = (f32[8192]{0:T(1024)S(1)}, f32[8192]{0:T(1024)S(1)}, u32[]{:S(2)}, u32[]{:S(2)}) collective-permute-start(f32[8192]{0:T(1024)S(1)} %get-tuple-element.29), channel_id=1, source_target_pairs={{4,0},{8,4},{12,8},{16,12},{20,16},{24,20},{28,24},{0,28},{5,1},{9... | collective-permute-start | bytes 98312 | tf_op jit(solution)/shard_map/ppermute | solution.py:64
  8.4 0.1 broadcast_add_fusion.7
  8.6 0.8 add_rsqrt_fusion
  9.3 0.4 multiply_reduce_fusion.1
  9.8 0.3 convolution_bitcast_fusion
  10.1 0.1 broadcast_add_fusion.8
  10.3 0.1 broadcast_add_fusion.1
  10.4 0.1 broadcast_add_fusion
  10.6 0.1 add.404
  10.7 13.0 %multiply_reduce_fusion = f32[11776]{0:T(1024)S(1)} fusion(f32[512]{0:T(512)S(1)} %bitcast.178, f32[512]{0:T(512)S(1)} %add.406, f32[11776]{0:T(1024)S(1)} %stack_broadcast_in_dim.53, f32[512]{0:T(512)S(1)} %bitcast.180, f32[11776]{0:T(1024)S(1)} %stack_broadcast_in_dim.49, f32[512]{0:T(512)S(1)} %bitcast.179, f32[11776]{0:T(1024)S(1)} %stack_broadcast_in_dim.45), kind=kLoop, calls=%fused_computation.12 | loop fusion | flops 66310656 | bytes 196608 | tf_op jit(solution)/shard_map/reduce_sum | solution.py:29
  23.8 0.8 scatter_custom_fusion
  24.7 3.3 %collective-permute-start.4 = (f32[8,2,2,256]{3,2,1,0:T(2,128)S(1)}, f32[8,2,2,256]{3,2,1,0:T(2,128)S(1)}, u32[]{:S(2)}, u32[]{:S(2)}) collective-permute-start(f32[8,2,2,256]{3,2,1,0:T(2,128)S(1)} %slice.340), channel_id=1, source_target_pairs={{0,2},{1,3},{2,0},{3,1},{4,6},{5,7},{6,4},{7,5},{8,10},{9,11},{10,... | collective-permute-start | bytes 98312 | tf_op jit(solution)/shard_map/ppermute | solution.py:223
  28.1 0.1 subtract_multiply_fusion.2
  28.2 0.3 iota_compare_fusion
  28.6 0.1 subtract_multiply_fusion
  28.7 0.1 broadcast_add_fusion.4
  28.8 0.1 pad_maximum_fusion.base_ref
  28.9 1.0 collective-permute-done.4
  29.9 2.0 %collective-permute-start.5 = (f32[8,1,2,256]{3,2,1,0:T(2,128)S(1)}, f32[8,1,2,256]{3,2,1,0:T(2,128)S(1)}, u32[]{:S(2)}, u32[]{:S(2)}) collective-permute-start(f32[8,1,2,256]{3,2,1,0:T(2,128)S(1)} %slice.342), channel_id=1, source_target_pairs={{0,1},{1,2},{2,3},{3,0},{4,5},{5,6},{6,7},{7,4},{8,9},{9,10},{10,1... | collective-permute-start | bytes 49160 | tf_op jit(solution)/shard_map/ppermute | solution.py:223
  31.9 3.9 %collective-permute-done.5 = f32[8,1,2,256]{3,2,1,0:T(2,128)S(1)} collective-permute-done((f32[8,1,2,256]{3,2,1,0:T(2,128)S(1)}, f32[8,1,2,256]{3,2,1,0:T(2,128)S(1)}, u32[]{:S(2)}, u32[]{:S(2)}) %collective-permute-start.5) | collective-permute-done | bytes 16416 | tf_op jit(solution)/shard_map/ppermute | solution.py:223
  35.9 1.6 %collective-permute-start.6 = (f32[4,1,2,256]{3,2,1,0:T(2,128)S(1)}, f32[4,1,2,256]{3,2,1,0:T(2,128)S(1)}, u32[]{:S(2)}, u32[]{:S(2)}) collective-permute-start(f32[4,1,2,256]{3,2,1,0:T(2,128)S(1)} %slice.344), channel_id=1, source_target_pairs={{0,16},{4,20},{8,24},{12,28},{16,0},{20,4},{24,8},{28,12},{1,17},{... | collective-permute-start | bytes 24584 | tf_op jit(solution)/shard_map/ppermute | solution.py:223
  37.5 2.1 %collective-permute-done.6 = f32[4,1,2,256]{3,2,1,0:T(2,128)S(1)} collective-permute-done((f32[4,1,2,256]{3,2,1,0:T(2,128)S(1)}, f32[4,1,2,256]{3,2,1,0:T(2,128)S(1)}, u32[]{:S(2)}, u32[]{:S(2)}) %collective-permute-start.6) | collective-permute-done | bytes 8224 | tf_op jit(solution)/shard_map/ppermute | solution.py:223
  39.6 0.9 collective-permute-start.7
  40.6 3.6 %collective-permute-done.7 = f32[2,1,2,256]{3,2,1,0:T(2,128)S(1)} collective-permute-done((f32[2,1,2,256]{3,2,1,0:T(2,128)S(1)}, f32[2,1,2,256]{3,2,1,0:T(2,128)S(1)}, u32[]{:S(2)}, u32[]{:S(2)}) %collective-permute-start.7) | collective-permute-done | bytes 4128 | tf_op jit(solution)/shard_map/ppermute | solution.py:223
  44.2 0.1 collective-permute-start.2
  44.3 3.8 %collective-permute-start.3 = (f32[20480]{0:T(1024)S(1)}, f32[20480]{0:T(1024)S(1)}, u32[]{:S(2)}, u32[]{:S(2)}) collective-permute-start(f32[20480]{0:T(1024)S(1)} %get-tuple-element.12), channel_id=1, source_target_pairs={{1,0},{2,1},{3,2},{0,3},{5,4},{6,5},{7,6},{4,7},{9,8},{10,9},{11,1... | collective-permute-start | bytes 245768 | tf_op jit(solution)/shard_map/ppermute | solution.py:64
  48.1 0.3 fusion.28
  48.4 0.1 mul.471
  48.4 1.3 %multiply_reduce_fusion.2 = f32[2,2,4,128]{3,2,1,0:T(4,128)S(1)} fusion(f32[4,256]{1,0:T(4,128)S(1)} %mul.471, f32[256]{0:T(256)S(1)} %bitcast.175, f32[2,2,4,128]{3,2,1,0:T(4,128)S(1)} %get-tuple-element.27, f32[256]{0:T(256)S(1)} %bitcast.177, f32[2,2,4,128]{3,2,1,0:T(4,128)S(1)} %get-tuple-element.20, f32[256]{0:T(256)S(1)} %bitcast.173, ...), kind=kLoop, calls=%fused_computation.14 | loop fusion | flops 5765120 | bytes 39936 | tf_op jit(solution)/shard_map/reduce_sum | solution.py:29
  49.8 1.6 %collective-permute-done.2 = f32[20480]{0:T(1024)S(1)} collective-permute-done((f32[20480]{0:T(1024)S(1)}, f32[20480]{0:T(1024)S(1)}, u32[]{:S(2)}, u32[]{:S(2)}) %collective-permute-start.2) | collective-permute-done | bytes 81952 | tf_op jit(solution)/shard_map/ppermute | solution.py:63
  51.4 0.1 select_maximum_fusion
  51.6 0.1 fusion.17
  51.7 0.1 fusion.16
  51.8 0.1 fusion.15
  51.9 0.1 fusion.14
  52.0 0.1 fusion.13
  52.1 0.1 fusion.12
  52.2 0.3 copy.25
  52.5 0.2 copy-done.1
  52.8 47.3 %shard_map.163 = f32[16,256]{1,0:T(8,128)S(1)} custom-call(f32[474]{0:T(512)S(1)} %copy-done.2, s32[1264]{0:T(1024)S(1)} %copy-done.1, f32[3,256,256]{2,1,0:T(8,128)S(1)} %pad_maximum_fusion.base_ref, f32[448,4,256]{2,1,0:T(4,128)S(1)} %bitcast.133), custom_call_target="tpu_custom_call" | custom-call | flops 2133065728 | bytes 2637824 | tf_op jit(solution)/shard_map/pallas_call | solution.py:130
  100.1 0.3 fusion.19
  100.5 1.3 %multiply_reduce_fusion.3 = f32[2,2,4,128]{3,2,1,0:T(4,128)S(1)} fusion(f32[2,2,4,256]{3,2,1,0:T(4,128)S(1)} %fusion.19, f32[256]{0:T(256)S(1)} %bitcast.184, f32[2,2,4,128]{3,2,1,0:T(4,128)S(1)} %get-tuple-element.24, f32[256]{0:T(256)S(1)} %bitcast.182, f32[2,2,4,128]{3,2,1,0:T(4,128)S(1)} %get-tuple-element.23, f32[256]{0:T(256)S(1)} %bitcast.186, ...), kind=kLoop, calls=%fused_computation.16 | loop fusion | flops 5765120 | bytes 52224 | tf_op jit(solution)/shard_map/reduce_sum | solution.py:29
  101.9 0.1 copy.29
  102.0 2.3 %gather_fusion = f32[432,4,128]{2,1,0:T(4,128)S(1)} fusion(f32[4,96,128]{2,0,1:T(4,128)S(1)} %bitcast.134, s32[1024]{0:T(1024)S(1)} %pad_clamp_fusion), kind=kCustom, calls=%fused_computation | custom fusion | bytes 1771200 | tf_op jit(solution)/shard_map/jit(_take)/gather | solution.py:270
  104.3 0.5 copy.55
  104.8 0.1 fusion.33
  104.9 0.1 copy.56
  105.1 0.1 copy.57
  105.2 0.1 copy.58
  105.3 0.1 copy.59
  105.5 0.0 copy-done.11
  105.5 0.0 copy-done.12
  105.5 0.0 copy-done.13
  105.6 20.0 %fusion.5 = f32[16,128]{1,0:T(8,128)S(1)} fusion(f32[3456]{0:T(1024)S(1)} %copy-done.13, f32[3456]{0:T(1024)S(1)} %copy-done.12, f32[3456]{0:T(1024)S(1)} %copy-done.11, f32[16,3456]{1,0:T(8,128)S(1)} %bitcast.142, f32[16,3456]{1,0:T(8,128)S(1)} %bitcast.143, f32[16,128]{1,0:T(8,128)S(1)} %bitcast.167, f32[16,3456]{1,0:T(8,128)S(1)} %bitcast.144, ...), kind=kLoop, calls=%fused_computation.8 | loop fusion | flops 106166272 | bytes 1401344 | tf_op jit(solution)/shard_map/reduce_sum | solution.py:285
  125.5 0.7 add_select_fusion
  (101 shorter events, 1.2 us)
Async XLA Ops:
  0.0 3.5 %copy-start = (f32[256,256]{1,0:T(8,128)S(1)}, f32[256,256]{1,0:T(8,128)}, u32[]{:S(2)}) copy-start(f32[256,256]{1,0:T(8,128)} %param.20) | copy-start | bytes 786436
  4.6 27.3 %collective-permute-start = (f32[8192]{0:T(1024)S(1)}, f32[8192]{0:T(1024)S(1)}, u32[]{:S(2)}, u32[]{:S(2)}) collective-permute-start(f32[8192]{0:T(1024)S(1)} %get-tuple-element.28), channel_id=1, source_target_pairs={{0,4},{4,8},{8,12},{12,16},{16,20},{20,24},{24,28},{28,0},{1,5},{5... | collective-permute-start | bytes 98312 | tf_op jit(solution)/shard_map/ppermute | solution.py:63
  5.1 26.8 %collective-permute-start.1 = (f32[8192]{0:T(1024)S(1)}, f32[8192]{0:T(1024)S(1)}, u32[]{:S(2)}, u32[]{:S(2)}) collective-permute-start(f32[8192]{0:T(1024)S(1)} %get-tuple-element.29), channel_id=1, source_target_pairs={{4,0},{8,4},{12,8},{16,12},{20,16},{24,20},{28,24},{0,28},{5,1},{9... | collective-permute-start | bytes 98312 | tf_op jit(solution)/shard_map/ppermute | solution.py:64
  8.5 1.3 %copy-start.5 = (f32[256,256]{1,0:T(8,128)S(1)}, f32[256,256]{1,0:T(8,128)}, u32[]{:S(2)}) copy-start(f32[256,256]{1,0:T(8,128)} %param.22) | copy-start | bytes 786436
  8.5 1.7 %copy-start.9 = (f32[23]{0:T(128)S(1)}, f32[23]{0:T(128)}, u32[]{:S(2)}) copy-start(f32[23]{0:T(128)} %constant.135) | copy-start | bytes 280
  8.5 1.9 %copy-start.10 = (f32[23]{0:T(128)S(1)}, f32[23]{0:T(128)}, u32[]{:S(2)}) copy-start(f32[23]{0:T(128)} %constant.136) | copy-start | bytes 280
  10.7 18.0 %copy-start.3 = (f32[3,2,2,4,128]{4,3,2,1,0:T(4,128)S(1)}, f32[3,2,2,4,128]{4,3,2,1,0:T(4,128)}, u32[]{:S(2)}) copy-start(f32[3,2,2,4,128]{4,3,2,1,0:T(4,128)} %param.17) | copy-start | bytes 73732
  23.7 5.1 %copy-start.8 = (s32[432]{0:T(512)S(1)}, s32[432]{0:T(512)}, u32[]{:S(2)}) copy-start(s32[432]{0:T(512)} %constant.137) | copy-start | bytes 5188
  24.6 23.5 %copy-start.6 = (f32[256,256]{1,0:T(8,128)S(1)}, f32[256,256]{1,0:T(8,128)}, u32[]{:S(2)}) copy-start(f32[256,256]{1,0:T(8,128)} %param.23) | copy-start | bytes 786436
  24.7 5.2 %collective-permute-start.4 = (f32[8,2,2,256]{3,2,1,0:T(2,128)S(1)}, f32[8,2,2,256]{3,2,1,0:T(2,128)S(1)}, u32[]{:S(2)}, u32[]{:S(2)}) collective-permute-start(f32[8,2,2,256]{3,2,1,0:T(2,128)S(1)} %slice.340), channel_id=1, source_target_pairs={{0,2},{1,3},{2,0},{3,1},{4,6},{5,7},{6,4},{7,5},{8,10},{9,11},{10,... | collective-permute-start | bytes 98312 | tf_op jit(solution)/shard_map/ppermute | solution.py:223
  29.9 5.9 %collective-permute-start.5 = (f32[8,1,2,256]{3,2,1,0:T(2,128)S(1)}, f32[8,1,2,256]{3,2,1,0:T(2,128)S(1)}, u32[]{:S(2)}, u32[]{:S(2)}) collective-permute-start(f32[8,1,2,256]{3,2,1,0:T(2,128)S(1)} %slice.342), channel_id=1, source_target_pairs={{0,1},{1,2},{2,3},{3,0},{4,5},{5,6},{6,7},{7,4},{8,9},{9,10},{10,1... | collective-permute-start | bytes 49160 | tf_op jit(solution)/shard_map/ppermute | solution.py:223
  35.9 3.7 %collective-permute-start.6 = (f32[4,1,2,256]{3,2,1,0:T(2,128)S(1)}, f32[4,1,2,256]{3,2,1,0:T(2,128)S(1)}, u32[]{:S(2)}, u32[]{:S(2)}) collective-permute-start(f32[4,1,2,256]{3,2,1,0:T(2,128)S(1)} %slice.344), channel_id=1, source_target_pairs={{0,16},{4,20},{8,24},{12,28},{16,0},{20,4},{24,8},{28,12},{1,17},{... | collective-permute-start | bytes 24584 | tf_op jit(solution)/shard_map/ppermute | solution.py:223
  39.6 4.6 %collective-permute-start.7 = (f32[2,1,2,256]{3,2,1,0:T(2,128)S(1)}, f32[2,1,2,256]{3,2,1,0:T(2,128)S(1)}, u32[]{:S(2)}, u32[]{:S(2)}) collective-permute-start(f32[2,1,2,256]{3,2,1,0:T(2,128)S(1)} %slice.346), channel_id=1, source_target_pairs={{0,8},{4,12},{8,16},{12,20},{16,24},{20,28},{24,0},{28,4},{1,9},{5... | collective-permute-start | bytes 12296 | tf_op jit(solution)/shard_map/ppermute | solution.py:223
  44.2 3.9 %collective-permute-start.8 = (f32[1,1,2,256]{3,2,1,0:T(2,128)S(1)}, f32[1,1,2,256]{3,2,1,0:T(2,128)S(1)}, u32[]{:S(2)}, u32[]{:S(2)}) collective-permute-start(f32[1,1,2,256]{3,2,1,0:T(2,128)S(1)} %slice.348), channel_id=1, source_target_pairs={{0,4},{4,8},{8,12},{12,16},{16,20},{20,24},{24,28},{28,0},{1,5},{5... | collective-permute-start | bytes 6152 | tf_op jit(solution)/shard_map/ppermute | solution.py:223
  44.2 7.1 %collective-permute-start.2 = (f32[20480]{0:T(1024)S(1)}, f32[20480]{0:T(1024)S(1)}, u32[]{:S(2)}, u32[]{:S(2)}) collective-permute-start(f32[20480]{0:T(1024)S(1)} %get-tuple-element.11), channel_id=1, source_target_pairs={{0,1},{1,2},{2,3},{3,0},{4,5},{5,6},{6,7},{7,4},{8,9},{9,10},{10,1... | collective-permute-start | bytes 245768 | tf_op jit(solution)/shard_map/ppermute | solution.py:63
  44.3 7.1 %collective-permute-start.3 = (f32[20480]{0:T(1024)S(1)}, f32[20480]{0:T(1024)S(1)}, u32[]{:S(2)}, u32[]{:S(2)}) collective-permute-start(f32[20480]{0:T(1024)S(1)} %get-tuple-element.12), channel_id=1, source_target_pairs={{1,0},{2,1},{3,2},{0,3},{5,4},{6,5},{7,6},{4,7},{9,8},{10,9},{11,1... | collective-permute-start | bytes 245768 | tf_op jit(solution)/shard_map/ppermute | solution.py:64
  52.1 0.7 copy-start.1
  52.1 0.7 copy-start.2
  52.8 47.3 %copy-start.4 = (f32[256,256]{1,0:T(8,128)S(1)}, f32[256,256]{1,0:T(8,128)}, u32[]{:S(2)}) copy-start(f32[256,256]{1,0:T(8,128)} %param.21) | copy-start | bytes 786436
  104.8 0.7 copy-start.11
  104.8 0.7 copy-start.12
  104.8 0.7 copy-start.13
  105.5 20.0 %copy-start.7 = (s32[2,2,4]{2,1,0:T(2,128)S(1)}, s32[2,2,4]{2,1,0:T(2,128)}, u32[]{:S(2)}) copy-start(s32[2,2,4]{2,1,0:T(2,128)} %param.19) | copy-start | bytes 196

commit v10 on v6

--- a/solution.py
+++ b/solution.py
@@ -140,7 +140,7 @@
     shift_count = table.shape[0] // 3
     points = windows.shape[-1]
     return pl.pallas_call(
-        functools.partial(m2l_kernel, shift_count, 128),
+        functools.partial(m2l_kernel, shift_count, 256),
         out_shape=jax.ShapeDtypeStruct((vectors, points), jnp.float32),
         in_specs=[
             pl.BlockSpec(memory_space=pltpu.SMEM),

time: 121 us -> 122 us (level)
    pallas_call x1, Pallas kernels: 47.3 us -> 48.5 us  [m2l(): pl.pallas_call(functools.partial(m2l_kernel, shift_count, 256), out_shape...]
where the time goes in v10:
time: 122 us
  Pallas kernels  48.5 us (40%)
  other arithmetic  41.4 us (34%)
  starting transfers between devices  16.5 us (14%)
  local copies, waits for them, and re-layouts  6.79 us (6%)
  waiting for transfers between devices  6.51 us (5%)
    pallas_call x1, Pallas kernels, m2l(): pl.pallas_call(functools.partial(m2l_kernel, shift_count, 256), out_shape...  48.5 us
    reduce_sum x1, other arithmetic, shards(): jnp.sum(kernel * source[3][..., None, :], axis=-1)  20 us
    reduce_sum x5, other arithmetic, point_sum(): return jnp.sum(kernel * weights[..., None, :], axis=-1)  15.8 us
    ppermute x5, starting transfers between devices, rel_gather(): lax.ppermute(part, axis, [(j, (j - have) % count) for j in range(count)])  8.79 us
    ppermute x5, waiting for transfers between devices, rel_gather(): lax.ppermute(part, axis, [(j, (j - have) % count) for j in range(count)])  6.49 us
    ppermute x2, starting transfers between devices, exchange(): lax.ppermute(sent_head, axis, [((i + 1) % count, i) for i in range(count)])  5.55 us
    gather x2, local copies, waits for them, and re-layouts, shards(): jnp.take(padded_around.reshape(4, -1, slot_count), box_rows, axis=1)  2.79 us
  transfers between devices with their start and end apart: 9, of which 3 were waited for; matrix products, arithmetic and copies ran while one was open for 14% of the time, Pallas kernels for 0%

profile of v10, /device:TPU:0, one launch (start us, length us, event | category | flops | bytes accessed | tf_op | source)
XLA Modules:
  0.0 121.7 jit_solution(12888971946021432319)
XLA Ops:
  0.0 0.1 cosine_multiply_fusion.1
  0.1 0.1 sine_multiply_fusion.1
  0.1 0.8 fusion.24
  0.9 0.8 fusion.46
  1.7 0.7 fusion.35
  2.4 1.1 multiply_reduce_fusion.4
  3.5 0.3 fusion.21
  3.9 0.7 fusion.23
  4.6 0.5 collective-permute-start
  5.1 2.9 %collective-permute-start.1 = (f32[8192]{0:T(1024)S(1)}, f32[8192]{0:T(1024)S(1)}, u32[]{:S(2)}, u32[]{:S(2)}) collective-permute-start(f32[8192]{0:T(1024)S(1)} %get-tuple-element.29), channel_id=1, source_target_pairs={{4,0},{8,4},{12,8},{16,12},{20,16},{24,20},{28,24},{0,28},{5,1},{9... | collective-permute-start | bytes 98312 | tf_op jit(solution)/shard_map/ppermute | solution.py:76
  8.3 0.1 broadcast_add_fusion.8
  8.4 0.8 add_rsqrt_fusion
  9.2 0.4 multiply_reduce_fusion.1
  9.7 0.3 convolution_bitcast_fusion
  10.0 4.4 %collective-permute-start.4 = (f32[1,1,2,256]{3,2,1,0:T(2,128)S(1)}, f32[1,1,2,256]{3,2,1,0:T(2,128)S(1)}, u32[]{:S(2)}, u32[]{:S(2)}) collective-permute-start(f32[1,1,2,256]{3,2,1,0:T(2,128)S(1)} %convolution_bitcast_fusion), channel_id=1, source_target_pairs={{0,3},{1,0},{2,1},{3,2},{4,7},{5,4},{6,5},{7,6},{8,11},{9,8},{10,9... | collective-permute-start | bytes 6152 | tf_op jit(solution)/shard_map/ppermute | solution.py:61
  14.4 0.1 fusion.28
  14.5 0.1 fusion.30
  14.7 0.1 subtract_multiply_fusion.2
  14.8 0.3 iota_compare_fusion
  15.1 0.1 subtract_multiply_fusion.3
  15.2 0.1 broadcast_add_fusion.4
  15.2 0.1 subtract_multiply_fusion
  15.4 0.1 broadcast_add_fusion.5
  15.4 0.1 broadcast_add_fusion.1
  15.5 0.1 broadcast_add_fusion
  15.6 1.2 %collective-permute-start.5 = (f32[1,2,2,256]{3,2,1,0:T(2,128)S(1)}, f32[1,2,2,256]{3,2,1,0:T(2,128)S(1)}, u32[]{:S(2)}, u32[]{:S(2)}) collective-permute-start(f32[1,2,2,256]{3,2,1,0:T(2,128)S(1)} %pad_maximum_fusion.14), channel_id=1, source_target_pairs={{0,2},{1,3},{2,0},{3,1},{4,6},{5,7},{6,4},{7,5},{8,10},{9,11},{10,... | collective-permute-start | bytes 12296 | tf_op jit(solution)/shard_map/ppermute | solution.py:61
  16.9 0.1 pad_maximum_fusion.base_ref
  16.9 3.3 %collective-permute-done.5 = f32[1,2,2,256]{3,2,1,0:T(2,128)S(1)} collective-permute-done((f32[1,2,2,256]{3,2,1,0:T(2,128)S(1)}, f32[1,2,2,256]{3,2,1,0:T(2,128)S(1)}, u32[]{:S(2)}, u32[]{:S(2)}) %collective-permute-start.5) | collective-permute-done | bytes 4128 | tf_op jit(solution)/shard_map/ppermute | solution.py:61
  20.3 1.3 %collective-permute-done.6 = f32[1,4,2,256]{3,2,1,0:T(2,128)S(1)} collective-permute-done((f32[1,4,2,256]{3,2,1,0:T(2,128)S(1)}, f32[1,4,2,256]{3,2,1,0:T(2,128)S(1)}, u32[]{:S(2)}, u32[]{:S(2)}) %collective-permute-start.6) | collective-permute-done | bytes 8224 | tf_op jit(solution)/shard_map/ppermute | solution.py:61
  21.6 1.6 %collective-permute-start.7 = (f32[2,4,2,256]{3,2,1,0:T(2,128)S(1)}, f32[2,4,2,256]{3,2,1,0:T(2,128)S(1)}, u32[]{:S(2)}, u32[]{:S(2)}) collective-permute-start(f32[2,4,2,256]{3,2,1,0:T(2,128)S(1)} %pad_maximum_fusion.11), channel_id=1, source_target_pairs={{0,24},{4,28},{8,0},{12,4},{16,8},{20,12},{24,16},{28,20},{1,25},{... | collective-permute-start | bytes 49160 | tf_op jit(solution)/shard_map/ppermute | solution.py:61
  23.2 0.1 stack_broadcast_in_dim.41
  23.5 1.9 %collective-permute-done.7 = f32[2,4,2,256]{3,2,1,0:T(2,128)S(1)} collective-permute-done((f32[2,4,2,256]{3,2,1,0:T(2,128)S(1)}, f32[2,4,2,256]{3,2,1,0:T(2,128)S(1)}, u32[]{:S(2)}, u32[]{:S(2)}) %collective-permute-start.7) | collective-permute-done | bytes 16416 | tf_op jit(solution)/shard_map/ppermute | solution.py:61
  25.4 1.6 %collective-permute-start.8 = (f32[4,4,2,256]{3,2,1,0:T(2,128)S(1)}, f32[4,4,2,256]{3,2,1,0:T(2,128)S(1)}, u32[]{:S(2)}, u32[]{:S(2)}) collective-permute-start(f32[4,4,2,256]{3,2,1,0:T(2,128)S(1)} %pad_maximum_fusion.9), channel_id=1, source_target_pairs={{0,16},{4,20},{8,24},{12,28},{16,0},{20,4},{24,8},{28,12},{1,17},{... | collective-permute-start | bytes 98312 | tf_op jit(solution)/shard_map/ppermute | solution.py:61
  27.2 1.7 %collective-permute-start.2 = (f32[20480]{0:T(1024)S(1)}, f32[20480]{0:T(1024)S(1)}, u32[]{:S(2)}, u32[]{:S(2)}) collective-permute-start(f32[20480]{0:T(1024)S(1)} %get-tuple-element.11), channel_id=1, source_target_pairs={{0,1},{1,2},{2,3},{3,0},{4,5},{5,6},{6,7},{7,4},{8,9},{9,10},{10,1... | collective-permute-start | bytes 245768 | tf_op jit(solution)/shard_map/ppermute | solution.py:75
  28.9 2.6 %collective-permute-start.3 = (f32[20480]{0:T(1024)S(1)}, f32[20480]{0:T(1024)S(1)}, u32[]{:S(2)}, u32[]{:S(2)}) collective-permute-start(f32[20480]{0:T(1024)S(1)} %get-tuple-element.12), channel_id=1, source_target_pairs={{1,0},{2,1},{3,2},{0,3},{5,4},{6,5},{7,6},{4,7},{9,8},{10,9},{11,1... | collective-permute-start | bytes 245768 | tf_op jit(solution)/shard_map/ppermute | solution.py:76
  31.5 0.6 gather_fusion.1
  32.2 11.7 %multiply_reduce_fusion = f32[2,256]{1,0:T(2,128)S(1)} fusion(f32[11776]{0:T(1024)S(1)} %select_n.55, f32[2,11776]{1,0:T(2,128)S(1)} %stack_broadcast_in_dim.41, f32[256]{0:T(256)S(1)} %bitcast.181, f32[11776]{0:T(1024)S(1)} %stack_broadcast_in_dim.39, f32[256]{0:T(256)S(1)} %bitcast.182, f32[11776]{0:T(1024)S(1)} %stack_broadcast_in_dim.37, f32[256]{0:T(256)S(1)} %bitcast.180), kind=kLoop, calls=%fused_computation.12 | loop fusion | flops 66321920 | bytes 240640 | tf_op jit(solution)/shard_map/reduce_sum | solution.py:29
  43.9 0.3 fusion.39
  44.1 0.1 mul.507
  44.2 1.3 %multiply_reduce_fusion.2 = f32[2,2,4,128]{3,2,1,0:T(4,128)S(1)} fusion(f32[4,256]{1,0:T(4,128)S(1)} %mul.507, f32[256]{0:T(256)S(1)} %bitcast.171, f32[2,2,4,128]{3,2,1,0:T(4,128)S(1)} %get-tuple-element.27, f32[256]{0:T(256)S(1)} %bitcast.173, f32[2,2,4,128]{3,2,1,0:T(4,128)S(1)} %get-tuple-element.20, f32[256]{0:T(256)S(1)} %bitcast.169, ...), kind=kLoop, calls=%fused_computation.14 | loop fusion | flops 5765120 | bytes 39936 | tf_op jit(solution)/shard_map/reduce_sum | solution.py:29
  45.6 0.1 select_maximum_fusion
  45.8 0.1 fusion.17
  45.9 0.1 fusion.16
  46.0 0.1 fusion.15
  46.1 0.1 fusion.14
  46.2 0.1 fusion.13
  46.3 0.1 fusion.12
  46.4 0.3 copy.24
  46.8 0.2 copy-done.1
  47.0 48.5 %shard_map.154 = f32[16,256]{1,0:T(8,128)S(1)} custom-call(f32[474]{0:T(512)S(1)} %copy-done.2, s32[1264]{0:T(1024)S(1)} %copy-done.1, f32[3,256,256]{2,1,0:T(8,128)S(1)} %pad_maximum_fusion.base_ref, f32[448,4,256]{2,1,0:T(4,128)S(1)} %bitcast.130), custom_call_target="tpu_custom_call" | custom-call | flops 2133065728 | bytes 2637824 | tf_op jit(solution)/shard_map/pallas_call | solution.py:142
  95.6 0.3 fusion.19
  95.9 1.3 %multiply_reduce_fusion.3 = f32[2,2,4,128]{3,2,1,0:T(4,128)S(1)} fusion(f32[2,2,4,256]{3,2,1,0:T(4,128)S(1)} %fusion.19, f32[256]{0:T(256)S(1)} %bitcast.177, f32[2,2,4,128]{3,2,1,0:T(4,128)S(1)} %get-tuple-element.24, f32[256]{0:T(256)S(1)} %bitcast.175, f32[2,2,4,128]{3,2,1,0:T(4,128)S(1)} %get-tuple-element.23, f32[256]{0:T(256)S(1)} %bitcast.179, ...), kind=kLoop, calls=%fused_computation.16 | loop fusion | flops 5765120 | bytes 52224 | tf_op jit(solution)/shard_map/reduce_sum | solution.py:29
  97.3 0.1 copy.28
  97.4 2.3 %gather_fusion = f32[432,4,128]{2,1,0:T(4,128)S(1)} fusion(f32[4,96,128]{2,0,1:T(4,128)S(1)} %bitcast.131, s32[1024]{0:T(1024)S(1)} %pad_clamp_fusion.1), kind=kCustom, calls=%fused_computation | custom fusion | bytes 1771200 | tf_op jit(solution)/shard_map/jit(_take)/gather | solution.py:267
  99.7 0.5 copy.50
  100.3 0.1 fusion.31
  100.4 0.1 copy.51
  100.5 0.1 copy.52
  100.6 0.1 copy.53
  100.8 0.1 copy.54
  100.9 0.0 copy-done.12
  101.0 0.0 copy-done.13
  101.0 20.0 %fusion.5 = f32[16,128]{1,0:T(8,128)S(1)} fusion(f32[3456]{0:T(1024)S(1)} %copy-done.14, f32[3456]{0:T(1024)S(1)} %copy-done.13, f32[3456]{0:T(1024)S(1)} %copy-done.12, f32[16,3456]{1,0:T(8,128)S(1)} %bitcast.139, f32[16,3456]{1,0:T(8,128)S(1)} %bitcast.140, f32[16,128]{1,0:T(8,128)S(1)} %bitcast.165, f32[16,3456]{1,0:T(8,128)S(1)} %bitcast.141, ...), kind=kLoop, calls=%fused_computation.8 | loop fusion | flops 106166272 | bytes 1401344 | tf_op jit(solution)/shard_map/reduce_sum | solution.py:282
  121.0 0.7 add_select_fusion
  (95 shorter events, 1.1 us)
Async XLA Ops:
  0.0 3.5 %copy-start = (f32[256,256]{1,0:T(8,128)S(1)}, f32[256,256]{1,0:T(8,128)}, u32[]{:S(2)}) copy-start(f32[256,256]{1,0:T(8,128)} %param.19) | copy-start | bytes 786436
  4.6 22.4 %collective-permute-start = (f32[8192]{0:T(1024)S(1)}, f32[8192]{0:T(1024)S(1)}, u32[]{:S(2)}, u32[]{:S(2)}) collective-permute-start(f32[8192]{0:T(1024)S(1)} %get-tuple-element.28), channel_id=1, source_target_pairs={{0,4},{4,8},{8,12},{12,16},{16,20},{20,24},{24,28},{28,0},{1,5},{5... | collective-permute-start | bytes 98312 | tf_op jit(solution)/shard_map/ppermute | solution.py:75
  5.1 21.9 %collective-permute-start.1 = (f32[8192]{0:T(1024)S(1)}, f32[8192]{0:T(1024)S(1)}, u32[]{:S(2)}, u32[]{:S(2)}) collective-permute-start(f32[8192]{0:T(1024)S(1)} %get-tuple-element.29), channel_id=1, source_target_pairs={{4,0},{8,4},{12,8},{16,12},{20,16},{24,20},{28,24},{0,28},{5,1},{9... | collective-permute-start | bytes 98312 | tf_op jit(solution)/shard_map/ppermute | solution.py:76
  8.4 1.3 %copy-start.5 = (f32[256,256]{1,0:T(8,128)S(1)}, f32[256,256]{1,0:T(8,128)}, u32[]{:S(2)}) copy-start(f32[256,256]{1,0:T(8,128)} %param.21) | copy-start | bytes 786436
  8.4 6.7 %copy-start.3 = (f32[3,2,2,4,128]{4,3,2,1,0:T(4,128)S(1)}, f32[3,2,2,4,128]{4,3,2,1,0:T(4,128)}, u32[]{:S(2)}) copy-start(f32[3,2,2,4,128]{4,3,2,1,0:T(4,128)} %param.16) | copy-start | bytes 73732
  9.2 6.2 %copy-start.10 = (f32[23]{0:T(128)S(1)}, f32[23]{0:T(128)}, u32[]{:S(2)}) copy-start(f32[23]{0:T(128)} %constant.139) | copy-start | bytes 280
  9.2 6.3 %copy-start.11 = (f32[23]{0:T(128)S(1)}, f32[23]{0:T(128)}, u32[]{:S(2)}) copy-start(f32[23]{0:T(128)} %constant.140) | copy-start | bytes 280
  9.7 10.6 %copy-start.8 = (s32[432]{0:T(512)S(1)}, s32[432]{0:T(512)}, u32[]{:S(2)}) copy-start(s32[432]{0:T(512)} %constant.150) | copy-start | bytes 5188
  9.7 13.5 %copy-start.9 = (s32[23]{0:T(128)S(1)}, s32[23]{0:T(128)}, u32[]{:S(2)}) copy-start(s32[23]{0:T(128)} %constant.151) | copy-start | bytes 280
  10.0 5.7 %collective-permute-start.4 = (f32[1,1,2,256]{3,2,1,0:T(2,128)S(1)}, f32[1,1,2,256]{3,2,1,0:T(2,128)S(1)}, u32[]{:S(2)}, u32[]{:S(2)}) collective-permute-start(f32[1,1,2,256]{3,2,1,0:T(2,128)S(1)} %convolution_bitcast_fusion), channel_id=1, source_target_pairs={{0,3},{1,0},{2,1},{3,2},{4,7},{5,4},{6,5},{7,6},{8,11},{9,8},{10,9... | collective-permute-start | bytes 6152 | tf_op jit(solution)/shard_map/ppermute | solution.py:61
  15.6 4.6 %collective-permute-start.5 = (f32[1,2,2,256]{3,2,1,0:T(2,128)S(1)}, f32[1,2,2,256]{3,2,1,0:T(2,128)S(1)}, u32[]{:S(2)}, u32[]{:S(2)}) collective-permute-start(f32[1,2,2,256]{3,2,1,0:T(2,128)S(1)} %pad_maximum_fusion.14), channel_id=1, source_target_pairs={{0,2},{1,3},{2,0},{3,1},{4,6},{5,7},{6,4},{7,5},{8,10},{9,11},{10,... | collective-permute-start | bytes 12296 | tf_op jit(solution)/shard_map/ppermute | solution.py:61
  20.2 1.4 %collective-permute-start.6 = (f32[1,4,2,256]{3,2,1,0:T(2,128)S(1)}, f32[1,4,2,256]{3,2,1,0:T(2,128)S(1)}, u32[]{:S(2)}, u32[]{:S(2)}) collective-permute-start(f32[1,4,2,256]{3,2,1,0:T(2,128)S(1)} %pad_maximum_fusion.12), channel_id=1, source_target_pairs={{0,28},{4,0},{8,4},{12,8},{16,12},{20,16},{24,20},{28,24},{1,29},{... | collective-permute-start | bytes 24584 | tf_op jit(solution)/shard_map/ppermute | solution.py:61
  21.6 3.8 %collective-permute-start.7 = (f32[2,4,2,256]{3,2,1,0:T(2,128)S(1)}, f32[2,4,2,256]{3,2,1,0:T(2,128)S(1)}, u32[]{:S(2)}, u32[]{:S(2)}) collective-permute-start(f32[2,4,2,256]{3,2,1,0:T(2,128)S(1)} %pad_maximum_fusion.11), channel_id=1, source_target_pairs={{0,24},{4,28},{8,0},{12,4},{16,8},{20,12},{24,16},{28,20},{1,25},{... | collective-permute-start | bytes 49160 | tf_op jit(solution)/shard_map/ppermute | solution.py:61
  25.4 6.1 %collective-permute-start.8 = (f32[4,4,2,256]{3,2,1,0:T(2,128)S(1)}, f32[4,4,2,256]{3,2,1,0:T(2,128)S(1)}, u32[]{:S(2)}, u32[]{:S(2)}) collective-permute-start(f32[4,4,2,256]{3,2,1,0:T(2,128)S(1)} %pad_maximum_fusion.9), channel_id=1, source_target_pairs={{0,16},{4,20},{8,24},{12,28},{16,0},{20,4},{24,8},{28,12},{1,17},{... | collective-permute-start | bytes 98312 | tf_op jit(solution)/shard_map/ppermute | solution.py:61
  27.2 18.3 %collective-permute-start.2 = (f32[20480]{0:T(1024)S(1)}, f32[20480]{0:T(1024)S(1)}, u32[]{:S(2)}, u32[]{:S(2)}) collective-permute-start(f32[20480]{0:T(1024)S(1)} %get-tuple-element.11), channel_id=1, source_target_pairs={{0,1},{1,2},{2,3},{3,0},{4,5},{5,6},{6,7},{7,4},{8,9},{9,10},{10,1... | collective-permute-start | bytes 245768 | tf_op jit(solution)/shard_map/ppermute | solution.py:75
  28.9 16.7 %collective-permute-start.3 = (f32[20480]{0:T(1024)S(1)}, f32[20480]{0:T(1024)S(1)}, u32[]{:S(2)}, u32[]{:S(2)}) collective-permute-start(f32[20480]{0:T(1024)S(1)} %get-tuple-element.12), channel_id=1, source_target_pairs={{1,0},{2,1},{3,2},{0,3},{5,4},{6,5},{7,6},{4,7},{9,8},{10,9},{11,1... | collective-permute-start | bytes 245768 | tf_op jit(solution)/shard_map/ppermute | solution.py:76
  32.2 11.7 %copy-start.6 = (f32[256,256]{1,0:T(8,128)S(1)}, f32[256,256]{1,0:T(8,128)}, u32[]{:S(2)}) copy-start(f32[256,256]{1,0:T(8,128)} %param.22) | copy-start | bytes 786436
  46.3 0.7 copy-start.1
  46.3 0.7 copy-start.2
  47.0 48.6 %copy-start.4 = (f32[256,256]{1,0:T(8,128)S(1)}, f32[256,256]{1,0:T(8,128)}, u32[]{:S(2)}) copy-start(f32[256,256]{1,0:T(8,128)} %param.20) | copy-start | bytes 786436
  100.2 0.7 copy-start.12
  100.2 0.7 copy-start.13
  100.3 0.7 copy-start.14
  101.0 20.0 %copy-start.7 = (s32[2,2,4]{2,1,0:T(2,128)S(1)}, s32[2,2,4]{2,1,0:T(2,128)}, u32[]{:S(2)}) copy-start(s32[2,2,4]{2,1,0:T(2,128)} %param.18) | copy-start | bytes 196

commit v11 on v6

--- a/solution.py
+++ b/solution.py
@@ -52,9 +52,8 @@
     return jnp.stack([along_x, along_y, along_z]).reshape(3, 8 * point_count)
 
 
-def rel_gather(buf, axis, dim):
+def rel_gather(buf, axis, dim, have=1):
     count = lax.axis_size(axis)
-    have = 1
     while have < count:
         step = min(have, count - have)
         part = lax.slice_in_dim(buf, 0, step, axis=dim)
@@ -64,14 +63,16 @@
     return buf
 
 
-def exchange(items, axis):
+def exchange(items, axis, rider=None):
     count = lax.axis_size(axis)
     heads, tails = [], []
     for cells, dim, width in items:
         heads.append(lax.slice_in_dim(cells, 0, width, axis=dim))
         tails.append(lax.slice_in_dim(cells, cells.shape[dim] - width, cells.shape[dim], axis=dim))
     sent_tail = jnp.concatenate([t.reshape(-1) for t in tails])
-    sent_head = jnp.concatenate([h.reshape(-1) for h in heads])
+    sent_head = jnp.concatenate(
+        [h.reshape(-1) for h in heads] + ([] if rider is None else [rider.reshape(-1)])
+    )
     from_left = lax.ppermute(sent_tail, axis, [(i, (i + 1) % count) for i in range(count)])
     from_right = lax.ppermute(sent_head, axis, [((i + 1) % count, i) for i in range(count)])
     out, start = [], 0
@@ -81,6 +82,8 @@
         after = from_right[start : start + size].reshape(head.shape)
         out.append(jnp.concatenate([before, cells, after], axis=dim))
         start += size
+    if rider is not None:
+        out.append(from_right[start:].reshape(rider.shape))
     return out
 
 
@@ -180,8 +183,6 @@
     leaf_check_pts = 0.5 + 1.8 * unit_sphere
     leaf_check = point_sum(leaf_check_pts[:, None, None, None, :], offsets, weights)
     leaf_eq = jnp.einsum("ec,xyzc->xyze", c2e_leaf_up, leaf_check, precision=highest)
-    packed_x, eq_x = exchange([(packed, 1, 1), (leaf_eq, 0, 2)], "gx")
-    beside_all, cycle = exchange([(packed_x, 2, 1), (eq_x, 1, 2)], "gy")
     children = child_points(unit_sphere)
     parent_weights = (
         leaf_eq.reshape(2, 2, parent_layers, 2, points)
@@ -194,7 +195,14 @@
     count_x = lax.axis_size("gx")
     count_y = lax.axis_size("gy")
 
-    gathered = rel_gather(rel_gather(parent_eq[None, None], "gy", 1), "gx", 0)
+    packed_x, eq_x, right_eq = exchange(
+        [(packed, 1, 1), (leaf_eq, 0, 2)], "gx", rider=parent_eq
+    )
+    beside_all, cycle = exchange([(packed_x, 2, 1), (eq_x, 1, 2)], "gy")
+    pair = jnp.stack([parent_eq, right_eq])[:, None]
+    if count_x == 1:
+        pair = parent_eq[None, None]
+    gathered = rel_gather(rel_gather(pair, "gx", 0, min(2, count_x)), "gy", 1)
     kept = []
     for rel_x in range(count_x):
         for rel_y in range(count_y):

time: 121 us -> 121 us (level)
  waiting for transfers between devices: 6.51 us -> 10.6 us
  starting transfers between devices: 16.5 us -> 13 us
    ppermute x5 -> x4, starting transfers between devices: 8.79 us -> 5.73 us  [rel_gather(): lax.ppermute(part, axis, [(j, (j - have) % count) for j in range(count)])]
    ppermute x2, waiting for transfers between devices: 0.01 us -> 2.54 us  [exchange(): lax.ppermute(sent_tail, axis, [(i, (i + 1) % count) for i in range(count)])]
    ppermute x2, starting transfers between devices: 5.55 us -> 3.89 us  [exchange(): lax.ppermute(sent_head, axis, [((i + 1) % count, i) for i in range(count)])]
    ppermute x5 -> x4, waiting for transfers between devices: 6.49 us -> 8.06 us  [rel_gather(): lax.ppermute(part, axis, [(j, (j - have) % count) for j in range(count)])]
  transfers between devices with their start and end apart: 9 -> 8, of which waited for: 3 -> 4; matrix products, arithmetic and copies ran while one was open for 14% -> 13% of each run, Pallas kernels for 0% -> 0%
where the time goes in v11:
time: 121 us; the launch traced here: 120 us
  Pallas kernels  47.3 us (39%)
  other arithmetic  40.7 us (34%)
  starting transfers between devices  13 us (11%)
  waiting for transfers between devices  10.6 us (9%)
  local copies, waits for them, and re-layouts  6.88 us (6%)
    pallas_call x1, Pallas kernels, m2l(): pl.pallas_call(functools.partial(m2l_kernel, shift_count, 128), out_shape...  47.3 us
    reduce_sum x1, other arithmetic, shards(): jnp.sum(kernel * source[3][..., None, :], axis=-1)  20 us
    reduce_sum x5, other arithmetic, point_sum(): return jnp.sum(kernel * weights[..., None, :], axis=-1)  15.8 us
    ppermute x4, waiting for transfers between devices, rel_gather(): lax.ppermute(part, axis, [(j, (j - have) % count) for j in range(count)])  8.06 us
    ppermute x4, starting transfers between devices, rel_gather(): lax.ppermute(part, axis, [(j, (j - have) % count) for j in range(count)])  5.73 us
    ppermute x2, starting transfers between devices, exchange(): lax.ppermute(sent_head, axis, [((i + 1) % count, i) for i in range(count)])  3.89 us
    ppermute x2, starting transfers between devices, exchange(): lax.ppermute(sent_tail, axis, [(i, (i + 1) % count) for i in range(count)])  3.37 us
    gather x2, local copies, waits for them, and re-layouts, shards(): jnp.take(padded_around.reshape(4, -1, slot_count), box_rows, axis=1)  2.79 us
  transfers between devices with their start and end apart: 8, of which 4 were waited for; matrix products, arithmetic and copies ran while one was open for 13% of the time, Pallas kernels for 0%

profile of v11, /device:TPU:0, one launch (start us, length us, event | category | flops | bytes accessed | tf_op | source)
XLA Modules:
  0.0 120.4 jit_solution(11185764597657178817)
XLA Ops:
  0.0 0.1 cosine_multiply_fusion.1
  0.1 0.1 sine_multiply_fusion.1
  0.2 0.8 fusion.24
  1.0 0.8 fusion.47
  1.8 0.7 fusion.35
  2.5 1.1 multiply_reduce_fusion.4
  3.6 0.3 fusion.21
  4.0 0.1 broadcast_add_fusion.8
  4.2 0.8 add_rsqrt_fusion
  5.0 0.4 multiply_reduce_fusion.1
  5.5 0.3 fusion.39
  5.7 0.1 copy.31
  5.9 3.4 %collective-permute-start.1 = (f32[8704]{0:T(1024)S(1)}, f32[8704]{0:T(1024)S(1)}, u32[]{:S(2)}, u32[]{:S(2)}) collective-permute-start(f32[8704]{0:T(1024)S(1)} %pad_maximum_fusion.7), channel_id=1, source_target_pairs={{4,0},{8,4},{12,8},{16,12},{20,16},{24,20},{28,24},{0,28},{5,1},{9... | collective-permute-start | bytes 104456 | tf_op jit(solution)/shard_map/ppermute | solution.py:77
  9.4 0.1 fusion.28
  9.4 0.1 fusion.30
  9.6 0.1 subtract_multiply_fusion.2
  9.7 0.3 iota_compare_fusion
  10.0 0.1 subtract_multiply_fusion.3
  10.1 0.1 broadcast_add_fusion.4
  10.2 0.1 subtract_multiply_fusion
  10.3 0.1 broadcast_add_fusion.5
  10.4 0.1 broadcast_add_fusion.1
  10.5 0.1 broadcast_add_fusion
  10.6 0.1 pad_maximum_fusion.base_ref
  10.7 0.1 stack_broadcast_in_dim.44
  10.9 2.5 %collective-permute-done = f32[8192]{0:T(1024)S(1)} collective-permute-done((f32[8192]{0:T(1024)S(1)}, f32[8192]{0:T(1024)S(1)}, u32[]{:S(2)}, u32[]{:S(2)}) %collective-permute-start) | collective-permute-done | bytes 32800 | tf_op jit(solution)/shard_map/ppermute | solution.py:76
  13.5 0.1 collective-permute-start.4
  13.7 3.6 %collective-permute-done.4 = f32[2,1,2,256]{3,2,0,1:T(2,128)S(1)} collective-permute-done((f32[2,1,2,256]{3,2,0,1:T(2,128)S(1)}, f32[2,1,2,256]{3,2,0,1:T(2,128)S(1)}, u32[]{:S(2)}, u32[]{:S(2)}) %collective-permute-start.4) | collective-permute-done | bytes 4128 | tf_op jit(solution)/shard_map/ppermute | solution.py:60
  17.2 0.5 collective-permute-start.5
  17.8 3.1 %collective-permute-done.5 = f32[4,1,2,256]{3,2,0,1:T(2,128)S(1)} collective-permute-done((f32[4,1,2,256]{3,2,0,1:T(2,128)S(1)}, f32[4,1,2,256]{3,2,0,1:T(2,128)S(1)}, u32[]{:S(2)}, u32[]{:S(2)}) %collective-permute-start.5) | collective-permute-done | bytes 8224 | tf_op jit(solution)/shard_map/ppermute | solution.py:60
  20.9 3.7 %collective-permute-start.6 = (f32[8,1,2,256]{3,2,0,1:T(2,128)S(1)}, f32[8,1,2,256]{3,2,0,1:T(2,128)S(1)}, u32[]{:S(2)}, u32[]{:S(2)}) collective-permute-start(f32[8,1,2,256]{3,2,0,1:T(2,128)S(1)} %pad_maximum_fusion.11), channel_id=1, source_target_pairs={{0,3},{1,0},{2,1},{3,2},{4,7},{5,4},{6,5},{7,6},{8,11},{9,8},{10,9... | collective-permute-start | bytes 49160 | tf_op jit(solution)/shard_map/ppermute | solution.py:60
  24.6 1.4 %collective-permute-done.6 = f32[8,1,2,256]{3,2,0,1:T(2,128)S(1)} collective-permute-done((f32[8,1,2,256]{3,2,0,1:T(2,128)S(1)}, f32[8,1,2,256]{3,2,0,1:T(2,128)S(1)}, u32[]{:S(2)}, u32[]{:S(2)}) %collective-permute-start.6) | collective-permute-done | bytes 16416 | tf_op jit(solution)/shard_map/ppermute | solution.py:60
  26.0 1.5 %collective-permute-start.7 = (f32[8,2,2,256]{3,2,0,1:T(2,128)S(1)}, f32[8,2,2,256]{3,2,0,1:T(2,128)S(1)}, u32[]{:S(2)}, u32[]{:S(2)}) collective-permute-start(f32[8,2,2,256]{3,2,0,1:T(2,128)S(1)} %pad_maximum_fusion.9), channel_id=1, source_target_pairs={{0,2},{1,3},{2,0},{3,1},{4,6},{5,7},{6,4},{7,5},{8,10},{9,11},{10,... | collective-permute-start | bytes 98312 | tf_op jit(solution)/shard_map/ppermute | solution.py:60
  27.5 3.4 %collective-permute-start.2 = (f32[20480]{0:T(1024)S(1)}, f32[20480]{0:T(1024)S(1)}, u32[]{:S(2)}, u32[]{:S(2)}) collective-permute-start(f32[20480]{0:T(1024)S(1)} %get-tuple-element.11), channel_id=1, source_target_pairs={{0,1},{1,2},{2,3},{3,0},{4,5},{5,6},{6,7},{7,4},{8,9},{9,10},{10,1... | collective-permute-start | bytes 245768 | tf_op jit(solution)/shard_map/ppermute | solution.py:76
  30.9 0.5 collective-permute-start.3
  31.5 0.6 gather_fusion.1
  32.1 11.7 %multiply_reduce_fusion = f32[2,256]{1,0:T(2,128)S(1)} fusion(f32[11776]{0:T(1024)S(1)} %select_n.55, f32[2,11776]{1,0:T(2,128)S(1)} %stack_broadcast_in_dim.44, f32[256]{0:T(256)S(1)} %bitcast.188, f32[11776]{0:T(1024)S(1)} %stack_broadcast_in_dim.42, f32[256]{0:T(256)S(1)} %bitcast.189, f32[11776]{0:T(1024)S(1)} %stack_broadcast_in_dim.40, f32[256]{0:T(256)S(1)} %bitcast.187), kind=kLoop, calls=%fused_computation.12 | loop fusion | flops 66321920 | bytes 240640 | tf_op jit(solution)/shard_map/reduce_sum | solution.py:29
  43.8 0.3 fusion.40
  44.1 0.1 mul.507
  44.1 1.3 %multiply_reduce_fusion.2 = f32[2,2,4,128]{3,2,1,0:T(4,128)S(1)} fusion(f32[4,256]{1,0:T(4,128)S(1)} %mul.507, f32[256]{0:T(256)S(1)} %bitcast.178, f32[2,2,4,128]{3,2,1,0:T(4,128)S(1)} %get-tuple-element.27, f32[256]{0:T(256)S(1)} %bitcast.180, f32[2,2,4,128]{3,2,1,0:T(4,128)S(1)} %get-tuple-element.20, f32[256]{0:T(256)S(1)} %bitcast.176, ...), kind=kLoop, calls=%fused_computation.14 | loop fusion | flops 5765120 | bytes 39936 | tf_op jit(solution)/shard_map/reduce_sum | solution.py:29
  45.6 0.1 select_maximum_fusion
  45.8 0.1 fusion.17
  45.9 0.1 fusion.16
  46.0 0.1 fusion.15
  46.1 0.1 fusion.14
  46.1 0.1 fusion.13
  46.3 0.1 fusion.12
  46.4 0.3 copy.26
  46.7 0.2 copy-done.1
  46.9 47.3 %shard_map.154 = f32[16,256]{1,0:T(8,128)S(1)} custom-call(f32[474]{0:T(512)S(1)} %copy-done.2, s32[1264]{0:T(1024)S(1)} %copy-done.1, f32[3,256,256]{2,1,0:T(8,128)S(1)} %pad_maximum_fusion.base_ref, f32[448,4,256]{2,1,0:T(4,128)S(1)} %bitcast.133), custom_call_target="tpu_custom_call" | custom-call | flops 2133065728 | bytes 2637824 | tf_op jit(solution)/shard_map/pallas_call | solution.py:145
  94.3 0.3 fusion.19
  94.6 1.3 %multiply_reduce_fusion.3 = f32[2,2,4,128]{3,2,1,0:T(4,128)S(1)} fusion(f32[2,2,4,256]{3,2,1,0:T(4,128)S(1)} %fusion.19, f32[256]{0:T(256)S(1)} %bitcast.184, f32[2,2,4,128]{3,2,1,0:T(4,128)S(1)} %get-tuple-element.24, f32[256]{0:T(256)S(1)} %bitcast.182, f32[2,2,4,128]{3,2,1,0:T(4,128)S(1)} %get-tuple-element.23, f32[256]{0:T(256)S(1)} %bitcast.186, ...), kind=kLoop, calls=%fused_computation.15 | loop fusion | flops 5765120 | bytes 52224 | tf_op jit(solution)/shard_map/reduce_sum | solution.py:29
  96.0 0.1 copy.30
  96.1 2.3 %gather_fusion = f32[432,4,128]{2,1,0:T(4,128)S(1)} fusion(f32[4,96,128]{2,0,1:T(4,128)S(1)} %bitcast.134, s32[1024]{0:T(1024)S(1)} %get-tuple-element.48), kind=kCustom, calls=%fused_computation | custom fusion | bytes 1771200 | tf_op jit(solution)/shard_map/jit(_take)/gather | solution.py:275
  98.4 0.5 copy.53
  99.0 0.1 fusion.31
  99.1 0.1 copy.54
  99.2 0.1 copy.55
  99.3 0.1 copy.56
  99.5 0.1 copy.57
  99.6 0.0 copy-done.12
  99.7 0.0 copy-done.13
  99.7 20.0 %fusion.5 = f32[16,128]{1,0:T(8,128)S(1)} fusion(f32[3456]{0:T(1024)S(1)} %copy-done.14, f32[3456]{0:T(1024)S(1)} %copy-done.13, f32[3456]{0:T(1024)S(1)} %copy-done.12, f32[16,3456]{1,0:T(8,128)S(1)} %bitcast.142, f32[16,3456]{1,0:T(8,128)S(1)} %bitcast.143, f32[16,128]{1,0:T(8,128)S(1)} %bitcast.171, f32[16,3456]{1,0:T(8,128)S(1)} %bitcast.144, ...), kind=kLoop, calls=%fused_computation.8 | loop fusion | flops 106166272 | bytes 1401344 | tf_op jit(solution)/shard_map/reduce_sum | solution.py:290
  119.7 0.7 add_select_fusion
  (97 shorter events, 1.2 us)
Async XLA Ops:
  0.0 3.6 %copy-start = (f32[256,256]{1,0:T(8,128)S(1)}, f32[256,256]{1,0:T(8,128)}, u32[]{:S(2)}) copy-start(f32[256,256]{1,0:T(8,128)} %param.19) | copy-start | bytes 786436
  4.2 1.3 %copy-start.5 = (f32[256,256]{1,0:T(8,128)S(1)}, f32[256,256]{1,0:T(8,128)}, u32[]{:S(2)}) copy-start(f32[256,256]{1,0:T(8,128)} %param.21) | copy-start | bytes 786436
  4.2 1.6 %copy-start.3 = (f32[3,2,2,4,128]{4,3,2,1,0:T(4,128)S(1)}, f32[3,2,2,4,128]{4,3,2,1,0:T(4,128)}, u32[]{:S(2)}) copy-start(f32[3,2,2,4,128]{4,3,2,1,0:T(4,128)} %param.16) | copy-start | bytes 73732
  5.0 5.4 %copy-start.9 = (f32[23]{0:T(128)S(1)}, f32[23]{0:T(128)}, u32[]{:S(2)}) copy-start(f32[23]{0:T(128)} %constant.139) | copy-start | bytes 280
  5.0 5.5 %copy-start.10 = (f32[23]{0:T(128)S(1)}, f32[23]{0:T(128)}, u32[]{:S(2)}) copy-start(f32[23]{0:T(128)} %constant.140) | copy-start | bytes 280
  5.4 5.2 %copy-start.8 = (s32[432]{0:T(512)S(1)}, s32[432]{0:T(512)}, u32[]{:S(2)}) copy-start(s32[432]{0:T(512)} %constant.150) | copy-start | bytes 5188
  5.5 5.2 %copy-start.11 = (s32[23]{0:T(128)S(1)}, s32[23]{0:T(128)}, u32[]{:S(2)}) copy-start(s32[23]{0:T(128)} %constant.151) | copy-start | bytes 280
  5.9 7.7 %collective-permute-start.1 = (f32[8704]{0:T(1024)S(1)}, f32[8704]{0:T(1024)S(1)}, u32[]{:S(2)}, u32[]{:S(2)}) collective-permute-start(f32[8704]{0:T(1024)S(1)} %pad_maximum_fusion.7), channel_id=1, source_target_pairs={{4,0},{8,4},{12,8},{16,12},{20,16},{24,20},{28,24},{0,28},{5,1},{9... | collective-permute-start | bytes 104456 | tf_op jit(solution)/shard_map/ppermute | solution.py:77
  9.2 4.2 %collective-permute-start = (f32[8192]{0:T(1024)S(1)}, f32[8192]{0:T(1024)S(1)}, u32[]{:S(2)}, u32[]{:S(2)}) collective-permute-start(f32[8192]{0:T(1024)S(1)} %pad_maximum_fusion.8), channel_id=1, source_target_pairs={{0,4},{4,8},{8,12},{12,16},{16,20},{20,24},{24,28},{28,0},{1,5},{5... | collective-permute-start | bytes 98312 | tf_op jit(solution)/shard_map/ppermute | solution.py:76
  13.5 3.7 %collective-permute-start.4 = (f32[2,1,2,256]{3,2,0,1:T(2,128)S(1)}, f32[2,1,2,256]{3,2,0,1:T(2,128)S(1)}, u32[]{:S(2)}, u32[]{:S(2)}) collective-permute-start(f32[2,1,2,256]{3,2,0,1:T(2,128)S(1)} %maximum_bitcast_fusion), channel_id=1, source_target_pairs={{0,24},{4,28},{8,0},{12,4},{16,8},{20,12},{24,16},{28,20},{1,25},{... | collective-permute-start | bytes 12296 | tf_op jit(solution)/shard_map/ppermute | solution.py:60
  17.2 3.7 %collective-permute-start.5 = (f32[4,1,2,256]{3,2,0,1:T(2,128)S(1)}, f32[4,1,2,256]{3,2,0,1:T(2,128)S(1)}, u32[]{:S(2)}, u32[]{:S(2)}) collective-permute-start(f32[4,1,2,256]{3,2,0,1:T(2,128)S(1)} %pad_maximum_fusion.12), channel_id=1, source_target_pairs={{0,16},{4,20},{8,24},{12,28},{16,0},{20,4},{24,8},{28,12},{1,17},{... | collective-permute-start | bytes 24584 | tf_op jit(solution)/shard_map/ppermute | solution.py:60
  20.9 5.1 %collective-permute-start.6 = (f32[8,1,2,256]{3,2,0,1:T(2,128)S(1)}, f32[8,1,2,256]{3,2,0,1:T(2,128)S(1)}, u32[]{:S(2)}, u32[]{:S(2)}) collective-permute-start(f32[8,1,2,256]{3,2,0,1:T(2,128)S(1)} %pad_maximum_fusion.11), channel_id=1, source_target_pairs={{0,3},{1,0},{2,1},{3,2},{4,7},{5,4},{6,5},{7,6},{8,11},{9,8},{10,9... | collective-permute-start | bytes 49160 | tf_op jit(solution)/shard_map/ppermute | solution.py:60
  26.0 5.4 %collective-permute-start.7 = (f32[8,2,2,256]{3,2,0,1:T(2,128)S(1)}, f32[8,2,2,256]{3,2,0,1:T(2,128)S(1)}, u32[]{:S(2)}, u32[]{:S(2)}) collective-permute-start(f32[8,2,2,256]{3,2,0,1:T(2,128)S(1)} %pad_maximum_fusion.9), channel_id=1, source_target_pairs={{0,2},{1,3},{2,0},{3,1},{4,6},{5,7},{6,4},{7,5},{8,10},{9,11},{10,... | collective-permute-start | bytes 98312 | tf_op jit(solution)/shard_map/ppermute | solution.py:60
  27.5 17.9 %collective-permute-start.2 = (f32[20480]{0:T(1024)S(1)}, f32[20480]{0:T(1024)S(1)}, u32[]{:S(2)}, u32[]{:S(2)}) collective-permute-start(f32[20480]{0:T(1024)S(1)} %get-tuple-element.11), channel_id=1, source_target_pairs={{0,1},{1,2},{2,3},{3,0},{4,5},{5,6},{6,7},{7,4},{8,9},{9,10},{10,1... | collective-permute-start | bytes 245768 | tf_op jit(solution)/shard_map/ppermute | solution.py:76
  30.9 14.6 %collective-permute-start.3 = (f32[20480]{0:T(1024)S(1)}, f32[20480]{0:T(1024)S(1)}, u32[]{:S(2)}, u32[]{:S(2)}) collective-permute-start(f32[20480]{0:T(1024)S(1)} %get-tuple-element.12), channel_id=1, source_target_pairs={{1,0},{2,1},{3,2},{0,3},{5,4},{6,5},{7,6},{4,7},{9,8},{10,9},{11,1... | collective-permute-start | bytes 245768 | tf_op jit(solution)/shard_map/ppermute | solution.py:77
  32.1 11.7 %copy-start.6 = (f32[256,256]{1,0:T(8,128)S(1)}, f32[256,256]{1,0:T(8,128)}, u32[]{:S(2)}) copy-start(f32[256,256]{1,0:T(8,128)} %param.22) | copy-start | bytes 786436
  46.2 0.7 copy-start.1
  46.3 0.7 copy-start.2
  46.9 47.3 %copy-start.4 = (f32[256,256]{1,0:T(8,128)S(1)}, f32[256,256]{1,0:T(8,128)}, u32[]{:S(2)}) copy-start(f32[256,256]{1,0:T(8,128)} %param.20) | copy-start | bytes 786436
  98.9 0.7 copy-start.12
  99.0 0.7 copy-start.13
  99.0 0.7 copy-start.14
  99.7 20.0 %copy-start.7 = (s32[2,2,4]{2,1,0:T(2,128)S(1)}, s32[2,2,4]{2,1,0:T(2,128)}, u32[]{:S(2)}) copy-start(s32[2,2,4]{2,1,0:T(2,128)} %param.18) | copy-start | bytes 196

commit v12 on v11

--- a/solution.py
+++ b/solution.py
@@ -113,18 +113,20 @@
         return jnp.concatenate([top, block - top], axis=0).astype(jnp.bfloat16)
 
     def body(index, carry):
-        shift_x = table_ref[3 * index]
-        shift_y = table_ref[3 * index + 1]
-        shift_z = table_ref[3 * index + 2]
+        scale_x = table_ref[4 * index]
+        scale_y = table_ref[4 * index + 1]
+        scale_z = table_ref[4 * index + 2]
+        offset = table_ref[4 * index + 3]
         fwd = gathered(0, index)
         back = gathered(1, index)
         for row in range(0, base_ref.shape[1], rows):
-            delta_x = base_ref[0, row : row + rows, :] - shift_x
-            delta_y = base_ref[1, row : row + rows, :] - shift_y
-            delta_z = base_ref[2, row : row + rows, :] - shift_z
-            matrix = lax.rsqrt(
-                delta_x * delta_x + delta_y * delta_y + delta_z * delta_z + softening_sq
+            square = (
+                (base_ref[3, row : row + rows, :] + offset)
+                + scale_x * base_ref[0, row : row + rows, :]
+                + scale_y * base_ref[1, row : row + rows, :]
+                + scale_z * base_ref[2, row : row + rows, :]
             )
+            matrix = lax.rsqrt(square)
             matrix_top = split_top(matrix)
             matrix_high = matrix_top.astype(jnp.bfloat16)
             matrix_low = (matrix - matrix_top).astype(jnp.bfloat16)
@@ -140,7 +142,7 @@
 
 
 def m2l(table, window_index, base, windows, vectors):
-    shift_count = table.shape[0] // 3
+    shift_count = table.shape[0] // 4
     points = windows.shape[-1]
     return pl.pallas_call(
         functools.partial(m2l_kernel, shift_count, 128),
@@ -250,7 +252,12 @@
     base = jnp.stack(
         [0.9 * (unit_sphere[i][:, None] - unit_sphere[i][None, :]) for i in range(3)]
     )
-    table = jnp.asarray(np.array(shifts, np.float32).reshape(-1))
+    base = jnp.concatenate([base, jnp.sum(base * base, axis=0)[None]], axis=0)
+    shift_array = np.array(shifts, np.float64)
+    table = np.concatenate(
+        [-2.0 * shift_array, (shift_array**2).sum(1, keepdims=True) + softening_sq], axis=1
+    )
+    table = jnp.asarray(table.astype(np.float32).reshape(-1))
     leaf_down_check = m2l(table, jnp.asarray(window_index), base, depth_windows, 4 * layers).reshape(
         2, 2, layers, points
     )

time: 121 us -> 118 us (0.975)
  Pallas kernels: 47.3 us -> 44.7 us
    pallas_call x1, Pallas kernels: 47.3 us -> 44.7 us  [m2l(): pl.pallas_call(functools.partial(m2l_kernel, shift_count, 128), out_shape...]
where the time goes in v12:
time: 118 us
  Pallas kernels  44.7 us (38%)
  other arithmetic  40.8 us (35%)
  starting transfers between devices  13 us (11%)
  waiting for transfers between devices  10.5 us (9%)
  local copies, waits for them, and re-layouts  6.89 us (6%)
  matrix products  1.18 us (1%)
    pallas_call x1, Pallas kernels, m2l(): pl.pallas_call(functools.partial(m2l_kernel, shift_count, 128), out_shape...  44.7 us
    reduce_sum x1, other arithmetic, shards(): jnp.sum(kernel * source[3][..., None, :], axis=-1)  20 us
    reduce_sum x5, other arithmetic, point_sum(): return jnp.sum(kernel * weights[..., None, :], axis=-1)  15.8 us
    ppermute x4, waiting for transfers between devices, rel_gather(): lax.ppermute(part, axis, [(j, (j - have) % count) for j in range(count)])  8.06 us
    ppermute x4, starting transfers between devices, rel_gather(): lax.ppermute(part, axis, [(j, (j - have) % count) for j in range(count)])  5.73 us
    ppermute x2, starting transfers between devices, exchange(): lax.ppermute(sent_head, axis, [((i + 1) % count, i) for i in range(count)])  3.89 us
    ppermute x2, starting transfers between devices, exchange(): lax.ppermute(sent_tail, axis, [(i, (i + 1) % count) for i in range(count)])  3.38 us
    gather x2, local copies, waits for them, and re-layouts, shards(): jnp.take(padded_around.reshape(4, -1, slot_count), box_rows, axis=1)  2.79 us
  transfers between devices with their start and end apart: 8, of which 4 were waited for; matrix products, arithmetic and copies ran while one was open for 13% of the time, Pallas kernels for 0%

profile of v12, /device:TPU:0, one launch (start us, length us, event | category | flops | bytes accessed | tf_op | source)
XLA Modules:
  0.0 117.7 jit_solution(16671207760506218683)
XLA Ops:
  0.0 0.1 cosine_multiply_fusion.1
  0.1 0.1 sine_multiply_fusion.1
  0.2 0.8 fusion.25
  1.0 0.8 fusion.48
  1.8 0.7 fusion.36
  2.5 1.1 multiply_reduce_fusion.4
  3.6 0.3 fusion.22
  4.0 0.1 broadcast_add_fusion.8
  4.2 0.8 add_rsqrt_fusion
  5.0 0.4 multiply_reduce_fusion.1
  5.4 0.3 fusion.40
  5.7 0.1 copy.31
  5.8 3.4 %collective-permute-start.1 = (f32[8704]{0:T(1024)S(1)}, f32[8704]{0:T(1024)S(1)}, u32[]{:S(2)}, u32[]{:S(2)}) collective-permute-start(f32[8704]{0:T(1024)S(1)} %pad_maximum_fusion.7), channel_id=1, source_target_pairs={{4,0},{8,4},{12,8},{16,12},{20,16},{24,20},{28,24},{0,28},{5,1},{9... | collective-permute-start | bytes 104456 | tf_op jit(solution)/shard_map/ppermute | solution.py:77
  9.3 0.1 fusion.29
  9.4 0.1 fusion.31
  9.6 0.1 subtract_multiply_fusion.2
  9.7 0.1 subtract_multiply_fusion
  9.9 0.1 fusion.12
  9.9 0.1 pad_maximum_fusion.base_ref
  10.0 0.3 iota_compare_fusion
  10.3 0.1 subtract_multiply_fusion.3
  10.4 0.1 broadcast_add_fusion.4
  10.5 0.1 broadcast_add_fusion.5
  10.6 0.1 broadcast_add_fusion.1
  10.6 0.1 broadcast_add_fusion
  10.8 0.1 stack_broadcast_in_dim.44
  11.0 2.4 %collective-permute-done = f32[8192]{0:T(1024)S(1)} collective-permute-done((f32[8192]{0:T(1024)S(1)}, f32[8192]{0:T(1024)S(1)}, u32[]{:S(2)}, u32[]{:S(2)}) %collective-permute-start) | collective-permute-done | bytes 32800 | tf_op jit(solution)/shard_map/ppermute | solution.py:76
  13.5 0.1 collective-permute-start.4
  13.6 3.6 %collective-permute-done.4 = f32[2,1,2,256]{3,2,0,1:T(2,128)S(1)} collective-permute-done((f32[2,1,2,256]{3,2,0,1:T(2,128)S(1)}, f32[2,1,2,256]{3,2,0,1:T(2,128)S(1)}, u32[]{:S(2)}, u32[]{:S(2)}) %collective-permute-start.4) | collective-permute-done | bytes 4128 | tf_op jit(solution)/shard_map/ppermute | solution.py:60
  17.2 0.5 collective-permute-start.5
  17.7 3.1 %collective-permute-done.5 = f32[4,1,2,256]{3,2,0,1:T(2,128)S(1)} collective-permute-done((f32[4,1,2,256]{3,2,0,1:T(2,128)S(1)}, f32[4,1,2,256]{3,2,0,1:T(2,128)S(1)}, u32[]{:S(2)}, u32[]{:S(2)}) %collective-permute-start.5) | collective-permute-done | bytes 8224 | tf_op jit(solution)/shard_map/ppermute | solution.py:60
  20.8 3.7 %collective-permute-start.6 = (f32[8,1,2,256]{3,2,0,1:T(2,128)S(1)}, f32[8,1,2,256]{3,2,0,1:T(2,128)S(1)}, u32[]{:S(2)}, u32[]{:S(2)}) collective-permute-start(f32[8,1,2,256]{3,2,0,1:T(2,128)S(1)} %pad_maximum_fusion.11), channel_id=1, source_target_pairs={{0,3},{1,0},{2,1},{3,2},{4,7},{5,4},{6,5},{7,6},{8,11},{9,8},{10,9... | collective-permute-start | bytes 49160 | tf_op jit(solution)/shard_map/ppermute | solution.py:60
  24.5 1.4 %collective-permute-done.6 = f32[8,1,2,256]{3,2,0,1:T(2,128)S(1)} collective-permute-done((f32[8,1,2,256]{3,2,0,1:T(2,128)S(1)}, f32[8,1,2,256]{3,2,0,1:T(2,128)S(1)}, u32[]{:S(2)}, u32[]{:S(2)}) %collective-permute-start.6) | collective-permute-done | bytes 16416 | tf_op jit(solution)/shard_map/ppermute | solution.py:60
  25.9 1.5 %collective-permute-start.7 = (f32[8,2,2,256]{3,2,0,1:T(2,128)S(1)}, f32[8,2,2,256]{3,2,0,1:T(2,128)S(1)}, u32[]{:S(2)}, u32[]{:S(2)}) collective-permute-start(f32[8,2,2,256]{3,2,0,1:T(2,128)S(1)} %pad_maximum_fusion.9), channel_id=1, source_target_pairs={{0,2},{1,3},{2,0},{3,1},{4,6},{5,7},{6,4},{7,5},{8,10},{9,11},{10,... | collective-permute-start | bytes 98312 | tf_op jit(solution)/shard_map/ppermute | solution.py:60
  27.5 3.4 %collective-permute-start.2 = (f32[20480]{0:T(1024)S(1)}, f32[20480]{0:T(1024)S(1)}, u32[]{:S(2)}, u32[]{:S(2)}) collective-permute-start(f32[20480]{0:T(1024)S(1)} %get-tuple-element.11), channel_id=1, source_target_pairs={{0,1},{1,2},{2,3},{3,0},{4,5},{5,6},{6,7},{7,4},{8,9},{9,10},{10,1... | collective-permute-start | bytes 245768 | tf_op jit(solution)/shard_map/ppermute | solution.py:76
  30.8 0.5 collective-permute-start.3
  31.4 0.6 gather_fusion.1
  32.1 11.7 %multiply_reduce_fusion = f32[2,256]{1,0:T(2,128)S(1)} fusion(f32[11776]{0:T(1024)S(1)} %select_n.55, f32[2,11776]{1,0:T(2,128)S(1)} %stack_broadcast_in_dim.44, f32[256]{0:T(256)S(1)} %bitcast.190, f32[11776]{0:T(1024)S(1)} %stack_broadcast_in_dim.42, f32[256]{0:T(256)S(1)} %bitcast.191, f32[11776]{0:T(1024)S(1)} %stack_broadcast_in_dim.40, f32[256]{0:T(256)S(1)} %bitcast.189), kind=kLoop, calls=%fused_computation.12 | loop fusion | flops 66321920 | bytes 240640 | tf_op jit(solution)/shard_map/reduce_sum | solution.py:29
  43.8 0.3 fusion.41
  44.0 0.1 mul.529
  44.1 1.3 %multiply_reduce_fusion.2 = f32[2,2,4,128]{3,2,1,0:T(4,128)S(1)} fusion(f32[4,256]{1,0:T(4,128)S(1)} %mul.529, f32[256]{0:T(256)S(1)} %bitcast.180, f32[2,2,4,128]{3,2,1,0:T(4,128)S(1)} %get-tuple-element.27, f32[256]{0:T(256)S(1)} %bitcast.182, f32[2,2,4,128]{3,2,1,0:T(4,128)S(1)} %get-tuple-element.20, f32[256]{0:T(256)S(1)} %bitcast.178, ...), kind=kLoop, calls=%fused_computation.14 | loop fusion | flops 5765120 | bytes 39936 | tf_op jit(solution)/shard_map/reduce_sum | solution.py:29
  45.5 0.1 select_maximum_fusion
  45.7 0.1 fusion.18
  45.8 0.1 fusion.17
  45.9 0.1 fusion.16
  46.0 0.1 fusion.15
  46.1 0.1 fusion.14
  46.2 0.1 fusion.13
  46.3 0.3 copy.26
  46.7 0.2 copy-done.1
  46.9 44.7 %shard_map.154 = f32[16,256]{1,0:T(8,128)S(1)} custom-call(f32[632]{0:T(1024)S(1)} %copy-done.2, s32[1264]{0:T(1024)S(1)} %copy-done.1, f32[4,256,256]{2,1,0:T(8,128)S(1)} %pad_maximum_fusion.base_ref, f32[448,4,256]{2,1,0:T(4,128)S(1)} %bitcast.134), custom_call_target="tpu_custom_call" | custom-call | flops 2133065728 | bytes 2899968 | tf_op jit(solution)/shard_map/pallas_call | solution.py:147
  91.6 0.3 fusion.20
  91.9 1.3 %multiply_reduce_fusion.3 = f32[2,2,4,128]{3,2,1,0:T(4,128)S(1)} fusion(f32[2,2,4,256]{3,2,1,0:T(4,128)S(1)} %fusion.20, f32[256]{0:T(256)S(1)} %bitcast.186, f32[2,2,4,128]{3,2,1,0:T(4,128)S(1)} %get-tuple-element.24, f32[256]{0:T(256)S(1)} %bitcast.184, f32[2,2,4,128]{3,2,1,0:T(4,128)S(1)} %get-tuple-element.23, f32[256]{0:T(256)S(1)} %bitcast.188, ...), kind=kLoop, calls=%fused_computation.15 | loop fusion | flops 5765120 | bytes 52224 | tf_op jit(solution)/shard_map/reduce_sum | solution.py:29
  93.3 0.1 copy.30
  93.5 2.3 %gather_fusion = f32[432,4,128]{2,1,0:T(4,128)S(1)} fusion(f32[4,96,128]{2,0,1:T(4,128)S(1)} %bitcast.135, s32[1024]{0:T(1024)S(1)} %get-tuple-element.48), kind=kCustom, calls=%fused_computation | custom fusion | bytes 1771200 | tf_op jit(solution)/shard_map/jit(_take)/gather | solution.py:282
  95.8 0.5 copy.53
  96.3 0.1 fusion.32
  96.4 0.1 copy.54
  96.5 0.1 copy.55
  96.7 0.1 copy.56
  96.8 0.1 copy.57
  97.0 0.0 copy-done.12
  97.0 20.0 %fusion.5 = f32[16,128]{1,0:T(8,128)S(1)} fusion(f32[3456]{0:T(1024)S(1)} %copy-done.14, f32[3456]{0:T(1024)S(1)} %copy-done.13, f32[3456]{0:T(1024)S(1)} %copy-done.12, f32[16,3456]{1,0:T(8,128)S(1)} %bitcast.144, f32[16,3456]{1,0:T(8,128)S(1)} %bitcast.145, f32[16,128]{1,0:T(8,128)S(1)} %bitcast.173, f32[16,3456]{1,0:T(8,128)S(1)} %bitcast.146, ...), kind=kLoop, calls=%fused_computation.8 | loop fusion | flops 106166272 | bytes 1401344 | tf_op jit(solution)/shard_map/reduce_sum | solution.py:297
  117.0 0.7 add_select_fusion
  (98 shorter events, 1.2 us)
Async XLA Ops:
  0.0 3.6 %copy-start = (f32[256,256]{1,0:T(8,128)S(1)}, f32[256,256]{1,0:T(8,128)}, u32[]{:S(2)}) copy-start(f32[256,256]{1,0:T(8,128)} %param.19) | copy-start | bytes 786436
  4.2 1.2 %copy-start.5 = (f32[256,256]{1,0:T(8,128)S(1)}, f32[256,256]{1,0:T(8,128)}, u32[]{:S(2)}) copy-start(f32[256,256]{1,0:T(8,128)} %param.21) | copy-start | bytes 786436
  4.2 1.6 %copy-start.3 = (f32[3,2,2,4,128]{4,3,2,1,0:T(4,128)S(1)}, f32[3,2,2,4,128]{4,3,2,1,0:T(4,128)}, u32[]{:S(2)}) copy-start(f32[3,2,2,4,128]{4,3,2,1,0:T(4,128)} %param.16) | copy-start | bytes 73732
  5.8 7.7 %collective-permute-start.1 = (f32[8704]{0:T(1024)S(1)}, f32[8704]{0:T(1024)S(1)}, u32[]{:S(2)}, u32[]{:S(2)}) collective-permute-start(f32[8704]{0:T(1024)S(1)} %pad_maximum_fusion.7), channel_id=1, source_target_pairs={{4,0},{8,4},{12,8},{16,12},{20,16},{24,20},{28,24},{0,28},{5,1},{9... | collective-permute-start | bytes 104456 | tf_op jit(solution)/shard_map/ppermute | solution.py:77
  9.2 4.2 %collective-permute-start = (f32[8192]{0:T(1024)S(1)}, f32[8192]{0:T(1024)S(1)}, u32[]{:S(2)}, u32[]{:S(2)}) collective-permute-start(f32[8192]{0:T(1024)S(1)} %pad_maximum_fusion.8), channel_id=1, source_target_pairs={{0,4},{4,8},{8,12},{12,16},{16,20},{20,24},{24,28},{28,0},{1,5},{5... | collective-permute-start | bytes 98312 | tf_op jit(solution)/shard_map/ppermute | solution.py:76
  9.7 0.9 copy-start.9
  9.7 1.0 copy-start.10
  9.7 1.0 copy-start.8
  9.7 1.0 copy-start.11
  13.5 3.7 %collective-permute-start.4 = (f32[2,1,2,256]{3,2,0,1:T(2,128)S(1)}, f32[2,1,2,256]{3,2,0,1:T(2,128)S(1)}, u32[]{:S(2)}, u32[]{:S(2)}) collective-permute-start(f32[2,1,2,256]{3,2,0,1:T(2,128)S(1)} %maximum_bitcast_fusion), channel_id=1, source_target_pairs={{0,24},{4,28},{8,0},{12,4},{16,8},{20,12},{24,16},{28,20},{1,25},{... | collective-permute-start | bytes 12296 | tf_op jit(solution)/shard_map/ppermute | solution.py:60
  17.2 3.7 %collective-permute-start.5 = (f32[4,1,2,256]{3,2,0,1:T(2,128)S(1)}, f32[4,1,2,256]{3,2,0,1:T(2,128)S(1)}, u32[]{:S(2)}, u32[]{:S(2)}) collective-permute-start(f32[4,1,2,256]{3,2,0,1:T(2,128)S(1)} %pad_maximum_fusion.12), channel_id=1, source_target_pairs={{0,16},{4,20},{8,24},{12,28},{16,0},{20,4},{24,8},{28,12},{1,17},{... | collective-permute-start | bytes 24584 | tf_op jit(solution)/shard_map/ppermute | solution.py:60
  20.8 5.1 %collective-permute-start.6 = (f32[8,1,2,256]{3,2,0,1:T(2,128)S(1)}, f32[8,1,2,256]{3,2,0,1:T(2,128)S(1)}, u32[]{:S(2)}, u32[]{:S(2)}) collective-permute-start(f32[8,1,2,256]{3,2,0,1:T(2,128)S(1)} %pad_maximum_fusion.11), channel_id=1, source_target_pairs={{0,3},{1,0},{2,1},{3,2},{4,7},{5,4},{6,5},{7,6},{8,11},{9,8},{10,9... | collective-permute-start | bytes 49160 | tf_op jit(solution)/shard_map/ppermute | solution.py:60
  25.9 5.4 %collective-permute-start.7 = (f32[8,2,2,256]{3,2,0,1:T(2,128)S(1)}, f32[8,2,2,256]{3,2,0,1:T(2,128)S(1)}, u32[]{:S(2)}, u32[]{:S(2)}) collective-permute-start(f32[8,2,2,256]{3,2,0,1:T(2,128)S(1)} %pad_maximum_fusion.9), channel_id=1, source_target_pairs={{0,2},{1,3},{2,0},{3,1},{4,6},{5,7},{6,4},{7,5},{8,10},{9,11},{10,... | collective-permute-start | bytes 98312 | tf_op jit(solution)/shard_map/ppermute | solution.py:60
  27.5 18.0 %collective-permute-start.2 = (f32[20480]{0:T(1024)S(1)}, f32[20480]{0:T(1024)S(1)}, u32[]{:S(2)}, u32[]{:S(2)}) collective-permute-start(f32[20480]{0:T(1024)S(1)} %get-tuple-element.11), channel_id=1, source_target_pairs={{0,1},{1,2},{2,3},{3,0},{4,5},{5,6},{6,7},{7,4},{8,9},{9,10},{10,1... | collective-permute-start | bytes 245768 | tf_op jit(solution)/shard_map/ppermute | solution.py:76
  30.8 14.6 %collective-permute-start.3 = (f32[20480]{0:T(1024)S(1)}, f32[20480]{0:T(1024)S(1)}, u32[]{:S(2)}, u32[]{:S(2)}) collective-permute-start(f32[20480]{0:T(1024)S(1)} %get-tuple-element.12), channel_id=1, source_target_pairs={{1,0},{2,1},{3,2},{0,3},{5,4},{6,5},{7,6},{4,7},{9,8},{10,9},{11,1... | collective-permute-start | bytes 245768 | tf_op jit(solution)/shard_map/ppermute | solution.py:77
  32.1 11.7 %copy-start.6 = (f32[256,256]{1,0:T(8,128)S(1)}, f32[256,256]{1,0:T(8,128)}, u32[]{:S(2)}) copy-start(f32[256,256]{1,0:T(8,128)} %param.22) | copy-start | bytes 786436
  46.2 0.7 copy-start.1
  46.2 0.7 copy-start.2
  46.9 44.7 %copy-start.4 = (f32[256,256]{1,0:T(8,128)S(1)}, f32[256,256]{1,0:T(8,128)}, u32[]{:S(2)}) copy-start(f32[256,256]{1,0:T(8,128)} %param.20) | copy-start | bytes 786436
  96.3 0.7 copy-start.12
  96.3 0.7 copy-start.13
  96.3 0.7 copy-start.14
  97.0 20.0 %copy-start.7 = (s32[2,2,4]{2,1,0:T(2,128)S(1)}, s32[2,2,4]{2,1,0:T(2,128)}, u32[]{:S(2)}) copy-start(s32[2,2,4]{2,1,0:T(2,128)} %param.18) | copy-start | bytes 196

commit v13 on v12

--- a/solution.py
+++ b/solution.py
@@ -290,11 +290,10 @@
     delta_y = own[1][..., :, None] - source[1][..., None, :] - move[:, 1]
     delta_z = own[2][..., :, None] - source[2][..., None, :] - move[:, 2]
     kernel = lax.rsqrt(delta_x * delta_x + delta_y * delta_y + delta_z * delta_z + softening_sq)
-    centre = moves.index((0, 0, 0))
-    column = jnp.arange(len(moves) * slot_count)[None, :]
-    itself = column == jnp.arange(slot_count)[:, None] + centre * slot_count
-    kernel = jnp.where(itself, 0.0, kernel)
-    near = jnp.sum(kernel * source[3][..., None, :], axis=-1).reshape(2, 2, layers, slot_count)
+    itself = lax.rsqrt(jnp.full((), softening_sq, jnp.float32)) * own[3]
+    near = (jnp.sum(kernel * source[3][..., None, :], axis=-1) - itself).reshape(
+        2, 2, layers, slot_count
+    )
 
     leaf_down_pts = 0.5 + 1.8 * unit_sphere
     leaf_far = point_sum(offsets, leaf_down_pts[:, None, None, None, :], leaf_local)

time: 118 us -> 115 us (0.975)
  other arithmetic: 40.8 us -> 37.5 us
    reduce_sum x1, other arithmetic: 20 us -> 17 us  [shards(): jnp.sum(kernel * source[3][..., None, :], axis=-1) - itself]
where the time goes in v13:
time: 115 us
  Pallas kernels  44.7 us (39%)
  other arithmetic  37.5 us (33%)
  starting transfers between devices  13 us (11%)
  waiting for transfers between devices  10.8 us (9%)
  local copies, waits for them, and re-layouts  6.82 us (6%)
  matrix products  1.18 us (1%)
    pallas_call x1, Pallas kernels, m2l(): pl.pallas_call(functools.partial(m2l_kernel, shift_count, 128), out_shape...  44.7 us
    reduce_sum x1, other arithmetic, shards(): jnp.sum(kernel * source[3][..., None, :], axis=-1) - itself  17 us
    reduce_sum x5, other arithmetic, point_sum(): return jnp.sum(kernel * weights[..., None, :], axis=-1)  15.8 us
    ppermute x4, waiting for transfers between devices, rel_gather(): lax.ppermute(part, axis, [(j, (j - have) % count) for j in range(count)])  8.06 us
    ppermute x4, starting transfers between devices, rel_gather(): lax.ppermute(part, axis, [(j, (j - have) % count) for j in range(count)])  5.76 us
    ppermute x2, starting transfers between devices, exchange(): lax.ppermute(sent_head, axis, [((i + 1) % count, i) for i in range(count)])  3.84 us
    ppermute x2, starting transfers between devices, exchange(): lax.ppermute(sent_tail, axis, [(i, (i + 1) % count) for i in range(count)])  3.43 us
    gather x2, local copies, waits for them, and re-layouts, shards(): jnp.take(padded_around.reshape(4, -1, slot_count), box_rows, axis=1)  2.79 us
  transfers between devices with their start and end apart: 8, of which 4 were waited for; matrix products, arithmetic and copies ran while one was open for 13% of the time, Pallas kernels for 0%

profile of v13, /device:TPU:0, one launch (start us, length us, event | category | flops | bytes accessed | tf_op | source)
XLA Modules:
  0.0 114.8 jit_solution(3790172930140864081)
XLA Ops:
  0.0 0.1 cosine_multiply_fusion.1
  0.1 0.1 sine_multiply_fusion.1
  0.2 0.8 fusion.24
  1.0 0.8 fusion.47
  1.8 0.7 fusion.35
  2.5 1.1 multiply_reduce_fusion.4
  3.6 0.3 fusion.21
  4.0 0.1 broadcast_add_fusion.8
  4.2 0.8 add_rsqrt_fusion
  5.0 0.4 multiply_reduce_fusion.1
  5.4 0.3 fusion.39
  5.7 0.1 copy.31
  5.8 0.0 copy-start.10
  5.9 3.4 %collective-permute-start.1 = (f32[8704]{0:T(1024)S(1)}, f32[8704]{0:T(1024)S(1)}, u32[]{:S(2)}, u32[]{:S(2)}) collective-permute-start(f32[8704]{0:T(1024)S(1)} %pad_maximum_fusion.7), channel_id=1, source_target_pairs={{4,0},{8,4},{12,8},{16,12},{20,16},{24,20},{28,24},{0,28},{5,1},{9... | collective-permute-start | bytes 104456 | tf_op jit(solution)/shard_map/ppermute | solution.py:77
  9.4 0.1 fusion.28
  9.4 0.1 fusion.30
  9.6 0.1 subtract_multiply_fusion.2
  9.7 0.1 subtract_multiply_fusion
  9.9 0.1 fusion.11
  9.9 0.1 pad_maximum_fusion.base_ref
  10.0 0.1 subtract_multiply_fusion.3
  10.1 0.1 broadcast_add_fusion.4
  10.2 0.1 broadcast_add_fusion.5
  10.3 0.1 broadcast_add_fusion.1
  10.3 0.1 broadcast_add_fusion
  10.5 0.1 stack_broadcast_in_dim.44
  10.7 2.8 %collective-permute-done = f32[8192]{0:T(1024)S(1)} collective-permute-done((f32[8192]{0:T(1024)S(1)}, f32[8192]{0:T(1024)S(1)}, u32[]{:S(2)}, u32[]{:S(2)}) %collective-permute-start) | collective-permute-done | bytes 32800 | tf_op jit(solution)/shard_map/ppermute | solution.py:76
  13.6 0.1 collective-permute-start.4
  13.7 3.6 %collective-permute-done.4 = f32[2,1,2,256]{3,2,0,1:T(2,128)S(1)} collective-permute-done((f32[2,1,2,256]{3,2,0,1:T(2,128)S(1)}, f32[2,1,2,256]{3,2,0,1:T(2,128)S(1)}, u32[]{:S(2)}, u32[]{:S(2)}) %collective-permute-start.4) | collective-permute-done | bytes 4128 | tf_op jit(solution)/shard_map/ppermute | solution.py:60
  17.2 0.5 collective-permute-start.5
  17.8 3.1 %collective-permute-done.5 = f32[4,1,2,256]{3,2,0,1:T(2,128)S(1)} collective-permute-done((f32[4,1,2,256]{3,2,0,1:T(2,128)S(1)}, f32[4,1,2,256]{3,2,0,1:T(2,128)S(1)}, u32[]{:S(2)}, u32[]{:S(2)}) %collective-permute-start.5) | collective-permute-done | bytes 8224 | tf_op jit(solution)/shard_map/ppermute | solution.py:60
  20.9 3.7 %collective-permute-start.6 = (f32[8,1,2,256]{3,2,0,1:T(2,128)S(1)}, f32[8,1,2,256]{3,2,0,1:T(2,128)S(1)}, u32[]{:S(2)}, u32[]{:S(2)}) collective-permute-start(f32[8,1,2,256]{3,2,0,1:T(2,128)S(1)} %pad_maximum_fusion.11), channel_id=1, source_target_pairs={{0,3},{1,0},{2,1},{3,2},{4,7},{5,4},{6,5},{7,6},{8,11},{9,8},{10,9... | collective-permute-start | bytes 49160 | tf_op jit(solution)/shard_map/ppermute | solution.py:60
  24.6 1.4 %collective-permute-done.6 = f32[8,1,2,256]{3,2,0,1:T(2,128)S(1)} collective-permute-done((f32[8,1,2,256]{3,2,0,1:T(2,128)S(1)}, f32[8,1,2,256]{3,2,0,1:T(2,128)S(1)}, u32[]{:S(2)}, u32[]{:S(2)}) %collective-permute-start.6) | collective-permute-done | bytes 16416 | tf_op jit(solution)/shard_map/ppermute | solution.py:60
  26.0 1.5 %collective-permute-start.7 = (f32[8,2,2,256]{3,2,0,1:T(2,128)S(1)}, f32[8,2,2,256]{3,2,0,1:T(2,128)S(1)}, u32[]{:S(2)}, u32[]{:S(2)}) collective-permute-start(f32[8,2,2,256]{3,2,0,1:T(2,128)S(1)} %pad_maximum_fusion.9), channel_id=1, source_target_pairs={{0,2},{1,3},{2,0},{3,1},{4,6},{5,7},{6,4},{7,5},{8,10},{9,11},{10,... | collective-permute-start | bytes 98312 | tf_op jit(solution)/shard_map/ppermute | solution.py:60
  27.5 3.4 %collective-permute-start.2 = (f32[20480]{0:T(1024)S(1)}, f32[20480]{0:T(1024)S(1)}, u32[]{:S(2)}, u32[]{:S(2)}) collective-permute-start(f32[20480]{0:T(1024)S(1)} %get-tuple-element.11), channel_id=1, source_target_pairs={{0,1},{1,2},{2,3},{3,0},{4,5},{5,6},{6,7},{7,4},{8,9},{9,10},{10,1... | collective-permute-start | bytes 245768 | tf_op jit(solution)/shard_map/ppermute | solution.py:76
  31.0 0.5 collective-permute-start.3
  31.5 0.6 gather_fusion.1
  32.2 11.7 %multiply_reduce_fusion = f32[2,256]{1,0:T(2,128)S(1)} fusion(f32[11776]{0:T(1024)S(1)} %select_n.50, f32[2,11776]{1,0:T(2,128)S(1)} %stack_broadcast_in_dim.44, f32[256]{0:T(256)S(1)} %bitcast.190, f32[11776]{0:T(1024)S(1)} %stack_broadcast_in_dim.42, f32[256]{0:T(256)S(1)} %bitcast.191, f32[11776]{0:T(1024)S(1)} %stack_broadcast_in_dim.40, f32[256]{0:T(256)S(1)} %bitcast.189), kind=kLoop, calls=%fused_computation.11 | loop fusion | flops 66321920 | bytes 240640 | tf_op jit(solution)/shard_map/reduce_sum | solution.py:29
  43.8 0.3 fusion.40
  44.1 0.1 mul.538
  44.2 1.3 %multiply_reduce_fusion.2 = f32[2,2,4,128]{3,2,1,0:T(4,128)S(1)} fusion(f32[4,256]{1,0:T(4,128)S(1)} %mul.538, f32[256]{0:T(256)S(1)} %bitcast.180, f32[2,2,4,128]{3,2,1,0:T(4,128)S(1)} %get-tuple-element.27, f32[256]{0:T(256)S(1)} %bitcast.182, f32[2,2,4,128]{3,2,1,0:T(4,128)S(1)} %get-tuple-element.20, f32[256]{0:T(256)S(1)} %bitcast.178, ...), kind=kLoop, calls=%fused_computation.13 | loop fusion | flops 5765120 | bytes 39936 | tf_op jit(solution)/shard_map/reduce_sum | solution.py:29
  45.6 0.1 copy.30
  45.7 2.3 %gather_fusion = f32[432,4,128]{2,1,0:T(4,128)S(1)} fusion(f32[4,96,128]{2,0,1:T(4,128)S(1)} %bitcast.135, s32[1024]{0:T(1024)S(1)} %get-tuple-element.48), kind=kCustom, calls=%fused_computation | custom fusion | bytes 1771200 | tf_op jit(solution)/shard_map/jit(_take)/gather | solution.py:282
  48.0 0.5 copy.53
  48.5 0.1 fusion.31
  48.6 0.1 copy.54
  48.7 0.1 copy.55
  48.9 0.1 copy.56
  49.0 0.1 copy.57
  49.3 0.1 select_maximum_fusion
  49.4 0.1 fusion.17
  49.5 0.1 fusion.16
  49.6 0.1 fusion.15
  49.7 0.1 fusion.14
  49.8 0.1 fusion.13
  49.9 0.1 fusion.12
  50.0 0.3 copy.26
  50.4 0.2 copy-done.1
  50.6 0.0 copy-done.2
  50.6 44.7 %shard_map.154 = f32[16,256]{1,0:T(8,128)S(1)} custom-call(f32[632]{0:T(1024)S(1)} %copy-done.2, s32[1264]{0:T(1024)S(1)} %copy-done.1, f32[4,256,256]{2,1,0:T(8,128)S(1)} %pad_maximum_fusion.base_ref, f32[448,4,256]{2,1,0:T(4,128)S(1)} %bitcast.134), custom_call_target="tpu_custom_call" | custom-call | flops 2133065728 | bytes 2899968 | tf_op jit(solution)/shard_map/pallas_call | solution.py:147
  95.3 0.3 fusion.19
  95.7 1.3 %multiply_reduce_fusion.3 = f32[2,2,4,128]{3,2,1,0:T(4,128)S(1)} fusion(f32[2,2,4,256]{3,2,1,0:T(4,128)S(1)} %fusion.19, f32[256]{0:T(256)S(1)} %bitcast.186, f32[2,2,4,128]{3,2,1,0:T(4,128)S(1)} %get-tuple-element.24, f32[256]{0:T(256)S(1)} %bitcast.184, f32[2,2,4,128]{3,2,1,0:T(4,128)S(1)} %get-tuple-element.23, f32[256]{0:T(256)S(1)} %bitcast.188, ...), kind=kLoop, calls=%fused_computation.14 | loop fusion | flops 5765120 | bytes 52224 | tf_op jit(solution)/shard_map/reduce_sum | solution.py:29
  97.1 17.0 %fusion.4 = f32[16,128]{1,0:T(8,128)S(1)} fusion(f32[3456]{0:T(1024)S(1)} %copy-done.15, f32[3456]{0:T(1024)S(1)} %copy-done.14, f32[3456]{0:T(1024)S(1)} %copy-done.13, f32[16,3456]{1,0:T(8,128)S(1)} %bitcast.144, f32[16,3456]{1,0:T(8,128)S(1)} %bitcast.145, f32[16,128]{1,0:T(8,128)S(1)} %bitcast.173, f32[16,3456]{1,0:T(8,128)S(1)} %bitcast.146, ...), kind=kLoop, calls=%fused_computation.7 | loop fusion | flops 99088384 | bytes 958976 | tf_op jit(solution)/shard_map/reduce_sum | solution.py:294
  114.1 0.7 add_select_fusion
  (98 shorter events, 1.2 us)
Async XLA Ops:
  0.0 3.6 %copy-start = (f32[256,256]{1,0:T(8,128)S(1)}, f32[256,256]{1,0:T(8,128)}, u32[]{:S(2)}) copy-start(f32[256,256]{1,0:T(8,128)} %param.19) | copy-start | bytes 786436
  4.2 1.3 %copy-start.5 = (f32[256,256]{1,0:T(8,128)S(1)}, f32[256,256]{1,0:T(8,128)}, u32[]{:S(2)}) copy-start(f32[256,256]{1,0:T(8,128)} %param.21) | copy-start | bytes 786436
  4.2 1.6 %copy-start.3 = (f32[3,2,2,4,128]{4,3,2,1,0:T(4,128)S(1)}, f32[3,2,2,4,128]{4,3,2,1,0:T(4,128)}, u32[]{:S(2)}) copy-start(f32[3,2,2,4,128]{4,3,2,1,0:T(4,128)} %param.16) | copy-start | bytes 73732
  5.8 4.5 %copy-start.10 = (f32[23]{0:T(128)S(1)}, f32[23]{0:T(128)}, u32[]{:S(2)}) copy-start(f32[23]{0:T(128)} %constant.139) | copy-start | bytes 280
  5.8 4.5 %copy-start.11 = (f32[23]{0:T(128)S(1)}, f32[23]{0:T(128)}, u32[]{:S(2)}) copy-start(f32[23]{0:T(128)} %constant.140) | copy-start | bytes 280
  5.8 4.6 %copy-start.9 = (s32[432]{0:T(512)S(1)}, s32[432]{0:T(512)}, u32[]{:S(2)}) copy-start(s32[432]{0:T(512)} %constant.150) | copy-start | bytes 5188
  5.9 4.5 %copy-start.12 = (s32[23]{0:T(128)S(1)}, s32[23]{0:T(128)}, u32[]{:S(2)}) copy-start(s32[23]{0:T(128)} %constant.151) | copy-start | bytes 280
  5.9 7.7 %collective-permute-start.1 = (f32[8704]{0:T(1024)S(1)}, f32[8704]{0:T(1024)S(1)}, u32[]{:S(2)}, u32[]{:S(2)}) collective-permute-start(f32[8704]{0:T(1024)S(1)} %pad_maximum_fusion.7), channel_id=1, source_target_pairs={{4,0},{8,4},{12,8},{16,12},{20,16},{24,20},{28,24},{0,28},{5,1},{9... | collective-permute-start | bytes 104456 | tf_op jit(solution)/shard_map/ppermute | solution.py:77
  9.3 4.2 %collective-permute-start = (f32[8192]{0:T(1024)S(1)}, f32[8192]{0:T(1024)S(1)}, u32[]{:S(2)}, u32[]{:S(2)}) collective-permute-start(f32[8192]{0:T(1024)S(1)} %pad_maximum_fusion.8), channel_id=1, source_target_pairs={{0,4},{4,8},{8,12},{12,16},{16,20},{20,24},{24,28},{28,0},{1,5},{5... | collective-permute-start | bytes 98312 | tf_op jit(solution)/shard_map/ppermute | solution.py:76
  13.6 3.7 %collective-permute-start.4 = (f32[2,1,2,256]{3,2,0,1:T(2,128)S(1)}, f32[2,1,2,256]{3,2,0,1:T(2,128)S(1)}, u32[]{:S(2)}, u32[]{:S(2)}) collective-permute-start(f32[2,1,2,256]{3,2,0,1:T(2,128)S(1)} %maximum_bitcast_fusion), channel_id=1, source_target_pairs={{0,24},{4,28},{8,0},{12,4},{16,8},{20,12},{24,16},{28,20},{1,25},{... | collective-permute-start | bytes 12296 | tf_op jit(solution)/shard_map/ppermute | solution.py:60
  17.2 3.7 %collective-permute-start.5 = (f32[4,1,2,256]{3,2,0,1:T(2,128)S(1)}, f32[4,1,2,256]{3,2,0,1:T(2,128)S(1)}, u32[]{:S(2)}, u32[]{:S(2)}) collective-permute-start(f32[4,1,2,256]{3,2,0,1:T(2,128)S(1)} %pad_maximum_fusion.12), channel_id=1, source_target_pairs={{0,16},{4,20},{8,24},{12,28},{16,0},{20,4},{24,8},{28,12},{1,17},{... | collective-permute-start | bytes 24584 | tf_op jit(solution)/shard_map/ppermute | solution.py:60
  20.9 5.1 %collective-permute-start.6 = (f32[8,1,2,256]{3,2,0,1:T(2,128)S(1)}, f32[8,1,2,256]{3,2,0,1:T(2,128)S(1)}, u32[]{:S(2)}, u32[]{:S(2)}) collective-permute-start(f32[8,1,2,256]{3,2,0,1:T(2,128)S(1)} %pad_maximum_fusion.11), channel_id=1, source_target_pairs={{0,3},{1,0},{2,1},{3,2},{4,7},{5,4},{6,5},{7,6},{8,11},{9,8},{10,9... | collective-permute-start | bytes 49160 | tf_op jit(solution)/shard_map/ppermute | solution.py:60
  26.0 5.4 %collective-permute-start.7 = (f32[8,2,2,256]{3,2,0,1:T(2,128)S(1)}, f32[8,2,2,256]{3,2,0,1:T(2,128)S(1)}, u32[]{:S(2)}, u32[]{:S(2)}) collective-permute-start(f32[8,2,2,256]{3,2,0,1:T(2,128)S(1)} %pad_maximum_fusion.9), channel_id=1, source_target_pairs={{0,2},{1,3},{2,0},{3,1},{4,6},{5,7},{6,4},{7,5},{8,10},{9,11},{10,... | collective-permute-start | bytes 98312 | tf_op jit(solution)/shard_map/ppermute | solution.py:60
  27.5 18.0 %collective-permute-start.2 = (f32[20480]{0:T(1024)S(1)}, f32[20480]{0:T(1024)S(1)}, u32[]{:S(2)}, u32[]{:S(2)}) collective-permute-start(f32[20480]{0:T(1024)S(1)} %get-tuple-element.11), channel_id=1, source_target_pairs={{0,1},{1,2},{2,3},{3,0},{4,5},{5,6},{6,7},{7,4},{8,9},{9,10},{10,1... | collective-permute-start | bytes 245768 | tf_op jit(solution)/shard_map/ppermute | solution.py:76
  31.0 14.5 %collective-permute-start.3 = (f32[20480]{0:T(1024)S(1)}, f32[20480]{0:T(1024)S(1)}, u32[]{:S(2)}, u32[]{:S(2)}) collective-permute-start(f32[20480]{0:T(1024)S(1)} %get-tuple-element.12), channel_id=1, source_target_pairs={{1,0},{2,1},{3,2},{0,3},{5,4},{6,5},{7,6},{4,7},{9,8},{10,9},{11,1... | collective-permute-start | bytes 245768 | tf_op jit(solution)/shard_map/ppermute | solution.py:77
  32.1 11.7 %copy-start.6 = (f32[256,256]{1,0:T(8,128)S(1)}, f32[256,256]{1,0:T(8,128)}, u32[]{:S(2)}) copy-start(f32[256,256]{1,0:T(8,128)} %param.22) | copy-start | bytes 786436
  49.9 0.7 copy-start.1
  49.9 0.7 copy-start.2
  50.6 44.7 %copy-start.4 = (f32[256,256]{1,0:T(8,128)S(1)}, f32[256,256]{1,0:T(8,128)}, u32[]{:S(2)}) copy-start(f32[256,256]{1,0:T(8,128)} %param.20) | copy-start | bytes 786436
  50.6 46.4 %copy-start.13 = (f32[3456]{0:T(1024)S(1)}, f32[3456]{0:T(1024)}, u32[]{:S(2)}) copy-start(f32[3456]{0:T(1024)} %constant.136) | copy-start | bytes 41476
  50.6 46.4 %copy-start.14 = (f32[3456]{0:T(1024)S(1)}, f32[3456]{0:T(1024)}, u32[]{:S(2)}) copy-start(f32[3456]{0:T(1024)} %constant.137) | copy-start | bytes 41476
  50.6 46.4 %copy-start.15 = (f32[3456]{0:T(1024)S(1)}, f32[3456]{0:T(1024)}, u32[]{:S(2)}) copy-start(f32[3456]{0:T(1024)} %constant.138) | copy-start | bytes 41476
  97.0 17.0 %copy-start.7 = (f32[2,2,4,128]{3,2,1,0:T(4,128)S(1)}, f32[2,2,4,128]{3,2,1,0:T(4,128)}, u32[]{:S(2)}) copy-start(f32[2,2,4,128]{3,2,1,0:T(4,128)} %param.17) | copy-start | bytes 24580
  97.0 17.0 %copy-start.8 = (s32[2,2,4]{2,1,0:T(2,128)S(1)}, s32[2,2,4]{2,1,0:T(2,128)}, u32[]{:S(2)}) copy-start(s32[2,2,4]{2,1,0:T(2,128)} %param.18) | copy-start | bytes 196

commit v14 on v13

--- a/solution.py
+++ b/solution.py
@@ -286,9 +286,10 @@
     source = source.reshape(4, 4 * layers, len(moves) * slot_count)
     move = np.repeat(np.array(moves, np.float32), slot_count, axis=0)
     own = packed.reshape(4, 4 * layers, slot_count)
-    delta_x = own[0][..., :, None] - source[0][..., None, :] - move[:, 0]
-    delta_y = own[1][..., :, None] - source[1][..., None, :] - move[:, 1]
-    delta_z = own[2][..., :, None] - source[2][..., None, :] - move[:, 2]
+    placed = lax.optimization_barrier(source[:3] + move.T[:, None, :])
+    delta_x = own[0][..., :, None] - placed[0][..., None, :]
+    delta_y = own[1][..., :, None] - placed[1][..., None, :]
+    delta_z = own[2][..., :, None] - placed[2][..., None, :]
     kernel = lax.rsqrt(delta_x * delta_x + delta_y * delta_y + delta_z * delta_z + softening_sq)
     itself = lax.rsqrt(jnp.full((), softening_sq, jnp.float32)) * own[3]
     near = (jnp.sum(kernel * source[3][..., None, :], axis=-1) - itself).reshape(

time: 115 us -> 111 us (0.965)
  other arithmetic: 37.5 us -> 33 us
    reduce_sum x1, other arithmetic: 17 us -> 12.5 us  [shards(): jnp.sum(kernel * source[3][..., None, :], axis=-1) - itself]
  transfers between devices with their start and end apart: 8 -> 8, of which waited for: 4 -> 4; matrix products, arithmetic and copies ran while one was open for 13% -> 14% of each run, Pallas kernels for 0% -> 0%
where the time goes in v14:
time: 111 us
  Pallas kernels  44.7 us (40%)
  other arithmetic  33 us (30%)
  starting transfers between devices  13 us (12%)
  waiting for transfers between devices  10.8 us (10%)
  local copies, waits for them, and re-layouts  7.16 us (6%)
  matrix products  1.18 us (1%)
    pallas_call x1, Pallas kernels, m2l(): pl.pallas_call(functools.partial(m2l_kernel, shift_count, 128), out_shape...  44.7 us
    reduce_sum x5, other arithmetic, point_sum(): return jnp.sum(kernel * weights[..., None, :], axis=-1)  15.8 us
    reduce_sum x1, other arithmetic, shards(): jnp.sum(kernel * source[3][..., None, :], axis=-1) - itself  12.5 us
    ppermute x4, waiting for transfers between devices, rel_gather(): lax.ppermute(part, axis, [(j, (j - have) % count) for j in range(count)])  8.06 us
    ppermute x4, starting transfers between devices, rel_gather(): lax.ppermute(part, axis, [(j, (j - have) % count) for j in range(count)])  5.76 us
    ppermute x2, starting transfers between devices, exchange(): lax.ppermute(sent_head, axis, [((i + 1) % count, i) for i in range(count)])  3.84 us
    ppermute x2, starting transfers between devices, exchange(): lax.ppermute(sent_tail, axis, [(i, (i + 1) % count) for i in range(count)])  3.43 us
    gather x2, local copies, waits for them, and re-layouts, shards(): jnp.take(padded_around.reshape(4, -1, slot_count), box_rows, axis=1)  2.79 us
  transfers between devices with their start and end apart: 8, of which 4 were waited for; matrix products, arithmetic and copies ran while one was open for 14% of the time, Pallas kernels for 0%

profile of v14, /device:TPU:0, one launch (start us, length us, event | category | flops | bytes accessed | tf_op | source)
XLA Modules:
  0.0 110.6 jit_solution(8326534470063806377)
XLA Ops:
  0.0 0.1 cosine_multiply_fusion.1
  0.1 0.1 sine_multiply_fusion.1
  0.2 0.8 fusion.18
  1.0 0.8 fusion.40
  1.8 0.7 fusion.28
  2.5 1.1 multiply_reduce_fusion.5
  3.6 0.3 fusion.15
  4.0 0.1 broadcast_add_fusion.9
  4.2 0.8 add_rsqrt_fusion
  5.0 0.4 multiply_reduce_fusion.2
  5.4 0.3 fusion.32
  5.7 0.1 copy.29
  5.8 0.0 copy-start.11
  5.9 3.4 %collective-permute-start.1 = (f32[8704]{0:T(1024)S(1)}, f32[8704]{0:T(1024)S(1)}, u32[]{:S(2)}, u32[]{:S(2)}) collective-permute-start(f32[8704]{0:T(1024)S(1)} %pad_maximum_fusion.7), channel_id=1, source_target_pairs={{4,0},{8,4},{12,8},{16,12},{20,16},{24,20},{28,24},{0,28},{5,1},{9... | collective-permute-start | bytes 104456 | tf_op jit(solution)/shard_map/ppermute | solution.py:77
  9.3 0.1 fusion.22
  9.4 0.1 fusion.24
  9.6 0.1 subtract_multiply_fusion.2
  9.7 0.1 subtract_multiply_fusion
  9.8 0.1 fusion.5
  9.9 0.1 pad_maximum_fusion.base_ref
  10.0 0.1 subtract_multiply_fusion.3
  10.1 0.1 broadcast_add_fusion.5
  10.2 0.1 broadcast_add_fusion.6
  10.2 0.1 broadcast_add_fusion.2
  10.3 0.1 broadcast_add_fusion.1
  10.4 0.1 stack_broadcast_in_dim.44
  10.7 2.8 %collective-permute-done = f32[8192]{0:T(1024)S(1)} collective-permute-done((f32[8192]{0:T(1024)S(1)}, f32[8192]{0:T(1024)S(1)}, u32[]{:S(2)}, u32[]{:S(2)}) %collective-permute-start) | collective-permute-done | bytes 32800 | tf_op jit(solution)/shard_map/ppermute | solution.py:76
  13.5 0.1 collective-permute-start.4
  13.7 3.6 %collective-permute-done.4 = f32[2,1,2,256]{3,2,0,1:T(2,128)S(1)} collective-permute-done((f32[2,1,2,256]{3,2,0,1:T(2,128)S(1)}, f32[2,1,2,256]{3,2,0,1:T(2,128)S(1)}, u32[]{:S(2)}, u32[]{:S(2)}) %collective-permute-start.4) | collective-permute-done | bytes 4128 | tf_op jit(solution)/shard_map/ppermute | solution.py:60
  17.2 0.5 collective-permute-start.5
  17.8 3.1 %collective-permute-done.5 = f32[4,1,2,256]{3,2,0,1:T(2,128)S(1)} collective-permute-done((f32[4,1,2,256]{3,2,0,1:T(2,128)S(1)}, f32[4,1,2,256]{3,2,0,1:T(2,128)S(1)}, u32[]{:S(2)}, u32[]{:S(2)}) %collective-permute-start.5) | collective-permute-done | bytes 8224 | tf_op jit(solution)/shard_map/ppermute | solution.py:60
  20.9 3.7 %collective-permute-start.6 = (f32[8,1,2,256]{3,2,0,1:T(2,128)S(1)}, f32[8,1,2,256]{3,2,0,1:T(2,128)S(1)}, u32[]{:S(2)}, u32[]{:S(2)}) collective-permute-start(f32[8,1,2,256]{3,2,0,1:T(2,128)S(1)} %pad_maximum_fusion.11), channel_id=1, source_target_pairs={{0,3},{1,0},{2,1},{3,2},{4,7},{5,4},{6,5},{7,6},{8,11},{9,8},{10,9... | collective-permute-start | bytes 49160 | tf_op jit(solution)/shard_map/ppermute | solution.py:60
  24.6 1.4 %collective-permute-done.6 = f32[8,1,2,256]{3,2,0,1:T(2,128)S(1)} collective-permute-done((f32[8,1,2,256]{3,2,0,1:T(2,128)S(1)}, f32[8,1,2,256]{3,2,0,1:T(2,128)S(1)}, u32[]{:S(2)}, u32[]{:S(2)}) %collective-permute-start.6) | collective-permute-done | bytes 16416 | tf_op jit(solution)/shard_map/ppermute | solution.py:60
  26.0 1.5 %collective-permute-start.7 = (f32[8,2,2,256]{3,2,0,1:T(2,128)S(1)}, f32[8,2,2,256]{3,2,0,1:T(2,128)S(1)}, u32[]{:S(2)}, u32[]{:S(2)}) collective-permute-start(f32[8,2,2,256]{3,2,0,1:T(2,128)S(1)} %pad_maximum_fusion.9), channel_id=1, source_target_pairs={{0,2},{1,3},{2,0},{3,1},{4,6},{5,7},{6,4},{7,5},{8,10},{9,11},{10,... | collective-permute-start | bytes 98312 | tf_op jit(solution)/shard_map/ppermute | solution.py:60
  27.5 3.4 %collective-permute-start.2 = (f32[20480]{0:T(1024)S(1)}, f32[20480]{0:T(1024)S(1)}, u32[]{:S(2)}, u32[]{:S(2)}) collective-permute-start(f32[20480]{0:T(1024)S(1)} %get-tuple-element.10), channel_id=1, source_target_pairs={{0,1},{1,2},{2,3},{3,0},{4,5},{5,6},{6,7},{7,4},{8,9},{9,10},{10,1... | collective-permute-start | bytes 245768 | tf_op jit(solution)/shard_map/ppermute | solution.py:76
  31.0 0.5 collective-permute-start.3
  31.5 0.6 gather_fusion.1
  32.1 11.7 %multiply_reduce_fusion.1 = f32[2,256]{1,0:T(2,128)S(1)} fusion(f32[11776]{0:T(1024)S(1)} %select_n.50, f32[2,11776]{1,0:T(2,128)S(1)} %stack_broadcast_in_dim.44, f32[256]{0:T(256)S(1)} %bitcast.176, f32[11776]{0:T(1024)S(1)} %stack_broadcast_in_dim.42, f32[256]{0:T(256)S(1)} %bitcast.177, f32[11776]{0:T(1024)S(1)} %stack_broadcast_in_dim.40, ...), kind=kLoop, calls=%fused_computation.3 | loop fusion | flops 66321920 | bytes 240640 | tf_op jit(solution)/shard_map/reduce_sum | solution.py:29
  43.8 0.3 fusion.33
  44.1 0.1 mul.538
  44.2 1.3 %multiply_reduce_fusion.3 = f32[2,2,4,128]{3,2,1,0:T(4,128)S(1)} fusion(f32[4,256]{1,0:T(4,128)S(1)} %mul.538, f32[256]{0:T(256)S(1)} %bitcast.166, f32[2,2,4,128]{3,2,1,0:T(4,128)S(1)} %get-tuple-element.26, f32[256]{0:T(256)S(1)} %bitcast.168, f32[2,2,4,128]{3,2,1,0:T(4,128)S(1)} %get-tuple-element.19, f32[256]{0:T(256)S(1)} %bitcast.164, ...), kind=kLoop, calls=%fused_computation.5 | loop fusion | flops 5765120 | bytes 39936 | tf_op jit(solution)/shard_map/reduce_sum | solution.py:29
  45.6 0.1 copy.28
  45.7 2.3 %gather_fusion = f32[432,4,128]{2,1,0:T(4,128)S(1)} fusion(f32[4,96,128]{2,0,1:T(4,128)S(1)} %bitcast.126, s32[1024]{0:T(1024)S(1)} %get-tuple-element.49), kind=kCustom, calls=%fused_computation | custom fusion | bytes 1771200 | tf_op jit(solution)/shard_map/jit(_take)/gather | solution.py:282
  48.0 0.5 copy.45
  48.5 0.1 slice.300
  48.6 0.1 slice.259
  48.7 0.6 copy-done.8
  49.3 0.1 broadcast_add_fusion
  49.5 0.1 copy.46
  49.7 0.1 select_maximum_fusion
  49.9 0.1 fusion.11
  50.0 0.1 fusion.10
  50.1 0.1 fusion.9
  50.2 0.1 fusion.8
  50.2 0.1 fusion.7
  50.4 0.1 fusion.6
  50.5 0.3 copy.24
  50.8 0.2 copy-done.1
  51.0 0.0 copy-done.2
  51.0 44.7 %shard_map.136 = f32[16,256]{1,0:T(8,128)S(1)} custom-call(f32[632]{0:T(1024)S(1)} %copy-done.2, s32[1264]{0:T(1024)S(1)} %copy-done.1, f32[4,256,256]{2,1,0:T(8,128)S(1)} %pad_maximum_fusion.base_ref, f32[448,4,256]{2,1,0:T(4,128)S(1)} %bitcast.125), custom_call_target="tpu_custom_call" | custom-call | flops 2133065728 | bytes 2899968 | tf_op jit(solution)/shard_map/pallas_call | solution.py:147
  95.8 0.3 fusion.13
  96.1 1.3 %multiply_reduce_fusion.4 = f32[2,2,4,128]{3,2,1,0:T(4,128)S(1)} fusion(f32[2,2,4,256]{3,2,1,0:T(4,128)S(1)} %fusion.13, f32[256]{0:T(256)S(1)} %bitcast.172, f32[2,2,4,128]{3,2,1,0:T(4,128)S(1)} %get-tuple-element.23, f32[256]{0:T(256)S(1)} %bitcast.170, f32[2,2,4,128]{3,2,1,0:T(4,128)S(1)} %get-tuple-element.22, f32[256]{0:T(256)S(1)} %bitcast.174, ...), kind=kLoop, calls=%fused_computation.6 | loop fusion | flops 5765120 | bytes 52224 | tf_op jit(solution)/shard_map/reduce_sum | solution.py:29
  97.4 12.5 %multiply_reduce_fusion = f32[16,128]{1,0:T(8,128)S(1)} fusion(f32[16,3456]{1,0:T(8,128)S(1)} %bitcast.133, f32[16,3456]{1,0:T(8,128)S(1)} %get-tuple-element.6, f32[16,128]{1,0:T(8,128)S(1)} %bitcast.159, f32[16,3456]{1,0:T(8,128)S(1)} %get-tuple-element.7, f32[16,128]{1,0:T(8,128)S(1)} %bitcast.160, f32[16,3456]{1,0:T(8,128)S(1)} %get-tuple-element.5, ...), kind=kLoop, calls=%fused_computation.2 | loop fusion | flops 77854720 | bytes 917504 | tf_op jit(solution)/shard_map/reduce_sum | solution.py:295
  109.9 0.7 add_select_fusion
  (95 shorter events, 1.2 us)
Async XLA Ops:
  0.0 3.6 %copy-start = (f32[256,256]{1,0:T(8,128)S(1)}, f32[256,256]{1,0:T(8,128)}, u32[]{:S(2)}) copy-start(f32[256,256]{1,0:T(8,128)} %param.17) | copy-start | bytes 786436
  4.2 1.2 %copy-start.5 = (f32[256,256]{1,0:T(8,128)S(1)}, f32[256,256]{1,0:T(8,128)}, u32[]{:S(2)}) copy-start(f32[256,256]{1,0:T(8,128)} %param.19) | copy-start | bytes 786436
  4.2 1.6 %copy-start.3 = (f32[3,2,2,4,128]{4,3,2,1,0:T(4,128)S(1)}, f32[3,2,2,4,128]{4,3,2,1,0:T(4,128)}, u32[]{:S(2)}) copy-start(f32[3,2,2,4,128]{4,3,2,1,0:T(4,128)} %param.14) | copy-start | bytes 73732
  5.8 4.5 %copy-start.11 = (f32[23]{0:T(128)S(1)}, f32[23]{0:T(128)}, u32[]{:S(2)}) copy-start(f32[23]{0:T(128)} %constant.131) | copy-start | bytes 280
  5.8 4.5 %copy-start.12 = (f32[23]{0:T(128)S(1)}, f32[23]{0:T(128)}, u32[]{:S(2)}) copy-start(f32[23]{0:T(128)} %constant.132) | copy-start | bytes 280
  5.8 4.6 %copy-start.10 = (s32[432]{0:T(512)S(1)}, s32[432]{0:T(512)}, u32[]{:S(2)}) copy-start(s32[432]{0:T(512)} %constant.142) | copy-start | bytes 5188
  5.8 4.5 %copy-start.13 = (s32[23]{0:T(128)S(1)}, s32[23]{0:T(128)}, u32[]{:S(2)}) copy-start(s32[23]{0:T(128)} %constant.143) | copy-start | bytes 280
  5.9 7.7 %collective-permute-start.1 = (f32[8704]{0:T(1024)S(1)}, f32[8704]{0:T(1024)S(1)}, u32[]{:S(2)}, u32[]{:S(2)}) collective-permute-start(f32[8704]{0:T(1024)S(1)} %pad_maximum_fusion.7), channel_id=1, source_target_pairs={{4,0},{8,4},{12,8},{16,12},{20,16},{24,20},{28,24},{0,28},{5,1},{9... | collective-permute-start | bytes 104456 | tf_op jit(solution)/shard_map/ppermute | solution.py:77
  9.2 4.2 %collective-permute-start = (f32[8192]{0:T(1024)S(1)}, f32[8192]{0:T(1024)S(1)}, u32[]{:S(2)}, u32[]{:S(2)}) collective-permute-start(f32[8192]{0:T(1024)S(1)} %pad_maximum_fusion.8), channel_id=1, source_target_pairs={{0,4},{4,8},{8,12},{12,16},{16,20},{20,24},{24,28},{28,0},{1,5},{5... | collective-permute-start | bytes 98312 | tf_op jit(solution)/shard_map/ppermute | solution.py:76
  13.5 3.7 %collective-permute-start.4 = (f32[2,1,2,256]{3,2,0,1:T(2,128)S(1)}, f32[2,1,2,256]{3,2,0,1:T(2,128)S(1)}, u32[]{:S(2)}, u32[]{:S(2)}) collective-permute-start(f32[2,1,2,256]{3,2,0,1:T(2,128)S(1)} %maximum_bitcast_fusion), channel_id=1, source_target_pairs={{0,24},{4,28},{8,0},{12,4},{16,8},{20,12},{24,16},{28,20},{1,25},{... | collective-permute-start | bytes 12296 | tf_op jit(solution)/shard_map/ppermute | solution.py:60
  17.2 3.7 %collective-permute-start.5 = (f32[4,1,2,256]{3,2,0,1:T(2,128)S(1)}, f32[4,1,2,256]{3,2,0,1:T(2,128)S(1)}, u32[]{:S(2)}, u32[]{:S(2)}) collective-permute-start(f32[4,1,2,256]{3,2,0,1:T(2,128)S(1)} %pad_maximum_fusion.12), channel_id=1, source_target_pairs={{0,16},{4,20},{8,24},{12,28},{16,0},{20,4},{24,8},{28,12},{1,17},{... | collective-permute-start | bytes 24584 | tf_op jit(solution)/shard_map/ppermute | solution.py:60
  20.9 5.1 %collective-permute-start.6 = (f32[8,1,2,256]{3,2,0,1:T(2,128)S(1)}, f32[8,1,2,256]{3,2,0,1:T(2,128)S(1)}, u32[]{:S(2)}, u32[]{:S(2)}) collective-permute-start(f32[8,1,2,256]{3,2,0,1:T(2,128)S(1)} %pad_maximum_fusion.11), channel_id=1, source_target_pairs={{0,3},{1,0},{2,1},{3,2},{4,7},{5,4},{6,5},{7,6},{8,11},{9,8},{10,9... | collective-permute-start | bytes 49160 | tf_op jit(solution)/shard_map/ppermute | solution.py:60
  26.0 5.4 %collective-permute-start.7 = (f32[8,2,2,256]{3,2,0,1:T(2,128)S(1)}, f32[8,2,2,256]{3,2,0,1:T(2,128)S(1)}, u32[]{:S(2)}, u32[]{:S(2)}) collective-permute-start(f32[8,2,2,256]{3,2,0,1:T(2,128)S(1)} %pad_maximum_fusion.9), channel_id=1, source_target_pairs={{0,2},{1,3},{2,0},{3,1},{4,6},{5,7},{6,4},{7,5},{8,10},{9,11},{10,... | collective-permute-start | bytes 98312 | tf_op jit(solution)/shard_map/ppermute | solution.py:60
  27.5 18.0 %collective-permute-start.2 = (f32[20480]{0:T(1024)S(1)}, f32[20480]{0:T(1024)S(1)}, u32[]{:S(2)}, u32[]{:S(2)}) collective-permute-start(f32[20480]{0:T(1024)S(1)} %get-tuple-element.10), channel_id=1, source_target_pairs={{0,1},{1,2},{2,3},{3,0},{4,5},{5,6},{6,7},{7,4},{8,9},{9,10},{10,1... | collective-permute-start | bytes 245768 | tf_op jit(solution)/shard_map/ppermute | solution.py:76
  31.0 14.6 %collective-permute-start.3 = (f32[20480]{0:T(1024)S(1)}, f32[20480]{0:T(1024)S(1)}, u32[]{:S(2)}, u32[]{:S(2)}) collective-permute-start(f32[20480]{0:T(1024)S(1)} %get-tuple-element.11), channel_id=1, source_target_pairs={{1,0},{2,1},{3,2},{0,3},{5,4},{6,5},{7,6},{4,7},{9,8},{10,9},{11,1... | collective-permute-start | bytes 245768 | tf_op jit(solution)/shard_map/ppermute | solution.py:77
  32.1 11.7 %copy-start.6 = (f32[256,256]{1,0:T(8,128)S(1)}, f32[256,256]{1,0:T(8,128)}, u32[]{:S(2)}) copy-start(f32[256,256]{1,0:T(8,128)} %param.20) | copy-start | bytes 786436
  48.5 0.8 copy-start.8
  50.3 0.7 copy-start.1
  50.4 0.7 copy-start.2
  51.0 44.7 %copy-start.4 = (f32[256,256]{1,0:T(8,128)S(1)}, f32[256,256]{1,0:T(8,128)}, u32[]{:S(2)}) copy-start(f32[256,256]{1,0:T(8,128)} %param.18) | copy-start | bytes 786436
  97.4 12.5 %copy-start.7 = (f32[2,2,4,128]{3,2,1,0:T(4,128)S(1)}, f32[2,2,4,128]{3,2,1,0:T(4,128)}, u32[]{:S(2)}) copy-start(f32[2,2,4,128]{3,2,1,0:T(4,128)} %param.15) | copy-start | bytes 24580
  97.4 12.5 %copy-start.9 = (s32[2,2,4]{2,1,0:T(2,128)S(1)}, s32[2,2,4]{2,1,0:T(2,128)}, u32[]{:S(2)}) copy-start(s32[2,2,4]{2,1,0:T(2,128)} %param.16) | copy-start | bytes 196

commit v15 on v14

--- a/solution.py
+++ b/solution.py
@@ -127,7 +127,7 @@
                 + scale_z * base_ref[2, row : row + rows, :]
             )
             matrix = lax.rsqrt(square)
-            matrix_top = split_top(matrix)
+            matrix_top = lax.reduce_precision(matrix, exponent_bits=8, mantissa_bits=7)
             matrix_high = matrix_top.astype(jnp.bfloat16)
             matrix_low = (matrix - matrix_top).astype(jnp.bfloat16)
             out_ref[:, row : row + rows] += split_dot(

time: 111 us -> 117 us (1.054)
  Pallas kernels: 44.7 us -> 50.9 us
    pallas_call x1, Pallas kernels: 44.7 us -> 50.9 us  [m2l(): pl.pallas_call(functools.partial(m2l_kernel, shift_count, 128), out_shape...]
  transfers between devices with their start and end apart: 8 -> 8, of which waited for: 4 -> 4; matrix products, arithmetic and copies ran while one was open for 14% -> 13% of each run, Pallas kernels for 0% -> 0%
where the time goes in v15:
time: 117 us
  Pallas kernels  50.9 us (44%)
  other arithmetic  33 us (28%)
  starting transfers between devices  13 us (11%)
  waiting for transfers between devices  10.8 us (9%)
  local copies, waits for them, and re-layouts  7.16 us (6%)
  matrix products  1.18 us (1%)
    pallas_call x1, Pallas kernels, m2l(): pl.pallas_call(functools.partial(m2l_kernel, shift_count, 128), out_shape...  50.9 us
    reduce_sum x5, other arithmetic, point_sum(): return jnp.sum(kernel * weights[..., None, :], axis=-1)  15.8 us
    reduce_sum x1, other arithmetic, shards(): jnp.sum(kernel * source[3][..., None, :], axis=-1) - itself  12.5 us
    ppermute x4, waiting for transfers between devices, rel_gather(): lax.ppermute(part, axis, [(j, (j - have) % count) for j in range(count)])  8.06 us
    ppermute x4, starting transfers between devices, rel_gather(): lax.ppermute(part, axis, [(j, (j - have) % count) for j in range(count)])  5.76 us
    ppermute x2, starting transfers between devices, exchange(): lax.ppermute(sent_head, axis, [((i + 1) % count, i) for i in range(count)])  3.84 us
    ppermute x2, starting transfers between devices, exchange(): lax.ppermute(sent_tail, axis, [(i, (i + 1) % count) for i in range(count)])  3.43 us
    gather x2, local copies, waits for them, and re-layouts, shards(): jnp.take(padded_around.reshape(4, -1, slot_count), box_rows, axis=1)  2.79 us
  transfers between devices with their start and end apart: 8, of which 4 were waited for; matrix products, arithmetic and copies ran while one was open for 13% of the time, Pallas kernels for 0%

profile of v15, /device:TPU:0, one launch (start us, length us, event | category | flops | bytes accessed | tf_op | source)
XLA Modules:
  0.0 116.8 jit_solution(12702907860584926876)
XLA Ops:
  0.0 0.1 cosine_multiply_fusion.1
  0.1 0.1 sine_multiply_fusion.1
  0.2 0.8 fusion.18
  1.0 0.8 fusion.40
  1.8 0.7 fusion.28
  2.5 1.1 multiply_reduce_fusion.5
  3.6 0.3 fusion.15
  4.0 0.1 broadcast_add_fusion.9
  4.2 0.8 add_rsqrt_fusion
  5.0 0.4 multiply_reduce_fusion.2
  5.4 0.3 fusion.32
  5.7 0.1 copy.29
  5.8 0.0 copy-start.11
  5.9 3.4 %collective-permute-start.1 = (f32[8704]{0:T(1024)S(1)}, f32[8704]{0:T(1024)S(1)}, u32[]{:S(2)}, u32[]{:S(2)}) collective-permute-start(f32[8704]{0:T(1024)S(1)} %pad_maximum_fusion.7), channel_id=1, source_target_pairs={{4,0},{8,4},{12,8},{16,12},{20,16},{24,20},{28,24},{0,28},{5,1},{9... | collective-permute-start | bytes 104456 | tf_op jit(solution)/shard_map/ppermute | solution.py:77
  9.3 0.1 fusion.22
  9.4 0.1 fusion.24
  9.6 0.1 subtract_multiply_fusion.2
  9.7 0.1 subtract_multiply_fusion
  9.8 0.1 fusion.5
  9.9 0.1 pad_maximum_fusion.base_ref
  10.0 0.1 subtract_multiply_fusion.3
  10.1 0.1 broadcast_add_fusion.5
  10.2 0.1 broadcast_add_fusion.6
  10.2 0.1 broadcast_add_fusion.2
  10.3 0.1 broadcast_add_fusion.1
  10.4 0.1 stack_broadcast_in_dim.44
  10.7 2.8 %collective-permute-done = f32[8192]{0:T(1024)S(1)} collective-permute-done((f32[8192]{0:T(1024)S(1)}, f32[8192]{0:T(1024)S(1)}, u32[]{:S(2)}, u32[]{:S(2)}) %collective-permute-start) | collective-permute-done | bytes 32800 | tf_op jit(solution)/shard_map/ppermute | solution.py:76
  13.5 0.1 collective-permute-start.4
  13.7 3.6 %collective-permute-done.4 = f32[2,1,2,256]{3,2,0,1:T(2,128)S(1)} collective-permute-done((f32[2,1,2,256]{3,2,0,1:T(2,128)S(1)}, f32[2,1,2,256]{3,2,0,1:T(2,128)S(1)}, u32[]{:S(2)}, u32[]{:S(2)}) %collective-permute-start.4) | collective-permute-done | bytes 4128 | tf_op jit(solution)/shard_map/ppermute | solution.py:60
  17.2 0.5 collective-permute-start.5
  17.8 3.1 %collective-permute-done.5 = f32[4,1,2,256]{3,2,0,1:T(2,128)S(1)} collective-permute-done((f32[4,1,2,256]{3,2,0,1:T(2,128)S(1)}, f32[4,1,2,256]{3,2,0,1:T(2,128)S(1)}, u32[]{:S(2)}, u32[]{:S(2)}) %collective-permute-start.5) | collective-permute-done | bytes 8224 | tf_op jit(solution)/shard_map/ppermute | solution.py:60
  20.9 3.7 %collective-permute-start.6 = (f32[8,1,2,256]{3,2,0,1:T(2,128)S(1)}, f32[8,1,2,256]{3,2,0,1:T(2,128)S(1)}, u32[]{:S(2)}, u32[]{:S(2)}) collective-permute-start(f32[8,1,2,256]{3,2,0,1:T(2,128)S(1)} %pad_maximum_fusion.11), channel_id=1, source_target_pairs={{0,3},{1,0},{2,1},{3,2},{4,7},{5,4},{6,5},{7,6},{8,11},{9,8},{10,9... | collective-permute-start | bytes 49160 | tf_op jit(solution)/shard_map/ppermute | solution.py:60
  24.6 1.4 %collective-permute-done.6 = f32[8,1,2,256]{3,2,0,1:T(2,128)S(1)} collective-permute-done((f32[8,1,2,256]{3,2,0,1:T(2,128)S(1)}, f32[8,1,2,256]{3,2,0,1:T(2,128)S(1)}, u32[]{:S(2)}, u32[]{:S(2)}) %collective-permute-start.6) | collective-permute-done | bytes 16416 | tf_op jit(solution)/shard_map/ppermute | solution.py:60
  26.0 1.5 %collective-permute-start.7 = (f32[8,2,2,256]{3,2,0,1:T(2,128)S(1)}, f32[8,2,2,256]{3,2,0,1:T(2,128)S(1)}, u32[]{:S(2)}, u32[]{:S(2)}) collective-permute-start(f32[8,2,2,256]{3,2,0,1:T(2,128)S(1)} %pad_maximum_fusion.9), channel_id=1, source_target_pairs={{0,2},{1,3},{2,0},{3,1},{4,6},{5,7},{6,4},{7,5},{8,10},{9,11},{10,... | collective-permute-start | bytes 98312 | tf_op jit(solution)/shard_map/ppermute | solution.py:60
  27.5 3.4 %collective-permute-start.2 = (f32[20480]{0:T(1024)S(1)}, f32[20480]{0:T(1024)S(1)}, u32[]{:S(2)}, u32[]{:S(2)}) collective-permute-start(f32[20480]{0:T(1024)S(1)} %get-tuple-element.10), channel_id=1, source_target_pairs={{0,1},{1,2},{2,3},{3,0},{4,5},{5,6},{6,7},{7,4},{8,9},{9,10},{10,1... | collective-permute-start | bytes 245768 | tf_op jit(solution)/shard_map/ppermute | solution.py:76
  31.0 0.5 collective-permute-start.3
  31.5 0.6 gather_fusion.1
  32.1 11.7 %multiply_reduce_fusion.1 = f32[2,256]{1,0:T(2,128)S(1)} fusion(f32[11776]{0:T(1024)S(1)} %select_n.50, f32[2,11776]{1,0:T(2,128)S(1)} %stack_broadcast_in_dim.44, f32[256]{0:T(256)S(1)} %bitcast.176, f32[11776]{0:T(1024)S(1)} %stack_broadcast_in_dim.42, f32[256]{0:T(256)S(1)} %bitcast.177, f32[11776]{0:T(1024)S(1)} %stack_broadcast_in_dim.40, ...), kind=kLoop, calls=%fused_computation.3 | loop fusion | flops 66321920 | bytes 240640 | tf_op jit(solution)/shard_map/reduce_sum | solution.py:29
  43.8 0.3 fusion.33
  44.1 0.1 mul.538
  44.2 1.3 %multiply_reduce_fusion.3 = f32[2,2,4,128]{3,2,1,0:T(4,128)S(1)} fusion(f32[4,256]{1,0:T(4,128)S(1)} %mul.538, f32[256]{0:T(256)S(1)} %bitcast.166, f32[2,2,4,128]{3,2,1,0:T(4,128)S(1)} %get-tuple-element.26, f32[256]{0:T(256)S(1)} %bitcast.168, f32[2,2,4,128]{3,2,1,0:T(4,128)S(1)} %get-tuple-element.19, f32[256]{0:T(256)S(1)} %bitcast.164, ...), kind=kLoop, calls=%fused_computation.5 | loop fusion | flops 5765120 | bytes 39936 | tf_op jit(solution)/shard_map/reduce_sum | solution.py:29
  45.6 0.1 copy.28
  45.7 2.3 %gather_fusion = f32[432,4,128]{2,1,0:T(4,128)S(1)} fusion(f32[4,96,128]{2,0,1:T(4,128)S(1)} %bitcast.126, s32[1024]{0:T(1024)S(1)} %get-tuple-element.49), kind=kCustom, calls=%fused_computation | custom fusion | bytes 1771200 | tf_op jit(solution)/shard_map/jit(_take)/gather | solution.py:282
  48.0 0.5 copy.45
  48.5 0.1 slice.300
  48.6 0.1 slice.259
  48.7 0.6 copy-done.8
  49.3 0.1 broadcast_add_fusion
  49.5 0.1 copy.46
  49.7 0.1 select_maximum_fusion
  49.9 0.1 fusion.11
  50.0 0.1 fusion.10
  50.1 0.1 fusion.9
  50.2 0.1 fusion.8
  50.2 0.1 fusion.7
  50.4 0.1 fusion.6
  50.5 0.3 copy.24
  50.8 0.2 copy-done.1
  51.0 0.0 copy-done.2
  51.0 50.9 %shard_map.136 = f32[16,256]{1,0:T(8,128)S(1)} custom-call(f32[632]{0:T(1024)S(1)} %copy-done.2, s32[1264]{0:T(1024)S(1)} %copy-done.1, f32[4,256,256]{2,1,0:T(8,128)S(1)} %pad_maximum_fusion.base_ref, f32[448,4,256]{2,1,0:T(4,128)S(1)} %bitcast.125), custom_call_target="tpu_custom_call" | custom-call | flops 2133065728 | bytes 2899968 | tf_op jit(solution)/shard_map/pallas_call | solution.py:147
  102.0 0.3 fusion.13
  102.3 1.3 %multiply_reduce_fusion.4 = f32[2,2,4,128]{3,2,1,0:T(4,128)S(1)} fusion(f32[2,2,4,256]{3,2,1,0:T(4,128)S(1)} %fusion.13, f32[256]{0:T(256)S(1)} %bitcast.172, f32[2,2,4,128]{3,2,1,0:T(4,128)S(1)} %get-tuple-element.23, f32[256]{0:T(256)S(1)} %bitcast.170, f32[2,2,4,128]{3,2,1,0:T(4,128)S(1)} %get-tuple-element.22, f32[256]{0:T(256)S(1)} %bitcast.174, ...), kind=kLoop, calls=%fused_computation.6 | loop fusion | flops 5765120 | bytes 52224 | tf_op jit(solution)/shard_map/reduce_sum | solution.py:29
  103.7 12.5 %multiply_reduce_fusion = f32[16,128]{1,0:T(8,128)S(1)} fusion(f32[16,3456]{1,0:T(8,128)S(1)} %bitcast.133, f32[16,3456]{1,0:T(8,128)S(1)} %get-tuple-element.6, f32[16,128]{1,0:T(8,128)S(1)} %bitcast.159, f32[16,3456]{1,0:T(8,128)S(1)} %get-tuple-element.7, f32[16,128]{1,0:T(8,128)S(1)} %bitcast.160, f32[16,3456]{1,0:T(8,128)S(1)} %get-tuple-element.5, ...), kind=kLoop, calls=%fused_computation.2 | loop fusion | flops 77854720 | bytes 917504 | tf_op jit(solution)/shard_map/reduce_sum | solution.py:295
  116.2 0.7 add_select_fusion
  (95 shorter events, 1.2 us)
Async XLA Ops:
  0.0 3.6 %copy-start = (f32[256,256]{1,0:T(8,128)S(1)}, f32[256,256]{1,0:T(8,128)}, u32[]{:S(2)}) copy-start(f32[256,256]{1,0:T(8,128)} %param.17) | copy-start | bytes 786436
  4.2 1.2 %copy-start.5 = (f32[256,256]{1,0:T(8,128)S(1)}, f32[256,256]{1,0:T(8,128)}, u32[]{:S(2)}) copy-start(f32[256,256]{1,0:T(8,128)} %param.19) | copy-start | bytes 786436
  4.2 1.6 %copy-start.3 = (f32[3,2,2,4,128]{4,3,2,1,0:T(4,128)S(1)}, f32[3,2,2,4,128]{4,3,2,1,0:T(4,128)}, u32[]{:S(2)}) copy-start(f32[3,2,2,4,128]{4,3,2,1,0:T(4,128)} %param.14) | copy-start | bytes 73732
  5.8 4.5 %copy-start.11 = (f32[23]{0:T(128)S(1)}, f32[23]{0:T(128)}, u32[]{:S(2)}) copy-start(f32[23]{0:T(128)} %constant.131) | copy-start | bytes 280
  5.8 4.5 %copy-start.12 = (f32[23]{0:T(128)S(1)}, f32[23]{0:T(128)}, u32[]{:S(2)}) copy-start(f32[23]{0:T(128)} %constant.132) | copy-start | bytes 280
  5.8 4.6 %copy-start.10 = (s32[432]{0:T(512)S(1)}, s32[432]{0:T(512)}, u32[]{:S(2)}) copy-start(s32[432]{0:T(512)} %constant.142) | copy-start | bytes 5188
  5.8 4.5 %copy-start.13 = (s32[23]{0:T(128)S(1)}, s32[23]{0:T(128)}, u32[]{:S(2)}) copy-start(s32[23]{0:T(128)} %constant.143) | copy-start | bytes 280
  5.9 7.7 %collective-permute-start.1 = (f32[8704]{0:T(1024)S(1)}, f32[8704]{0:T(1024)S(1)}, u32[]{:S(2)}, u32[]{:S(2)}) collective-permute-start(f32[8704]{0:T(1024)S(1)} %pad_maximum_fusion.7), channel_id=1, source_target_pairs={{4,0},{8,4},{12,8},{16,12},{20,16},{24,20},{28,24},{0,28},{5,1},{9... | collective-permute-start | bytes 104456 | tf_op jit(solution)/shard_map/ppermute | solution.py:77
  9.2 4.2 %collective-permute-start = (f32[8192]{0:T(1024)S(1)}, f32[8192]{0:T(1024)S(1)}, u32[]{:S(2)}, u32[]{:S(2)}) collective-permute-start(f32[8192]{0:T(1024)S(1)} %pad_maximum_fusion.8), channel_id=1, source_target_pairs={{0,4},{4,8},{8,12},{12,16},{16,20},{20,24},{24,28},{28,0},{1,5},{5... | collective-permute-start | bytes 98312 | tf_op jit(solution)/shard_map/ppermute | solution.py:76
  13.5 3.7 %collective-permute-start.4 = (f32[2,1,2,256]{3,2,0,1:T(2,128)S(1)}, f32[2,1,2,256]{3,2,0,1:T(2,128)S(1)}, u32[]{:S(2)}, u32[]{:S(2)}) collective-permute-start(f32[2,1,2,256]{3,2,0,1:T(2,128)S(1)} %maximum_bitcast_fusion), channel_id=1, source_target_pairs={{0,24},{4,28},{8,0},{12,4},{16,8},{20,12},{24,16},{28,20},{1,25},{... | collective-permute-start | bytes 12296 | tf_op jit(solution)/shard_map/ppermute | solution.py:60
  17.2 3.7 %collective-permute-start.5 = (f32[4,1,2,256]{3,2,0,1:T(2,128)S(1)}, f32[4,1,2,256]{3,2,0,1:T(2,128)S(1)}, u32[]{:S(2)}, u32[]{:S(2)}) collective-permute-start(f32[4,1,2,256]{3,2,0,1:T(2,128)S(1)} %pad_maximum_fusion.12), channel_id=1, source_target_pairs={{0,16},{4,20},{8,24},{12,28},{16,0},{20,4},{24,8},{28,12},{1,17},{... | collective-permute-start | bytes 24584 | tf_op jit(solution)/shard_map/ppermute | solution.py:60
  20.9 5.1 %collective-permute-start.6 = (f32[8,1,2,256]{3,2,0,1:T(2,128)S(1)}, f32[8,1,2,256]{3,2,0,1:T(2,128)S(1)}, u32[]{:S(2)}, u32[]{:S(2)}) collective-permute-start(f32[8,1,2,256]{3,2,0,1:T(2,128)S(1)} %pad_maximum_fusion.11), channel_id=1, source_target_pairs={{0,3},{1,0},{2,1},{3,2},{4,7},{5,4},{6,5},{7,6},{8,11},{9,8},{10,9... | collective-permute-start | bytes 49160 | tf_op jit(solution)/shard_map/ppermute | solution.py:60
  26.0 5.4 %collective-permute-start.7 = (f32[8,2,2,256]{3,2,0,1:T(2,128)S(1)}, f32[8,2,2,256]{3,2,0,1:T(2,128)S(1)}, u32[]{:S(2)}, u32[]{:S(2)}) collective-permute-start(f32[8,2,2,256]{3,2,0,1:T(2,128)S(1)} %pad_maximum_fusion.9), channel_id=1, source_target_pairs={{0,2},{1,3},{2,0},{3,1},{4,6},{5,7},{6,4},{7,5},{8,10},{9,11},{10,... | collective-permute-start | bytes 98312 | tf_op jit(solution)/shard_map/ppermute | solution.py:60
  27.5 18.0 %collective-permute-start.2 = (f32[20480]{0:T(1024)S(1)}, f32[20480]{0:T(1024)S(1)}, u32[]{:S(2)}, u32[]{:S(2)}) collective-permute-start(f32[20480]{0:T(1024)S(1)} %get-tuple-element.10), channel_id=1, source_target_pairs={{0,1},{1,2},{2,3},{3,0},{4,5},{5,6},{6,7},{7,4},{8,9},{9,10},{10,1... | collective-permute-start | bytes 245768 | tf_op jit(solution)/shard_map/ppermute | solution.py:76
  31.0 14.6 %collective-permute-start.3 = (f32[20480]{0:T(1024)S(1)}, f32[20480]{0:T(1024)S(1)}, u32[]{:S(2)}, u32[]{:S(2)}) collective-permute-start(f32[20480]{0:T(1024)S(1)} %get-tuple-element.11), channel_id=1, source_target_pairs={{1,0},{2,1},{3,2},{0,3},{5,4},{6,5},{7,6},{4,7},{9,8},{10,9},{11,1... | collective-permute-start | bytes 245768 | tf_op jit(solution)/shard_map/ppermute | solution.py:77
  32.1 11.7 %copy-start.6 = (f32[256,256]{1,0:T(8,128)S(1)}, f32[256,256]{1,0:T(8,128)}, u32[]{:S(2)}) copy-start(f32[256,256]{1,0:T(8,128)} %param.20) | copy-start | bytes 786436
  48.5 0.8 copy-start.8
  50.3 0.7 copy-start.1
  50.4 0.7 copy-start.2
  51.0 50.9 %copy-start.4 = (f32[256,256]{1,0:T(8,128)S(1)}, f32[256,256]{1,0:T(8,128)}, u32[]{:S(2)}) copy-start(f32[256,256]{1,0:T(8,128)} %param.18) | copy-start | bytes 786436
  103.6 12.5 %copy-start.7 = (f32[2,2,4,128]{3,2,1,0:T(4,128)S(1)}, f32[2,2,4,128]{3,2,1,0:T(4,128)}, u32[]{:S(2)}) copy-start(f32[2,2,4,128]{3,2,1,0:T(4,128)} %param.15) | copy-start | bytes 24580
  103.6 12.5 %copy-start.9 = (s32[2,2,4]{2,1,0:T(2,128)S(1)}, s32[2,2,4]{2,1,0:T(2,128)}, u32[]{:S(2)}) copy-start(s32[2,2,4]{2,1,0:T(2,128)} %param.16) | copy-start | bytes 196

commit v16 on v14

--- a/solution.py
+++ b/solution.py
@@ -226,11 +226,18 @@
             jnp.broadcast_to(depth_pairs[:, None, :, None] + 1.8 * unit_sphere[2], far_shape),
         ]
     ).reshape(3, parent_layers, -1)
-    far_check = point_sum(
-        jnp.broadcast_to(1.8 * unit_sphere[:, None, :], (3, parent_layers, points)),
-        source_pts,
-        far_sources.reshape(-1),
-    )
+    check_far = 1.8 * unit_sphere
+    check_square = jnp.sum(check_far * check_far, axis=0)
+    source_square, source_scaled = lax.optimization_barrier(
+        (jnp.sum(source_pts * source_pts, axis=0) + softening_sq, -2.0 * source_pts)
+    )
+    far_square = (
+        (check_square[:, None] + source_square[:, None, :])
+        + check_far[0][:, None] * source_scaled[0][:, None, :]
+        + check_far[1][:, None] * source_scaled[1][:, None, :]
+        + check_far[2][:, None] * source_scaled[2][:, None, :]
+    )
+    far_check = jnp.sum(lax.rsqrt(far_square) * far_sources.reshape(-1), axis=-1)
 
     framed = jnp.pad(cycle, ((1, 1), (1, 1), (3, 3), (0, 0)))
     shifts = far_shifts(3)

time: 111 us -> 115 us (1.036)
  other arithmetic: 33 us -> 37.1 us
    reduce_sum x0 -> x2, other arithmetic: none -> 15.6 us  [the longest x1 15.5 us: shards(): jnp.sum(lax.rsqrt(far_square) * far_sources.reshape(-1), axis=-1)]
    reduce_sum x5 -> x4, other arithmetic: 15.8 us -> 4.15 us  [point_sum(): return jnp.sum(kernel * weights[..., None, :], axis=-1)]
  transfers between devices with their start and end apart: 8 -> 8, of which waited for: 4 -> 4; matrix products, arithmetic and copies ran while one was open for 14% -> 17% of each run, Pallas kernels for 0% -> 0%
where the time goes in v16:
time: 115 us; the launch traced here: 114 us
  Pallas kernels  44.7 us (39%)
  other arithmetic  37.1 us (32%)
  starting transfers between devices  13 us (11%)
  waiting for transfers between devices  10.4 us (9%)
  local copies, waits for them, and re-layouts  7.45 us (6%)
  matrix products  1.18 us (1%)
    pallas_call x1, Pallas kernels, m2l(): pl.pallas_call(functools.partial(m2l_kernel, shift_count, 128), out_shape...  44.7 us
    reduce_sum x1, other arithmetic, shards(): jnp.sum(lax.rsqrt(far_square) * far_sources.reshape(-1), axis=-1)  15.5 us
    reduce_sum x1, other arithmetic, shards(): jnp.sum(kernel * source[3][..., None, :], axis=-1) - itself  12.5 us
    ppermute x4, waiting for transfers between devices, rel_gather(): lax.ppermute(part, axis, [(j, (j - have) % count) for j in range(count)])  8.06 us
    ppermute x4, starting transfers between devices, rel_gather(): lax.ppermute(part, axis, [(j, (j - have) % count) for j in range(count)])  5.74 us
    reduce_sum x4, other arithmetic, point_sum(): return jnp.sum(kernel * weights[..., None, :], axis=-1)  4.15 us
    ppermute x2, starting transfers between devices, exchange(): lax.ppermute(sent_head, axis, [((i + 1) % count, i) for i in range(count)])  3.9 us
    ppermute x2, starting transfers between devices, exchange(): lax.ppermute(sent_tail, axis, [(i, (i + 1) % count) for i in range(count)])  3.37 us
  transfers between devices with their start and end apart: 8, of which 4 were waited for; matrix products, arithmetic and copies ran while one was open for 17% of the time, Pallas kernels for 0%

profile of v16, /device:TPU:0, one launch (start us, length us, event | category | flops | bytes accessed | tf_op | source)
XLA Modules:
  0.0 114.5 jit_solution(11749439202604984456)
XLA Ops:
  0.0 0.1 cosine_multiply_fusion.1
  0.1 0.1 sine_multiply_fusion.1
  0.2 0.8 fusion.18
  1.0 0.8 fusion.38
  1.8 0.1 broadcast_add_fusion.11
  1.9 0.7 fusion.26
  2.7 1.1 multiply_reduce_fusion.5
  3.8 0.3 fusion.15
  4.2 0.8 add_rsqrt_fusion
  5.0 0.4 multiply_reduce_fusion.2
  5.4 0.3 fusion.30
  5.7 0.1 copy.29
  5.9 3.4 %collective-permute-start.1 = (f32[8704]{0:T(1024)S(1)}, f32[8704]{0:T(1024)S(1)}, u32[]{:S(2)}, u32[]{:S(2)}) collective-permute-start(f32[8704]{0:T(1024)S(1)} %pad_maximum_fusion.8), channel_id=1, source_target_pairs={{4,0},{8,4},{12,8},{16,12},{20,16},{24,20},{28,24},{0,28},{5,1},{9... | collective-permute-start | bytes 104456 | tf_op jit(solution)/shard_map/ppermute | solution.py:77
  9.5 0.1 subtract_multiply_fusion.2
  9.6 0.1 subtract_multiply_fusion
  9.7 0.1 fusion.5
  9.8 0.1 pad_maximum_fusion.base_ref
  9.9 0.1 subtract_multiply_fusion.3
  10.0 0.1 broadcast_add_fusion.7
  10.0 0.1 broadcast_add_fusion.3
  10.1 0.1 broadcast_add_fusion.2
  10.3 0.2 broadcast_multiply_fusion
  10.5 0.3 mul.532
  10.9 0.1 broadcast_add_fusion.1
  10.9 0.1 add.453
  11.1 0.1 broadcast_add_fusion.6
  11.2 2.3 %collective-permute-done = f32[8192]{0:T(1024)S(1)} collective-permute-done((f32[8192]{0:T(1024)S(1)}, f32[8192]{0:T(1024)S(1)}, u32[]{:S(2)}, u32[]{:S(2)}) %collective-permute-start) | collective-permute-done | bytes 32800 | tf_op jit(solution)/shard_map/ppermute | solution.py:76
  13.5 0.1 collective-permute-start.4
  13.6 3.6 %collective-permute-done.4 = f32[2,1,2,256]{3,2,0,1:T(2,128)S(1)} collective-permute-done((f32[2,1,2,256]{3,2,0,1:T(2,128)S(1)}, f32[2,1,2,256]{3,2,0,1:T(2,128)S(1)}, u32[]{:S(2)}, u32[]{:S(2)}) %collective-permute-start.4) | collective-permute-done | bytes 4128 | tf_op jit(solution)/shard_map/ppermute | solution.py:60
  17.2 0.5 collective-permute-start.5
  17.8 3.1 %collective-permute-done.5 = f32[4,1,2,256]{3,2,0,1:T(2,128)S(1)} collective-permute-done((f32[4,1,2,256]{3,2,0,1:T(2,128)S(1)}, f32[4,1,2,256]{3,2,0,1:T(2,128)S(1)}, u32[]{:S(2)}, u32[]{:S(2)}) %collective-permute-start.5) | collective-permute-done | bytes 8224 | tf_op jit(solution)/shard_map/ppermute | solution.py:60
  20.9 3.7 %collective-permute-start.6 = (f32[8,1,2,256]{3,2,0,1:T(2,128)S(1)}, f32[8,1,2,256]{3,2,0,1:T(2,128)S(1)}, u32[]{:S(2)}, u32[]{:S(2)}) collective-permute-start(f32[8,1,2,256]{3,2,0,1:T(2,128)S(1)} %pad_maximum_fusion.12), channel_id=1, source_target_pairs={{0,3},{1,0},{2,1},{3,2},{4,7},{5,4},{6,5},{7,6},{8,11},{9,8},{10,9... | collective-permute-start | bytes 49160 | tf_op jit(solution)/shard_map/ppermute | solution.py:60
  24.6 1.4 %collective-permute-done.6 = f32[8,1,2,256]{3,2,0,1:T(2,128)S(1)} collective-permute-done((f32[8,1,2,256]{3,2,0,1:T(2,128)S(1)}, f32[8,1,2,256]{3,2,0,1:T(2,128)S(1)}, u32[]{:S(2)}, u32[]{:S(2)}) %collective-permute-start.6) | collective-permute-done | bytes 16416 | tf_op jit(solution)/shard_map/ppermute | solution.py:60
  26.0 1.5 %collective-permute-start.7 = (f32[8,2,2,256]{3,2,0,1:T(2,128)S(1)}, f32[8,2,2,256]{3,2,0,1:T(2,128)S(1)}, u32[]{:S(2)}, u32[]{:S(2)}) collective-permute-start(f32[8,2,2,256]{3,2,0,1:T(2,128)S(1)} %pad_maximum_fusion.10), channel_id=1, source_target_pairs={{0,2},{1,3},{2,0},{3,1},{4,6},{5,7},{6,4},{7,5},{8,10},{9,11},{10,... | collective-permute-start | bytes 98312 | tf_op jit(solution)/shard_map/ppermute | solution.py:60
  27.5 3.4 %collective-permute-start.2 = (f32[20480]{0:T(1024)S(1)}, f32[20480]{0:T(1024)S(1)}, u32[]{:S(2)}, u32[]{:S(2)}) collective-permute-start(f32[20480]{0:T(1024)S(1)} %get-tuple-element.19), channel_id=1, source_target_pairs={{0,1},{1,2},{2,3},{3,0},{4,5},{5,6},{6,7},{7,4},{8,9},{9,10},{10,1... | collective-permute-start | bytes 245768 | tf_op jit(solution)/shard_map/ppermute | solution.py:76
  30.9 0.5 collective-permute-start.3
  31.5 0.6 gather_fusion.1
  32.1 15.5 %multiply_reduce_fusion.1 = f32[2,256]{1,0:T(2,128)S(1)} fusion(f32[11776]{0:T(1024)S(1)} %select_n.50, f32[2,11776]{1,0:T(2,128)S(1)} %get-tuple-element.13, f32[256]{0:T(256)S(1)} %bitcast.166, f32[2,11776]{1,0:T(2,128)S(1)} %get-tuple-element.14, f32[256]{0:T(256)S(1)} %bitcast.167, f32[2,11776]{1,0:T(2,128)S(1)} %get-tuple-element.12, ...), kind=kLoop, calls=%fused_computation.3 | loop fusion | flops 54263296 | bytes 430080 | tf_op jit(solution)/shard_map/reduce_sum | solution.py:240
  47.7 0.3 fusion.31
  47.9 0.1 mul.550
  48.0 1.3 %multiply_reduce_fusion.3 = f32[2,2,4,128]{3,2,1,0:T(4,128)S(1)} fusion(f32[4,256]{1,0:T(4,128)S(1)} %mul.550, f32[256]{0:T(256)S(1)} %bitcast.162, f32[2,2,4,128]{3,2,1,0:T(4,128)S(1)} %get-tuple-element.35, f32[256]{0:T(256)S(1)} %bitcast.160, f32[2,2,4,128]{3,2,1,0:T(4,128)S(1)} %get-tuple-element.28, f32[256]{0:T(256)S(1)} %bitcast.164, ...), kind=kLoop, calls=%fused_computation.5 | loop fusion | flops 5765120 | bytes 39936 | tf_op jit(solution)/shard_map/reduce_sum | solution.py:29
  49.4 0.1 copy.28
  49.6 2.3 %gather_fusion = f32[432,4,128]{2,1,0:T(4,128)S(1)} fusion(f32[4,96,128]{2,0,1:T(4,128)S(1)} %bitcast.122, s32[1024]{0:T(1024)S(1)} %get-tuple-element.58), kind=kCustom, calls=%fused_computation | custom fusion | bytes 1771200 | tf_op jit(solution)/shard_map/jit(_take)/gather | solution.py:289
  51.8 0.5 copy.41
  52.4 0.1 slice.300
  52.5 0.1 slice.256
  52.6 0.6 copy-done.8
  53.2 0.1 broadcast_add_fusion
  53.3 0.1 copy.42
  53.5 0.1 select_maximum_fusion
  53.7 0.1 fusion.11
  53.8 0.1 fusion.10
  53.9 0.1 fusion.9
  54.0 0.1 fusion.8
  54.1 0.1 fusion.7
  54.2 0.1 fusion.6
  54.3 0.3 copy.24
  54.7 0.2 copy-done.1
  54.9 0.0 copy-done.2
  54.9 44.7 %shard_map.136 = f32[16,256]{1,0:T(8,128)S(1)} custom-call(f32[632]{0:T(1024)S(1)} %copy-done.2, s32[1264]{0:T(1024)S(1)} %copy-done.1, f32[4,256,256]{2,1,0:T(8,128)S(1)} %pad_maximum_fusion.base_ref, f32[448,4,256]{2,1,0:T(4,128)S(1)} %bitcast.121), custom_call_target="tpu_custom_call" | custom-call | flops 2133065728 | bytes 2899968 | tf_op jit(solution)/shard_map/pallas_call | solution.py:147
  99.6 0.3 fusion.13
  99.9 1.3 %multiply_reduce_fusion.4 = f32[2,2,4,128]{3,2,1,0:T(4,128)S(1)} fusion(f32[2,2,4,256]{3,2,1,0:T(4,128)S(1)} %fusion.13, f32[256]{0:T(256)S(1)} %bitcast.171, f32[2,2,4,128]{3,2,1,0:T(4,128)S(1)} %get-tuple-element.32, f32[256]{0:T(256)S(1)} %bitcast.173, f32[2,2,4,128]{3,2,1,0:T(4,128)S(1)} %get-tuple-element.31, f32[256]{0:T(256)S(1)} %bitcast.169, ...), kind=kLoop, calls=%fused_computation.6 | loop fusion | flops 5765120 | bytes 52224 | tf_op jit(solution)/shard_map/reduce_sum | solution.py:29
  101.3 12.5 %multiply_reduce_fusion = f32[16,128]{1,0:T(8,128)S(1)} fusion(f32[16,3456]{1,0:T(8,128)S(1)} %bitcast.129, f32[16,3456]{1,0:T(8,128)S(1)} %get-tuple-element.10, f32[16,128]{1,0:T(8,128)S(1)} %bitcast.155, f32[16,3456]{1,0:T(8,128)S(1)} %get-tuple-element.11, f32[16,128]{1,0:T(8,128)S(1)} %bitcast.156, f32[16,3456]{1,0:T(8,128)S(1)} %get-tuple-element.9, ...), kind=kLoop, calls=%fused_computation.2 | loop fusion | flops 77854720 | bytes 917504 | tf_op jit(solution)/shard_map/reduce_sum | solution.py:302
  113.8 0.7 add_select_fusion
  (94 shorter events, 1.2 us)
Async XLA Ops:
  0.0 3.8 %copy-start = (f32[256,256]{1,0:T(8,128)S(1)}, f32[256,256]{1,0:T(8,128)}, u32[]{:S(2)}) copy-start(f32[256,256]{1,0:T(8,128)} %param.17) | copy-start | bytes 786436
  4.2 1.2 %copy-start.5 = (f32[256,256]{1,0:T(8,128)S(1)}, f32[256,256]{1,0:T(8,128)}, u32[]{:S(2)}) copy-start(f32[256,256]{1,0:T(8,128)} %param.19) | copy-start | bytes 786436
  4.2 1.6 %copy-start.3 = (f32[3,2,2,4,128]{4,3,2,1,0:T(4,128)S(1)}, f32[3,2,2,4,128]{4,3,2,1,0:T(4,128)}, u32[]{:S(2)}) copy-start(f32[3,2,2,4,128]{4,3,2,1,0:T(4,128)} %param.14) | copy-start | bytes 73732
  5.8 4.2 %copy-start.11 = (f32[23]{0:T(128)S(1)}, f32[23]{0:T(128)}, u32[]{:S(2)}) copy-start(f32[23]{0:T(128)} %constant.132) | copy-start | bytes 280
  5.8 4.3 %copy-start.12 = (f32[23]{0:T(128)S(1)}, f32[23]{0:T(128)}, u32[]{:S(2)}) copy-start(f32[23]{0:T(128)} %constant.133) | copy-start | bytes 280
  5.9 7.7 %collective-permute-start.1 = (f32[8704]{0:T(1024)S(1)}, f32[8704]{0:T(1024)S(1)}, u32[]{:S(2)}, u32[]{:S(2)}) collective-permute-start(f32[8704]{0:T(1024)S(1)} %pad_maximum_fusion.8), channel_id=1, source_target_pairs={{4,0},{8,4},{12,8},{16,12},{20,16},{24,20},{28,24},{0,28},{5,1},{9... | collective-permute-start | bytes 104456 | tf_op jit(solution)/shard_map/ppermute | solution.py:77
  9.2 4.2 %collective-permute-start = (f32[8192]{0:T(1024)S(1)}, f32[8192]{0:T(1024)S(1)}, u32[]{:S(2)}, u32[]{:S(2)}) collective-permute-start(f32[8192]{0:T(1024)S(1)} %pad_maximum_fusion.9), channel_id=1, source_target_pairs={{0,4},{4,8},{8,12},{12,16},{16,20},{20,24},{24,28},{28,0},{1,5},{5... | collective-permute-start | bytes 98312 | tf_op jit(solution)/shard_map/ppermute | solution.py:76
  9.8 1.4 %copy-start.10 = (s32[432]{0:T(512)S(1)}, s32[432]{0:T(512)}, u32[]{:S(2)}) copy-start(s32[432]{0:T(512)} %constant.143) | copy-start | bytes 5188
  9.8 1.3 %copy-start.13 = (s32[23]{0:T(128)S(1)}, s32[23]{0:T(128)}, u32[]{:S(2)}) copy-start(s32[23]{0:T(128)} %constant.144) | copy-start | bytes 280
  13.5 3.7 %collective-permute-start.4 = (f32[2,1,2,256]{3,2,0,1:T(2,128)S(1)}, f32[2,1,2,256]{3,2,0,1:T(2,128)S(1)}, u32[]{:S(2)}, u32[]{:S(2)}) collective-permute-start(f32[2,1,2,256]{3,2,0,1:T(2,128)S(1)} %maximum_bitcast_fusion), channel_id=1, source_target_pairs={{0,24},{4,28},{8,0},{12,4},{16,8},{20,12},{24,16},{28,20},{1,25},{... | collective-permute-start | bytes 12296 | tf_op jit(solution)/shard_map/ppermute | solution.py:60
  17.2 3.7 %collective-permute-start.5 = (f32[4,1,2,256]{3,2,0,1:T(2,128)S(1)}, f32[4,1,2,256]{3,2,0,1:T(2,128)S(1)}, u32[]{:S(2)}, u32[]{:S(2)}) collective-permute-start(f32[4,1,2,256]{3,2,0,1:T(2,128)S(1)} %pad_maximum_fusion.13), channel_id=1, source_target_pairs={{0,16},{4,20},{8,24},{12,28},{16,0},{20,4},{24,8},{28,12},{1,17},{... | collective-permute-start | bytes 24584 | tf_op jit(solution)/shard_map/ppermute | solution.py:60
  20.9 5.1 %collective-permute-start.6 = (f32[8,1,2,256]{3,2,0,1:T(2,128)S(1)}, f32[8,1,2,256]{3,2,0,1:T(2,128)S(1)}, u32[]{:S(2)}, u32[]{:S(2)}) collective-permute-start(f32[8,1,2,256]{3,2,0,1:T(2,128)S(1)} %pad_maximum_fusion.12), channel_id=1, source_target_pairs={{0,3},{1,0},{2,1},{3,2},{4,7},{5,4},{6,5},{7,6},{8,11},{9,8},{10,9... | collective-permute-start | bytes 49160 | tf_op jit(solution)/shard_map/ppermute | solution.py:60
  26.0 5.4 %collective-permute-start.7 = (f32[8,2,2,256]{3,2,0,1:T(2,128)S(1)}, f32[8,2,2,256]{3,2,0,1:T(2,128)S(1)}, u32[]{:S(2)}, u32[]{:S(2)}) collective-permute-start(f32[8,2,2,256]{3,2,0,1:T(2,128)S(1)} %pad_maximum_fusion.10), channel_id=1, source_target_pairs={{0,2},{1,3},{2,0},{3,1},{4,6},{5,7},{6,4},{7,5},{8,10},{9,11},{10,... | collective-permute-start | bytes 98312 | tf_op jit(solution)/shard_map/ppermute | solution.py:60
  27.5 21.8 %collective-permute-start.2 = (f32[20480]{0:T(1024)S(1)}, f32[20480]{0:T(1024)S(1)}, u32[]{:S(2)}, u32[]{:S(2)}) collective-permute-start(f32[20480]{0:T(1024)S(1)} %get-tuple-element.19), channel_id=1, source_target_pairs={{0,1},{1,2},{2,3},{3,0},{4,5},{5,6},{6,7},{7,4},{8,9},{9,10},{10,1... | collective-permute-start | bytes 245768 | tf_op jit(solution)/shard_map/ppermute | solution.py:76
  30.9 18.5 %collective-permute-start.3 = (f32[20480]{0:T(1024)S(1)}, f32[20480]{0:T(1024)S(1)}, u32[]{:S(2)}, u32[]{:S(2)}) collective-permute-start(f32[20480]{0:T(1024)S(1)} %get-tuple-element.20), channel_id=1, source_target_pairs={{1,0},{2,1},{3,2},{0,3},{5,4},{6,5},{7,6},{4,7},{9,8},{10,9},{11,1... | collective-permute-start | bytes 245768 | tf_op jit(solution)/shard_map/ppermute | solution.py:77
  32.1 15.5 %copy-start.6 = (f32[256,256]{1,0:T(8,128)S(1)}, f32[256,256]{1,0:T(8,128)}, u32[]{:S(2)}) copy-start(f32[256,256]{1,0:T(8,128)} %param.20) | copy-start | bytes 786436
  52.4 0.8 copy-start.8
  54.2 0.7 copy-start.1
  54.2 0.7 copy-start.2
  54.9 44.7 %copy-start.4 = (f32[256,256]{1,0:T(8,128)S(1)}, f32[256,256]{1,0:T(8,128)}, u32[]{:S(2)}) copy-start(f32[256,256]{1,0:T(8,128)} %param.18) | copy-start | bytes 786436
  101.3 12.5 %copy-start.7 = (f32[2,2,4,128]{3,2,1,0:T(4,128)S(1)}, f32[2,2,4,128]{3,2,1,0:T(4,128)}, u32[]{:S(2)}) copy-start(f32[2,2,4,128]{3,2,1,0:T(4,128)} %param.15) | copy-start | bytes 24580
  101.3 12.5 %copy-start.9 = (s32[2,2,4]{2,1,0:T(2,128)S(1)}, s32[2,2,4]{2,1,0:T(2,128)}, u32[]{:S(2)}) copy-start(s32[2,2,4]{2,1,0:T(2,128)} %param.16) | copy-start | bytes 196

commit v17 on v14

--- a/solution.py
+++ b/solution.py
@@ -92,8 +92,9 @@
     return scaled - (scaled - values)
 
 
-def m2l_kernel(shift_count, rows, table_ref, index_ref, base_ref, windows_ref, out_ref):
+def m2l_kernel(shift_count, rows, table_ref, index_ref, base_ref, windows_ref, out_ref, turned_ref):
     out_ref[...] = jnp.zeros_like(out_ref)
+    turned_ref[...] = jnp.zeros_like(turned_ref)
     vectors = out_ref.shape[0]
     pieces = index_ref.shape[0] // (2 * shift_count)
 
@@ -130,15 +131,21 @@
             matrix_top = split_top(matrix)
             matrix_high = matrix_top.astype(jnp.bfloat16)
             matrix_low = (matrix - matrix_top).astype(jnp.bfloat16)
-            out_ref[:, row : row + rows] += split_dot(
-                fwd, matrix_high, matrix_low, (((1,), (1,)), ((), ()))
-            )
+            both = lax.dot_general(
+                matrix_high, fwd, (((1,), (1,)), ((), ())), preferred_element_type=jnp.float32
+            )
+            cross = lax.dot_general(
+                matrix_low, fwd[:vectors], (((1,), (1,)), ((), ())),
+                preferred_element_type=jnp.float32,
+            )
+            turned_ref[row : row + rows, :] += both[:, :vectors] + both[:, vectors:] + cross
             out_ref[...] += split_dot(
                 back[:, row : row + rows], matrix_high, matrix_low, (((1,), (0,)), ((), ()))
             )
         return carry
 
     lax.fori_loop(0, shift_count, body, 0)
+    out_ref[...] += turned_ref[...].T
 
 
 def m2l(table, window_index, base, windows, vectors):
@@ -154,6 +161,7 @@
             pl.BlockSpec(memory_space=pltpu.VMEM),
         ],
         out_specs=pl.BlockSpec(memory_space=pltpu.VMEM),
+        scratch_shapes=[pltpu.VMEM((points, vectors), jnp.float32)],
         compiler_params=pltpu.CompilerParams(vmem_limit_bytes=48 * 1024 * 1024),
         cost_estimate=pl.CostEstimate(
             flops=12 * shift_count * vectors * points * points + 14 * shift_count * points * points,

time: 111 us -> 118 us (1.063)
  Pallas kernels: 44.7 us -> 51.3 us
    pallas_call x1, Pallas kernels: 44.7 us -> 51.3 us  [m2l(): pl.pallas_call(functools.partial(m2l_kernel, shift_count, 128), out_shape...]
  transfers between devices with their start and end apart: 8 -> 8, of which waited for: 4 -> 4; matrix products, arithmetic and copies ran while one was open for 14% -> 13% of each run, Pallas kernels for 0% -> 0%
where the time goes in v17:
time: 118 us; the launch traced here: 117 us
  Pallas kernels  51.3 us (43%)
  other arithmetic  33 us (28%)
  starting transfers between devices  13 us (11%)
  waiting for transfers between devices  10.8 us (9%)
  local copies, waits for them, and re-layouts  7.15 us (6%)
  matrix products  1.18 us (1%)
    pallas_call x1, Pallas kernels, m2l(): pl.pallas_call(functools.partial(m2l_kernel, shift_count, 128), out_shape...  51.3 us
    reduce_sum x5, other arithmetic, point_sum(): return jnp.sum(kernel * weights[..., None, :], axis=-1)  15.8 us
    reduce_sum x1, other arithmetic, shards(): jnp.sum(kernel * source[3][..., None, :], axis=-1) - itself  12.5 us
    ppermute x4, waiting for transfers between devices, rel_gather(): lax.ppermute(part, axis, [(j, (j - have) % count) for j in range(count)])  8.06 us
    ppermute x4, starting transfers between devices, rel_gather(): lax.ppermute(part, axis, [(j, (j - have) % count) for j in range(count)])  5.76 us
    ppermute x2, starting transfers between devices, exchange(): lax.ppermute(sent_head, axis, [((i + 1) % count, i) for i in range(count)])  3.84 us
    ppermute x2, starting transfers between devices, exchange(): lax.ppermute(sent_tail, axis, [(i, (i + 1) % count) for i in range(count)])  3.43 us
    gather x2, local copies, waits for them, and re-layouts, shards(): jnp.take(padded_around.reshape(4, -1, slot_count), box_rows, axis=1)  2.79 us
  transfers between devices with their start and end apart: 8, of which 4 were waited for; matrix products, arithmetic and copies ran while one was open for 13% of the time, Pallas kernels for 0%

profile of v17, /device:TPU:0, one launch (start us, length us, event | category | flops | bytes accessed | tf_op | source)
XLA Modules:
  0.0 117.3 jit_solution(16132378831331346198)
XLA Ops:
  0.0 0.1 cosine_multiply_fusion.1
  0.1 0.1 sine_multiply_fusion.1
  0.2 0.8 fusion.18
  1.0 0.8 fusion.40
  1.8 0.7 fusion.28
  2.5 1.1 multiply_reduce_fusion.5
  3.6 0.3 fusion.15
  4.0 0.1 broadcast_add_fusion.9
  4.2 0.8 add_rsqrt_fusion
  5.0 0.4 multiply_reduce_fusion.2
  5.4 0.3 fusion.32
  5.7 0.1 copy.29
  5.8 0.0 copy-start.11
  5.9 3.4 %collective-permute-start.1 = (f32[8704]{0:T(1024)S(1)}, f32[8704]{0:T(1024)S(1)}, u32[]{:S(2)}, u32[]{:S(2)}) collective-permute-start(f32[8704]{0:T(1024)S(1)} %pad_maximum_fusion.7), channel_id=1, source_target_pairs={{4,0},{8,4},{12,8},{16,12},{20,16},{24,20},{28,24},{0,28},{5,1},{9... | collective-permute-start | bytes 104456 | tf_op jit(solution)/shard_map/ppermute | solution.py:77
  9.3 0.1 fusion.22
  9.4 0.1 fusion.24
  9.6 0.1 subtract_multiply_fusion.2
  9.7 0.1 subtract_multiply_fusion
  9.8 0.1 fusion.5
  9.9 0.1 pad_maximum_fusion.base_ref
  10.0 0.1 subtract_multiply_fusion.3
  10.1 0.1 broadcast_add_fusion.5
  10.2 0.1 broadcast_add_fusion.6
  10.2 0.1 broadcast_add_fusion.2
  10.3 0.1 broadcast_add_fusion.1
  10.4 0.1 stack_broadcast_in_dim.44
  10.7 2.8 %collective-permute-done = f32[8192]{0:T(1024)S(1)} collective-permute-done((f32[8192]{0:T(1024)S(1)}, f32[8192]{0:T(1024)S(1)}, u32[]{:S(2)}, u32[]{:S(2)}) %collective-permute-start) | collective-permute-done | bytes 32800 | tf_op jit(solution)/shard_map/ppermute | solution.py:76
  13.5 0.1 collective-permute-start.4
  13.7 3.6 %collective-permute-done.4 = f32[2,1,2,256]{3,2,0,1:T(2,128)S(1)} collective-permute-done((f32[2,1,2,256]{3,2,0,1:T(2,128)S(1)}, f32[2,1,2,256]{3,2,0,1:T(2,128)S(1)}, u32[]{:S(2)}, u32[]{:S(2)}) %collective-permute-start.4) | collective-permute-done | bytes 4128 | tf_op jit(solution)/shard_map/ppermute | solution.py:60
  17.2 0.5 collective-permute-start.5
  17.8 3.1 %collective-permute-done.5 = f32[4,1,2,256]{3,2,0,1:T(2,128)S(1)} collective-permute-done((f32[4,1,2,256]{3,2,0,1:T(2,128)S(1)}, f32[4,1,2,256]{3,2,0,1:T(2,128)S(1)}, u32[]{:S(2)}, u32[]{:S(2)}) %collective-permute-start.5) | collective-permute-done | bytes 8224 | tf_op jit(solution)/shard_map/ppermute | solution.py:60
  20.9 3.7 %collective-permute-start.6 = (f32[8,1,2,256]{3,2,0,1:T(2,128)S(1)}, f32[8,1,2,256]{3,2,0,1:T(2,128)S(1)}, u32[]{:S(2)}, u32[]{:S(2)}) collective-permute-start(f32[8,1,2,256]{3,2,0,1:T(2,128)S(1)} %pad_maximum_fusion.11), channel_id=1, source_target_pairs={{0,3},{1,0},{2,1},{3,2},{4,7},{5,4},{6,5},{7,6},{8,11},{9,8},{10,9... | collective-permute-start | bytes 49160 | tf_op jit(solution)/shard_map/ppermute | solution.py:60
  24.6 1.4 %collective-permute-done.6 = f32[8,1,2,256]{3,2,0,1:T(2,128)S(1)} collective-permute-done((f32[8,1,2,256]{3,2,0,1:T(2,128)S(1)}, f32[8,1,2,256]{3,2,0,1:T(2,128)S(1)}, u32[]{:S(2)}, u32[]{:S(2)}) %collective-permute-start.6) | collective-permute-done | bytes 16416 | tf_op jit(solution)/shard_map/ppermute | solution.py:60
  26.0 1.5 %collective-permute-start.7 = (f32[8,2,2,256]{3,2,0,1:T(2,128)S(1)}, f32[8,2,2,256]{3,2,0,1:T(2,128)S(1)}, u32[]{:S(2)}, u32[]{:S(2)}) collective-permute-start(f32[8,2,2,256]{3,2,0,1:T(2,128)S(1)} %pad_maximum_fusion.9), channel_id=1, source_target_pairs={{0,2},{1,3},{2,0},{3,1},{4,6},{5,7},{6,4},{7,5},{8,10},{9,11},{10,... | collective-permute-start | bytes 98312 | tf_op jit(solution)/shard_map/ppermute | solution.py:60
  27.5 3.4 %collective-permute-start.2 = (f32[20480]{0:T(1024)S(1)}, f32[20480]{0:T(1024)S(1)}, u32[]{:S(2)}, u32[]{:S(2)}) collective-permute-start(f32[20480]{0:T(1024)S(1)} %get-tuple-element.10), channel_id=1, source_target_pairs={{0,1},{1,2},{2,3},{3,0},{4,5},{5,6},{6,7},{7,4},{8,9},{9,10},{10,1... | collective-permute-start | bytes 245768 | tf_op jit(solution)/shard_map/ppermute | solution.py:76
  31.0 0.5 collective-permute-start.3
  31.5 0.6 gather_fusion.1
  32.1 11.7 %multiply_reduce_fusion.1 = f32[2,256]{1,0:T(2,128)S(1)} fusion(f32[11776]{0:T(1024)S(1)} %select_n.50, f32[2,11776]{1,0:T(2,128)S(1)} %stack_broadcast_in_dim.44, f32[256]{0:T(256)S(1)} %bitcast.176, f32[11776]{0:T(1024)S(1)} %stack_broadcast_in_dim.42, f32[256]{0:T(256)S(1)} %bitcast.177, f32[11776]{0:T(1024)S(1)} %stack_broadcast_in_dim.40, ...), kind=kLoop, calls=%fused_computation.3 | loop fusion | flops 66321920 | bytes 240640 | tf_op jit(solution)/shard_map/reduce_sum | solution.py:29
  43.8 0.3 fusion.33
  44.1 0.1 mul.538
  44.2 1.3 %multiply_reduce_fusion.3 = f32[2,2,4,128]{3,2,1,0:T(4,128)S(1)} fusion(f32[4,256]{1,0:T(4,128)S(1)} %mul.538, f32[256]{0:T(256)S(1)} %bitcast.166, f32[2,2,4,128]{3,2,1,0:T(4,128)S(1)} %get-tuple-element.26, f32[256]{0:T(256)S(1)} %bitcast.168, f32[2,2,4,128]{3,2,1,0:T(4,128)S(1)} %get-tuple-element.19, f32[256]{0:T(256)S(1)} %bitcast.164, ...), kind=kLoop, calls=%fused_computation.5 | loop fusion | flops 5765120 | bytes 39936 | tf_op jit(solution)/shard_map/reduce_sum | solution.py:29
  45.6 0.1 copy.28
  45.7 2.3 %gather_fusion = f32[432,4,128]{2,1,0:T(4,128)S(1)} fusion(f32[4,96,128]{2,0,1:T(4,128)S(1)} %bitcast.126, s32[1024]{0:T(1024)S(1)} %get-tuple-element.49), kind=kCustom, calls=%fused_computation | custom fusion | bytes 1771200 | tf_op jit(solution)/shard_map/jit(_take)/gather | solution.py:290
  48.0 0.5 copy.45
  48.5 0.1 slice.300
  48.6 0.1 slice.259
  48.7 0.6 copy-done.8
  49.3 0.1 broadcast_add_fusion
  49.5 0.1 copy.46
  49.7 0.1 select_maximum_fusion
  49.9 0.1 fusion.11
  50.0 0.1 fusion.10
  50.1 0.1 fusion.9
  50.2 0.1 fusion.8
  50.2 0.1 fusion.7
  50.4 0.1 fusion.6
  50.5 0.3 copy.24
  50.8 0.2 copy-done.1
  51.0 0.0 copy-done.2
  51.0 51.3 %shard_map.136 = f32[16,256]{1,0:T(8,128)S(1)} custom-call(f32[632]{0:T(1024)S(1)} %copy-done.2, s32[1264]{0:T(1024)S(1)} %copy-done.1, f32[4,256,256]{2,1,0:T(8,128)S(1)} %pad_maximum_fusion.base_ref, f32[448,4,256]{2,1,0:T(4,128)S(1)} %bitcast.125), custom_call_target="tpu_custom_call" | custom-call | flops 2133065728 | bytes 2899968 | tf_op jit(solution)/shard_map/pallas_call | solution.py:154
  102.4 0.3 fusion.13
  102.7 1.3 %multiply_reduce_fusion.4 = f32[2,2,4,128]{3,2,1,0:T(4,128)S(1)} fusion(f32[2,2,4,256]{3,2,1,0:T(4,128)S(1)} %fusion.13, f32[256]{0:T(256)S(1)} %bitcast.172, f32[2,2,4,128]{3,2,1,0:T(4,128)S(1)} %get-tuple-element.23, f32[256]{0:T(256)S(1)} %bitcast.170, f32[2,2,4,128]{3,2,1,0:T(4,128)S(1)} %get-tuple-element.22, f32[256]{0:T(256)S(1)} %bitcast.174, ...), kind=kLoop, calls=%fused_computation.6 | loop fusion | flops 5765120 | bytes 52224 | tf_op jit(solution)/shard_map/reduce_sum | solution.py:29
  104.1 12.5 %multiply_reduce_fusion = f32[16,128]{1,0:T(8,128)S(1)} fusion(f32[16,3456]{1,0:T(8,128)S(1)} %bitcast.133, f32[16,3456]{1,0:T(8,128)S(1)} %get-tuple-element.6, f32[16,128]{1,0:T(8,128)S(1)} %bitcast.159, f32[16,3456]{1,0:T(8,128)S(1)} %get-tuple-element.7, f32[16,128]{1,0:T(8,128)S(1)} %bitcast.160, f32[16,3456]{1,0:T(8,128)S(1)} %get-tuple-element.5, ...), kind=kLoop, calls=%fused_computation.2 | loop fusion | flops 77854720 | bytes 917504 | tf_op jit(solution)/shard_map/reduce_sum | solution.py:303
  116.6 0.7 add_select_fusion
  (95 shorter events, 1.2 us)
Async XLA Ops:
  0.0 3.6 %copy-start = (f32[256,256]{1,0:T(8,128)S(1)}, f32[256,256]{1,0:T(8,128)}, u32[]{:S(2)}) copy-start(f32[256,256]{1,0:T(8,128)} %param.17) | copy-start | bytes 786436
  4.2 1.2 %copy-start.5 = (f32[256,256]{1,0:T(8,128)S(1)}, f32[256,256]{1,0:T(8,128)}, u32[]{:S(2)}) copy-start(f32[256,256]{1,0:T(8,128)} %param.19) | copy-start | bytes 786436
  4.2 1.6 %copy-start.3 = (f32[3,2,2,4,128]{4,3,2,1,0:T(4,128)S(1)}, f32[3,2,2,4,128]{4,3,2,1,0:T(4,128)}, u32[]{:S(2)}) copy-start(f32[3,2,2,4,128]{4,3,2,1,0:T(4,128)} %param.14) | copy-start | bytes 73732
  5.8 4.5 %copy-start.11 = (f32[23]{0:T(128)S(1)}, f32[23]{0:T(128)}, u32[]{:S(2)}) copy-start(f32[23]{0:T(128)} %constant.131) | copy-start | bytes 280
  5.8 4.5 %copy-start.12 = (f32[23]{0:T(128)S(1)}, f32[23]{0:T(128)}, u32[]{:S(2)}) copy-start(f32[23]{0:T(128)} %constant.132) | copy-start | bytes 280
  5.8 4.6 %copy-start.10 = (s32[432]{0:T(512)S(1)}, s32[432]{0:T(512)}, u32[]{:S(2)}) copy-start(s32[432]{0:T(512)} %constant.142) | copy-start | bytes 5188
  5.8 4.5 %copy-start.13 = (s32[23]{0:T(128)S(1)}, s32[23]{0:T(128)}, u32[]{:S(2)}) copy-start(s32[23]{0:T(128)} %constant.143) | copy-start | bytes 280
  5.9 7.7 %collective-permute-start.1 = (f32[8704]{0:T(1024)S(1)}, f32[8704]{0:T(1024)S(1)}, u32[]{:S(2)}, u32[]{:S(2)}) collective-permute-start(f32[8704]{0:T(1024)S(1)} %pad_maximum_fusion.7), channel_id=1, source_target_pairs={{4,0},{8,4},{12,8},{16,12},{20,16},{24,20},{28,24},{0,28},{5,1},{9... | collective-permute-start | bytes 104456 | tf_op jit(solution)/shard_map/ppermute | solution.py:77
  9.2 4.2 %collective-permute-start = (f32[8192]{0:T(1024)S(1)}, f32[8192]{0:T(1024)S(1)}, u32[]{:S(2)}, u32[]{:S(2)}) collective-permute-start(f32[8192]{0:T(1024)S(1)} %pad_maximum_fusion.8), channel_id=1, source_target_pairs={{0,4},{4,8},{8,12},{12,16},{16,20},{20,24},{24,28},{28,0},{1,5},{5... | collective-permute-start | bytes 98312 | tf_op jit(solution)/shard_map/ppermute | solution.py:76
  13.5 3.7 %collective-permute-start.4 = (f32[2,1,2,256]{3,2,0,1:T(2,128)S(1)}, f32[2,1,2,256]{3,2,0,1:T(2,128)S(1)}, u32[]{:S(2)}, u32[]{:S(2)}) collective-permute-start(f32[2,1,2,256]{3,2,0,1:T(2,128)S(1)} %maximum_bitcast_fusion), channel_id=1, source_target_pairs={{0,24},{4,28},{8,0},{12,4},{16,8},{20,12},{24,16},{28,20},{1,25},{... | collective-permute-start | bytes 12296 | tf_op jit(solution)/shard_map/ppermute | solution.py:60
  17.2 3.7 %collective-permute-start.5 = (f32[4,1,2,256]{3,2,0,1:T(2,128)S(1)}, f32[4,1,2,256]{3,2,0,1:T(2,128)S(1)}, u32[]{:S(2)}, u32[]{:S(2)}) collective-permute-start(f32[4,1,2,256]{3,2,0,1:T(2,128)S(1)} %pad_maximum_fusion.12), channel_id=1, source_target_pairs={{0,16},{4,20},{8,24},{12,28},{16,0},{20,4},{24,8},{28,12},{1,17},{... | collective-permute-start | bytes 24584 | tf_op jit(solution)/shard_map/ppermute | solution.py:60
  20.9 5.1 %collective-permute-start.6 = (f32[8,1,2,256]{3,2,0,1:T(2,128)S(1)}, f32[8,1,2,256]{3,2,0,1:T(2,128)S(1)}, u32[]{:S(2)}, u32[]{:S(2)}) collective-permute-start(f32[8,1,2,256]{3,2,0,1:T(2,128)S(1)} %pad_maximum_fusion.11), channel_id=1, source_target_pairs={{0,3},{1,0},{2,1},{3,2},{4,7},{5,4},{6,5},{7,6},{8,11},{9,8},{10,9... | collective-permute-start | bytes 49160 | tf_op jit(solution)/shard_map/ppermute | solution.py:60
  26.0 5.4 %collective-permute-start.7 = (f32[8,2,2,256]{3,2,0,1:T(2,128)S(1)}, f32[8,2,2,256]{3,2,0,1:T(2,128)S(1)}, u32[]{:S(2)}, u32[]{:S(2)}) collective-permute-start(f32[8,2,2,256]{3,2,0,1:T(2,128)S(1)} %pad_maximum_fusion.9), channel_id=1, source_target_pairs={{0,2},{1,3},{2,0},{3,1},{4,6},{5,7},{6,4},{7,5},{8,10},{9,11},{10,... | collective-permute-start | bytes 98312 | tf_op jit(solution)/shard_map/ppermute | solution.py:60
  27.5 18.0 %collective-permute-start.2 = (f32[20480]{0:T(1024)S(1)}, f32[20480]{0:T(1024)S(1)}, u32[]{:S(2)}, u32[]{:S(2)}) collective-permute-start(f32[20480]{0:T(1024)S(1)} %get-tuple-element.10), channel_id=1, source_target_pairs={{0,1},{1,2},{2,3},{3,0},{4,5},{5,6},{6,7},{7,4},{8,9},{9,10},{10,1... | collective-permute-start | bytes 245768 | tf_op jit(solution)/shard_map/ppermute | solution.py:76
  31.0 14.6 %collective-permute-start.3 = (f32[20480]{0:T(1024)S(1)}, f32[20480]{0:T(1024)S(1)}, u32[]{:S(2)}, u32[]{:S(2)}) collective-permute-start(f32[20480]{0:T(1024)S(1)} %get-tuple-element.11), channel_id=1, source_target_pairs={{1,0},{2,1},{3,2},{0,3},{5,4},{6,5},{7,6},{4,7},{9,8},{10,9},{11,1... | collective-permute-start | bytes 245768 | tf_op jit(solution)/shard_map/ppermute | solution.py:77
  32.1 11.7 %copy-start.6 = (f32[256,256]{1,0:T(8,128)S(1)}, f32[256,256]{1,0:T(8,128)}, u32[]{:S(2)}) copy-start(f32[256,256]{1,0:T(8,128)} %param.20) | copy-start | bytes 786436
  48.5 0.8 copy-start.8
  50.3 0.7 copy-start.1
  50.4 0.7 copy-start.2
  51.0 51.3 %copy-start.4 = (f32[256,256]{1,0:T(8,128)S(1)}, f32[256,256]{1,0:T(8,128)}, u32[]{:S(2)}) copy-start(f32[256,256]{1,0:T(8,128)} %param.18) | copy-start | bytes 786436
  104.1 12.5 %copy-start.7 = (f32[2,2,4,128]{3,2,1,0:T(4,128)S(1)}, f32[2,2,4,128]{3,2,1,0:T(4,128)}, u32[]{:S(2)}) copy-start(f32[2,2,4,128]{3,2,1,0:T(4,128)} %param.15) | copy-start | bytes 24580
  104.1 12.5 %copy-start.9 = (s32[2,2,4]{2,1,0:T(2,128)S(1)}, s32[2,2,4]{2,1,0:T(2,128)}, u32[]{:S(2)}) copy-start(s32[2,2,4]{2,1,0:T(2,128)} %param.16) | copy-start | bytes 196

commit v18 on v13

--- a/solution.py
+++ b/solution.py
@@ -266,34 +266,61 @@
 
     padded_around = jnp.pad(beside_all, ((0, 0), (0, 0), (0, 0), (1, 1), (0, 0)))
     around_shape = padded_around.shape[1:4]
-    moves = [(mx, my, mz) for mx in (-1, 0, 1) for my in (-1, 0, 1) for mz in (-1, 0, 1)]
-    box_rows = np.array(
-        [
+    targets = [(bx, by, bz) for bx in range(2) for by in range(2) for bz in range(layers)]
+
+    def neighbour_moves(bz):
+        return [
+            (mx, my, mz)
+            for mx in (-1, 0, 1)
+            for my in (-1, 0, 1)
+            for mz in (-1, 0, 1)
+            if 0 <= bz + mz < layers
+        ]
+
+    groups = {}
+    for index, (bx, by, bz) in enumerate(targets):
+        groups.setdefault(len(neighbour_moves(bz)), []).append(index)
+    own = packed.reshape(4, 4 * layers, slot_count)
+    around_rows = padded_around.reshape(4, -1, slot_count)
+    self_term = lax.rsqrt(jnp.full((), softening_sq, jnp.float32))
+    near_parts, order = [], []
+    for members in groups.values():
+        rows = np.array(
             [
-                np.ravel_multi_index((bx + 1 + mx, by + 1 + my, bz + 1 + mz), around_shape)
-                for bx in range(2)
-                for by in range(2)
-                for bz in range(layers)
-            ]
-            for mx, my, mz in moves
-        ],
-        np.int32,
-    )
-    source = jnp.take(
-        padded_around.reshape(4, -1, slot_count), box_rows, axis=1
-    ).reshape(4, len(moves), 2, 2, layers, slot_count)
-    source = source.reshape(4, len(moves), 4 * layers, slot_count).transpose(0, 2, 1, 3)
-    source = source.reshape(4, 4 * layers, len(moves) * slot_count)
-    move = np.repeat(np.array(moves, np.float32), slot_count, axis=0)
-    own = packed.reshape(4, 4 * layers, slot_count)
-    delta_x = own[0][..., :, None] - source[0][..., None, :] - move[:, 0]
-    delta_y = own[1][..., :, None] - source[1][..., None, :] - move[:, 1]
-    delta_z = own[2][..., :, None] - source[2][..., None, :] - move[:, 2]
-    kernel = lax.rsqrt(delta_x * delta_x + delta_y * delta_y + delta_z * delta_z + softening_sq)
-    itself = lax.rsqrt(jnp.full((), softening_sq, jnp.float32)) * own[3]
-    near = (jnp.sum(kernel * source[3][..., None, :], axis=-1) - itself).reshape(
-        2, 2, layers, slot_count
-    )
+                [
+                    np.ravel_multi_index(
+                        (targets[t][0] + 1 + mx, targets[t][1] + 1 + my, targets[t][2] + 1 + mz),
+                        around_shape,
+                    )
+                    for mx, my, mz in neighbour_moves(targets[t][2])
+                ]
+                for t in members
+            ],
+            np.int32,
+        )
+        move = np.stack(
+            [
+                np.repeat(np.array(neighbour_moves(targets[t][2]), np.float32), slot_count, axis=0).T
+                for t in members
+            ],
+            axis=1,
+        )
+        source = jnp.take(around_rows, rows.reshape(-1), axis=1).reshape(4, len(members), -1)
+        mine = own[:, np.array(members)]
+        placed = lax.optimization_barrier(source[:3] + move)
+        delta_x = mine[0][..., :, None] - placed[0][..., None, :]
+        delta_y = mine[1][..., :, None] - placed[1][..., None, :]
+        delta_z = mine[2][..., :, None] - placed[2][..., None, :]
+        kernel = lax.rsqrt(
+            delta_x * delta_x + delta_y * delta_y + delta_z * delta_z + softening_sq
+        )
+        near_parts.append(
+            jnp.sum(kernel * source[3][..., None, :], axis=-1) - self_term * mine[3]
+        )
+        order += members
+    near = jnp.take(
+        jnp.concatenate(near_parts, axis=0), np.argsort(np.array(order)), axis=0
+    ).reshape(2, 2, layers, slot_count)
 
     leaf_down_pts = 0.5 + 1.8 * unit_sphere
     leaf_far = point_sum(offsets, leaf_down_pts[:, None, None, None, :], leaf_local)

time: 115 us -> 108 us (0.939)
  other arithmetic: 37.5 us -> 31.6 us
  waiting for transfers between devices: 10.8 us -> 9.47 us
    reduce_sum x1 -> x2, other arithmetic: 17 us -> 11 us  [shards(): jnp.sum(kernel * source[3][..., None, :], axis=-1) - self_term * mine[3]]
    ppermute x2, waiting for transfers between devices: 2.78 us -> 1.4 us  [exchange(): lax.ppermute(sent_tail, axis, [(i, (i + 1) % count) for i in range(count)])]
    gather x2 -> x8, local copies, waits for them, and re-layouts: 2.79 us -> 3.47 us  [the longest x4 1.75 us: shards(): jnp.take(around_rows, rows.reshape(-1), axis=1).reshape(4, len(members), -1)]
  transfers between devices with their start and end apart: 8 -> 8, of which waited for: 4 -> 4; matrix products, arithmetic and copies ran while one was open for 13% -> 15% of each run, Pallas kernels for 0% -> 0%
where the time goes in v18:
time: 108 us
  Pallas kernels  44.7 us (41%)
  other arithmetic  31.6 us (29%)
  starting transfers between devices  12.9 us (12%)
  waiting for transfers between devices  9.47 us (9%)
  local copies, waits for them, and re-layouts  7.11 us (7%)
  matrix products  1.18 us (1%)
    pallas_call x1, Pallas kernels, m2l(): pl.pallas_call(functools.partial(m2l_kernel, shift_count, 128), out_shape...  44.7 us
    reduce_sum x5, other arithmetic, point_sum(): return jnp.sum(kernel * weights[..., None, :], axis=-1)  15.8 us
    reduce_sum x2, other arithmetic, shards(): jnp.sum(kernel * source[3][..., None, :], axis=-1) - self_term * mine[3]  11 us
    ppermute x4, waiting for transfers between devices, rel_gather(): lax.ppermute(part, axis, [(j, (j - have) % count) for j in range(count)])  8.06 us
    ppermute x4, starting transfers between devices, rel_gather(): lax.ppermute(part, axis, [(j, (j - have) % count) for j in range(count)])  5.57 us
    ppermute x2, starting transfers between devices, exchange(): lax.ppermute(sent_head, axis, [((i + 1) % count, i) for i in range(count)])  3.67 us
    ppermute x2, starting transfers between devices, exchange(): lax.ppermute(sent_tail, axis, [(i, (i + 1) % count) for i in range(count)])  3.65 us
  transfers between devices with their start and end apart: 8, of which 4 were waited for; matrix products, arithmetic and copies ran while one was open for 15% of the time, Pallas kernels for 0%

profile of v18, /device:TPU:0, one launch (start us, length us, event | category | flops | bytes accessed | tf_op | source)
XLA Modules:
  0.0 107.8 jit_solution(3956847593679376284)
XLA Ops:
  0.0 0.1 cosine_multiply_fusion.1
  0.1 0.1 sine_multiply_fusion.1
  0.2 0.8 fusion.18
  1.0 0.8 fusion.41
  1.8 0.7 slice_bitcast_fusion.15
  2.5 1.1 %multiply_reduce_fusion.6 = f32[2,2,4,256]{3,2,1,0:T(4,128)S(1)} fusion(f32[2,2,4,128]{3,2,1,0:T(4,128)S(1)} %fusion.18, f32[2,2,4,128]{3,2,1,0:T(4,128)S(1)} %get-tuple-element.25, f32[256]{0:T(256)S(1)} %bitcast.202, f32[2,2,4,128]{3,2,1,0:T(4,128)S(1)} %get-tuple-element.26, f32[256]{0:T(256)S(1)} %bitcast.200, ...), kind=kLoop, calls=%fused_computation.13 | loop fusion | flops 5763072 | bytes 52224 | tf_op jit(solution)/shard_map/reduce_sum | solution.py:29
  3.6 0.3 fusion.15
  4.0 0.1 broadcast_add_fusion.8
  4.2 0.8 add_rsqrt_fusion
  5.0 0.4 multiply_reduce_fusion.3
  5.4 0.3 fusion.33
  5.7 0.1 copy.60
  5.8 3.4 %collective-permute-start.1 = (f32[8704]{0:T(1024)S(1)}, f32[8704]{0:T(1024)S(1)}, u32[]{:S(2)}, u32[]{:S(2)}) collective-permute-start(f32[8704]{0:T(1024)S(1)} %pad_maximum_fusion.7), channel_id=1, source_target_pairs={{4,0},{8,4},{12,8},{16,12},{20,16},{24,20},{28,24},{0,28},{5,1},{9... | collective-permute-start | bytes 104456 | tf_op jit(solution)/shard_map/ppermute | solution.py:77
  9.2 0.1 collective-permute-start
  9.4 0.1 fusion.24
  9.5 0.1 fusion.26
  9.7 0.1 subtract_multiply_fusion.2
  9.8 0.1 subtract_multiply_fusion
  10.0 0.1 fusion.5
  10.0 0.1 pad_maximum_fusion.base_ref
  10.2 0.6 gather_fusion
  10.8 0.6 gather_fusion.2
  11.4 0.1 subtract_multiply_fusion.3
  11.5 0.1 broadcast_add_fusion.4
  11.6 0.1 broadcast_add_fusion.5
  11.7 0.1 broadcast_add_fusion.1
  11.7 0.1 broadcast_add_fusion
  11.8 0.1 stack_broadcast_in_dim.44
  12.1 1.4 %collective-permute-done = f32[8192]{0:T(1024)S(1)} collective-permute-done((f32[8192]{0:T(1024)S(1)}, f32[8192]{0:T(1024)S(1)}, u32[]{:S(2)}, u32[]{:S(2)}) %collective-permute-start) | collective-permute-done | bytes 32800 | tf_op jit(solution)/shard_map/ppermute | solution.py:76
  13.6 0.1 collective-permute-start.4
  13.7 3.6 %collective-permute-done.4 = f32[2,1,2,256]{3,2,0,1:T(2,128)S(1)} collective-permute-done((f32[2,1,2,256]{3,2,0,1:T(2,128)S(1)}, f32[2,1,2,256]{3,2,0,1:T(2,128)S(1)}, u32[]{:S(2)}, u32[]{:S(2)}) %collective-permute-start.4) | collective-permute-done | bytes 4128 | tf_op jit(solution)/shard_map/ppermute | solution.py:60
  17.2 0.5 collective-permute-start.5
  17.8 3.1 %collective-permute-done.5 = f32[4,1,2,256]{3,2,0,1:T(2,128)S(1)} collective-permute-done((f32[4,1,2,256]{3,2,0,1:T(2,128)S(1)}, f32[4,1,2,256]{3,2,0,1:T(2,128)S(1)}, u32[]{:S(2)}, u32[]{:S(2)}) %collective-permute-start.5) | collective-permute-done | bytes 8224 | tf_op jit(solution)/shard_map/ppermute | solution.py:60
  20.9 3.7 %collective-permute-start.6 = (f32[8,1,2,256]{3,2,0,1:T(2,128)S(1)}, f32[8,1,2,256]{3,2,0,1:T(2,128)S(1)}, u32[]{:S(2)}, u32[]{:S(2)}) collective-permute-start(f32[8,1,2,256]{3,2,0,1:T(2,128)S(1)} %pad_maximum_fusion.12), channel_id=1, source_target_pairs={{0,3},{1,0},{2,1},{3,2},{4,7},{5,4},{6,5},{7,6},{8,11},{9,8},{10,9... | collective-permute-start | bytes 49160 | tf_op jit(solution)/shard_map/ppermute | solution.py:60
  24.6 1.4 %collective-permute-done.6 = f32[8,1,2,256]{3,2,0,1:T(2,128)S(1)} collective-permute-done((f32[8,1,2,256]{3,2,0,1:T(2,128)S(1)}, f32[8,1,2,256]{3,2,0,1:T(2,128)S(1)}, u32[]{:S(2)}, u32[]{:S(2)}) %collective-permute-start.6) | collective-permute-done | bytes 16416 | tf_op jit(solution)/shard_map/ppermute | solution.py:60
  26.0 1.3 %collective-permute-start.7 = (f32[8,2,2,256]{3,2,0,1:T(2,128)S(1)}, f32[8,2,2,256]{3,2,0,1:T(2,128)S(1)}, u32[]{:S(2)}, u32[]{:S(2)}) collective-permute-start(f32[8,2,2,256]{3,2,0,1:T(2,128)S(1)} %pad_maximum_fusion.10), channel_id=1, source_target_pairs={{0,2},{1,3},{2,0},{3,1},{4,6},{5,7},{6,4},{7,5},{8,10},{9,11},{10,... | collective-permute-start | bytes 98312 | tf_op jit(solution)/shard_map/ppermute | solution.py:60
  27.4 3.6 %collective-permute-start.2 = (f32[20480]{0:T(1024)S(1)}, f32[20480]{0:T(1024)S(1)}, u32[]{:S(2)}, u32[]{:S(2)}) collective-permute-start(f32[20480]{0:T(1024)S(1)} %get-tuple-element.13), channel_id=1, source_target_pairs={{0,1},{1,2},{2,3},{3,0},{4,5},{5,6},{6,7},{7,4},{8,9},{9,10},{10,1... | collective-permute-start | bytes 245768 | tf_op jit(solution)/shard_map/ppermute | solution.py:76
  31.0 0.3 collective-permute-start.3
  31.3 0.6 gather_fusion.5
  32.0 11.6 %multiply_reduce_fusion = f32[2,256]{1,0:T(2,128)S(1)} fusion(f32[11776]{0:T(1024)S(1)} %select_n.80, f32[2,11776]{1,0:T(2,128)S(1)} %stack_broadcast_in_dim.44, f32[256]{0:T(256)S(1)} %bitcast.207, f32[11776]{0:T(1024)S(1)} %stack_broadcast_in_dim.42, f32[256]{0:T(256)S(1)} %bitcast.208, f32[11776]{0:T(1024)S(1)} %stack_broadcast_in_dim.40, f32[256]{0:T(256)S(1)} %bitcast.206), kind=kLoop, calls=%fused_computation.6 | loop fusion | flops 66321920 | bytes 240640 | tf_op jit(solution)/shard_map/reduce_sum | solution.py:29
  43.7 0.3 fusion.34
  43.9 0.1 mul.570
  44.0 1.3 %multiply_reduce_fusion.4 = f32[2,2,4,128]{3,2,1,0:T(4,128)S(1)} fusion(f32[4,256]{1,0:T(4,128)S(1)} %mul.570, f32[256]{0:T(256)S(1)} %bitcast.194, f32[2,2,4,128]{3,2,1,0:T(4,128)S(1)} %get-tuple-element.23, f32[256]{0:T(256)S(1)} %bitcast.196, f32[2,2,4,128]{3,2,1,0:T(4,128)S(1)} %get-tuple-element.22, f32[256]{0:T(256)S(1)} %bitcast.192, ...), kind=kLoop, calls=%fused_computation.10 | loop fusion | flops 5765120 | bytes 39936 | tf_op jit(solution)/shard_map/reduce_sum | solution.py:29
  45.4 0.1 select_maximum_fusion
  45.6 0.1 fusion.11
  45.7 0.1 fusion.10
  45.8 0.1 fusion.9
  45.9 0.1 fusion.8
  46.0 0.1 fusion.7
  46.1 0.1 fusion.6
  46.2 0.3 copy.55
  46.6 0.2 copy-done.1
  46.8 0.0 copy-done.2
  46.8 44.7 %shard_map.199 = f32[16,256]{1,0:T(8,128)S(1)} custom-call(f32[632]{0:T(1024)S(1)} %copy-done.2, s32[1264]{0:T(1024)S(1)} %copy-done.1, f32[4,256,256]{2,1,0:T(8,128)S(1)} %pad_maximum_fusion.base_ref, f32[448,4,256]{2,1,0:T(4,128)S(1)} %bitcast.149), custom_call_target="tpu_custom_call" | custom-call | flops 2133065728 | bytes 2899968 | tf_op jit(solution)/shard_map/pallas_call | solution.py:147
  91.5 0.3 fusion.13
  91.9 1.3 %multiply_reduce_fusion.5 = f32[2,2,4,128]{3,2,1,0:T(4,128)S(1)} fusion(f32[2,2,4,256]{3,2,1,0:T(4,128)S(1)} %fusion.13, f32[256]{0:T(256)S(1)} %bitcast.203, f32[2,2,4,128]{3,2,1,0:T(4,128)S(1)} %get-tuple-element.25, f32[256]{0:T(256)S(1)} %bitcast.201, f32[2,2,4,128]{3,2,1,0:T(4,128)S(1)} %get-tuple-element.26, f32[256]{0:T(256)S(1)} %bitcast.205, ...), kind=kLoop, calls=%fused_computation.11 | loop fusion | flops 5765120 | bytes 52224 | tf_op jit(solution)/shard_map/reduce_sum | solution.py:29
  93.2 0.1 copy.59
  93.4 0.8 gather_fusion.1
  94.4 0.9 gather_fusion.3
  95.4 0.1 reshape.855
  95.5 6.5 %multiply_reduce_fusion.1 = f32[8,128]{1,0:T(8,128)S(1)} fusion(f32[8,3456]{1,0:T(8,128)S(1)} %mul.542, f32[8,3456]{1,0:T(8,128)S(1)} %get-tuple-element.6, f32[8,128]{1,0:T(8,128)S(1)} %get-tuple-element.32, f32[8,3456]{1,0:T(8,128)S(1)} %get-tuple-element.7, f32[8,128]{1,0:T(8,128)S(1)} %get-tuple-element.33, f32[8,3456]{1,0:T(8,128)S(1)} %get-tuple-element.5, ...), kind=kLoop, calls=%fused_computation.7 | loop fusion | flops 38927360 | bytes 458752 | tf_op jit(solution)/shard_map/reduce_sum | solution.py:318
  102.1 4.5 %multiply_reduce_fusion.2 = f32[8,128]{1,0:T(8,128)S(1)} fusion(f32[8,2304]{1,0:T(8,128)S(1)} %mul.534, f32[8,2304]{1,0:T(8,128)S(1)} %get-tuple-element.9, f32[8,128]{1,0:T(8,128)S(1)} %bitcast.197, f32[8,2304]{1,0:T(8,128)S(1)} %get-tuple-element.10, f32[8,128]{1,0:T(8,128)S(1)} %bitcast.198, f32[8,2304]{1,0:T(8,128)S(1)} %get-tuple-element.8, ...), kind=kLoop, calls=%fused_computation.8 | loop fusion | flops 25951232 | bytes 311296 | tf_op jit(solution)/shard_map/reduce_sum | solution.py:318
  106.6 0.6 gather_fusion.4
  107.2 0.7 add_select_fusion
  (124 shorter events, 1.5 us)
Async XLA Ops:
  0.0 3.6 %copy-start = (f32[256,256]{1,0:T(8,128)S(1)}, f32[256,256]{1,0:T(8,128)}, u32[]{:S(2)}) copy-start(f32[256,256]{1,0:T(8,128)} %param.24) | copy-start | bytes 786436
  4.2 1.2 %copy-start.6 = (f32[256,256]{1,0:T(8,128)S(1)}, f32[256,256]{1,0:T(8,128)}, u32[]{:S(2)}) copy-start(f32[256,256]{1,0:T(8,128)} %param.26) | copy-start | bytes 786436
  4.2 1.6 %copy-start.3 = (f32[3,2,2,4,128]{4,3,2,1,0:T(4,128)S(1)}, f32[3,2,2,4,128]{4,3,2,1,0:T(4,128)}, u32[]{:S(2)}) copy-start(f32[3,2,2,4,128]{4,3,2,1,0:T(4,128)} %param.21) | copy-start | bytes 73732
  5.8 4.3 %copy-start.11 = (s32[144]{0:T(256)S(1)}, s32[144]{0:T(256)}, u32[]{:S(2)}) copy-start(s32[144]{0:T(256)} %constant.208) | copy-start | bytes 1732
  5.8 4.3 %copy-start.17 = (s32[8]{0:T(128)S(1)}, s32[8]{0:T(128)}, u32[]{:S(2)}) copy-start(s32[8]{0:T(128)} %constant.207) | copy-start | bytes 100
  5.8 7.7 %collective-permute-start.1 = (f32[8704]{0:T(1024)S(1)}, f32[8704]{0:T(1024)S(1)}, u32[]{:S(2)}, u32[]{:S(2)}) collective-permute-start(f32[8704]{0:T(1024)S(1)} %pad_maximum_fusion.7), channel_id=1, source_target_pairs={{4,0},{8,4},{12,8},{16,12},{20,16},{24,20},{28,24},{0,28},{5,1},{9... | collective-permute-start | bytes 104456 | tf_op jit(solution)/shard_map/ppermute | solution.py:77
  9.2 1.5 %copy-start.10 = (s32[216]{0:T(256)S(1)}, s32[216]{0:T(256)}, u32[]{:S(2)}) copy-start(s32[216]{0:T(256)} %constant.210) | copy-start | bytes 2596
  9.2 1.5 %copy-start.16 = (s32[8]{0:T(128)S(1)}, s32[8]{0:T(128)}, u32[]{:S(2)}) copy-start(s32[8]{0:T(128)} %constant.209) | copy-start | bytes 100
  9.2 4.3 %collective-permute-start = (f32[8192]{0:T(1024)S(1)}, f32[8192]{0:T(1024)S(1)}, u32[]{:S(2)}, u32[]{:S(2)}) collective-permute-start(f32[8192]{0:T(1024)S(1)} %pad_maximum_fusion.9), channel_id=1, source_target_pairs={{0,4},{4,8},{8,12},{12,16},{16,20},{20,24},{24,28},{28,0},{1,5},{5... | collective-permute-start | bytes 98312 | tf_op jit(solution)/shard_map/ppermute | solution.py:76
  9.7 2.0 %copy-start.15 = (f32[23]{0:T(128)S(1)}, f32[23]{0:T(128)}, u32[]{:S(2)}) copy-start(f32[23]{0:T(128)} %constant.192) | copy-start | bytes 280
  9.7 2.1 %copy-start.14 = (f32[23]{0:T(128)S(1)}, f32[23]{0:T(128)}, u32[]{:S(2)}) copy-start(f32[23]{0:T(128)} %constant.193) | copy-start | bytes 280
  9.8 2.0 %copy-start.12 = (s32[16]{0:T(128)S(1)}, s32[16]{0:T(128)}, u32[]{:S(2)}) copy-start(s32[16]{0:T(128)} %constant.211) | copy-start | bytes 196
  9.8 2.0 %copy-start.13 = (s32[23]{0:T(128)S(1)}, s32[23]{0:T(128)}, u32[]{:S(2)}) copy-start(s32[23]{0:T(128)} %constant.212) | copy-start | bytes 280
  13.6 3.7 %collective-permute-start.4 = (f32[2,1,2,256]{3,2,0,1:T(2,128)S(1)}, f32[2,1,2,256]{3,2,0,1:T(2,128)S(1)}, u32[]{:S(2)}, u32[]{:S(2)}) collective-permute-start(f32[2,1,2,256]{3,2,0,1:T(2,128)S(1)} %maximum_bitcast_fusion), channel_id=1, source_target_pairs={{0,24},{4,28},{8,0},{12,4},{16,8},{20,12},{24,16},{28,20},{1,25},{... | collective-permute-start | bytes 12296 | tf_op jit(solution)/shard_map/ppermute | solution.py:60
  17.2 3.7 %collective-permute-start.5 = (f32[4,1,2,256]{3,2,0,1:T(2,128)S(1)}, f32[4,1,2,256]{3,2,0,1:T(2,128)S(1)}, u32[]{:S(2)}, u32[]{:S(2)}) collective-permute-start(f32[4,1,2,256]{3,2,0,1:T(2,128)S(1)} %pad_maximum_fusion.14), channel_id=1, source_target_pairs={{0,16},{4,20},{8,24},{12,28},{16,0},{20,4},{24,8},{28,12},{1,17},{... | collective-permute-start | bytes 24584 | tf_op jit(solution)/shard_map/ppermute | solution.py:60
  20.9 5.1 %collective-permute-start.6 = (f32[8,1,2,256]{3,2,0,1:T(2,128)S(1)}, f32[8,1,2,256]{3,2,0,1:T(2,128)S(1)}, u32[]{:S(2)}, u32[]{:S(2)}) collective-permute-start(f32[8,1,2,256]{3,2,0,1:T(2,128)S(1)} %pad_maximum_fusion.12), channel_id=1, source_target_pairs={{0,3},{1,0},{2,1},{3,2},{4,7},{5,4},{6,5},{7,6},{8,11},{9,8},{10,9... | collective-permute-start | bytes 49160 | tf_op jit(solution)/shard_map/ppermute | solution.py:60
  26.0 5.2 %collective-permute-start.7 = (f32[8,2,2,256]{3,2,0,1:T(2,128)S(1)}, f32[8,2,2,256]{3,2,0,1:T(2,128)S(1)}, u32[]{:S(2)}, u32[]{:S(2)}) collective-permute-start(f32[8,2,2,256]{3,2,0,1:T(2,128)S(1)} %pad_maximum_fusion.10), channel_id=1, source_target_pairs={{0,2},{1,3},{2,0},{3,1},{4,6},{5,7},{6,4},{7,5},{8,10},{9,11},{10,... | collective-permute-start | bytes 98312 | tf_op jit(solution)/shard_map/ppermute | solution.py:60
  27.4 17.9 %collective-permute-start.2 = (f32[20480]{0:T(1024)S(1)}, f32[20480]{0:T(1024)S(1)}, u32[]{:S(2)}, u32[]{:S(2)}) collective-permute-start(f32[20480]{0:T(1024)S(1)} %get-tuple-element.13), channel_id=1, source_target_pairs={{0,1},{1,2},{2,3},{3,0},{4,5},{5,6},{6,7},{7,4},{8,9},{9,10},{10,1... | collective-permute-start | bytes 245768 | tf_op jit(solution)/shard_map/ppermute | solution.py:76
  31.0 14.4 %collective-permute-start.3 = (f32[20480]{0:T(1024)S(1)}, f32[20480]{0:T(1024)S(1)}, u32[]{:S(2)}, u32[]{:S(2)}) collective-permute-start(f32[20480]{0:T(1024)S(1)} %get-tuple-element.14), channel_id=1, source_target_pairs={{1,0},{2,1},{3,2},{0,3},{5,4},{6,5},{7,6},{4,7},{9,8},{10,9},{11,1... | collective-permute-start | bytes 245768 | tf_op jit(solution)/shard_map/ppermute | solution.py:77
  32.0 11.7 %copy-start.7 = (f32[256,256]{1,0:T(8,128)S(1)}, f32[256,256]{1,0:T(8,128)}, u32[]{:S(2)}) copy-start(f32[256,256]{1,0:T(8,128)} %param.27) | copy-start | bytes 786436
  46.1 0.7 copy-start.1
  46.1 0.7 copy-start.2
  46.8 44.7 %copy-start.5 = (f32[256,256]{1,0:T(8,128)S(1)}, f32[256,256]{1,0:T(8,128)}, u32[]{:S(2)}) copy-start(f32[256,256]{1,0:T(8,128)} %param.25) | copy-start | bytes 786436
  91.5 2.8 %copy-start.8 = (f32[3,144,128]{2,1,0:T(8,128)S(1)}, f32[3,144,128]{2,1,0:T(8,128)}, u32[]{:S(2)}) copy-start(f32[3,144,128]{2,1,0:T(8,128)} %constant.205) | copy-start | bytes 663556
  94.2 1.2 %copy-start.4 = (f32[3,216,128]{2,1,0:T(8,128)S(1)}, f32[3,216,128]{2,1,0:T(8,128)}, u32[]{:S(2)}) copy-start(f32[3,216,128]{2,1,0:T(8,128)} %constant.206) | copy-start | bytes 995332
  102.1 5.1 %copy-start.9 = (s32[2,2,4]{2,1,0:T(2,128)S(1)}, s32[2,2,4]{2,1,0:T(2,128)}, u32[]{:S(2)}) copy-start(s32[2,2,4]{2,1,0:T(2,128)} %param.23) | copy-start | bytes 196

commit v19 on v18

--- a/solution.py
+++ b/solution.py
@@ -216,21 +216,32 @@
     kept_x = np.array([2.0 * k[1] for k in kept], np.float32)
     kept_y = np.array([2.0 * k[2] for k in kept], np.float32)
     far_sources = jnp.take(gathered.reshape(count_x * count_y, parent_layers, points), kept_index, axis=0)
-    layer_float = jnp.arange(parent_layers).astype(jnp.float32)
-    depth_pairs = 2.0 * (layer_float[None, :] - layer_float[:, None])
-    far_shape = (parent_layers, len(kept), parent_layers, points)
+    steps = list(range(1 - parent_layers, parent_layers))
+    step_shape = (len(steps), len(kept), points)
+    step_float = 2.0 * np.array(steps, np.float32)
     source_pts = jnp.stack(
         [
-            jnp.broadcast_to(kept_x[None, :, None, None] + 1.8 * unit_sphere[0], far_shape),
-            jnp.broadcast_to(kept_y[None, :, None, None] + 1.8 * unit_sphere[1], far_shape),
-            jnp.broadcast_to(depth_pairs[:, None, :, None] + 1.8 * unit_sphere[2], far_shape),
+            jnp.broadcast_to(kept_x[None, :, None] + 1.8 * unit_sphere[0], step_shape),
+            jnp.broadcast_to(kept_y[None, :, None] + 1.8 * unit_sphere[1], step_shape),
+            jnp.broadcast_to(step_float[:, None, None] + 1.8 * unit_sphere[2], step_shape),
         ]
-    ).reshape(3, parent_layers, -1)
-    far_check = point_sum(
-        jnp.broadcast_to(1.8 * unit_sphere[:, None, :], (3, parent_layers, points)),
-        source_pts,
-        far_sources.reshape(-1),
-    )
+    ).reshape(3, -1)
+    check_far = 1.8 * unit_sphere
+    delta_x = check_far[0][:, None] - source_pts[0][None, :]
+    delta_y = check_far[1][:, None] - source_pts[1][None, :]
+    delta_z = check_far[2][:, None] - source_pts[2][None, :]
+    far_kernel = lax.rsqrt(delta_x * delta_x + delta_y * delta_y + delta_z * delta_z + softening_sq)
+    zero_layer = jnp.zeros((len(kept), points), jnp.float32)
+    far_rows = []
+    for target in range(parent_layers):
+        weight = jnp.stack(
+            [
+                far_sources[:, target + g] if 0 <= target + g < parent_layers else zero_layer
+                for g in steps
+            ]
+        ).reshape(-1)
+        far_rows.append(jnp.sum(far_kernel * weight, axis=-1))
+    far_check = jnp.stack(far_rows)
 
     framed = jnp.pad(cycle, ((1, 1), (1, 1), (3, 3), (0, 0)))
     shifts = far_shifts(3)

time: 108 us -> 113 us (1.046)
  other arithmetic: 31.6 us -> 35.7 us
    reduce_sum x0 -> x1, other arithmetic: none -> 15.8 us  [shards(): far_rows.append(jnp.sum(far_kernel * weight, axis=-1))]
    reduce_sum x5 -> x4, other arithmetic: 15.8 us -> 4.15 us  [point_sum(): return jnp.sum(kernel * weights[..., None, :], axis=-1)]
  transfers between devices with their start and end apart: 8 -> 8, of which waited for: 4 -> 4; matrix products, arithmetic and copies ran while one was open for 15% -> 18% of each run, Pallas kernels for 0% -> 0%
where the time goes in v19:
time: 113 us; the launch traced here: 112 us
  Pallas kernels  44.7 us (40%)
  other arithmetic  35.7 us (32%)
  starting transfers between devices  12.9 us (11%)
  waiting for transfers between devices  9.85 us (9%)
  local copies, waits for them, and re-layouts  6.98 us (6%)
  matrix products  1.18 us (1%)
    pallas_call x1, Pallas kernels, m2l(): pl.pallas_call(functools.partial(m2l_kernel, shift_count, 128), out_shape...  44.7 us
    reduce_sum x1, other arithmetic, shards(): far_rows.append(jnp.sum(far_kernel * weight, axis=-1))  15.8 us
    reduce_sum x2, other arithmetic, shards(): jnp.sum(kernel * source[3][..., None, :], axis=-1) - self_term * mine[3]  11 us
    ppermute x4, waiting for transfers between devices, rel_gather(): lax.ppermute(part, axis, [(j, (j - have) % count) for j in range(count)])  8.06 us
    ppermute x4, starting transfers between devices, rel_gather(): lax.ppermute(part, axis, [(j, (j - have) % count) for j in range(count)])  5.57 us
    reduce_sum x4, other arithmetic, point_sum(): return jnp.sum(kernel * weights[..., None, :], axis=-1)  4.15 us
    ppermute x2, starting transfers between devices, exchange(): lax.ppermute(sent_head, axis, [((i + 1) % count, i) for i in range(count)])  3.73 us
    ppermute x2, starting transfers between devices, exchange(): lax.ppermute(sent_tail, axis, [(i, (i + 1) % count) for i in range(count)])  3.59 us
  transfers between devices with their start and end apart: 8, of which 4 were waited for; matrix products, arithmetic and copies ran while one was open for 18% of the time, Pallas kernels for 0%

profile of v19, /device:TPU:0, one launch (start us, length us, event | category | flops | bytes accessed | tf_op | source)
XLA Modules:
  0.0 112.2 jit_solution(11399282930189709031)
XLA Ops:
  0.0 0.1 cosine_multiply_fusion.1
  0.1 0.1 sine_multiply_fusion.1
  0.2 0.8 fusion.18
  1.0 0.8 fusion.42
  1.8 0.1 broadcast_add_fusion.9
  1.9 0.7 slice_bitcast_fusion.17
  2.7 1.1 multiply_reduce_fusion.7
  3.8 0.3 fusion.15
  4.2 0.8 add_rsqrt_fusion.1
  5.0 0.4 multiply_reduce_fusion.4
  5.4 0.3 fusion.36
  5.7 0.1 copy.67
  5.8 0.0 copy-start.11
  5.8 0.0 copy-start.17
  5.8 3.4 %collective-permute-start.1 = (f32[8704]{0:T(1024)S(1)}, f32[8704]{0:T(1024)S(1)}, u32[]{:S(2)}, u32[]{:S(2)}) collective-permute-start(f32[8704]{0:T(1024)S(1)} %pad_maximum_fusion.9), channel_id=1, source_target_pairs={{4,0},{8,4},{12,8},{16,12},{20,16},{24,20},{28,24},{0,28},{5,1},{9... | collective-permute-start | bytes 104456 | tf_op jit(solution)/shard_map/ppermute | solution.py:77
  9.2 0.1 collective-permute-start
  9.6 0.0 copy-start.15
  9.6 0.1 subtract_multiply_fusion.2
  9.7 0.1 subtract_multiply_fusion
  9.9 0.1 fusion.5
  9.9 0.1 pad_maximum_fusion.base_ref
  10.1 0.6 gather_fusion
  10.7 0.6 gather_fusion.2
  11.3 0.1 broadcast_add_fusion.1
  11.4 0.1 broadcast_add_fusion
  11.5 0.1 broadcast_add_fusion.5
  11.5 0.1 broadcast_add_fusion.4
  11.7 1.8 %collective-permute-done = f32[8192]{0:T(1024)S(1)} collective-permute-done((f32[8192]{0:T(1024)S(1)}, f32[8192]{0:T(1024)S(1)}, u32[]{:S(2)}, u32[]{:S(2)}) %collective-permute-start) | collective-permute-done | bytes 32800 | tf_op jit(solution)/shard_map/ppermute | solution.py:76
  13.6 0.1 collective-permute-start.4
  13.7 3.6 %collective-permute-done.4 = f32[2,1,2,256]{3,2,0,1:T(2,128)S(1)} collective-permute-done((f32[2,1,2,256]{3,2,0,1:T(2,128)S(1)}, f32[2,1,2,256]{3,2,0,1:T(2,128)S(1)}, u32[]{:S(2)}, u32[]{:S(2)}) %collective-permute-start.4) | collective-permute-done | bytes 4128 | tf_op jit(solution)/shard_map/ppermute | solution.py:60
  17.3 0.5 collective-permute-start.5
  17.8 3.1 %collective-permute-done.5 = f32[4,1,2,256]{3,2,0,1:T(2,128)S(1)} collective-permute-done((f32[4,1,2,256]{3,2,0,1:T(2,128)S(1)}, f32[4,1,2,256]{3,2,0,1:T(2,128)S(1)}, u32[]{:S(2)}, u32[]{:S(2)}) %collective-permute-start.5) | collective-permute-done | bytes 8224 | tf_op jit(solution)/shard_map/ppermute | solution.py:60
  20.9 3.7 %collective-permute-start.6 = (f32[8,1,2,256]{3,2,0,1:T(2,128)S(1)}, f32[8,1,2,256]{3,2,0,1:T(2,128)S(1)}, u32[]{:S(2)}, u32[]{:S(2)}) collective-permute-start(f32[8,1,2,256]{3,2,0,1:T(2,128)S(1)} %pad_maximum_fusion.14), channel_id=1, source_target_pairs={{0,3},{1,0},{2,1},{3,2},{4,7},{5,4},{6,5},{7,6},{8,11},{9,8},{10,9... | collective-permute-start | bytes 49160 | tf_op jit(solution)/shard_map/ppermute | solution.py:60
  24.6 1.4 %collective-permute-done.6 = f32[8,1,2,256]{3,2,0,1:T(2,128)S(1)} collective-permute-done((f32[8,1,2,256]{3,2,0,1:T(2,128)S(1)}, f32[8,1,2,256]{3,2,0,1:T(2,128)S(1)}, u32[]{:S(2)}, u32[]{:S(2)}) %collective-permute-start.6) | collective-permute-done | bytes 16416 | tf_op jit(solution)/shard_map/ppermute | solution.py:60
  26.0 1.3 %collective-permute-start.7 = (f32[8,2,2,256]{3,2,0,1:T(2,128)S(1)}, f32[8,2,2,256]{3,2,0,1:T(2,128)S(1)}, u32[]{:S(2)}, u32[]{:S(2)}) collective-permute-start(f32[8,2,2,256]{3,2,0,1:T(2,128)S(1)} %pad_maximum_fusion.12), channel_id=1, source_target_pairs={{0,2},{1,3},{2,0},{3,1},{4,6},{5,7},{6,4},{7,5},{8,10},{9,11},{10,... | collective-permute-start | bytes 98312 | tf_op jit(solution)/shard_map/ppermute | solution.py:60
  27.4 3.5 %collective-permute-start.2 = (f32[20480]{0:T(1024)S(1)}, f32[20480]{0:T(1024)S(1)}, u32[]{:S(2)}, u32[]{:S(2)}) collective-permute-start(f32[20480]{0:T(1024)S(1)} %get-tuple-element.17), channel_id=1, source_target_pairs={{0,1},{1,2},{2,3},{3,0},{4,5},{5,6},{6,7},{7,4},{8,9},{9,10},{10,1... | collective-permute-start | bytes 245768 | tf_op jit(solution)/shard_map/ppermute | solution.py:76
  30.9 0.3 collective-permute-start.3
  31.3 0.6 gather_fusion.5
  32.0 0.1 pad_maximum_fusion.3
  32.2 15.8 %multiply_reduce_fusion.1 = (f32[256]{0:T(256)S(1)}, f32[256]{0:T(256)S(1)}) fusion(f32[17664]{0:T(1024)S(1)} %mul.513, f32[17664]{0:T(1024)S(1)} %stack_broadcast_in_dim.44, f32[256]{0:T(256)S(1)} %bitcast.197, f32[17664]{0:T(1024)S(1)} %stack_broadcast_in_dim.42, f32[256]{0:T(256)S(1)} %bitcast.196, f32[17664]{0:T(1024)S(1)} %stack_broadcast_in_dim.40, ...), kind=kLoop, calls=%fused_computation.7 | loop fusion | flops 58785280 | bytes 358400 | tf_op jit(solution)/shard_map/reduce_sum | solution.py:243
  48.0 0.3 fusion.22
  48.3 0.1 mul.519
  48.4 1.3 %multiply_reduce_fusion.5 = f32[2,2,4,128]{3,2,1,0:T(4,128)S(1)} fusion(f32[4,256]{1,0:T(4,128)S(1)} %mul.519, f32[256]{0:T(256)S(1)} %bitcast.187, f32[2,2,4,128]{3,2,1,0:T(4,128)S(1)} %get-tuple-element.29, f32[256]{0:T(256)S(1)} %bitcast.185, f32[2,2,4,128]{3,2,1,0:T(4,128)S(1)} %get-tuple-element.28, f32[256]{0:T(256)S(1)} %bitcast.189, ...), kind=kLoop, calls=%fused_computation.12 | loop fusion | flops 5765120 | bytes 39936 | tf_op jit(solution)/shard_map/reduce_sum | solution.py:29
  49.8 0.1 select_maximum_fusion
  50.0 0.1 fusion.11
  50.1 0.1 fusion.10
  50.2 0.1 fusion.9
  50.3 0.1 fusion.8
  50.4 0.1 fusion.7
  50.5 0.1 fusion.6
  50.6 0.3 copy.60
  51.0 0.2 copy-done.1
  51.2 0.0 copy-done.2
  51.2 44.7 %shard_map.208 = f32[16,256]{1,0:T(8,128)S(1)} custom-call(f32[632]{0:T(1024)S(1)} %copy-done.2, s32[1264]{0:T(1024)S(1)} %copy-done.1, f32[4,256,256]{2,1,0:T(8,128)S(1)} %pad_maximum_fusion.base_ref, f32[448,4,256]{2,1,0:T(4,128)S(1)} %bitcast.142), custom_call_target="tpu_custom_call" | custom-call | flops 2133065728 | bytes 2899968 | tf_op jit(solution)/shard_map/pallas_call | solution.py:147
  95.9 0.3 fusion.13
  96.2 1.3 %multiply_reduce_fusion.6 = f32[2,2,4,128]{3,2,1,0:T(4,128)S(1)} fusion(f32[2,2,4,256]{3,2,1,0:T(4,128)S(1)} %fusion.13, f32[256]{0:T(256)S(1)} %bitcast.201, f32[2,2,4,128]{3,2,1,0:T(4,128)S(1)} %get-tuple-element.31, f32[256]{0:T(256)S(1)} %bitcast.203, f32[2,2,4,128]{3,2,1,0:T(4,128)S(1)} %get-tuple-element.32, f32[256]{0:T(256)S(1)} %bitcast.199, ...), kind=kLoop, calls=%fused_computation.13 | loop fusion | flops 5765120 | bytes 52224 | tf_op jit(solution)/shard_map/reduce_sum | solution.py:29
  97.6 0.1 copy.66
  97.8 0.8 gather_fusion.1
  98.8 0.9 gather_fusion.3
  99.8 0.1 reshape.818
  99.9 6.5 %multiply_reduce_fusion.2 = f32[8,128]{1,0:T(8,128)S(1)} fusion(f32[8,3456]{1,0:T(8,128)S(1)} %mul.490, f32[8,3456]{1,0:T(8,128)S(1)} %get-tuple-element.8, f32[8,128]{1,0:T(8,128)S(1)} %get-tuple-element.38, f32[8,3456]{1,0:T(8,128)S(1)} %get-tuple-element.9, f32[8,128]{1,0:T(8,128)S(1)} %get-tuple-element.39, f32[8,3456]{1,0:T(8,128)S(1)} %get-tuple-element.7, ...), kind=kLoop, calls=%fused_computation.9 | loop fusion | flops 38927360 | bytes 458752 | tf_op jit(solution)/shard_map/reduce_sum | solution.py:329
  106.5 4.5 %multiply_reduce_fusion.3 = f32[8,128]{1,0:T(8,128)S(1)} fusion(f32[8,2304]{1,0:T(8,128)S(1)} %mul.482, f32[8,2304]{1,0:T(8,128)S(1)} %get-tuple-element.11, f32[8,128]{1,0:T(8,128)S(1)} %bitcast.190, f32[8,2304]{1,0:T(8,128)S(1)} %get-tuple-element.12, f32[8,128]{1,0:T(8,128)S(1)} %bitcast.191, f32[8,2304]{1,0:T(8,128)S(1)} %get-tuple-element.10, ...), kind=kLoop, calls=%fused_computation.10 | loop fusion | flops 25951232 | bytes 311296 | tf_op jit(solution)/shard_map/reduce_sum | solution.py:329
  111.0 0.6 gather_fusion.4
  111.6 0.7 add_select_fusion
  (128 shorter events, 1.5 us)
Async XLA Ops:
  0.0 3.8 %copy-start = (f32[256,256]{1,0:T(8,128)S(1)}, f32[256,256]{1,0:T(8,128)}, u32[]{:S(2)}) copy-start(f32[256,256]{1,0:T(8,128)} %param.25) | copy-start | bytes 786436
  4.2 1.2 %copy-start.6 = (f32[256,256]{1,0:T(8,128)S(1)}, f32[256,256]{1,0:T(8,128)}, u32[]{:S(2)}) copy-start(f32[256,256]{1,0:T(8,128)} %param.27) | copy-start | bytes 786436
  4.2 1.6 %copy-start.3 = (f32[3,2,2,4,128]{4,3,2,1,0:T(4,128)S(1)}, f32[3,2,2,4,128]{4,3,2,1,0:T(4,128)}, u32[]{:S(2)}) copy-start(f32[3,2,2,4,128]{4,3,2,1,0:T(4,128)} %param.22) | copy-start | bytes 73732
  5.8 4.2 %copy-start.11 = (s32[144]{0:T(256)S(1)}, s32[144]{0:T(256)}, u32[]{:S(2)}) copy-start(s32[144]{0:T(256)} %constant.210) | copy-start | bytes 1732
  5.8 4.2 %copy-start.17 = (s32[8]{0:T(128)S(1)}, s32[8]{0:T(128)}, u32[]{:S(2)}) copy-start(s32[8]{0:T(128)} %constant.209) | copy-start | bytes 100
  5.8 7.7 %collective-permute-start.1 = (f32[8704]{0:T(1024)S(1)}, f32[8704]{0:T(1024)S(1)}, u32[]{:S(2)}, u32[]{:S(2)}) collective-permute-start(f32[8704]{0:T(1024)S(1)} %pad_maximum_fusion.9), channel_id=1, source_target_pairs={{4,0},{8,4},{12,8},{16,12},{20,16},{24,20},{28,24},{0,28},{5,1},{9... | collective-permute-start | bytes 104456 | tf_op jit(solution)/shard_map/ppermute | solution.py:77
  9.2 1.4 %copy-start.10 = (s32[216]{0:T(256)S(1)}, s32[216]{0:T(256)}, u32[]{:S(2)}) copy-start(s32[216]{0:T(256)} %constant.212) | copy-start | bytes 2596
  9.2 1.4 %copy-start.16 = (s32[8]{0:T(128)S(1)}, s32[8]{0:T(128)}, u32[]{:S(2)}) copy-start(s32[8]{0:T(128)} %constant.211) | copy-start | bytes 100
  9.2 4.3 %collective-permute-start = (f32[8192]{0:T(1024)S(1)}, f32[8192]{0:T(1024)S(1)}, u32[]{:S(2)}, u32[]{:S(2)}) collective-permute-start(f32[8192]{0:T(1024)S(1)} %pad_maximum_fusion.11), channel_id=1, source_target_pairs={{0,4},{4,8},{8,12},{12,16},{16,20},{20,24},{24,28},{28,0},{1,5},{5... | collective-permute-start | bytes 98312 | tf_op jit(solution)/shard_map/ppermute | solution.py:76
  9.6 1.8 %copy-start.15 = (f32[23]{0:T(128)S(1)}, f32[23]{0:T(128)}, u32[]{:S(2)}) copy-start(f32[23]{0:T(128)} %constant.193) | copy-start | bytes 280
  9.6 1.8 %copy-start.14 = (f32[23]{0:T(128)S(1)}, f32[23]{0:T(128)}, u32[]{:S(2)}) copy-start(f32[23]{0:T(128)} %constant.194) | copy-start | bytes 280
  9.6 1.9 %copy-start.18 = (f32[3]{0:T(128)S(1)}, f32[3]{0:T(128)}, u32[]{:S(2)}) copy-start(f32[3]{0:T(128)} %constant.195) | copy-start | bytes 40
  9.6 2.0 %copy-start.12 = (s32[16]{0:T(128)S(1)}, s32[16]{0:T(128)}, u32[]{:S(2)}) copy-start(s32[16]{0:T(128)} %constant.213) | copy-start | bytes 196
  9.6 2.0 %copy-start.13 = (s32[23]{0:T(128)S(1)}, s32[23]{0:T(128)}, u32[]{:S(2)}) copy-start(s32[23]{0:T(128)} %constant.214) | copy-start | bytes 280
  13.6 3.7 %collective-permute-start.4 = (f32[2,1,2,256]{3,2,0,1:T(2,128)S(1)}, f32[2,1,2,256]{3,2,0,1:T(2,128)S(1)}, u32[]{:S(2)}, u32[]{:S(2)}) collective-permute-start(f32[2,1,2,256]{3,2,0,1:T(2,128)S(1)} %maximum_bitcast_fusion), channel_id=1, source_target_pairs={{0,24},{4,28},{8,0},{12,4},{16,8},{20,12},{24,16},{28,20},{1,25},{... | collective-permute-start | bytes 12296 | tf_op jit(solution)/shard_map/ppermute | solution.py:60
  17.3 3.7 %collective-permute-start.5 = (f32[4,1,2,256]{3,2,0,1:T(2,128)S(1)}, f32[4,1,2,256]{3,2,0,1:T(2,128)S(1)}, u32[]{:S(2)}, u32[]{:S(2)}) collective-permute-start(f32[4,1,2,256]{3,2,0,1:T(2,128)S(1)} %pad_maximum_fusion.16), channel_id=1, source_target_pairs={{0,16},{4,20},{8,24},{12,28},{16,0},{20,4},{24,8},{28,12},{1,17},{... | collective-permute-start | bytes 24584 | tf_op jit(solution)/shard_map/ppermute | solution.py:60
  20.9 5.1 %collective-permute-start.6 = (f32[8,1,2,256]{3,2,0,1:T(2,128)S(1)}, f32[8,1,2,256]{3,2,0,1:T(2,128)S(1)}, u32[]{:S(2)}, u32[]{:S(2)}) collective-permute-start(f32[8,1,2,256]{3,2,0,1:T(2,128)S(1)} %pad_maximum_fusion.14), channel_id=1, source_target_pairs={{0,3},{1,0},{2,1},{3,2},{4,7},{5,4},{6,5},{7,6},{8,11},{9,8},{10,9... | collective-permute-start | bytes 49160 | tf_op jit(solution)/shard_map/ppermute | solution.py:60
  26.0 5.2 %collective-permute-start.7 = (f32[8,2,2,256]{3,2,0,1:T(2,128)S(1)}, f32[8,2,2,256]{3,2,0,1:T(2,128)S(1)}, u32[]{:S(2)}, u32[]{:S(2)}) collective-permute-start(f32[8,2,2,256]{3,2,0,1:T(2,128)S(1)} %pad_maximum_fusion.12), channel_id=1, source_target_pairs={{0,2},{1,3},{2,0},{3,1},{4,6},{5,7},{6,4},{7,5},{8,10},{9,11},{10,... | collective-permute-start | bytes 98312 | tf_op jit(solution)/shard_map/ppermute | solution.py:60
  27.4 22.3 %collective-permute-start.2 = (f32[20480]{0:T(1024)S(1)}, f32[20480]{0:T(1024)S(1)}, u32[]{:S(2)}, u32[]{:S(2)}) collective-permute-start(f32[20480]{0:T(1024)S(1)} %get-tuple-element.17), channel_id=1, source_target_pairs={{0,1},{1,2},{2,3},{3,0},{4,5},{5,6},{6,7},{7,4},{8,9},{9,10},{10,1... | collective-permute-start | bytes 245768 | tf_op jit(solution)/shard_map/ppermute | solution.py:76
  30.9 18.8 %collective-permute-start.3 = (f32[20480]{0:T(1024)S(1)}, f32[20480]{0:T(1024)S(1)}, u32[]{:S(2)}, u32[]{:S(2)}) collective-permute-start(f32[20480]{0:T(1024)S(1)} %get-tuple-element.18), channel_id=1, source_target_pairs={{1,0},{2,1},{3,2},{0,3},{5,4},{6,5},{7,6},{4,7},{9,8},{10,9},{11,1... | collective-permute-start | bytes 245768 | tf_op jit(solution)/shard_map/ppermute | solution.py:77
  32.2 15.8 %copy-start.7 = (f32[256,256]{1,0:T(8,128)S(1)}, f32[256,256]{1,0:T(8,128)}, u32[]{:S(2)}) copy-start(f32[256,256]{1,0:T(8,128)} %param.28) | copy-start | bytes 786436
  50.5 0.7 copy-start.1
  50.5 0.7 copy-start.2
  51.2 44.7 %copy-start.5 = (f32[256,256]{1,0:T(8,128)S(1)}, f32[256,256]{1,0:T(8,128)}, u32[]{:S(2)}) copy-start(f32[256,256]{1,0:T(8,128)} %param.26) | copy-start | bytes 786436
  95.9 2.8 %copy-start.8 = (f32[3,144,128]{2,1,0:T(8,128)S(1)}, f32[3,144,128]{2,1,0:T(8,128)}, u32[]{:S(2)}) copy-start(f32[3,144,128]{2,1,0:T(8,128)} %constant.207) | copy-start | bytes 663556
  98.6 1.2 %copy-start.4 = (f32[3,216,128]{2,1,0:T(8,128)S(1)}, f32[3,216,128]{2,1,0:T(8,128)}, u32[]{:S(2)}) copy-start(f32[3,216,128]{2,1,0:T(8,128)} %constant.208) | copy-start | bytes 995332
  106.5 5.1 %copy-start.9 = (s32[2,2,4]{2,1,0:T(2,128)S(1)}, s32[2,2,4]{2,1,0:T(2,128)}, u32[]{:S(2)}) copy-start(s32[2,2,4]{2,1,0:T(2,128)} %param.24) | copy-start | bytes 196

commit v20 on v18

--- a/solution.py
+++ b/solution.py
@@ -323,20 +323,24 @@
     ).reshape(2, 2, layers, slot_count)
 
     leaf_down_pts = 0.5 + 1.8 * unit_sphere
-    leaf_far = point_sum(offsets, leaf_down_pts[:, None, None, None, :], leaf_local)
     parent_down_pts = 1.0 + 3.6 * unit_sphere
     local_float = jnp.arange(2).astype(jnp.float32)
     layer_parity = (jnp.arange(layers) % 2).astype(jnp.float32)
-    in_parent = jnp.stack(
+    box_shape = (3, 2, 2, layers, points)
+    parent_in_leaf = jnp.stack(
         [
-            local_float[:, None, None, None] + offsets[0],
-            local_float[None, :, None, None] + offsets[1],
-            layer_parity[None, None, :, None] + offsets[2],
+            jnp.broadcast_to(parent_down_pts[0] - local_float[:, None, None, None], box_shape[1:]),
+            jnp.broadcast_to(parent_down_pts[1] - local_float[None, :, None, None], box_shape[1:]),
+            jnp.broadcast_to(parent_down_pts[2] - layer_parity[None, None, :, None], box_shape[1:]),
         ]
     )
-    spread_local = jnp.repeat(parent_local, 2, axis=0)[None, None]
-    parent_far = point_sum(in_parent, parent_down_pts[:, None, None, None, :], spread_local)
-    total = near + leaf_far + parent_far
+    far_pts = jnp.concatenate(
+        [jnp.broadcast_to(leaf_down_pts[:, None, None, None, :], box_shape), parent_in_leaf], axis=-1
+    )
+    far_weights = jnp.concatenate(
+        [leaf_local, jnp.broadcast_to(jnp.repeat(parent_local, 2, axis=0), box_shape[1:])], axis=-1
+    )
+    total = near + point_sum(offsets, far_pts, far_weights)
     return jnp.where(slot_index < counts[..., None], total, 0.0)
 
 

time: 108 us -> 108 us (level)
    reduce_sum x5 -> x4, other arithmetic: 15.8 us -> 15.3 us  [point_sum(): return jnp.sum(kernel * weights[..., None, :], axis=-1)]
  transfers between devices with their start and end apart: 8 -> 8, of which waited for: 4 -> 4; matrix products, arithmetic and copies ran while one was open for 15% -> 14% of each run, Pallas kernels for 0% -> 0%
where the time goes in v20:
time: 108 us; the launch traced here: 107 us
  Pallas kernels  44.7 us (41%)
  other arithmetic  31.2 us (29%)
  starting transfers between devices  12.8 us (12%)
  waiting for transfers between devices  9.18 us (8%)
  local copies, waits for them, and re-layouts  7.26 us (7%)
  matrix products  1.18 us (1%)
    pallas_call x1, Pallas kernels, m2l(): pl.pallas_call(functools.partial(m2l_kernel, shift_count, 128), out_shape...  44.7 us
    reduce_sum x4, other arithmetic, point_sum(): return jnp.sum(kernel * weights[..., None, :], axis=-1)  15.3 us
    reduce_sum x2, other arithmetic, shards(): jnp.sum(kernel * source[3][..., None, :], axis=-1) - self_term * mine[3]  11 us
    ppermute x4, waiting for transfers between devices, rel_gather(): lax.ppermute(part, axis, [(j, (j - have) % count) for j in range(count)])  8.06 us
    ppermute x4, starting transfers between devices, rel_gather(): lax.ppermute(part, axis, [(j, (j - have) % count) for j in range(count)])  5.57 us
    ppermute x2, starting transfers between devices, exchange(): lax.ppermute(sent_head, axis, [((i + 1) % count, i) for i in range(count)])  3.73 us
    ppermute x2, starting transfers between devices, exchange(): lax.ppermute(sent_tail, axis, [(i, (i + 1) % count) for i in range(count)])  3.54 us
  transfers between devices with their start and end apart: 8, of which 4 were waited for; matrix products, arithmetic and copies ran while one was open for 14% of the time, Pallas kernels for 0%

profile of v20, /device:TPU:0, one launch (start us, length us, event | category | flops | bytes accessed | tf_op | source)
XLA Modules:
  0.0 107.3 jit_solution(13554830294831256254)
XLA Ops:
  0.0 0.1 cosine_multiply_fusion.1
  0.1 0.1 sine_multiply_fusion.1
  0.2 0.8 fusion.18
  1.0 0.8 fusion.41
  1.8 0.1 broadcast_add_fusion.5
  1.9 0.7 slice_bitcast_fusion.18
  2.7 1.1 %multiply_reduce_fusion.5 = f32[2,2,4,256]{3,2,1,0:T(4,128)S(1)} fusion(f32[2,2,4,128]{3,2,1,0:T(4,128)S(1)} %fusion.18, f32[2,2,4,128]{3,2,1,0:T(4,128)S(1)} %get-tuple-element.25, f32[256]{0:T(256)S(1)} %bitcast.201, f32[2,2,4,128]{3,2,1,0:T(4,128)S(1)} %get-tuple-element.26, f32[256]{0:T(256)S(1)} %bitcast.200, ...), kind=kLoop, calls=%fused_computation.12 | loop fusion | flops 5763072 | bytes 52224 | tf_op jit(solution)/shard_map/reduce_sum | solution.py:29
  3.8 0.3 fusion.15
  4.2 0.8 add_rsqrt_fusion
  5.0 0.4 multiply_reduce_fusion.4
  5.4 0.3 fusion.33
  5.7 0.1 copy.60
  5.8 3.4 %collective-permute-start.1 = (f32[8704]{0:T(1024)S(1)}, f32[8704]{0:T(1024)S(1)}, u32[]{:S(2)}, u32[]{:S(2)}) collective-permute-start(f32[8704]{0:T(1024)S(1)} %pad_maximum_fusion.7), channel_id=1, source_target_pairs={{4,0},{8,4},{12,8},{16,12},{20,16},{24,20},{28,24},{0,28},{5,1},{9... | collective-permute-start | bytes 104456 | tf_op jit(solution)/shard_map/ppermute | solution.py:77
  9.3 0.1 fusion.24
  9.4 0.1 fusion.26
  9.5 0.1 subtract_multiply_fusion.3
  9.6 0.1 broadcast_subtract_fusion.2
  9.7 0.1 subtract_multiply_fusion.2
  9.9 0.1 subtract_multiply_fusion
  10.1 0.1 fusion.5
  10.1 0.1 pad_maximum_fusion.base_ref
  10.2 0.1 broadcast_subtract_fusion
  10.4 0.1 copy-done.11
  10.5 0.6 gather_fusion
  11.1 0.6 gather_fusion.2
  11.7 0.1 broadcast_add_fusion.2
  11.8 0.1 broadcast_add_fusion.1
  11.9 0.1 broadcast_add_fusion
  12.1 0.1 stack_broadcast_in_dim.62
  12.3 1.1 %collective-permute-done = f32[8192]{0:T(1024)S(1)} collective-permute-done((f32[8192]{0:T(1024)S(1)}, f32[8192]{0:T(1024)S(1)}, u32[]{:S(2)}, u32[]{:S(2)}) %collective-permute-start) | collective-permute-done | bytes 32800 | tf_op jit(solution)/shard_map/ppermute | solution.py:76
  13.5 0.1 collective-permute-start.4
  13.6 3.6 %collective-permute-done.4 = f32[2,1,2,256]{3,2,0,1:T(2,128)S(1)} collective-permute-done((f32[2,1,2,256]{3,2,0,1:T(2,128)S(1)}, f32[2,1,2,256]{3,2,0,1:T(2,128)S(1)}, u32[]{:S(2)}, u32[]{:S(2)}) %collective-permute-start.4) | collective-permute-done | bytes 4128 | tf_op jit(solution)/shard_map/ppermute | solution.py:60
  17.2 0.5 collective-permute-start.5
  17.7 3.1 %collective-permute-done.5 = f32[4,1,2,256]{3,2,0,1:T(2,128)S(1)} collective-permute-done((f32[4,1,2,256]{3,2,0,1:T(2,128)S(1)}, f32[4,1,2,256]{3,2,0,1:T(2,128)S(1)}, u32[]{:S(2)}, u32[]{:S(2)}) %collective-permute-start.5) | collective-permute-done | bytes 8224 | tf_op jit(solution)/shard_map/ppermute | solution.py:60
  20.8 3.7 %collective-permute-start.6 = (f32[8,1,2,256]{3,2,0,1:T(2,128)S(1)}, f32[8,1,2,256]{3,2,0,1:T(2,128)S(1)}, u32[]{:S(2)}, u32[]{:S(2)}) collective-permute-start(f32[8,1,2,256]{3,2,0,1:T(2,128)S(1)} %pad_maximum_fusion.13), channel_id=1, source_target_pairs={{0,3},{1,0},{2,1},{3,2},{4,7},{5,4},{6,5},{7,6},{8,11},{9,8},{10,9... | collective-permute-start | bytes 49160 | tf_op jit(solution)/shard_map/ppermute | solution.py:60
  24.5 1.4 %collective-permute-done.6 = f32[8,1,2,256]{3,2,0,1:T(2,128)S(1)} collective-permute-done((f32[8,1,2,256]{3,2,0,1:T(2,128)S(1)}, f32[8,1,2,256]{3,2,0,1:T(2,128)S(1)}, u32[]{:S(2)}, u32[]{:S(2)}) %collective-permute-start.6) | collective-permute-done | bytes 16416 | tf_op jit(solution)/shard_map/ppermute | solution.py:60
  25.9 1.3 %collective-permute-start.7 = (f32[8,2,2,256]{3,2,0,1:T(2,128)S(1)}, f32[8,2,2,256]{3,2,0,1:T(2,128)S(1)}, u32[]{:S(2)}, u32[]{:S(2)}) collective-permute-start(f32[8,2,2,256]{3,2,0,1:T(2,128)S(1)} %pad_maximum_fusion.10), channel_id=1, source_target_pairs={{0,2},{1,3},{2,0},{3,1},{4,6},{5,7},{6,4},{7,5},{8,10},{9,11},{10,... | collective-permute-start | bytes 98312 | tf_op jit(solution)/shard_map/ppermute | solution.py:60
  27.3 3.5 %collective-permute-start.2 = (f32[20480]{0:T(1024)S(1)}, f32[20480]{0:T(1024)S(1)}, u32[]{:S(2)}, u32[]{:S(2)}) collective-permute-start(f32[20480]{0:T(1024)S(1)} %get-tuple-element.16), channel_id=1, source_target_pairs={{0,1},{1,2},{2,3},{3,0},{4,5},{5,6},{6,7},{7,4},{8,9},{9,10},{10,1... | collective-permute-start | bytes 245768 | tf_op jit(solution)/shard_map/ppermute | solution.py:76
  30.8 0.3 collective-permute-start.3
  31.2 0.6 gather_fusion.5
  31.9 11.7 %multiply_reduce_fusion = f32[2,256]{1,0:T(2,128)S(1)} fusion(f32[11776]{0:T(1024)S(1)} %select_n.80, f32[2,11776]{1,0:T(2,128)S(1)} %stack_broadcast_in_dim.62, f32[256]{0:T(256)S(1)} %bitcast.204, f32[11776]{0:T(1024)S(1)} %stack_broadcast_in_dim.60, f32[256]{0:T(256)S(1)} %bitcast.205, f32[11776]{0:T(1024)S(1)} %stack_broadcast_in_dim.58, f32[256]{0:T(256)S(1)} %bitcast.203), kind=kLoop, calls=%fused_computation.6 | loop fusion | flops 66321920 | bytes 240640 | tf_op jit(solution)/shard_map/reduce_sum | solution.py:29
  43.6 0.3 fusion.34
  43.9 0.1 reshape.923
  44.0 0.1 select_maximum_fusion
  44.2 0.1 fusion.11
  44.3 0.1 fusion.10
  44.4 0.1 fusion.9
  44.5 0.1 fusion.8
  44.6 0.1 fusion.7
  44.7 0.1 fusion.6
  44.8 0.3 copy.55
  45.2 0.2 copy-done.1
  45.4 0.0 copy-done.2
  45.4 44.7 %shard_map.199 = f32[16,256]{1,0:T(8,128)S(1)} custom-call(f32[632]{0:T(1024)S(1)} %copy-done.2, s32[1264]{0:T(1024)S(1)} %copy-done.1, f32[4,256,256]{2,1,0:T(8,128)S(1)} %pad_maximum_fusion.base_ref, f32[448,4,256]{2,1,0:T(4,128)S(1)} %bitcast.149), custom_call_target="tpu_custom_call" | custom-call | flops 2133065728 | bytes 2899968 | tf_op jit(solution)/shard_map/pallas_call | solution.py:147
  90.2 0.1 copy.59
  90.3 0.8 gather_fusion.1
  91.3 0.9 gather_fusion.3
  92.3 0.1 reshape.927
  92.5 6.5 %multiply_reduce_fusion.1 = f32[8,128]{1,0:T(8,128)S(1)} fusion(f32[8,3456]{1,0:T(8,128)S(1)} %mul.539, f32[8,3456]{1,0:T(8,128)S(1)} %get-tuple-element.6, f32[8,128]{1,0:T(8,128)S(1)} %get-tuple-element.32, f32[8,3456]{1,0:T(8,128)S(1)} %get-tuple-element.7, f32[8,128]{1,0:T(8,128)S(1)} %get-tuple-element.33, f32[8,3456]{1,0:T(8,128)S(1)} %get-tuple-element.5, ...), kind=kLoop, calls=%fused_computation.7 | loop fusion | flops 38927360 | bytes 458752 | tf_op jit(solution)/shard_map/reduce_sum | solution.py:318
  99.0 0.3 fusion.13
  99.4 4.5 %multiply_reduce_fusion.2 = f32[8,128]{1,0:T(8,128)S(1)} fusion(f32[8,2304]{1,0:T(8,128)S(1)} %mul.531, f32[8,2304]{1,0:T(8,128)S(1)} %get-tuple-element.9, f32[8,128]{1,0:T(8,128)S(1)} %bitcast.197, f32[8,2304]{1,0:T(8,128)S(1)} %get-tuple-element.10, f32[8,128]{1,0:T(8,128)S(1)} %bitcast.198, f32[8,2304]{1,0:T(8,128)S(1)} %get-tuple-element.8, ...), kind=kLoop, calls=%fused_computation.8 | loop fusion | flops 25951232 | bytes 311296 | tf_op jit(solution)/shard_map/reduce_sum | solution.py:318
  103.9 0.6 gather_fusion.4
  104.5 2.2 %multiply_reduce_fusion.3 = f32[2,2,4,128]{3,2,1,0:T(4,128)S(1)} fusion(f32[2,2,4,512]{3,2,1,0:T(4,128)S(1)} %pad_maximum_fusion.11, f32[2,2,4,512]{3,2,1,0:T(4,128)S(1)} %get-tuple-element.12, f32[2,2,4,128]{3,2,1,0:T(4,128)S(1)} %get-tuple-element.25, f32[2,2,4,512]{3,2,1,0:T(4,128)S(1)} %get-tuple-element.13, f32[2,2,4,128]{3,2,1,0:T(4,128)S(1)} %get-tuple-element.26, ...), kind=kLoop, calls=%fused_computation.9 | loop fusion | flops 11532288 | bytes 163840 | tf_op jit(solution)/shard_map/reduce_sum | solution.py:29
  106.7 0.7 add_select_fusion
  (132 shorter events, 1.6 us)
Async XLA Ops:
  0.0 3.8 %copy-start = (f32[256,256]{1,0:T(8,128)S(1)}, f32[256,256]{1,0:T(8,128)}, u32[]{:S(2)}) copy-start(f32[256,256]{1,0:T(8,128)} %param.24) | copy-start | bytes 786436
  4.2 1.2 %copy-start.6 = (f32[256,256]{1,0:T(8,128)S(1)}, f32[256,256]{1,0:T(8,128)}, u32[]{:S(2)}) copy-start(f32[256,256]{1,0:T(8,128)} %param.26) | copy-start | bytes 786436
  4.2 1.6 %copy-start.3 = (f32[3,2,2,4,128]{4,3,2,1,0:T(4,128)S(1)}, f32[3,2,2,4,128]{4,3,2,1,0:T(4,128)}, u32[]{:S(2)}) copy-start(f32[3,2,2,4,128]{4,3,2,1,0:T(4,128)} %param.21) | copy-start | bytes 73732
  5.8 7.7 %collective-permute-start.1 = (f32[8704]{0:T(1024)S(1)}, f32[8704]{0:T(1024)S(1)}, u32[]{:S(2)}, u32[]{:S(2)}) collective-permute-start(f32[8704]{0:T(1024)S(1)} %pad_maximum_fusion.7), channel_id=1, source_target_pairs={{4,0},{8,4},{12,8},{16,12},{20,16},{24,20},{28,24},{0,28},{5,1},{9... | collective-permute-start | bytes 104456 | tf_op jit(solution)/shard_map/ppermute | solution.py:77
  9.2 4.2 %collective-permute-start = (f32[8192]{0:T(1024)S(1)}, f32[8192]{0:T(1024)S(1)}, u32[]{:S(2)}, u32[]{:S(2)}) collective-permute-start(f32[8192]{0:T(1024)S(1)} %pad_maximum_fusion.9), channel_id=1, source_target_pairs={{0,4},{4,8},{8,12},{12,16},{16,20},{20,24},{24,28},{28,0},{1,5},{5... | collective-permute-start | bytes 98312 | tf_op jit(solution)/shard_map/ppermute | solution.py:76
  9.8 0.7 copy-start.11
  9.8 0.7 copy-start.17
  9.8 1.3 %copy-start.10 = (s32[216]{0:T(256)S(1)}, s32[216]{0:T(256)}, u32[]{:S(2)}) copy-start(s32[216]{0:T(256)} %constant.210) | copy-start | bytes 2596
  9.8 1.3 %copy-start.16 = (s32[8]{0:T(128)S(1)}, s32[8]{0:T(128)}, u32[]{:S(2)}) copy-start(s32[8]{0:T(128)} %constant.209) | copy-start | bytes 100
  9.9 2.0 %copy-start.15 = (f32[23]{0:T(128)S(1)}, f32[23]{0:T(128)}, u32[]{:S(2)}) copy-start(f32[23]{0:T(128)} %constant.192) | copy-start | bytes 280
  10.0 1.9 %copy-start.14 = (f32[23]{0:T(128)S(1)}, f32[23]{0:T(128)}, u32[]{:S(2)}) copy-start(f32[23]{0:T(128)} %constant.193) | copy-start | bytes 280
  10.0 2.0 %copy-start.12 = (s32[16]{0:T(128)S(1)}, s32[16]{0:T(128)}, u32[]{:S(2)}) copy-start(s32[16]{0:T(128)} %constant.211) | copy-start | bytes 196
  10.0 2.0 %copy-start.13 = (s32[23]{0:T(128)S(1)}, s32[23]{0:T(128)}, u32[]{:S(2)}) copy-start(s32[23]{0:T(128)} %constant.212) | copy-start | bytes 280
  13.5 3.7 %collective-permute-start.4 = (f32[2,1,2,256]{3,2,0,1:T(2,128)S(1)}, f32[2,1,2,256]{3,2,0,1:T(2,128)S(1)}, u32[]{:S(2)}, u32[]{:S(2)}) collective-permute-start(f32[2,1,2,256]{3,2,0,1:T(2,128)S(1)} %maximum_bitcast_fusion), channel_id=1, source_target_pairs={{0,24},{4,28},{8,0},{12,4},{16,8},{20,12},{24,16},{28,20},{1,25},{... | collective-permute-start | bytes 12296 | tf_op jit(solution)/shard_map/ppermute | solution.py:60
  17.2 3.7 %collective-permute-start.5 = (f32[4,1,2,256]{3,2,0,1:T(2,128)S(1)}, f32[4,1,2,256]{3,2,0,1:T(2,128)S(1)}, u32[]{:S(2)}, u32[]{:S(2)}) collective-permute-start(f32[4,1,2,256]{3,2,0,1:T(2,128)S(1)} %pad_maximum_fusion.15), channel_id=1, source_target_pairs={{0,16},{4,20},{8,24},{12,28},{16,0},{20,4},{24,8},{28,12},{1,17},{... | collective-permute-start | bytes 24584 | tf_op jit(solution)/shard_map/ppermute | solution.py:60
  20.8 5.1 %collective-permute-start.6 = (f32[8,1,2,256]{3,2,0,1:T(2,128)S(1)}, f32[8,1,2,256]{3,2,0,1:T(2,128)S(1)}, u32[]{:S(2)}, u32[]{:S(2)}) collective-permute-start(f32[8,1,2,256]{3,2,0,1:T(2,128)S(1)} %pad_maximum_fusion.13), channel_id=1, source_target_pairs={{0,3},{1,0},{2,1},{3,2},{4,7},{5,4},{6,5},{7,6},{8,11},{9,8},{10,9... | collective-permute-start | bytes 49160 | tf_op jit(solution)/shard_map/ppermute | solution.py:60
  25.9 5.2 %collective-permute-start.7 = (f32[8,2,2,256]{3,2,0,1:T(2,128)S(1)}, f32[8,2,2,256]{3,2,0,1:T(2,128)S(1)}, u32[]{:S(2)}, u32[]{:S(2)}) collective-permute-start(f32[8,2,2,256]{3,2,0,1:T(2,128)S(1)} %pad_maximum_fusion.10), channel_id=1, source_target_pairs={{0,2},{1,3},{2,0},{3,1},{4,6},{5,7},{6,4},{7,5},{8,10},{9,11},{10,... | collective-permute-start | bytes 98312 | tf_op jit(solution)/shard_map/ppermute | solution.py:60
  27.3 16.6 %collective-permute-start.2 = (f32[20480]{0:T(1024)S(1)}, f32[20480]{0:T(1024)S(1)}, u32[]{:S(2)}, u32[]{:S(2)}) collective-permute-start(f32[20480]{0:T(1024)S(1)} %get-tuple-element.16), channel_id=1, source_target_pairs={{0,1},{1,2},{2,3},{3,0},{4,5},{5,6},{6,7},{7,4},{8,9},{9,10},{10,1... | collective-permute-start | bytes 245768 | tf_op jit(solution)/shard_map/ppermute | solution.py:76
  30.8 13.1 %collective-permute-start.3 = (f32[20480]{0:T(1024)S(1)}, f32[20480]{0:T(1024)S(1)}, u32[]{:S(2)}, u32[]{:S(2)}) collective-permute-start(f32[20480]{0:T(1024)S(1)} %get-tuple-element.17), channel_id=1, source_target_pairs={{1,0},{2,1},{3,2},{0,3},{5,4},{6,5},{7,6},{4,7},{9,8},{10,9},{11,1... | collective-permute-start | bytes 245768 | tf_op jit(solution)/shard_map/ppermute | solution.py:77
  31.9 11.7 %copy-start.7 = (f32[256,256]{1,0:T(8,128)S(1)}, f32[256,256]{1,0:T(8,128)}, u32[]{:S(2)}) copy-start(f32[256,256]{1,0:T(8,128)} %param.27) | copy-start | bytes 786436
  44.7 0.7 copy-start.1
  44.7 0.7 copy-start.2
  90.1 1.1 %copy-start.8 = (f32[3,144,128]{2,1,0:T(8,128)S(1)}, f32[3,144,128]{2,1,0:T(8,128)}, u32[]{:S(2)}) copy-start(f32[3,144,128]{2,1,0:T(8,128)} %constant.205) | copy-start | bytes 663556
  91.1 1.2 %copy-start.4 = (f32[3,216,128]{2,1,0:T(8,128)S(1)}, f32[3,216,128]{2,1,0:T(8,128)}, u32[]{:S(2)}) copy-start(f32[3,216,128]{2,1,0:T(8,128)} %constant.206) | copy-start | bytes 995332
  92.4 6.6 %copy-start.5 = (f32[256,256]{1,0:T(8,128)S(1)}, f32[256,256]{1,0:T(8,128)}, u32[]{:S(2)}) copy-start(f32[256,256]{1,0:T(8,128)} %param.25) | copy-start | bytes 786436
  103.9 2.8 %copy-start.9 = (s32[2,2,4]{2,1,0:T(2,128)S(1)}, s32[2,2,4]{2,1,0:T(2,128)}, u32[]{:S(2)}) copy-start(s32[2,2,4]{2,1,0:T(2,128)} %param.23) | copy-start | bytes 196
